TPU v7x, 256 devices: a whole 4x4x8 slice. The times are simulated.
256 devices in a mesh: dp: 8 (over x, core), seq: 32 (over y, z).
Axes of the slice: x: 4, y: 4, z: 8, core: 2. Of those that a mesh axis runs over, the one named last changes fastest.
Arguments:
- activations: bfloat16 [8, 4096, 2048], P('dp', 'seq'), may hold values from -16 to 16
- w_query: bfloat16 [2048, 2048], P('seq')
- w_key: bfloat16 [2048, 256], P('seq')
- w_value: bfloat16 [2048, 256], P('seq'), may hold values from -0.125 to 0.125
- key_blocks: int32 [32, 32, 7], replicated, may hold values from 0 to 31, as said below
- random_count: int32 [32], replicated, may hold values from 1 to 3, 64 in all
- grad_out: bfloat16 [8, 4096, 2048], P('dp', 'seq'), may hold values from -6 to 6
Outputs:
- attn_out: bfloat16 [8, 4096, 2048], P('dp', 'seq')
- grad_x: bfloat16 [8, 4096, 2048], P('dp', 'seq')
- grad_wq: bfloat16 [2048, 2048], P('seq')
- grad_wk: bfloat16 [2048, 256], P('seq')
- grad_wv: bfloat16 [2048, 256], P('seq')
Inputs may be any that keep to these rules, and one draw needn't show every extreme that they name: `key_blocks`: row b of head h: columns 0 to 2 are b - 1, b and b + 1 modulo 32; column 3 is one block of the head, the same in all its rows; columns 4 to 6 are three blocks that differ from each other and from the row's first four entries. Head h uses the first random_count[h] of its three random key blocks; the counts sum to 64.
All inputs are finite; a program needn't handle non-finite values.
Results may differ from a plain program's by a relative error of at most 0.025.
The roundings to bfloat16 on the way count: a program that leaves them out, or rounds other values in their place, can miss the bound.
Values may be sent and summed in bfloat16 or wider, within the bound.
No kernel may reach another device: no remote copies, remote signals or barrier semaphores. Data moves between devices by JAX's collectives and lax.ppermute only.
A program may use at most 128 MiB of HBM per device.

v0:
```python
import math

import jax
import jax.numpy as jnp
from jax import lax
from jax.sharding import PartitionSpec as P

HD = 64
GROUP = 8


masked_score = -1e30
query_group = 4


def head_pass(queries, key_rows, value_rows, grad_head, blocks, extra_count):
    seq_len, head_width = queries.shape
    block_count, slot_count = blocks.shape
    block_len = seq_len // block_count
    score_scale = head_width ** (-0.5)
    key_tiles = key_rows.reshape(block_count, block_len, head_width)
    value_tiles = value_rows.reshape(block_count, block_len, head_width)
    usable = jnp.repeat(jnp.arange(slot_count) < 4 + extra_count, block_len)
    rounds = block_count // query_group
    query_steps = queries.reshape(rounds, query_group, block_len, head_width)
    grad_steps = grad_head.reshape(rounds, query_group, block_len, head_width)
    block_steps = blocks.reshape(rounds, query_group, slot_count)

    def one_step(running, inputs):
        q_part, g_part, chosen = inputs
        k_part = key_tiles[chosen].reshape(query_group, slot_count * block_len, head_width)
        v_part = value_tiles[chosen].reshape(query_group, slot_count * block_len, head_width)
        scores = (
            jnp.einsum("gqe,gke->gqk", q_part, k_part, preferred_element_type=jnp.float32)
            * score_scale
        )
        scores = jnp.where(usable, scores, masked_score)
        highest = jnp.max(scores, axis=-1, keepdims=True)
        exponent = jnp.exp(scores - highest)
        shares = exponent / jnp.sum(exponent, axis=-1, keepdims=True)
        shares_low = shares.astype(jnp.bfloat16)
        attended = jnp.einsum(
            "gqk,gke->gqe", shares_low, v_part, preferred_element_type=jnp.float32
        ).astype(jnp.bfloat16)
        grad_shares = jnp.einsum("gqe,gke->gqk", g_part, v_part, preferred_element_type=jnp.float32)
        weighted = jnp.sum(grad_shares * shares, axis=-1, keepdims=True)
        grad_scores = (shares * (grad_shares - weighted)).astype(jnp.bfloat16)
        grad_query = (
            jnp.einsum("gqk,gke->gqe", grad_scores, k_part, preferred_element_type=jnp.float32)
            * score_scale
        ).astype(jnp.bfloat16)
        grad_keys = (
            jnp.einsum("gqk,gqe->gke", grad_scores, q_part, preferred_element_type=jnp.float32)
            * score_scale
        )
        grad_values = jnp.einsum(
            "gqk,gqe->gke", shares_low, g_part, preferred_element_type=jnp.float32
        )
        pieces = jnp.concatenate([grad_keys, grad_values], axis=-1).reshape(
            query_group * slot_count, block_len, 2 * head_width
        )
        running = running.at[chosen.reshape(-1)].add(pieces)
        return (running, (attended, grad_query))

    initial = jnp.zeros((block_count, block_len, 2 * head_width), jnp.float32)
    summed, (attended, grad_query) = lax.scan(
        one_step, initial, (query_steps, grad_steps, block_steps)
    )
    return (
        attended.reshape(seq_len, head_width),
        grad_query.reshape(seq_len, head_width),
        summed.reshape(seq_len, 2 * head_width),
    )


def per_device(activations, w_query, w_key, w_value, key_blocks, random_count, grad_out):
    seq_devices = lax.axis_size("seq")
    dp_devices = lax.axis_size("dp")
    position = lax.axis_index("seq")
    tokens = activations[0]
    grad_rows = grad_out[0]
    tok_count = tokens.shape[0]
    heads = w_query.shape[1] // HD
    kv_heads = w_key.shape[1] // HD
    full_q, full_k, full_v = (
        lax.all_gather(w_query, "seq", axis=0, tiled=True),
        lax.all_gather(w_key, "seq", axis=0, tiled=True),
        lax.all_gather(w_value, "seq", axis=0, tiled=True),
    )
    queries = jnp.dot(tokens, full_q, preferred_element_type=jnp.float32).astype(jnp.bfloat16)
    key_proj = jnp.dot(tokens, full_k, preferred_element_type=jnp.float32).astype(jnp.bfloat16)
    value_proj = jnp.dot(tokens, full_v, preferred_element_type=jnp.float32).astype(jnp.bfloat16)
    query_pieces = queries.reshape(tok_count, heads, HD).transpose(1, 0, 2)
    grad_pieces = grad_rows.reshape(tok_count, heads, HD).transpose(1, 0, 2)
    paired = jnp.concatenate(
        [key_proj.reshape(tok_count, kv_heads, HD), value_proj.reshape(tok_count, kv_heads, HD)],
        axis=2,
    )
    kv_pieces = jnp.repeat(paired.transpose(1, 0, 2), GROUP, axis=0)
    head_q, head_grad, landed = (
        lax.all_to_all(query_pieces, "seq", split_axis=0, concat_axis=1, tiled=True),
        lax.all_to_all(grad_pieces, "seq", split_axis=0, concat_axis=1, tiled=True),
        lax.all_to_all(kv_pieces, "seq", split_axis=0, concat_axis=1, tiled=True),
    )
    head_kv = landed[0]
    blocks_mine = lax.dynamic_index_in_dim(key_blocks, position, 0, keepdims=False)
    count_mine = lax.dynamic_index_in_dim(random_count, position, 0, keepdims=False)
    attended, grad_query, grad_kv = head_pass(
        head_q[0], head_kv[:, :HD], head_kv[:, HD:], head_grad[0], blocks_mine, count_mine
    )
    grad_kv_low = grad_kv.astype(jnp.bfloat16).reshape(seq_devices, tok_count, 2 * HD)
    back_out, back_query, back_kv = (
        lax.all_to_all(
            attended.reshape(seq_devices, tok_count, HD),
            "seq",
            split_axis=0,
            concat_axis=0,
            tiled=True,
        ),
        lax.all_to_all(
            grad_query.reshape(seq_devices, tok_count, HD),
            "seq",
            split_axis=0,
            concat_axis=0,
            tiled=True,
        ),
        lax.all_to_all(grad_kv_low, "seq", split_axis=0, concat_axis=0, tiled=True),
    )
    out_rows = back_out.transpose(1, 0, 2).reshape(tok_count, heads * HD)
    grad_q_rows = back_query.transpose(1, 0, 2).reshape(tok_count, heads * HD)
    kv_sum = jnp.sum(
        back_kv.reshape(kv_heads, GROUP, tok_count, 2 * HD), axis=1, dtype=jnp.float32
    ).astype(jnp.bfloat16)
    grad_k_rows = kv_sum[:, :, :HD].transpose(1, 0, 2).reshape(tok_count, kv_heads * HD)
    grad_v_rows = kv_sum[:, :, HD:].transpose(1, 0, 2).reshape(tok_count, kv_heads * HD)
    contract = (((1,), (1,)), ((), ()))
    grad_x_rows = (
        lax.dot_general(grad_q_rows, full_q, contract, preferred_element_type=jnp.float32)
        + lax.dot_general(grad_k_rows, full_k, contract, preferred_element_type=jnp.float32)
        + lax.dot_general(grad_v_rows, full_v, contract, preferred_element_type=jnp.float32)
    ).astype(jnp.bfloat16)
    combined = jnp.concatenate([grad_q_rows, grad_k_rows, grad_v_rows], axis=1)
    factor = 1.0 / math.sqrt(tok_count * seq_devices * dp_devices)
    over_tokens = (((0,), (0,)), ((), ()))
    partial_seq = lax.psum_scatter(
        (
            lax.dot_general(tokens, combined, over_tokens, preferred_element_type=jnp.float32)
            * factor
        ).astype(jnp.bfloat16),
        "seq",
        scatter_dimension=0,
        tiled=True,
    )
    summed = lax.psum(partial_seq, "dp").astype(jnp.float32)
    grad_all = summed.astype(jnp.bfloat16)
    query_cols = heads * HD
    kv_cols = kv_heads * HD
    grad_wq = grad_all[:, :query_cols]
    grad_wk = grad_all[:, query_cols : query_cols + kv_cols]
    grad_wv = grad_all[:, query_cols + kv_cols :]
    return (out_rows[None], grad_x_rows[None], grad_wq, grad_wk, grad_wv)


def solution(mesh):
    placed = (
        P("dp", "seq", None),
        P("seq", None),
        P("seq", None),
        P("seq", None),
        P(),
        P(),
        P("dp", "seq", None),
    )
    return jax.shard_map(
        per_device,
        mesh=mesh,
        in_specs=placed,
        out_specs=(
            P("dp", "seq", None),
            P("dp", "seq", None),
            P("seq", None),
            P("seq", None),
            P("seq", None),
        ),
        check_vma=False,
    )
```

profile of v0, /device:TPU:1, one launch (start us, length us, event | category | flops | bytes accessed | tf_op | source)
XLA Modules:
  0.0 847.8 jit_solution(14132646041992996613)
XLA Ops:
  9.4 2.0 copy.64
  11.4 12.0 %all-to-all-start.2 = ((bf16[32,128,64]{1,2,0:T(8,128)(2,1)}), bf16[32,128,64]{1,2,0:T(8,128)(2,1)S(1)}, u32[]{:S(2)}, u32[]{:S(2)}) async-start(bf16[32,128,64]{1,2,0:T(8,128)(2,1)} %bitcast.12), calls=%async_computation.2 | async-start | bytes 1048576 | tf_op jit(solution)/shard_map/all_to_all | solution.py:102
  23.5 62.9 %all-gather.8.cloned.1.call-done = bf16[2048,256]{1,0:T(8,128)(2,1)} async-done(((bf16[64,256]{1,0:T(8,128)(2,1)}), bf16[2048,256]{1,0:T(8,128)(2,1)}) %all-gather.8.cloned.1.call-update) | async-done | bytes 1048592 | tf_op jit(solution)/shard_map/all_gather | solution.py:88
  88.1 74.8 %all-gather.6.cloned.1.call-done = bf16[2048,256]{1,0:T(8,128)(2,1)} async-done(((bf16[64,256]{1,0:T(8,128)(2,1)}), bf16[2048,256]{1,0:T(8,128)(2,1)}) %all-gather.6.cloned.1.call-update) | async-done | bytes 1048592 | tf_op jit(solution)/shard_map/all_gather | solution.py:87
  162.9 1.5 convolution_convert_fusion.3
  165.9 5.7 all-to-all-start.1
  173.7 96.2 %all-gather.4.cloned.1.call-done = bf16[2048,2048]{1,0:T(8,128)(2,1)} async-done(((bf16[64,2048]{1,0:T(8,128)(2,1)}), bf16[2048,2048]{1,0:T(8,128)(2,1)}) %all-gather.4.cloned.1.call-update) | async-done | bytes 8388624 | tf_op jit(solution)/shard_map/all_gather | solution.py:86
  269.9 4.6 convolution_convert_fusion.1
  275.5 5.4 all-to-all-start
  281.0 1.9 fusion.58
  283.0 11.9 %all-to-all-done = bf16[32,128,64]{1,2,0:T(8,128)(2,1)S(1)} async-done(((bf16[32,128,64]{1,2,0:T(8,128)(2,1)}), bf16[32,128,64]{1,2,0:T(8,128)(2,1)S(1)}, u32[]{:S(2)}, u32[]{:S(2)}) %all-to-all-start) | async-done | bytes 524320 | tf_op jit(solution)/shard_map/all_to_all | solution.py:101
  294.9 1.6 broadcast_in_dim.33
  296.4 160.1 %while.15 = (s32[]{:T(128)}, f32[32,128,128]{2,1,0:T(8,128)}, bf16[8,4,128,64]{2,3,1,0:T(8,128)(2,1)}, bf16[8,4,128,64]{2,3,1,0:T(8,128)(2,1)}, s32[8,4,7]{2,1,0...) while((s32[]{:T(128)}, f32[32,128,128]{2,1,0:T(8,128)}, ...), condition=%wide.region_5.6_spmd.clone, body=%wide.region_0.5_spmd.clone.sunk | while | flops 360449568 | bytes 49239564 | solution.py:66
  296.7 1.6 gather_fusion.1
  299.1 1.6 fusion.104
  300.7 2.4 fusion.106
  307.9 1.7 copy.78
  309.6 6.8 scatter_fusion
  316.7 1.6 gather_fusion.1
  319.1 1.6 fusion.104
  320.7 2.4 fusion.106
  327.9 1.7 copy.78
  329.6 6.9 scatter_fusion
  336.7 1.6 gather_fusion.1
  339.1 1.6 fusion.104
  340.7 2.4 fusion.106
  347.9 1.7 copy.78
  349.6 6.8 scatter_fusion
  356.7 1.6 gather_fusion.1
  359.1 1.6 fusion.104
  360.7 2.4 fusion.106
  367.9 1.7 copy.78
  369.6 6.8 scatter_fusion
  376.7 1.6 gather_fusion.1
  379.1 1.6 fusion.104
  380.7 2.4 fusion.106
  387.9 1.7 copy.78
  389.6 6.9 scatter_fusion
  396.8 1.6 gather_fusion.1
  399.1 1.6 fusion.104
  400.8 2.4 fusion.106
  407.9 1.7 copy.78
  409.6 6.9 scatter_fusion
  416.8 1.6 gather_fusion.1
  419.1 1.6 fusion.104
  420.8 2.4 fusion.106
  428.0 1.7 copy.78
  429.7 6.8 scatter_fusion
  436.8 1.6 gather_fusion.1
  439.1 1.6 fusion.104
  440.8 2.4 fusion.106
  448.0 1.7 copy.78
  449.7 6.9 scatter_fusion
  456.6 1.7 convert_element_type.41
  458.3 32.5 %all_to_all.42 = bf16[32,128,128]{2,1,0:T(8,128)(2,1)S(1)} all-to-all(bf16[32,128,128]{2,1,0:T(8,128)(2,1)S(1)} %convert_element_type.41), channel_id=1, replica_groups=mesh['dp'=8,'seq'=32] {'seq'}, dimensions={0} | all-to-all | bytes 2097152 | tf_op jit(solution)/shard_map/all_to_all | solution.py:127
  490.8 8.5 %all-to-all-start.4 = ((bf16[32,128,64]{1,2,0:T(8,128)(2,1)}), bf16[32,128,64]{1,2,0:T(8,128)(2,1)S(1)}, u32[]{:S(2)}, u32[]{:S(2)}) async-start(bf16[32,128,64]{1,2,0:T(8,128)(2,1)} %bitcast.19), calls=%async_computation.4 | async-start | bytes 1048576 | tf_op jit(solution)/shard_map/all_to_all | solution.py:120
  500.0 13.0 %all-to-all-done.4 = bf16[32,128,64]{1,2,0:T(8,128)(2,1)S(1)} async-done(((bf16[32,128,64]{1,2,0:T(8,128)(2,1)}), bf16[32,128,64]{1,2,0:T(8,128)(2,1)S(1)}, u32[]{:S(2)}, u32[]{:S(2)}) %all-to-all-start.4) | async-done | bytes 524320 | tf_op jit(solution)/shard_map/all_to_all | solution.py:120
  513.0 7.3 fusion.42
  520.3 13.7 %copy.75 = bf16[2048,2560]{1,0:T(8,128)(2,1)} copy(bf16[2048,2560]{0,1:T(8,128)(2,1)} %fusion.42) | data formatting | bytes 20971520
  535.1 21.6 %all_to_all.43 = bf16[32,128,64]{1,2,0:T(8,128)(2,1)S(1)} all-to-all(bf16[32,128,64]{1,2,0:T(8,128)(2,1)S(1)} %bitcast.154), channel_id=1, replica_groups=mesh['dp'=8,'seq'=32] {'seq'}, dimensions={0} | all-to-all | bytes 1048576 | tf_op jit(solution)/shard_map/all_to_all | solution.py:113
  557.7 6.5 fusion.60
  564.7 203.2 %reduce-scatter.4.cloned.1.call-done = bf16[64,2560]{1,0:T(8,128)(2,1)} async-done(((bf16[2048,2560]{1,0:T(8,128)(2,1)}), bf16[64,2560]{1,0:T(8,128)(2,1)}) %reduce-scatter.4.cloned.1.call-update) | async-done | bytes 327696
  768.0 2.1 copy.76
  771.4 65.7 %all-reduce.2.cloned.1.call-done = bf16[64,2560]{0,1:T(8,128)(2,1)} async-done(((bf16[64,2560]{0,1:T(8,128)(2,1)}), bf16[64,2560]{0,1:T(8,128)(2,1)}) %all-reduce.2.cloned.1.call-update) | async-done | bytes 327696 | tf_op jit(solution)/shard_map/psum | solution.py:154
  (267 shorter events, 62.5 us)
Async XLA Ops:
  7.2 79.3 %copy-start = (bf16[1,128,2048]{2,1,0:T(8,128)(2,1)S(1)}, bf16[1,128,2048]{2,1,0:T(8,128)(2,1)}, u32[]{:S(2)}) copy-start(bf16[1,128,2048]{2,1,0:T(8,128)(2,1)} %param.9) | copy-start | bytes 1572868
  7.2 79.2 %all-gather.8.cloned.1.call-start = ((), (), s32[]{:S(2)}) async-start(), calls=%async_computation.9 | async-start | bytes 1081344 | tf_op jit(solution)/shard_map/all_gather | solution.py:88
  7.9 154.9 %all-gather.6.cloned.1.call-start = ((), (), s32[]{:S(2)}) async-start(), calls=%async_computation.8 | async-start | bytes 1081344 | tf_op jit(solution)/shard_map/all_gather | solution.py:87
  8.7 261.2 %all-gather.4.cloned.1.call-start = ((), (), s32[]{:S(2)}) async-start(), calls=%async_computation.7 | async-start | bytes 8650752 | tf_op jit(solution)/shard_map/all_gather | solution.py:86
  11.4 153.2 %all-to-all-start.2 = ((bf16[32,128,64]{1,2,0:T(8,128)(2,1)}), bf16[32,128,64]{1,2,0:T(8,128)(2,1)S(1)}, u32[]{:S(2)}, u32[]{:S(2)}) async-start(bf16[32,128,64]{1,2,0:T(8,128)(2,1)} %bitcast.12), calls=%async_computation.2 | async-start | bytes 1048576 | tf_op jit(solution)/shard_map/all_to_all | solution.py:102
  164.5 7.1 copy-start.13
  164.7 1.2 copy-start.11
  165.9 109.6 %all-to-all-start.1 = ((bf16[32,128,128]{2,1,0:T(8,128)(2,1)}), bf16[32,128,128]{2,1,0:T(8,128)(2,1)S(1)}, u32[]{:S(2)}, u32[]{:S(2)}) async-start(bf16[32,128,128]{2,1,0:T(8,128)(2,1)} %bitcast.8), calls=%async_computation.1 | async-start | bytes 2097152 | tf_op jit(solution)/shard_map/all_to_all | solution.py:103
  275.5 5.5 copy-start.6
  275.5 19.3 %all-to-all-start = ((bf16[32,128,64]{1,2,0:T(8,128)(2,1)}), bf16[32,128,64]{1,2,0:T(8,128)(2,1)S(1)}, u32[]{:S(2)}, u32[]{:S(2)}) async-start(bf16[32,128,64]{1,2,0:T(8,128)(2,1)} %bitcast.3), calls=%async_computation | async-start | bytes 1048576 | tf_op jit(solution)/shard_map/all_to_all | solution.py:101
  296.4 1.9 copy-start.1
  296.4 2.6 copy-start.3
  296.4 2.6 copy-start.9
  303.1 1.3 copy-start.5
  306.2 1.2 copy-start.10
  309.6 6.9 copy-start.2
  309.6 6.9 copy-start.4
  316.4 1.9 copy-start.1
  316.4 2.6 copy-start.3
  316.4 2.6 copy-start.9
  323.1 1.3 copy-start.5
  329.6 6.9 copy-start.2
  329.6 6.9 copy-start.4
  336.4 1.9 copy-start.1
  336.4 2.6 copy-start.3
  336.4 2.6 copy-start.9
  343.1 1.3 copy-start.5
  349.6 6.8 copy-start.2
  349.6 6.8 copy-start.4
  356.4 1.9 copy-start.1
  356.4 2.6 copy-start.3
  356.4 2.6 copy-start.9
  363.1 1.3 copy-start.5
  369.6 6.8 copy-start.2
  369.6 6.8 copy-start.4
  376.4 1.9 copy-start.1
  376.4 2.6 copy-start.3
  376.4 2.6 copy-start.9
  383.1 1.3 copy-start.5
  389.6 6.9 copy-start.2
  389.6 6.9 copy-start.4
  396.5 1.9 copy-start.1
  396.5 2.6 copy-start.3
  396.5 2.6 copy-start.9
  403.2 1.3 copy-start.5
  409.6 6.9 copy-start.2
  409.6 6.9 copy-start.4
  416.5 1.9 copy-start.1
  416.5 2.6 copy-start.3
  416.5 2.6 copy-start.9
  423.2 1.3 copy-start.5
  429.7 6.8 copy-start.2
  429.7 6.8 copy-start.4
  436.5 1.9 copy-start.1
  436.5 2.6 copy-start.3
  436.5 2.6 copy-start.9
  443.2 1.3 copy-start.5
  449.7 6.9 copy-start.2
  449.7 6.9 copy-start.4
  490.8 22.3 %all-to-all-start.4 = ((bf16[32,128,64]{1,2,0:T(8,128)(2,1)}), bf16[32,128,64]{1,2,0:T(8,128)(2,1)S(1)}, u32[]{:S(2)}, u32[]{:S(2)}) async-start(bf16[32,128,64]{1,2,0:T(8,128)(2,1)} %bitcast.19), calls=%async_computation.4 | async-start | bytes 1048576 | tf_op jit(solution)/shard_map/all_to_all | solution.py:120
  499.3 268.7 %reduce-scatter.4.cloned.1.call-start = ((), (), s32[]{:S(2)}) async-start(), calls=%async_computation.11 | async-start | bytes 10813440
  534.1 302.9 %all-reduce.2.cloned.1.call-start = ((), (), s32[]{:S(2)}) async-start(), calls=%async_computation.10 | async-start | bytes 1310720 | tf_op jit(solution)/shard_map/psum | solution.py:154
  557.7 6.5 copy-start.7
  564.2 205.9 %copy-start.8 = (bf16[2048,256]{1,0:T(8,128)(2,1)S(1)}, bf16[2048,256]{1,0:T(8,128)(2,1)}, u32[]{:S(2)}) copy-start(bf16[2048,256]{1,0:T(8,128)(2,1)} %all-gather.8.cloned.1.call-done) | copy-start | bytes 3145732
  (8 other events, 9.4 us)
Sparse Core Ops, SparseCore 0:
  10.6 75.7 all-gather.7
  89.0 73.7 all-gather.5
  165.5 104.3 all-gather.3
  534.2 233.7 reduce-scatter.3
  770.3 66.7 all-reduce.1
where the time goes:
time: 852 us; the launch traced here: 848 us
  waiting for transfers between devices  530 us (62%)
  matrix products  89.5 us (11%)
  local copies, waits for them, and re-layouts  66.4 us (8%)
  other arithmetic  60.7 us (7%)
  blocking collectives  54.1 us (6%)
  starting transfers between devices  32 us (4%)
  between operations  14.7 us (2%)
    unnamed x6, waiting for transfers between devices  205 us
    all_gather x1, waiting for transfers between devices, per_device(): lax.all_gather(w_query, 'seq', axis=0, tiled=True)  96.2 us
    all_gather x1, waiting for transfers between devices, per_device(): lax.all_gather(w_key, 'seq', axis=0, tiled=True)  74.8 us
    psum x1, waiting for transfers between devices, per_device(): summed = lax.psum(partial_seq, 'dp').astype(jnp.float32)  65.7 us
    all_gather x1, waiting for transfers between devices, per_device(): lax.all_gather(w_value, 'seq', axis=0, tiled=True)  62.9 us
    scatter-add x8, other arithmetic, one_step(): running = running.at[chosen.reshape(-1)].add(pieces)  54.8 us
    all_to_all x1, blocking collectives, per_device(): lax.all_to_all(grad_kv_low, 'seq', split_axis=0, concat_axis=0, tiled=True)  32.5 us
    unnamed x21, local copies, waits for them, and re-layouts  22.2 us
  transfers between devices with their start and end apart: 9, of which 7 were waited for; matrix products, arithmetic and copies ran while one was open for 3% of the time, Pallas kernels for 0%

commit v1 on v0

--- a/solution.py
+++ b/solution.py
@@ -77,19 +77,21 @@
     seq_devices = lax.axis_size("seq")
     dp_devices = lax.axis_size("dp")
     position = lax.axis_index("seq")
+    dp_index = lax.axis_index("dp")
     tokens = activations[0]
     grad_rows = grad_out[0]
     tok_count = tokens.shape[0]
     heads = w_query.shape[1] // HD
     kv_heads = w_key.shape[1] // HD
-    full_q, full_k, full_v = (
-        lax.all_gather(w_query, "seq", axis=0, tiled=True),
-        lax.all_gather(w_key, "seq", axis=0, tiled=True),
-        lax.all_gather(w_value, "seq", axis=0, tiled=True),
-    )
-    queries = jnp.dot(tokens, full_q, preferred_element_type=jnp.float32).astype(jnp.bfloat16)
-    key_proj = jnp.dot(tokens, full_k, preferred_element_type=jnp.float32).astype(jnp.bfloat16)
-    value_proj = jnp.dot(tokens, full_v, preferred_element_type=jnp.float32).astype(jnp.bfloat16)
+    query_cols = heads * HD
+    kv_cols = kv_heads * HD
+    all_cols = query_cols + 2 * kv_cols
+    w_local = jnp.concatenate([w_query, w_key, w_value], axis=1)
+    w_full = lax.all_gather(w_local, "seq", axis=0, tiled=True)
+    projected = jnp.dot(tokens, w_full, preferred_element_type=jnp.float32).astype(jnp.bfloat16)
+    queries = projected[:, :query_cols]
+    key_proj = projected[:, query_cols : query_cols + kv_cols]
+    value_proj = projected[:, query_cols + kv_cols :]
     query_pieces = queries.reshape(tok_count, heads, HD).transpose(1, 0, 2)
     grad_pieces = grad_rows.reshape(tok_count, heads, HD).transpose(1, 0, 2)
     paired = jnp.concatenate(
@@ -97,35 +99,29 @@
         axis=2,
     )
     kv_pieces = jnp.repeat(paired.transpose(1, 0, 2), GROUP, axis=0)
-    head_q, head_grad, landed = (
-        lax.all_to_all(query_pieces, "seq", split_axis=0, concat_axis=1, tiled=True),
-        lax.all_to_all(grad_pieces, "seq", split_axis=0, concat_axis=1, tiled=True),
-        lax.all_to_all(kv_pieces, "seq", split_axis=0, concat_axis=1, tiled=True),
-    )
-    head_kv = landed[0]
+    sent = jnp.concatenate([query_pieces, grad_pieces, kv_pieces], axis=2)
+    landed = lax.all_to_all(sent, "seq", split_axis=0, concat_axis=1, tiled=True)[0]
+    head_q = landed[:, :HD]
+    head_grad = landed[:, HD : 2 * HD]
+    head_k = landed[:, 2 * HD : 3 * HD]
+    head_v = landed[:, 3 * HD :]
     blocks_mine = lax.dynamic_index_in_dim(key_blocks, position, 0, keepdims=False)
     count_mine = lax.dynamic_index_in_dim(random_count, position, 0, keepdims=False)
     attended, grad_query, grad_kv = head_pass(
-        head_q[0], head_kv[:, :HD], head_kv[:, HD:], head_grad[0], blocks_mine, count_mine
+        head_q, head_k, head_v, head_grad, blocks_mine, count_mine
     )
-    grad_kv_low = grad_kv.astype(jnp.bfloat16).reshape(seq_devices, tok_count, 2 * HD)
-    back_out, back_query, back_kv = (
-        lax.all_to_all(
+    back_sent = jnp.concatenate(
+        [
             attended.reshape(seq_devices, tok_count, HD),
-            "seq",
-            split_axis=0,
-            concat_axis=0,
-            tiled=True,
-        ),
-        lax.all_to_all(
             grad_query.reshape(seq_devices, tok_count, HD),
-            "seq",
-            split_axis=0,
-            concat_axis=0,
-            tiled=True,
-        ),
-        lax.all_to_all(grad_kv_low, "seq", split_axis=0, concat_axis=0, tiled=True),
+            grad_kv.astype(jnp.bfloat16).reshape(seq_devices, tok_count, 2 * HD),
+        ],
+        axis=2,
     )
+    back = lax.all_to_all(back_sent, "seq", split_axis=0, concat_axis=0, tiled=True)
+    back_out = back[:, :, :HD]
+    back_query = back[:, :, HD : 2 * HD]
+    back_kv = back[:, :, 2 * HD :]
     out_rows = back_out.transpose(1, 0, 2).reshape(tok_count, heads * HD)
     grad_q_rows = back_query.transpose(1, 0, 2).reshape(tok_count, heads * HD)
     kv_sum = jnp.sum(
@@ -133,28 +129,35 @@
     ).astype(jnp.bfloat16)
     grad_k_rows = kv_sum[:, :, :HD].transpose(1, 0, 2).reshape(tok_count, kv_heads * HD)
     grad_v_rows = kv_sum[:, :, HD:].transpose(1, 0, 2).reshape(tok_count, kv_heads * HD)
+    combined = jnp.concatenate([grad_q_rows, grad_k_rows, grad_v_rows], axis=1)
     contract = (((1,), (1,)), ((), ()))
-    grad_x_rows = (
-        lax.dot_general(grad_q_rows, full_q, contract, preferred_element_type=jnp.float32)
-        + lax.dot_general(grad_k_rows, full_k, contract, preferred_element_type=jnp.float32)
-        + lax.dot_general(grad_v_rows, full_v, contract, preferred_element_type=jnp.float32)
+    grad_x_rows = lax.dot_general(
+        combined, w_full, contract, preferred_element_type=jnp.float32
     ).astype(jnp.bfloat16)
-    combined = jnp.concatenate([grad_q_rows, grad_k_rows, grad_v_rows], axis=1)
     factor = 1.0 / math.sqrt(tok_count * seq_devices * dp_devices)
     over_tokens = (((0,), (0,)), ((), ()))
-    partial_seq = lax.psum_scatter(
-        (
-            lax.dot_general(tokens, combined, over_tokens, preferred_element_type=jnp.float32)
-            * factor
-        ).astype(jnp.bfloat16),
-        "seq",
-        scatter_dimension=0,
-        tiled=True,
-    )
-    summed = lax.psum(partial_seq, "dp").astype(jnp.float32)
-    grad_all = summed.astype(jnp.bfloat16)
-    query_cols = heads * HD
-    kv_cols = kv_heads * HD
+    term = (
+        lax.dot_general(tokens, combined, over_tokens, preferred_element_type=jnp.float32)
+        * factor
+    ).astype(jnp.bfloat16)
+    half = all_cols // 2
+    core = dp_index % 2
+    pairs = [(i, i ^ 1) for i in range(dp_devices)]
+    keep = lax.dynamic_slice_in_dim(term, core * half, half, axis=1)
+    give = lax.dynamic_slice_in_dim(term, (1 - core) * half, half, axis=1)
+    got = lax.ppermute(give, "dp", pairs)
+    chip_sum = (keep.astype(jnp.float32) + got.astype(jnp.float32)).astype(jnp.bfloat16)
+    part = lax.psum_scatter(chip_sum, "seq", scatter_dimension=0, tiled=True)
+    step = 2
+    while step < dp_devices:
+        mates = [(i, i ^ step) for i in range(dp_devices)]
+        other = lax.ppermute(part, "dp", mates)
+        part = (part.astype(jnp.float32) + other.astype(jnp.float32)).astype(jnp.bfloat16)
+        step *= 2
+    other_half = lax.ppermute(part, "dp", pairs)
+    first = jnp.where(core == 0, part, other_half)
+    second = jnp.where(core == 0, other_half, part)
+    grad_all = jnp.concatenate([first, second], axis=1)
     grad_wq = grad_all[:, :query_cols]
     grad_wk = grad_all[:, query_cols : query_cols + kv_cols]
     grad_wv = grad_all[:, query_cols + kv_cols :]

time: 852 us -> 731 us (0.86)
  waiting for transfers between devices: 530 us -> 449 us
  blocking collectives: 54.1 us -> 0 us
  other arithmetic: 60.7 us -> 73.7 us
    all_gather x3 -> x1, waiting for transfers between devices: 234 us -> 113 us  [per_device(): w_full = lax.all_gather(w_local, 'seq', axis=0, tiled=True)]
    all_to_all x4 -> x2, waiting for transfers between devices: 24.9 us -> 94.9 us  [the longest x1 48.4 us: per_device(): lax.all_to_all(back_sent, 'seq', split_axis=0, concat_axis=0, tiled=True)]
    psum x1 -> x0, waiting for transfers between devices: 65.7 us -> none  [per_device(): summed = lax.psum(partial_seq, 'dp').astype(jnp.float32)]
    all_to_all x2 -> x0, blocking collectives: 54.1 us -> none  [the longest x1 32.5 us: per_device(): lax.all_to_all(grad_kv_low, 'seq', split_axis=0, concat_axis=0, tiled=True)]
    ppermute x0 -> x4, waiting for transfers between devices: none -> 21.9 us  [the longest x2 13.3 us: per_device(): other = lax.ppermute(part, 'dp', mates)]
    all_to_all x4 -> x2, starting transfers between devices: 31.6 us -> 12.4 us  [the longest x1 6.93 us: per_device(): lax.all_to_all(back_sent, 'seq', split_axis=0, concat_axis=0, tiled=True)]
    unnamed x6 -> x3, waiting for transfers between devices: 205 us -> 219 us
    ppermute x0 -> x4, starting transfers between devices: none -> 11.7 us  [the longest x1 5.8 us: per_device(): other_half = lax.ppermute(part, 'dp', pairs)]
  transfers between devices with their start and end apart: 9 -> 8, of which waited for: 7 -> 7; matrix products, arithmetic and copies ran while one was open for 3% -> 2% of each run, Pallas kernels for 0% -> 0%
where the time goes in v1:
time: 731 us; the launch traced here: 728 us
  waiting for transfers between devices  449 us (61%)
  matrix products  93.4 us (13%)
  other arithmetic  73.7 us (10%)
  local copies, waits for them, and re-layouts  72 us (10%)
  starting transfers between devices  24.4 us (3%)
  between operations  14.9 us (2%)
    unnamed x3, waiting for transfers between devices  219 us
    all_gather x1, waiting for transfers between devices, per_device(): w_full = lax.all_gather(w_local, 'seq', axis=0, tiled=True)  113 us
    scatter-add x8, other arithmetic, one_step(): running = running.at[chosen.reshape(-1)].add(pieces)  55 us
    all_to_all x1, waiting for transfers between devices, per_device(): lax.all_to_all(back_sent, 'seq', split_axis=0, concat_axis=0, tiled=True)  48.4 us
    all_to_all x1, waiting for transfers between devices, per_device(): lax.all_to_all(sent, 'seq', split_axis=0, concat_axis=1, tiled=True)[0]  46.5 us
    unnamed x21, local copies, waits for them, and re-layouts  20.6 us
    dot_general x8, matrix products, one_step(): jnp.einsum('gqk,gke->gqe', shares_low, v_part, preferred_element_type=jnp...  19.1 us
  transfers between devices with their start and end apart: 8, of which 7 were waited for; matrix products, arithmetic and copies ran while one was open for 2% of the time, Pallas kernels for 0%

profile of v1, /device:TPU:1, one launch (start us, length us, event | category | flops | bytes accessed | tf_op | source)
XLA Modules:
  0.0 727.9 jit_solution(3099953773682184216)
XLA Ops:
  7.2 1.8 pad_maximum_fusion.5
  10.4 113.4 %all-gather.2.cloned.1.call-done = bf16[2048,2560]{1,0:T(8,128)(2,1)} async-done(((bf16[64,2560]{1,0:T(8,128)(2,1)}), bf16[2048,2560]{1,0:T(8,128)(2,1)}) %all-gather.2.cloned.1.call-update) | async-done | bytes 10485776 | tf_op jit(solution)/shard_map/all_gather | solution.py:90
  123.7 6.9 fusion.43
  132.5 5.4 all-to-all-start
  140.1 46.5 %all-to-all-done = bf16[32,128,256]{1,2,0:T(8,128)(2,1)S(1)} async-done(((bf16[32,128,256]{1,2,0:T(8,128)(2,1)}), bf16[32,128,256]{1,2,0:T(8,128)(2,1)S(1)}, u32[]{:S(2)}, u32[]{:S(2)}) %all-to-all-start) | async-done | bytes 2097184 | tf_op jit(solution)/shard_map/all_to_all | solution.py:103
  186.6 2.9 copy.68
  189.5 4.2 fusion.53
  193.7 2.3 copy.72
  196.0 2.3 copy.71
  199.9 167.5 %while.15 = (s32[]{:T(128)}, f32[32,128,128]{2,1,0:T(8,128)}, bf16[8,4,128,64]{2,3,1,0:T(8,128)(2,1)}, bf16[8,4,128,64]{2,3,1,0:T(8,128)(2,1)}, s32[8,4,7]{2,1,0...) while((s32[]{:T(128)}, f32[32,128,128]{2,1,0:T(8,128)}, ...), condition=%wide.region_5.6_spmd.clone, body=%wide.region_0.5_spmd.clone.sunk | while | flops 360449568 | bytes 45045204 | solution.py:66
  200.2 1.7 gather_fusion.1
  202.6 1.6 fusion.93
  204.3 2.4 fusion.95
  212.3 1.7 copy.89
  214.0 6.9 scatter_fusion
  221.1 1.7 gather_fusion.1
  223.5 1.6 fusion.93
  225.2 2.4 fusion.95
  233.2 1.7 copy.89
  234.9 6.9 scatter_fusion
  242.1 1.7 gather_fusion.1
  246.1 2.4 fusion.95
  254.1 1.7 copy.89
  255.8 6.9 scatter_fusion
  263.0 1.7 gather_fusion.1
  267.0 2.4 fusion.95
  275.0 1.7 copy.89
  276.8 6.9 scatter_fusion
  283.9 1.7 gather_fusion.1
  286.4 1.6 fusion.93
  288.0 2.4 fusion.95
  296.0 1.7 copy.89
  297.7 6.9 scatter_fusion
  304.9 1.7 gather_fusion.1
  307.3 1.6 fusion.93
  308.9 2.4 fusion.95
  316.9 1.7 copy.89
  318.6 6.9 scatter_fusion
  325.8 1.7 gather_fusion.1
  328.2 1.6 fusion.93
  329.9 2.4 fusion.95
  337.9 1.7 copy.89
  339.6 6.8 scatter_fusion
  346.7 1.7 gather_fusion.1
  349.1 1.6 fusion.93
  350.8 2.4 fusion.95
  358.8 1.7 copy.89
  360.5 6.9 scatter_fusion
  367.4 1.9 copy.73
  370.8 6.9 all-to-all-start.1
  378.0 48.4 %all-to-all-done.1 = bf16[32,128,256]{1,2,0:T(8,128)(2,1)S(1)} async-done(((bf16[32,128,256]{1,2,0:T(8,128)(2,1)}), bf16[32,128,256]{1,2,0:T(8,128)(2,1)S(1)}, u32[]{:S(2)}, u32[]{:S(2)}) %all-to-all-start.1) | async-done | bytes 2097184 | tf_op jit(solution)/shard_map/all_to_all | solution.py:121
  427.5 5.1 multiply_convert_fusion.1
  432.6 3.2 dynamic-slice_bitcast_fusion
  435.8 2.3 copy-done.1
  438.1 2.5 collective-permute-start
  440.5 8.6 %collective-permute-done = bf16[2048,1280]{0,1:T(8,128)(2,1)} collective-permute-done((bf16[2048,1280]{0,1:T(8,128)(2,1)}, bf16[2048,1280]{0,1:T(8,128)(2,1)}, u32[]{:S(2)}, u32[]{:S(2)}) %collective-permute-start) | collective-permute-done | bytes 5242912 | tf_op jit(solution)/shard_map/ppermute | solution.py:148
  449.2 9.4 %fusion.42 = bf16[2048,1280]{0,1:T(8,128)(2,1)} fusion(bf16[2048,1280]{0,1:T(8,128)(2,1)} %collective-permute-done, bf16[2560,2048]{1,0:T(8,128)(2,1)} %copy-done.1, s32[]{:T(128)S(6)} %select_n.59), kind=kLoop, calls=%fused_computation.54 | loop fusion | flops 10485760 | bytes 15728644 | tf_op jit(solution)/shard_map/convert_element_type | solution.py:149
  458.6 7.9 %copy.86 = bf16[2048,1280]{1,0:T(8,128)(2,1)} copy(bf16[2048,1280]{0,1:T(8,128)(2,1)} %fusion.42) | data formatting | bytes 10485760
  466.5 218.9 %reduce-scatter.4.cloned.1.call-done = bf16[64,1280]{1,0:T(8,128)(2,1)} async-done(((bf16[2048,1280]{1,0:T(8,128)(2,1)}), bf16[64,1280]{1,0:T(8,128)(2,1)}) %reduce-scatter.4.cloned.1.call-update) | async-done | bytes 163856
  687.3 5.3 collective-permute-done.1
  692.6 2.7 collective-permute-start.2
  695.4 8.0 %collective-permute-done.2 = bf16[64,1280]{0,1:T(8,128)(2,1)S(1)} collective-permute-done((bf16[64,1280]{0,1:T(8,128)(2,1)S(1)}, bf16[64,1280]{0,1:T(8,128)(2,1)S(1)}, u32[]{:S(2)}, u32[]{:S(2)}) %collective-permute-start.2) | collective-permute-done | bytes 163872 | tf_op jit(solution)/shard_map/ppermute | solution.py:154
  703.5 5.8 collective-permute-start.3
  709.3 8.3 %fusion.44 = bf16[1,128,2048]{2,1,0:T(8,128)(2,1)} fusion(bf16[2048,2560]{1,0:T(8,128)(2,1)} %all-gather.2.cloned.1.call-done, bf16[128,256]{0,1:T(8,128)(2,1)S(1)} %bitcast.151, bf16[128,256]{0,1:T(8,128)(2,1)S(1)} %bitcast.149, bf16[128,2048]{0,1:T(8,128)(2,1)S(1)} %bitcast.141), kind=kOutput, calls=%fused_computation.59 | convolution fusion | flops 1344405504 | bytes 11665408 | tf_op jit(solution)/shard_map/dot_general | solution.py:134
  (230 shorter events, 70.5 us)
Async XLA Ops:
  7.2 116.6 %copy-start = (bf16[1,128,2048]{2,1,0:T(8,128)(2,1)S(1)}, bf16[1,128,2048]{2,1,0:T(8,128)(2,1)}, u32[]{:S(2)}) copy-start(bf16[1,128,2048]{2,1,0:T(8,128)(2,1)} %param.9) | copy-start | bytes 1572868
  7.2 116.6 %all-gather.2.cloned.1.call-start = ((), (), s32[]{:S(2)}) async-start(), calls=%async_computation.3 | async-start | bytes 10813440 | tf_op jit(solution)/shard_map/all_gather | solution.py:90
  132.5 5.5 copy-start.10
  132.5 54.1 %all-to-all-start = ((bf16[32,128,256]{1,2,0:T(8,128)(2,1)}), bf16[32,128,256]{1,2,0:T(8,128)(2,1)S(1)}, u32[]{:S(2)}, u32[]{:S(2)}) async-start(bf16[32,128,256]{1,2,0:T(8,128)(2,1)} %pad_maximum_fusion.1), calls=%async_computation | async-start | bytes 4194304 | tf_op jit(solution)/shard_map/all_to_all | solution.py:103
  199.9 1.9 copy-start.2
  199.9 2.7 copy-start.4
  206.6 1.3 copy-start.6
  214.0 6.9 copy-start.3
  214.0 6.9 copy-start.5
  220.8 2.0 copy-start.2
  220.8 2.7 copy-start.4
  227.6 1.3 copy-start.6
  234.9 6.9 copy-start.3
  234.9 6.9 copy-start.5
  241.8 2.0 copy-start.2
  241.8 2.7 copy-start.4
  248.5 1.3 copy-start.6
  255.8 6.9 copy-start.3
  255.8 6.9 copy-start.5
  262.7 2.0 copy-start.2
  262.7 2.7 copy-start.4
  269.4 1.3 copy-start.6
  276.8 6.9 copy-start.3
  276.8 6.9 copy-start.5
  283.7 2.0 copy-start.2
  283.7 2.7 copy-start.4
  290.4 1.3 copy-start.6
  297.7 6.9 copy-start.3
  297.7 6.9 copy-start.5
  304.6 2.0 copy-start.2
  304.6 2.7 copy-start.4
  311.3 1.3 copy-start.6
  318.6 6.9 copy-start.3
  318.6 6.9 copy-start.5
  325.5 2.0 copy-start.2
  325.5 2.7 copy-start.4
  332.3 1.3 copy-start.6
  339.6 6.9 copy-start.3
  339.6 6.9 copy-start.5
  346.4 2.0 copy-start.2
  346.4 2.7 copy-start.4
  353.2 1.3 copy-start.6
  360.5 6.9 copy-start.3
  360.5 6.9 copy-start.5
  367.4 1.9 copy-start.8
  367.4 2.0 copy-start.9
  370.8 55.6 %all-to-all-start.1 = ((bf16[32,128,256]{1,2,0:T(8,128)(2,1)}), bf16[32,128,256]{1,2,0:T(8,128)(2,1)S(1)}, u32[]{:S(2)}, u32[]{:S(2)}) async-start(bf16[32,128,256]{1,2,0:T(8,128)(2,1)} %pad_maximum_fusion.2), calls=%async_computation.1 | async-start | bytes 4194304 | tf_op jit(solution)/shard_map/all_to_all | solution.py:121
  377.8 307.6 %reduce-scatter.4.cloned.1.call-start = ((), (), s32[]{:S(2)}) async-start(), calls=%async_computation.4 | async-start | bytes 5406720
  432.6 5.5 copy-start.1
  438.1 11.1 %collective-permute-start = (bf16[2048,1280]{0,1:T(8,128)(2,1)}, bf16[2048,1280]{0,1:T(8,128)(2,1)}, u32[]{:S(2)}, u32[]{:S(2)}) collective-permute-start(bf16[2048,1280]{0,1:T(8,128)(2,1)} %dynamic-slice_bitcast_fusion), channel_id=1, source_target_pairs={{0,32},{32,0},{64,96},{96,64},{128,160},{160,128},{192,224},{224,1... | collective-permute-start | bytes 15728648 | tf_op jit(solution)/shard_map/ppermute | solution.py:148
  686.5 6.0 collective-permute-start.1
  692.6 10.7 %collective-permute-start.2 = (bf16[64,1280]{0,1:T(8,128)(2,1)S(1)}, bf16[64,1280]{0,1:T(8,128)(2,1)S(1)}, u32[]{:S(2)}, u32[]{:S(2)}) collective-permute-start(bf16[64,1280]{0,1:T(8,128)(2,1)S(1)} %add_convert_fusion.1), channel_id=1, source_target_pairs={{0,128},{32,160},{64,192},{96,224},{128,0},{160,32},{192,64},{224,... | collective-permute-start | bytes 491528 | tf_op jit(solution)/shard_map/ppermute | solution.py:154
  703.5 14.1 %copy-start.7 = (bf16[32,128,64]{1,2,0:T(8,128)(2,1)S(1)}, bf16[32,128,64]{1,2,0:T(8,128)(2,1)}, u32[]{:S(2)}) copy-start(bf16[32,128,64]{1,2,0:T(8,128)(2,1)} %get-tuple-element.162) | copy-start | bytes 1572868
  703.5 15.1 %collective-permute-start.3 = (bf16[64,1280]{0,1:T(8,128)(2,1)S(1)}, bf16[64,1280]{0,1:T(8,128)(2,1)S(1)}, u32[]{:S(2)}, u32[]{:S(2)}) collective-permute-start(bf16[64,1280]{0,1:T(8,128)(2,1)S(1)} %add_convert_fusion), channel_id=1, source_target_pairs={{0,32},{32,0},{64,96},{96,64},{128,160},{160,128},{192,224},{224,1... | collective-permute-start | bytes 491528 | tf_op jit(solution)/shard_map/ppermute | solution.py:157
Sparse Core Ops, SparseCore 0:
  11.2 112.5 all-gather.1
  466.6 218.7 reduce-scatter.3

commit v2 on v1

--- a/solution.py
+++ b/solution.py
@@ -11,6 +11,7 @@
 
 masked_score = -1e30
 query_group = 4
+RING_Z = 8
 
 
 def head_pass(queries, key_rows, value_rows, grad_head, blocks, extra_count):
@@ -20,57 +21,75 @@
     score_scale = head_width ** (-0.5)
     key_tiles = key_rows.reshape(block_count, block_len, head_width)
     value_tiles = value_rows.reshape(block_count, block_len, head_width)
+    q_part = queries.reshape(block_count, block_len, head_width)
+    g_part = grad_head.reshape(block_count, block_len, head_width)
     usable = jnp.repeat(jnp.arange(slot_count) < 4 + extra_count, block_len)
-    rounds = block_count // query_group
-    query_steps = queries.reshape(rounds, query_group, block_len, head_width)
-    grad_steps = grad_head.reshape(rounds, query_group, block_len, head_width)
-    block_steps = blocks.reshape(rounds, query_group, slot_count)
-
-    def one_step(running, inputs):
-        q_part, g_part, chosen = inputs
-        k_part = key_tiles[chosen].reshape(query_group, slot_count * block_len, head_width)
-        v_part = value_tiles[chosen].reshape(query_group, slot_count * block_len, head_width)
-        scores = (
-            jnp.einsum("gqe,gke->gqk", q_part, k_part, preferred_element_type=jnp.float32)
-            * score_scale
-        )
-        scores = jnp.where(usable, scores, masked_score)
-        highest = jnp.max(scores, axis=-1, keepdims=True)
-        exponent = jnp.exp(scores - highest)
-        shares = exponent / jnp.sum(exponent, axis=-1, keepdims=True)
-        shares_low = shares.astype(jnp.bfloat16)
-        attended = jnp.einsum(
-            "gqk,gke->gqe", shares_low, v_part, preferred_element_type=jnp.float32
-        ).astype(jnp.bfloat16)
-        grad_shares = jnp.einsum("gqe,gke->gqk", g_part, v_part, preferred_element_type=jnp.float32)
-        weighted = jnp.sum(grad_shares * shares, axis=-1, keepdims=True)
-        grad_scores = (shares * (grad_shares - weighted)).astype(jnp.bfloat16)
-        grad_query = (
-            jnp.einsum("gqk,gke->gqe", grad_scores, k_part, preferred_element_type=jnp.float32)
-            * score_scale
-        ).astype(jnp.bfloat16)
-        grad_keys = (
-            jnp.einsum("gqk,gqe->gke", grad_scores, q_part, preferred_element_type=jnp.float32)
-            * score_scale
-        )
-        grad_values = jnp.einsum(
-            "gqk,gqe->gke", shares_low, g_part, preferred_element_type=jnp.float32
-        )
-        pieces = jnp.concatenate([grad_keys, grad_values], axis=-1).reshape(
-            query_group * slot_count, block_len, 2 * head_width
-        )
-        running = running.at[chosen.reshape(-1)].add(pieces)
-        return (running, (attended, grad_query))
-
-    initial = jnp.zeros((block_count, block_len, 2 * head_width), jnp.float32)
-    summed, (attended, grad_query) = lax.scan(
-        one_step, initial, (query_steps, grad_steps, block_steps)
-    )
+    k_part = key_tiles[blocks].reshape(block_count, slot_count * block_len, head_width)
+    v_part = value_tiles[blocks].reshape(block_count, slot_count * block_len, head_width)
+    scores = (
+        jnp.einsum("gqe,gke->gqk", q_part, k_part, preferred_element_type=jnp.float32)
+        * score_scale
+    )
+    scores = jnp.where(usable, scores, masked_score)
+    highest = jnp.max(scores, axis=-1, keepdims=True)
+    exponent = jnp.exp(scores - highest)
+    shares = exponent / jnp.sum(exponent, axis=-1, keepdims=True)
+    shares_low = shares.astype(jnp.bfloat16)
+    attended = jnp.einsum(
+        "gqk,gke->gqe", shares_low, v_part, preferred_element_type=jnp.float32
+    ).astype(jnp.bfloat16)
+    grad_shares = jnp.einsum("gqe,gke->gqk", g_part, v_part, preferred_element_type=jnp.float32)
+    weighted = jnp.sum(grad_shares * shares, axis=-1, keepdims=True)
+    grad_scores = (shares * (grad_shares - weighted)).astype(jnp.bfloat16)
+    grad_query = (
+        jnp.einsum("gqk,gke->gqe", grad_scores, k_part, preferred_element_type=jnp.float32)
+        * score_scale
+    ).astype(jnp.bfloat16)
+    grad_keys = (
+        jnp.einsum("gqk,gqe->gke", grad_scores, q_part, preferred_element_type=jnp.float32)
+        * score_scale
+    )
+    grad_values = jnp.einsum(
+        "gqk,gqe->gke", shares_low, g_part, preferred_element_type=jnp.float32
+    )
+    pieces = jnp.concatenate([grad_keys, grad_values], axis=-1).reshape(
+        block_count * slot_count, block_len * 2 * head_width
+    )
+    owner = (
+        blocks.reshape(1, block_count * slot_count)
+        == jnp.arange(block_count, dtype=blocks.dtype)[:, None]
+    ).astype(jnp.float32)
+    summed = jnp.dot(owner, pieces, precision=lax.Precision.HIGHEST)
     return (
         attended.reshape(seq_len, head_width),
         grad_query.reshape(seq_len, head_width),
         summed.reshape(seq_len, 2 * head_width),
     )
+
+
+def ring_reduce_scatter(parts, ring, stride, position):
+    seq_devices = lax.axis_size("seq")
+    group = ring * stride
+    me = (position // stride) % ring
+    width = parts.shape[-1] // 2
+    ahead = [
+        (s, (s // group) * group + (((s // stride) % ring + 1) % ring) * stride + s % stride)
+        for s in range(seq_devices)
+    ]
+    behind = [(b, a) for (a, b) in ahead]
+    total = []
+    for side, perm, sign in ((0, ahead, 1), (1, behind, -1)):
+        own = parts[..., side * width : (side + 1) * width]
+
+        def chunk(k):
+            return lax.dynamic_index_in_dim(own, (me - sign * (1 + k)) % ring, 0, keepdims=False)
+
+        buf = chunk(0)
+        for k in range(ring - 1):
+            got = lax.ppermute(buf, "seq", perm)
+            buf = (got.astype(jnp.float32) + chunk(k + 1).astype(jnp.float32)).astype(jnp.bfloat16)
+        total.append(buf)
+    return jnp.concatenate(total, axis=-1)
 
 
 def per_device(activations, w_query, w_key, w_value, key_blocks, random_count, grad_out):
@@ -147,7 +166,10 @@
     give = lax.dynamic_slice_in_dim(term, (1 - core) * half, half, axis=1)
     got = lax.ppermute(give, "dp", pairs)
     chip_sum = (keep.astype(jnp.float32) + got.astype(jnp.float32)).astype(jnp.bfloat16)
-    part = lax.psum_scatter(chip_sum, "seq", scatter_dimension=0, tiled=True)
+    rows = chip_sum.shape[0] // seq_devices
+    by_z = chip_sum.reshape(seq_devices // RING_Z, RING_Z, rows, half).transpose(1, 0, 2, 3)
+    by_y = ring_reduce_scatter(by_z, RING_Z, 1, position)
+    part = ring_reduce_scatter(by_y, seq_devices // RING_Z, RING_Z, position)
     step = 2
     while step < dp_devices:
         mates = [(i, i ^ step) for i in range(dp_devices)]

time: 731 us -> 572 us (0.78)
  waiting for transfers between devices: 449 us -> 258 us
  starting transfers between devices: 24.4 us -> 60.2 us
  local copies, waits for them, and re-layouts: 72 us -> 99.6 us
  other arithmetic: 73.7 us -> 55.6 us
  matrix products: 93.4 us -> 77.2 us
    unnamed x3 -> x1, waiting for transfers between devices: 219 us -> 0.02 us
    scatter-add x8 -> x0, other arithmetic: 55 us -> none  [one_step(): running = running.at[chosen.reshape(-1)].add(pieces)]
    ppermute x0 -> x20, waiting for transfers between devices: none -> 35.1 us  [ring_reduce_scatter(): got = lax.ppermute(buf, 'seq', perm)]
    reshape x8 -> x6, local copies, waits for them, and re-layouts: 0.67 us -> 35.4 us  [the longest x1 16 us: head_pass(): jnp.concatenate([grad_keys, grad_values], axis=-1)]
    convert_element_type x8 -> x21, other arithmetic: 2.78 us -> 33.5 us  [the longest x20 22.7 us: ring_reduce_scatter(): (got.astype(jnp.float32) + chunk(k + 1).astype(jnp.float32)).astype(jnp.b...]
    ppermute x0 -> x20, starting transfers between devices: none -> 27.9 us  [ring_reduce_scatter(): got = lax.ppermute(buf, 'seq', perm)]
    dot_general x40 -> x6, matrix products: 60 us -> 46.8 us  [the longest x1 11 us: head_pass(): jnp.einsum('gqe,gke->gqk', g_part, v_part, preferred_element_type=jnp.flo...]
    unnamed x21 -> x26, local copies, waits for them, and re-layouts: 20.6 us -> 8.56 us
  transfers between devices with their start and end apart: 8 -> 27, of which waited for: 7 -> 18; matrix products, arithmetic and copies ran while one was open for 2% -> 6% of each run, Pallas kernels for 0% -> 0%
where the time goes in v2:
time: 572 us; the launch traced here: 566 us
  waiting for transfers between devices  258 us (45%)
  local copies, waits for them, and re-layouts  99.6 us (17%)
  matrix products  77.2 us (13%)
  starting transfers between devices  60.2 us (11%)
  other arithmetic  55.6 us (10%)
  between operations  15.4 us (3%)
    all_gather x1, waiting for transfers between devices, per_device(): w_full = lax.all_gather(w_local, 'seq', axis=0, tiled=True)  113 us
    all_to_all x1, waiting for transfers between devices, per_device(): lax.all_to_all(back_sent, 'seq', split_axis=0, concat_axis=0, tiled=True)  48.6 us
    all_to_all x1, waiting for transfers between devices, per_device(): lax.all_to_all(sent, 'seq', split_axis=0, concat_axis=1, tiled=True)[0]  46.1 us
    ppermute x20, waiting for transfers between devices, ring_reduce_scatter(): got = lax.ppermute(buf, 'seq', perm)  35.1 us
    ppermute x20, starting transfers between devices, ring_reduce_scatter(): got = lax.ppermute(buf, 'seq', perm)  27.9 us
    convert_element_type x20, other arithmetic, ring_reduce_scatter(): (got.astype(jnp.float32) + chunk(k + 1).astype(jnp.float32)).astype(jnp.b...  22.7 us
    concatenate x1, local copies, waits for them, and re-layouts, head_pass(): jnp.concatenate([grad_keys, grad_values], axis=-1)  16.1 us
    reshape x1, local copies, waits for them, and re-layouts, head_pass(): jnp.concatenate([grad_keys, grad_values], axis=-1)  16 us
  transfers between devices with their start and end apart: 27, of which 18 were waited for; matrix products, arithmetic and copies ran while one was open for 6% of the time, Pallas kernels for 0%

profile of v2, /device:TPU:1, one launch (start us, length us, event | category | flops | bytes accessed | tf_op | source)
XLA Modules:
  0.0 566.1 jit_solution(12210671963242412984)
XLA Ops:
  10.4 113.4 %all-gather.2.cloned.1.call-done = bf16[2048,2560]{1,0:T(8,128)(2,1)} async-done(((bf16[64,2560]{1,0:T(8,128)(2,1)}), bf16[2048,2560]{1,0:T(8,128)(2,1)}) %all-gather.2.cloned.1.call-update) | async-done | bytes 10485776 | tf_op jit(solution)/shard_map/all_gather | solution.py:109
  123.7 6.9 %fusion.13 = bf16[128,2560]{0,1:T(8,128)(2,1)S(1)} fusion(bf16[2048,2560]{1,0:T(8,128)(2,1)} %all-gather.2.cloned.1.call-done, bf16[1,128,2048]{2,1,0:T(8,128)(2,1)S(1)} %copy-done), kind=kOutput, calls=%fused_computation.27 | convolution fusion | flops 1342504960 | bytes 11665408 | tf_op jit(solution)/shard_map/dot_general | solution.py:110
  132.5 5.6 all-to-all-start
  140.7 46.1 %all-to-all-done = bf16[32,128,256]{1,2,0:T(8,128)(2,1)} async-done(((bf16[32,128,256]{1,2,0:T(8,128)(2,1)}), bf16[32,128,256]{1,2,0:T(8,128)(2,1)}, u32[]{:S(2)}, u32[]{:S(2)}) %all-to-all-start) | async-done | bytes 2097184 | tf_op jit(solution)/shard_map/all_to_all | solution.py:122
  186.7 3.3 copy.117
  190.0 2.7 fusion.73
  195.9 2.9 gather_fusion
  198.8 6.2 %copy.122 = bf16[224,128,64]{1,0,2:T(8,128)(2,1)} copy(bf16[224,128,64]{1,2,0:T(8,128)(2,1)} %gather_fusion) | data formatting | bytes 7340032 | tf_op jit(solution)/shard_map/gather | solution.py:27
  205.0 7.8 %reshape.152 = bf16[32,896,64]{1,0,2:T(8,128)(2,1)} reshape(bf16[224,128,64]{1,0,2:T(8,128)(2,1)} %copy.122) | data formatting | bytes 7340032 | tf_op jit(solution)/shard_map/reshape | solution.py:27
  212.8 3.0 gather_fusion.1
  215.8 6.2 %copy.127 = bf16[224,128,64]{1,0,2:T(8,128)(2,1)} copy(bf16[224,128,64]{1,2,0:T(8,128)(2,1)} %gather_fusion.1) | data formatting | bytes 7340032 | tf_op jit(solution)/shard_map/gather | solution.py:28
  222.0 7.8 %reshape.154 = bf16[32,896,64]{1,0,2:T(8,128)(2,1)} reshape(bf16[224,128,64]{1,0,2:T(8,128)(2,1)} %copy.127) | data formatting | bytes 7340032 | tf_op jit(solution)/shard_map/reshape | solution.py:28
  229.8 10.8 %fusion.77 = (f32[32,128]{1,0:T(8,128)S(1)}, f32[32,128,896]{2,1,0:T(8,128)}) fusion(pred[896]{0:T(1024)(128)(4,1)S(1)} %broadcast_bitcast_fusion, bf16[32,128,64]{2,1,0:T(8,128)(2,1)S(1)} %bitcast.152, bf16[32,896,64]{1,0,2:T(8,128)(2,1)} %reshape.152), kind=kOutput, calls=%fused_computation.119 | convolution fusion | flops 484443008 | bytes 18891648 | tf_op jit(solution)/shard_map/sub | solution.py:35
  240.6 9.3 %fusion.31 = bf16[32,128,64]{1,2,0:T(8,128)(2,1)S(1)} fusion(bf16[32,896,64]{1,0,2:T(8,128)(2,1)} %reshape.154, f32[32,128,896]{2,1,0:T(8,128)} %get-tuple-element.49, f32[32,128]{1,0:T(8,128)S(1)} %get-tuple-element.48), kind=kOutput, calls=%fused_computation.42 | convolution fusion | flops 477364224 | bytes 18890752 | tf_op jit(solution)/shard_map/gqk,gke->gqe/dot_general | solution.py:38
  249.9 9.8 %fusion.9 = f32[32,896,64]{1,2,0:T(8,128)} fusion(bf16[32,128,64]{2,1,0:T(8,128)(2,1)S(1)} %bitcast.162, f32[32,128,896]{2,1,0:T(8,128)} %get-tuple-element.49, f32[32,128]{1,0:T(8,128)S(1)} %get-tuple-element.48), kind=kOutput, calls=%fused_computation.22 | convolution fusion | flops 477102080 | bytes 22560768 | tf_op jit(solution)/shard_map/gqk,gqe->gke/dot_general | solution.py:52
  259.7 11.0 %multiply_reduce_fusion = (f32[32,128]{1,0:T(8,128)S(1)}, f32[32,128,896]{2,1,0:T(8,128)}) fusion(f32[32,128,896]{2,1,0:T(8,128)} %get-tuple-element.49, f32[32,128]{1,0:T(8,128)S(1)} %get-tuple-element.48, bf16[32,128,64]{2,1,0:T(8,128)(2,1)S(1)} %bitcast.163, bf16[32,896,64]{1,0,2:T(8,128)(2,1)S(1)} %copy-done.7), kind=kOutput, calls=%fused_computation.9 | convolution fusion | flops 480768000 | bytes 33587200 | tf_op jit(solution)/shard_map/gqe,gke->gqk/dot_general | solution.py:41
  270.7 10.8 %multiply_convert_fusion.1 = bf16[32,128,896]{2,1,0:T(8,128)(2,1)S(1)} fusion(f32[32,128,896]{2,1,0:T(8,128)} %get-tuple-element.51, f32[32,128]{1,0:T(8,128)S(1)} %get-tuple-element.50, f32[32,128,896]{2,1,0:T(8,128)} %get-tuple-element.49, f32[32,128]{1,0:T(8,128)S(1)} %get-tuple-element.48), kind=kLoop, calls=%fused_computation.8 | loop fusion | flops 14680064 | bytes 36732928 | tf_op jit(solution)/shard_map/convert_element_type | solution.py:43
  281.5 3.4 fusion.28
  284.8 4.3 broadcast_multiply_fusion
  290.8 10.5 %pad_maximum_fusion = f32[32,896,128]{1,2,0:T(8,128)} fusion(f32[32,896,64]{1,2,0:T(8,128)} %fusion.9, f32[32,896,64]{1,2,0:T(8,128)} %broadcast_multiply_fusion), kind=kLoop, calls=%fused_computation.7 | loop fusion | flops 3670016 | bytes 29360128 | tf_op jit(solution)/shard_map/concatenate | solution.py:55
  301.3 16.1 %copy.136 = f32[32,896,128]{2,1,0:T(8,128)} copy(f32[32,896,128]{1,2,0:T(8,128)} %pad_maximum_fusion) | data formatting | bytes 29360128 | tf_op jit(solution)/shard_map/concatenate | solution.py:55
  317.4 16.0 %reshape.156 = f32[224,16384]{1,0:T(8,128)} reshape(f32[32,896,128]{2,1,0:T(8,128)} %copy.136) | data formatting | bytes 29360128 | tf_op jit(solution)/shard_map/reshape | solution.py:55
  335.1 9.1 %fusion.22 = bf16[32,128,128]{2,0,1:T(8,128)(2,1)S(1)} fusion(s32[224]{0:T(256)S(1)} %eq.47, f32[224,16384]{1,0:T(8,128)} %reshape.156), kind=kOutput, calls=%fused_computation.39 | convolution fusion | flops 1409817600 | bytes 15729536 | tf_op jit(solution)/shard_map/dot_general | solution.py:62
  345.3 2.5 copy.140
  347.9 7.1 %all-to-all-start.1 = ((bf16[32,128,256]{2,1,0:T(8,128)(2,1)}), bf16[32,128,256]{2,1,0:T(8,128)(2,1)S(1)}, u32[]{:S(2)}, u32[]{:S(2)}) async-start(bf16[32,128,256]{2,1,0:T(8,128)(2,1)} %copy.140), calls=%async_computation.1 | async-start | bytes 4194304 | tf_op jit(solution)/shard_map/all_to_all | solution.py:140
  355.0 48.6 %all-to-all-done.1 = bf16[32,128,256]{2,1,0:T(8,128)(2,1)S(1)} async-done(((bf16[32,128,256]{2,1,0:T(8,128)(2,1)}), bf16[32,128,256]{2,1,0:T(8,128)(2,1)S(1)}, u32[]{:S(2)}, u32[]{:S(2)}) %all-to-all-start.1) | async-done | bytes 2097184 | tf_op jit(solution)/shard_map/all_to_all | solution.py:140
  403.7 1.9 fusion.72
  407.9 4.2 multiply_convert_fusion
  412.2 2.9 dynamic-slice_bitcast_fusion
  415.1 2.7 copy-done.1
  417.8 2.5 collective-permute-start
  420.3 8.6 %collective-permute-done = bf16[2048,1280]{1,0:T(8,128)(2,1)} collective-permute-done((bf16[2048,1280]{1,0:T(8,128)(2,1)}, bf16[2048,1280]{1,0:T(8,128)(2,1)}, u32[]{:S(2)}, u32[]{:S(2)}) %collective-permute-start) | collective-permute-done | bytes 5242912 | tf_op jit(solution)/shard_map/ppermute | solution.py:167
  428.9 5.4 fusion.5
  439.9 7.0 %collective-permute-done.11 = bf16[4,64,640]{2,1,0:T(8,128)(2,1)} collective-permute-done((bf16[4,64,640]{2,1,0:T(8,128)(2,1)}, bf16[4,64,640]{2,1,0:T(8,128)(2,1)}, u32[]{:S(2)}, u32[]{:S(2)}) %collective-permute-start.11) | collective-permute-done | bytes 327712 | tf_op jit(solution)/shard_map/ppermute | solution.py:89
  446.9 1.9 fusion.46
  448.8 1.9 collective-permute-start.12
  450.7 1.8 fusion.53
  452.5 4.8 collective-permute-done.12
  457.3 1.9 fusion.45
  459.2 2.9 collective-permute-start.13
  462.1 1.8 fusion.52
  463.9 3.4 collective-permute-done.13
  467.3 1.9 fusion.44
  469.2 3.4 collective-permute-start.14
  472.6 1.8 fusion.51
  474.4 2.5 collective-permute-done.14
  476.9 1.9 fusion.43
  478.8 3.1 collective-permute-start.15
  483.7 2.5 collective-permute-done.15
  486.2 1.9 fusion.42
  488.1 3.1 collective-permute-start.16
  493.0 2.5 collective-permute-done.16
  495.6 1.9 fusion.41
  497.4 3.1 collective-permute-start.17
  501.7 3.2 collective-permute-done.17
  506.1 2.4 collective-permute-start.18
  511.3 2.1 collective-permute-start.19
  515.2 3.0 collective-permute-start.20
  519.8 4.4 collective-permute-done.10
  525.5 3.3 collective-permute-done.21
  528.8 2.8 collective-permute-start.22
  531.6 3.0 collective-permute-done.22
  534.7 13.0 %collective-permute-start.23 = (bf16[64,1280]{1,0:T(8,128)(2,1)S(1)}, bf16[64,1280]{1,0:T(8,128)(2,1)S(1)}, u32[]{:S(2)}, u32[]{:S(2)}) collective-permute-start(bf16[64,1280]{1,0:T(8,128)(2,1)S(1)} %add_convert_fusion), channel_id=1, source_target_pairs={{0,32},{32,0},{64,96},{96,64},{128,160},{160,128},{192,224},{224,1... | collective-permute-start | bytes 491528 | tf_op jit(solution)/shard_map/ppermute | solution.py:179
  547.7 8.5 %fusion.21 = bf16[1,128,2048]{2,1,0:T(8,128)(2,1)} fusion(bf16[2048,2560]{1,0:T(8,128)(2,1)} %all-gather.2.cloned.1.call-done, bf16[128,256]{0,1:T(8,128)(2,1)S(1)} %bitcast.165, bf16[128,256]{0,1:T(8,128)(2,1)S(1)} %bitcast.167, bf16[128,2048]{0,1:T(8,128)(2,1)} %bitcast.155), kind=kOutput, calls=%fused_computation.36 | convolution fusion | flops 1344405504 | bytes 11665408 | tf_op jit(solution)/shard_map/dot_general | solution.py:153
  (100 shorter events, 38.5 us)
Async XLA Ops:
  7.2 116.6 %copy-start = (bf16[1,128,2048]{2,1,0:T(8,128)(2,1)S(1)}, bf16[1,128,2048]{2,1,0:T(8,128)(2,1)}, u32[]{:S(2)}) copy-start(bf16[1,128,2048]{2,1,0:T(8,128)(2,1)} %param.7) | copy-start | bytes 1572868
  7.2 116.6 %all-gather.2.cloned.1.call-start = ((), (), s32[]{:S(2)}) async-start(), calls=%async_computation.2 | async-start | bytes 10813440 | tf_op jit(solution)/shard_map/all_gather | solution.py:109
  130.7 7.5 %copy-start.10 = (s32[32]{0:T(128)S(1)}, s32[32]{0:T(128)}, u32[]{:S(2)}) copy-start(s32[32]{0:T(128)} %param.12) | copy-start | bytes 388
  132.5 54.2 %all-to-all-start = ((bf16[32,128,256]{1,2,0:T(8,128)(2,1)}), bf16[32,128,256]{1,2,0:T(8,128)(2,1)}, u32[]{:S(2)}, u32[]{:S(2)}) async-start(bf16[32,128,256]{1,2,0:T(8,128)(2,1)} %pad_maximum_fusion.1), calls=%async_computation | async-start | bytes 4194304 | tf_op jit(solution)/shard_map/all_to_all | solution.py:122
  222.0 7.8 %copy-start.3 = (bf16[4096,64]{1,0:T(8,128)(2,1)S(1)}, bf16[4096,64]{1,0:T(8,128)(2,1)}, u32[]{:S(2)}) copy-start(bf16[4096,64]{1,0:T(8,128)(2,1)} %get-tuple-element.39) | copy-start | bytes 1572868
  240.6 9.3 %copy-start.8 = (bf16[4096,64]{1,0:T(8,128)(2,1)S(1)}, bf16[4096,64]{1,0:T(8,128)(2,1)}, u32[]{:S(2)}) copy-start(bf16[4096,64]{1,0:T(8,128)(2,1)} %get-tuple-element.37) | copy-start | bytes 1572868
  249.9 9.8 %copy-start.7 = (bf16[32,896,64]{1,0,2:T(8,128)(2,1)S(1)}, bf16[32,896,64]{1,0,2:T(8,128)(2,1)}, u32[]{:S(2)}) copy-start(bf16[32,896,64]{1,0,2:T(8,128)(2,1)} %reshape.154) | copy-start | bytes 11010052
  270.7 10.8 %copy-start.6 = (bf16[32,896,64]{1,0,2:T(8,128)(2,1)S(1)}, bf16[32,896,64]{1,0,2:T(8,128)(2,1)}, u32[]{:S(2)}) copy-start(bf16[32,896,64]{1,0,2:T(8,128)(2,1)} %reshape.152) | copy-start | bytes 11010052
  317.4 16.1 %copy-start.9 = (bf16[32,128,64]{1,2,0:T(8,128)(2,1)S(1)}, bf16[32,128,64]{1,2,0:T(8,128)(2,1)}, u32[]{:S(2)}) copy-start(bf16[32,128,64]{1,2,0:T(8,128)(2,1)} %fusion.28) | copy-start | bytes 1572868
  347.9 55.8 %all-to-all-start.1 = ((bf16[32,128,256]{2,1,0:T(8,128)(2,1)}), bf16[32,128,256]{2,1,0:T(8,128)(2,1)S(1)}, u32[]{:S(2)}, u32[]{:S(2)}) async-start(bf16[32,128,256]{2,1,0:T(8,128)(2,1)} %copy.140), calls=%async_computation.1 | async-start | bytes 4194304 | tf_op jit(solution)/shard_map/all_to_all | solution.py:140
  407.2 5.0 copy-start.4
  412.1 5.7 %copy-start.1 = (bf16[2560,2048]{0,1:T(8,128)(2,1)}, bf16[2560,2048]{0,1:T(8,128)(2,1)S(1)}, u32[]{:S(2)}) copy-start(bf16[2560,2048]{0,1:T(8,128)(2,1)S(1)} %multiply_convert_fusion) | copy-start | bytes 31457284
  417.8 11.1 %collective-permute-start = (bf16[2048,1280]{1,0:T(8,128)(2,1)}, bf16[2048,1280]{1,0:T(8,128)(2,1)}, u32[]{:S(2)}, u32[]{:S(2)}) collective-permute-start(bf16[2048,1280]{1,0:T(8,128)(2,1)} %dynamic-slice_bitcast_fusion), channel_id=1, source_target_pairs={{0,32},{32,0},{64,96},{96,64},{128,160},{160,128},{192,224},{224,1... | collective-permute-start | bytes 15728648 | tf_op jit(solution)/shard_map/ppermute | solution.py:167
  435.4 1.5 copy-start.2
  437.7 9.2 %collective-permute-start.11 = (bf16[4,64,640]{2,1,0:T(8,128)(2,1)}, bf16[4,64,640]{2,1,0:T(8,128)(2,1)}, u32[]{:S(2)}, u32[]{:S(2)}) collective-permute-start(bf16[4,64,640]{2,1,0:T(8,128)(2,1)} %dynamic-slice_bitcast_fusion.1), channel_id=1, source_target_pairs={{1,0},{2,1},{3,2},{4,3},{5,4},{6,5},{7,6},{0,7},{9,8},{10,9},{11,1... | collective-permute-start | bytes 983048 | tf_op jit(solution)/shard_map/ppermute | solution.py:89
  438.9 11.7 %collective-permute-start.1 = (bf16[4,64,640]{2,1,0:T(8,128)(2,1)}, bf16[4,64,640]{2,1,0:T(8,128)(2,1)}, u32[]{:S(2)}, u32[]{:S(2)}) collective-permute-start(bf16[4,64,640]{2,1,0:T(8,128)(2,1)} %dynamic-slice_bitcast_fusion.2), channel_id=1, source_target_pairs={{0,1},{1,2},{2,3},{3,4},{4,5},{5,6},{6,7},{7,0},{8,9},{9,10},{10,1... | collective-permute-start | bytes 983048 | tf_op jit(solution)/shard_map/ppermute | solution.py:89
  448.8 8.5 %collective-permute-start.12 = (bf16[4,64,640]{2,1,0:T(8,128)(2,1)}, bf16[4,64,640]{2,1,0:T(8,128)(2,1)}, u32[]{:S(2)}, u32[]{:S(2)}) collective-permute-start(bf16[4,64,640]{2,1,0:T(8,128)(2,1)} %fusion.46), channel_id=1, source_target_pairs={{1,0},{2,1},{3,2},{4,3},{5,4},{6,5},{7,6},{0,7},{9,8},{10,9},{11,1... | collective-permute-start | bytes 983048 | tf_op jit(solution)/shard_map/ppermute | solution.py:89
  452.5 9.6 %collective-permute-start.2 = (bf16[4,64,640]{2,1,0:T(8,128)(2,1)}, bf16[4,64,640]{2,1,0:T(8,128)(2,1)}, u32[]{:S(2)}, u32[]{:S(2)}) collective-permute-start(bf16[4,64,640]{2,1,0:T(8,128)(2,1)} %fusion.53), channel_id=1, source_target_pairs={{0,1},{1,2},{2,3},{3,4},{4,5},{5,6},{6,7},{7,0},{8,9},{9,10},{10,1... | collective-permute-start | bytes 983048 | tf_op jit(solution)/shard_map/ppermute | solution.py:89
  459.2 8.1 %collective-permute-start.13 = (bf16[4,64,640]{2,1,0:T(8,128)(2,1)}, bf16[4,64,640]{2,1,0:T(8,128)(2,1)}, u32[]{:S(2)}, u32[]{:S(2)}) collective-permute-start(bf16[4,64,640]{2,1,0:T(8,128)(2,1)} %fusion.45), channel_id=1, source_target_pairs={{1,0},{2,1},{3,2},{4,3},{5,4},{6,5},{7,6},{0,7},{9,8},{10,9},{11,1... | collective-permute-start | bytes 983048 | tf_op jit(solution)/shard_map/ppermute | solution.py:89
  463.9 8.7 %collective-permute-start.3 = (bf16[4,64,640]{2,1,0:T(8,128)(2,1)}, bf16[4,64,640]{2,1,0:T(8,128)(2,1)}, u32[]{:S(2)}, u32[]{:S(2)}) collective-permute-start(bf16[4,64,640]{2,1,0:T(8,128)(2,1)} %fusion.52), channel_id=1, source_target_pairs={{0,1},{1,2},{2,3},{3,4},{4,5},{5,6},{6,7},{7,0},{8,9},{9,10},{10,1... | collective-permute-start | bytes 983048 | tf_op jit(solution)/shard_map/ppermute | solution.py:89
  469.2 7.7 %collective-permute-start.14 = (bf16[4,64,640]{2,1,0:T(8,128)(2,1)}, bf16[4,64,640]{2,1,0:T(8,128)(2,1)}, u32[]{:S(2)}, u32[]{:S(2)}) collective-permute-start(bf16[4,64,640]{2,1,0:T(8,128)(2,1)} %fusion.44), channel_id=1, source_target_pairs={{1,0},{2,1},{3,2},{4,3},{5,4},{6,5},{7,6},{0,7},{9,8},{10,9},{11,1... | collective-permute-start | bytes 983048 | tf_op jit(solution)/shard_map/ppermute | solution.py:89
  474.4 7.5 %collective-permute-start.4 = (bf16[4,64,640]{2,1,0:T(8,128)(2,1)}, bf16[4,64,640]{2,1,0:T(8,128)(2,1)}, u32[]{:S(2)}, u32[]{:S(2)}) collective-permute-start(bf16[4,64,640]{2,1,0:T(8,128)(2,1)} %fusion.51), channel_id=1, source_target_pairs={{0,1},{1,2},{2,3},{3,4},{4,5},{5,6},{6,7},{7,0},{8,9},{9,10},{10,1... | collective-permute-start | bytes 983048 | tf_op jit(solution)/shard_map/ppermute | solution.py:89
  478.8 7.5 %collective-permute-start.15 = (bf16[4,64,640]{2,1,0:T(8,128)(2,1)}, bf16[4,64,640]{2,1,0:T(8,128)(2,1)}, u32[]{:S(2)}, u32[]{:S(2)}) collective-permute-start(bf16[4,64,640]{2,1,0:T(8,128)(2,1)} %fusion.43), channel_id=1, source_target_pairs={{1,0},{2,1},{3,2},{4,3},{5,4},{6,5},{7,6},{0,7},{9,8},{10,9},{11,1... | collective-permute-start | bytes 983048 | tf_op jit(solution)/shard_map/ppermute | solution.py:89
  483.7 7.5 %collective-permute-start.5 = (bf16[4,64,640]{2,1,0:T(8,128)(2,1)}, bf16[4,64,640]{2,1,0:T(8,128)(2,1)}, u32[]{:S(2)}, u32[]{:S(2)}) collective-permute-start(bf16[4,64,640]{2,1,0:T(8,128)(2,1)} %fusion.50), channel_id=1, source_target_pairs={{0,1},{1,2},{2,3},{3,4},{4,5},{5,6},{6,7},{7,0},{8,9},{9,10},{10,1... | collective-permute-start | bytes 983048 | tf_op jit(solution)/shard_map/ppermute | solution.py:89
  488.1 7.5 %collective-permute-start.16 = (bf16[4,64,640]{2,1,0:T(8,128)(2,1)}, bf16[4,64,640]{2,1,0:T(8,128)(2,1)}, u32[]{:S(2)}, u32[]{:S(2)}) collective-permute-start(bf16[4,64,640]{2,1,0:T(8,128)(2,1)} %fusion.42), channel_id=1, source_target_pairs={{1,0},{2,1},{3,2},{4,3},{5,4},{6,5},{7,6},{0,7},{9,8},{10,9},{11,1... | collective-permute-start | bytes 983048 | tf_op jit(solution)/shard_map/ppermute | solution.py:89
  493.0 7.5 %collective-permute-start.6 = (bf16[4,64,640]{2,1,0:T(8,128)(2,1)}, bf16[4,64,640]{2,1,0:T(8,128)(2,1)}, u32[]{:S(2)}, u32[]{:S(2)}) collective-permute-start(bf16[4,64,640]{2,1,0:T(8,128)(2,1)} %fusion.49), channel_id=1, source_target_pairs={{0,1},{1,2},{2,3},{3,4},{4,5},{5,6},{6,7},{7,0},{8,9},{9,10},{10,1... | collective-permute-start | bytes 983048 | tf_op jit(solution)/shard_map/ppermute | solution.py:89
  497.4 7.5 %collective-permute-start.17 = (bf16[4,64,640]{2,1,0:T(8,128)(2,1)}, bf16[4,64,640]{2,1,0:T(8,128)(2,1)}, u32[]{:S(2)}, u32[]{:S(2)}) collective-permute-start(bf16[4,64,640]{2,1,0:T(8,128)(2,1)} %fusion.41), channel_id=1, source_target_pairs={{1,0},{2,1},{3,2},{4,3},{5,4},{6,5},{7,6},{0,7},{9,8},{10,9},{11,1... | collective-permute-start | bytes 983048 | tf_op jit(solution)/shard_map/ppermute | solution.py:89
  501.6 8.4 %collective-permute-start.7 = (bf16[4,64,640]{2,1,0:T(8,128)(2,1)S(1)}, bf16[4,64,640]{2,1,0:T(8,128)(2,1)S(1)}, u32[]{:S(2)}, u32[]{:S(2)}) collective-permute-start(bf16[4,64,640]{2,1,0:T(8,128)(2,1)S(1)} %fusion.48), channel_id=1, source_target_pairs={{0,1},{1,2},{2,3},{3,4},{4,5},{5,6},{6,7},{7,0},{8,9},{9,10},{10,1... | collective-permute-start | bytes 983048 | tf_op jit(solution)/shard_map/ppermute | solution.py:89
  506.1 5.2 collective-permute-start.18
  510.1 4.9 collective-permute-start.8
  511.3 3.9 collective-permute-start.19
  515.0 4.6 collective-permute-start.9
  515.2 4.5 collective-permute-start.20
  519.6 4.6 collective-permute-start.10
  524.2 4.6 collective-permute-start.21
  528.8 5.8 %collective-permute-start.22 = (bf16[64,1280]{1,0:T(8,128)(2,1)S(1)}, bf16[64,1280]{1,0:T(8,128)(2,1)S(1)}, u32[]{:S(2)}, u32[]{:S(2)}) collective-permute-start(bf16[64,1280]{1,0:T(8,128)(2,1)S(1)} %add_convert_fusion.1), channel_id=1, source_target_pairs={{0,128},{32,160},{64,192},{96,224},{128,0},{160,32},{192,64},{224,... | collective-permute-start | bytes 491528 | tf_op jit(solution)/shard_map/ppermute | solution.py:176
  534.7 21.6 %copy-start.5 = (bf16[32,128,64]{2,1,0:T(8,128)(2,1)S(1)}, bf16[32,128,64]{2,1,0:T(8,128)(2,1)}, u32[]{:S(2)}) copy-start(bf16[32,128,64]{2,1,0:T(8,128)(2,1)} %get-tuple-element.35) | copy-start | bytes 1572868
  534.7 22.9 %collective-permute-start.23 = (bf16[64,1280]{1,0:T(8,128)(2,1)S(1)}, bf16[64,1280]{1,0:T(8,128)(2,1)S(1)}, u32[]{:S(2)}, u32[]{:S(2)}) collective-permute-start(bf16[64,1280]{1,0:T(8,128)(2,1)S(1)} %add_convert_fusion), channel_id=1, source_target_pairs={{0,32},{32,0},{64,96},{96,64},{128,160},{160,128},{192,224},{224,1... | collective-permute-start | bytes 491528 | tf_op jit(solution)/shard_map/ppermute | solution.py:179
Sparse Core Ops, SparseCore 0:
  11.2 112.5 all-gather.1

commit v3 on v2

--- a/solution.py
+++ b/solution.py
@@ -3,6 +3,8 @@
 import jax
 import jax.numpy as jnp
 from jax import lax
+from jax.experimental import pallas as pl
+from jax.experimental.pallas import tpu as pltpu
 from jax.sharding import PartitionSpec as P
 
 HD = 64
@@ -12,54 +14,103 @@
 masked_score = -1e30
 query_group = 4
 RING_Z = 8
+
+
+def head_kernel(table_ref, count_ref, q_ref, g_ref, k_ref, v_ref,
+                out_ref, gq_ref, dk_ref, dv_ref):
+    b = pl.program_id(0)
+    slot_count = table_ref.shape[0] // pl.num_programs(0)
+    head_width = q_ref.shape[-1]
+    score_scale = head_width ** (-0.5)
+
+    @pl.when(b == 0)
+    def _():
+        dk_ref[...] = jnp.zeros_like(dk_ref)
+        dv_ref[...] = jnp.zeros_like(dv_ref)
+
+    q = q_ref[0]
+    g = g_ref[0]
+    used = 4 + count_ref[0]
+    chosen = [table_ref[b * slot_count + j] for j in range(slot_count)]
+    keys = [k_ref[c] for c in chosen]
+    vals = [v_ref[c] for c in chosen]
+    nt = (((1,), (1,)), ((), ()))
+    tn = (((0,), (0,)), ((), ()))
+    scores = []
+    for j in range(slot_count):
+        s = lax.dot_general(q, keys[j], nt, preferred_element_type=jnp.float32) * score_scale
+        if j >= 4:
+            s = jnp.where(j < used, s, masked_score)
+        scores.append(s)
+    highest = scores[0].max(axis=-1, keepdims=True)
+    for s in scores[1:]:
+        highest = jnp.maximum(highest, s.max(axis=-1, keepdims=True))
+    exps = [jnp.exp(s - highest) for s in scores]
+    denom = exps[0].sum(axis=-1, keepdims=True)
+    for e in exps[1:]:
+        denom = denom + e.sum(axis=-1, keepdims=True)
+    shares = [e / denom for e in exps]
+    shares_low = [p.astype(jnp.bfloat16) for p in shares]
+    attended = jnp.dot(shares_low[0], vals[0], preferred_element_type=jnp.float32)
+    for j in range(1, slot_count):
+        attended = attended + jnp.dot(shares_low[j], vals[j], preferred_element_type=jnp.float32)
+    out_ref[0] = attended.astype(out_ref.dtype)
+    grad_shares = [lax.dot_general(g, vals[j], nt, preferred_element_type=jnp.float32)
+                   for j in range(slot_count)]
+    weighted = (grad_shares[0] * shares[0]).sum(axis=-1, keepdims=True)
+    for j in range(1, slot_count):
+        weighted = weighted + (grad_shares[j] * shares[j]).sum(axis=-1, keepdims=True)
+    grad_scores = [(shares[j] * (grad_shares[j] - weighted)).astype(jnp.bfloat16)
+                   for j in range(slot_count)]
+    grad_query = jnp.dot(grad_scores[0], keys[0], preferred_element_type=jnp.float32)
+    for j in range(1, slot_count):
+        grad_query = grad_query + jnp.dot(grad_scores[j], keys[j], preferred_element_type=jnp.float32)
+    gq_ref[0] = (grad_query * score_scale).astype(gq_ref.dtype)
+    for j in range(slot_count):
+        dk = lax.dot_general(grad_scores[j], q, tn, preferred_element_type=jnp.float32) * score_scale
+        dv = lax.dot_general(shares_low[j], g, tn, preferred_element_type=jnp.float32)
+        dk_ref[chosen[j]] += dk
+        dv_ref[chosen[j]] += dv
 
 
 def head_pass(queries, key_rows, value_rows, grad_head, blocks, extra_count):
     seq_len, head_width = queries.shape
     block_count, slot_count = blocks.shape
     block_len = seq_len // block_count
-    score_scale = head_width ** (-0.5)
-    key_tiles = key_rows.reshape(block_count, block_len, head_width)
-    value_tiles = value_rows.reshape(block_count, block_len, head_width)
-    q_part = queries.reshape(block_count, block_len, head_width)
-    g_part = grad_head.reshape(block_count, block_len, head_width)
-    usable = jnp.repeat(jnp.arange(slot_count) < 4 + extra_count, block_len)
-    k_part = key_tiles[blocks].reshape(block_count, slot_count * block_len, head_width)
-    v_part = value_tiles[blocks].reshape(block_count, slot_count * block_len, head_width)
-    scores = (
-        jnp.einsum("gqe,gke->gqk", q_part, k_part, preferred_element_type=jnp.float32)
-        * score_scale
-    )
-    scores = jnp.where(usable, scores, masked_score)
-    highest = jnp.max(scores, axis=-1, keepdims=True)
-    exponent = jnp.exp(scores - highest)
-    shares = exponent / jnp.sum(exponent, axis=-1, keepdims=True)
-    shares_low = shares.astype(jnp.bfloat16)
-    attended = jnp.einsum(
-        "gqk,gke->gqe", shares_low, v_part, preferred_element_type=jnp.float32
-    ).astype(jnp.bfloat16)
-    grad_shares = jnp.einsum("gqe,gke->gqk", g_part, v_part, preferred_element_type=jnp.float32)
-    weighted = jnp.sum(grad_shares * shares, axis=-1, keepdims=True)
-    grad_scores = (shares * (grad_shares - weighted)).astype(jnp.bfloat16)
-    grad_query = (
-        jnp.einsum("gqk,gke->gqe", grad_scores, k_part, preferred_element_type=jnp.float32)
-        * score_scale
-    ).astype(jnp.bfloat16)
-    grad_keys = (
-        jnp.einsum("gqk,gqe->gke", grad_scores, q_part, preferred_element_type=jnp.float32)
-        * score_scale
-    )
-    grad_values = jnp.einsum(
-        "gqk,gqe->gke", shares_low, g_part, preferred_element_type=jnp.float32
-    )
-    pieces = jnp.concatenate([grad_keys, grad_values], axis=-1).reshape(
-        block_count * slot_count, block_len * 2 * head_width
-    )
-    owner = (
-        blocks.reshape(1, block_count * slot_count)
-        == jnp.arange(block_count, dtype=blocks.dtype)[:, None]
-    ).astype(jnp.float32)
-    summed = jnp.dot(owner, pieces, precision=lax.Precision.HIGHEST)
+    tiles = (block_count, block_len, head_width)
+    one_block = pl.BlockSpec((1, block_len, head_width), lambda b, t, c: (b, 0, 0))
+    whole = pl.BlockSpec(tiles, lambda b, t, c: (0, 0, 0))
+    grid_spec = pltpu.PrefetchScalarGridSpec(
+        num_scalar_prefetch=2,
+        grid=(block_count,),
+        in_specs=[one_block, one_block, whole, whole],
+        out_specs=[one_block, one_block, whole, whole],
+    )
+    flops = 2 * seq_len * slot_count * block_len * head_width * 6
+    attended, grad_query, grad_k, grad_v = pl.pallas_call(
+        head_kernel,
+        grid_spec=grid_spec,
+        out_shape=[
+            jax.ShapeDtypeStruct(tiles, jnp.bfloat16),
+            jax.ShapeDtypeStruct(tiles, jnp.bfloat16),
+            jax.ShapeDtypeStruct(tiles, jnp.float32),
+            jax.ShapeDtypeStruct(tiles, jnp.float32),
+        ],
+        compiler_params=pltpu.CompilerParams(dimension_semantics=("arbitrary",)),
+        cost_estimate=pl.CostEstimate(
+            flops=flops,
+            transcendentals=seq_len * slot_count * block_len,
+            bytes_accessed=seq_len * head_width * 2 * 6 + seq_len * head_width * 4 * 2,
+        ),
+    )(
+        blocks.reshape(-1),
+        jnp.reshape(extra_count, (1,)),
+        queries.reshape(tiles),
+        grad_head.reshape(tiles),
+        key_rows.reshape(tiles),
+        value_rows.reshape(tiles),
+    )
+    summed = jnp.concatenate([grad_k, grad_v], axis=-1)
     return (
         attended.reshape(seq_len, head_width),
         grad_query.reshape(seq_len, head_width),

time: 572 us -> 471 us (0.82)
  local copies, waits for them, and re-layouts: 99.6 us -> 23.9 us
  matrix products: 77.2 us -> 19.5 us
  Pallas kernels: 0 us -> 48.1 us
  other arithmetic: 55.6 us -> 37.9 us
    pallas_call x0 -> x1, Pallas kernels: none -> 48.1 us  [head_pass(): pl.pallas_call(head_kernel, grid_spec=grid_spec, out_shape=[jax.ShapeDtyp...]
    dot_general x6 -> x0, matrix products: 46.8 us -> none  [the longest x1 11 us: head_pass(): jnp.einsum('gqe,gke->gqk', g_part, v_part, preferred_element_type=jnp.flo...]
    reshape x6 -> x1, local copies, waits for them, and re-layouts: 34.9 us -> 0.67 us  [head_pass(): blocks.reshape(-1)]
    concatenate x2 -> x0, local copies, waits for them, and re-layouts: 18.7 us -> none  [the longest x1 16.1 us: head_pass(): jnp.concatenate([grad_keys, grad_values], axis=-1)]
    gather x4 -> x0, local copies, waits for them, and re-layouts: 18.3 us -> none  [the longest x2 9.22 us: head_pass(): value_tiles[blocks].reshape(block_count, slot_count * block_len, head_width)]
    convert_element_type x1 -> x0, other arithmetic: 10.8 us -> none  [head_pass(): grad_scores = (shares * (grad_shares - weighted)).astype(jnp.bfloat16)]
    sub x1 -> x0, matrix products: 10.8 us -> none  [head_pass(): exponent = jnp.exp(scores - highest)]
    concatenate x1 -> x0, other arithmetic: 10.5 us -> none  [head_pass(): jnp.concatenate([grad_keys, grad_values], axis=-1)]
  transfers between devices with their start and end apart: 27 -> 27, of which waited for: 18 -> 17; matrix products, arithmetic and copies ran while one was open for 6% -> 8% of each run, Pallas kernels for 0% -> 0%
where the time goes in v3:
time: 471 us; the launch traced here: 463 us
  waiting for transfers between devices  258 us (55%)
  starting transfers between devices  60.1 us (13%)
  Pallas kernels  48.1 us (10%)
  other arithmetic  37.9 us (8%)
  local copies, waits for them, and re-layouts  23.9 us (5%)
  matrix products  19.5 us (4%)
  between operations  14.9 us (3%)
    all_gather x1, waiting for transfers between devices, per_device(): w_full = lax.all_gather(w_local, 'seq', axis=0, tiled=True)  113 us
    all_to_all x1, waiting for transfers between devices, per_device(): lax.all_to_all(back_sent, 'seq', split_axis=0, concat_axis=0, tiled=True)  48.6 us
    pallas_call x1, Pallas kernels, head_pass(): pl.pallas_call(head_kernel, grid_spec=grid_spec, out_shape=[jax.ShapeDtyp...  48.1 us
    all_to_all x1, waiting for transfers between devices, per_device(): lax.all_to_all(sent, 'seq', split_axis=0, concat_axis=1, tiled=True)[0]  46.5 us
    ppermute x20, waiting for transfers between devices, ring_reduce_scatter(): got = lax.ppermute(buf, 'seq', perm)  35.5 us
    ppermute x20, starting transfers between devices, ring_reduce_scatter(): got = lax.ppermute(buf, 'seq', perm)  27.5 us
    convert_element_type x20, other arithmetic, ring_reduce_scatter(): (got.astype(jnp.float32) + chunk(k + 1).astype(jnp.float32)).astype(jnp.b...  22.6 us
    ppermute x1, starting transfers between devices, per_device(): other_half = lax.ppermute(part, 'dp', pairs)  13 us
  transfers between devices with their start and end apart: 27, of which 17 were waited for; matrix products, arithmetic and copies ran while one was open for 8% of the time, Pallas kernels for 0%

profile of v3, /device:TPU:1, one launch (start us, length us, event | category | flops | bytes accessed | tf_op | source)
XLA Modules:
  0.0 462.7 jit_solution(12192594052468727858)
XLA Ops:
  7.2 1.8 pad_maximum_fusion.3
  9.0 1.3 copy.26
  10.9 112.9 %all-gather.2.cloned.1.call-done = bf16[2048,2560]{1,0:T(8,128)(2,1)} async-done(((bf16[64,2560]{1,0:T(8,128)(2,1)}), bf16[2048,2560]{1,0:T(8,128)(2,1)}) %all-gather.2.cloned.1.call-update) | async-done | bytes 10485776 | tf_op jit(solution)/shard_map/all_gather | solution.py:160
  123.7 6.9 %fusion.1 = bf16[128,2560]{0,1:T(8,128)(2,1)S(1)} fusion(bf16[2048,2560]{1,0:T(8,128)(2,1)} %all-gather.2.cloned.1.call-done, bf16[1,128,2048]{2,1,0:T(8,128)(2,1)S(1)} %copy-done), kind=kOutput, calls=%fused_computation.6 | convolution fusion | flops 1342504960 | bytes 11665408 | tf_op jit(solution)/shard_map/dot_general | solution.py:161
  131.6 2.4 pad_maximum_fusion
  134.0 5.4 %all-to-all-start = ((bf16[32,128,256]{2,1,0:T(8,128)(2,1)}), bf16[32,128,256]{2,1,0:T(8,128)(2,1)S(1)}, u32[]{:S(2)}, u32[]{:S(2)}) async-start(bf16[32,128,256]{2,1,0:T(8,128)(2,1)} %pad_maximum_fusion), calls=%async_computation | async-start | bytes 4194304 | tf_op jit(solution)/shard_map/all_to_all | solution.py:173
  141.5 46.5 %all-to-all-done = bf16[32,128,256]{2,1,0:T(8,128)(2,1)S(1)} async-done(((bf16[32,128,256]{2,1,0:T(8,128)(2,1)}), bf16[32,128,256]{2,1,0:T(8,128)(2,1)S(1)}, u32[]{:S(2)}, u32[]{:S(2)}) %all-to-all-start) | async-done | bytes 2097184 | tf_op jit(solution)/shard_map/all_to_all | solution.py:173
  188.0 2.7 fusion.28
  190.8 48.1 %shard_map.110 = (bf16[32,128,64]{2,1,0:T(8,128)(2,1)}, bf16[32,128,64]{2,1,0:T(8,128)(2,1)}, f32[32,128,64]{2,1,0:T(8,128)}, f32[32,128,64]{2,1,0:T(8,128)}) custom-call(s32[224]{0:T(256)} %reshape.100.table_ref, s32[1]{0:T(128)} %dynamic_slice.89.count_ref, bf16[32,128,64]{2,1,0:T(8,128)(2,1)} %bitcast.131, bf16[32,128,64]{2,1,0:T(8,128)(2,1)} %bitcast.130, ...), custom_call_target="tpu_custom_call" | custom-call | flops 2818572288 | bytes 5242880 | tf_op jit(solution)/shard_map/pallas_call | solution.py:90
  238.9 1.9 convert.29
  241.7 2.7 pad_maximum_fusion.1
  244.4 7.3 %all-to-all-start.1 = ((bf16[32,128,256]{2,1,0:T(8,128)(2,1)}), bf16[32,128,256]{2,1,0:T(8,128)(2,1)S(1)}, u32[]{:S(2)}, u32[]{:S(2)}) async-start(bf16[32,128,256]{2,1,0:T(8,128)(2,1)} %pad_maximum_fusion.1), calls=%async_computation.1 | async-start | bytes 4194304 | tf_op jit(solution)/shard_map/all_to_all | solution.py:191
  251.7 48.6 %all-to-all-done.1 = bf16[32,128,256]{2,1,0:T(8,128)(2,1)S(1)} async-done(((bf16[32,128,256]{2,1,0:T(8,128)(2,1)}), bf16[32,128,256]{2,1,0:T(8,128)(2,1)S(1)}, u32[]{:S(2)}, u32[]{:S(2)}) %all-to-all-start.1) | async-done | bytes 2097184 | tf_op jit(solution)/shard_map/all_to_all | solution.py:191
  300.9 1.9 slice_bitcast_fusion
  302.7 1.6 copy.31
  304.3 4.2 multiply_convert_fusion
  308.6 3.0 dynamic-slice_bitcast_fusion
  311.6 2.5 copy-done.2
  314.1 2.4 collective-permute-start
  316.5 8.6 %collective-permute-done = bf16[2048,1280]{1,0:T(8,128)(2,1)} collective-permute-done((bf16[2048,1280]{1,0:T(8,128)(2,1)}, bf16[2048,1280]{1,0:T(8,128)(2,1)}, u32[]{:S(2)}, u32[]{:S(2)}) %collective-permute-start) | collective-permute-done | bytes 5242912 | tf_op jit(solution)/shard_map/ppermute | solution.py:218
  325.2 5.4 %fusion = bf16[2048,1280]{1,0:T(8,128)(2,1)S(1)} fusion(bf16[2048,1280]{1,0:T(8,128)(2,1)} %collective-permute-done, bf16[2560,2048]{0,1:T(8,128)(2,1)} %copy-done.2, s32[]{:T(128)S(6)} %select_n.217), kind=kLoop, calls=%fused_computation.2 | loop fusion | flops 10485760 | bytes 15728644 | tf_op jit(solution)/shard_map/convert_element_type | solution.py:219
  331.7 1.6 copy-done.3
  335.3 1.0 collective-permute-start.1
  336.3 7.0 %collective-permute-done.11 = bf16[4,64,640]{2,1,0:T(8,128)(2,1)} collective-permute-done((bf16[4,64,640]{2,1,0:T(8,128)(2,1)}, bf16[4,64,640]{2,1,0:T(8,128)(2,1)}, u32[]{:S(2)}, u32[]{:S(2)}) %collective-permute-start.11) | collective-permute-done | bytes 327712 | tf_op jit(solution)/shard_map/ppermute | solution.py:140
  343.3 1.9 fusion.9
  345.2 1.7 collective-permute-start.12
  346.9 1.8 fusion.16
  348.6 4.9 %collective-permute-done.12 = bf16[4,64,640]{2,1,0:T(8,128)(2,1)} collective-permute-done((bf16[4,64,640]{2,1,0:T(8,128)(2,1)}, bf16[4,64,640]{2,1,0:T(8,128)(2,1)}, u32[]{:S(2)}, u32[]{:S(2)}) %collective-permute-start.12) | collective-permute-done | bytes 327712 | tf_op jit(solution)/shard_map/ppermute | solution.py:140
  353.5 1.9 fusion.8
  355.4 2.9 collective-permute-start.13
  358.3 1.8 fusion.15
  360.0 3.4 collective-permute-done.13
  363.5 1.9 fusion.7
  365.3 3.6 collective-permute-start.14
  368.9 1.8 fusion.14
  370.7 2.6 collective-permute-done.14
  373.3 1.9 fusion.6
  375.1 3.1 collective-permute-start.15
  378.3 1.8 fusion.13
  380.0 2.6 collective-permute-done.15
  382.6 1.9 fusion.5
  384.5 3.1 collective-permute-start.16
  387.6 1.8 fusion.12
  389.4 2.6 collective-permute-done.16
  391.9 1.9 fusion.4
  393.8 3.1 collective-permute-start.17
  396.9 1.1 fusion.11
  398.1 3.2 collective-permute-done.17
  401.3 1.2 fusion.3
  402.4 2.4 collective-permute-start.18
  404.8 1.5 collective-permute-done.7
  406.4 1.2 collective-permute-start.8
  407.6 1.8 collective-permute-start.19
  409.5 1.9 collective-permute-done.8
  411.5 2.9 collective-permute-start.20
  414.4 1.6 collective-permute-done.9
  416.1 4.4 collective-permute-done.10
  420.6 1.3 collective-permute-start.21
  421.9 3.3 collective-permute-done.21
  425.2 3.0 collective-permute-start.22
  428.2 3.0 collective-permute-done.22
  431.3 13.0 %collective-permute-start.23 = (bf16[64,1280]{1,0:T(8,128)(2,1)S(1)}, bf16[64,1280]{1,0:T(8,128)(2,1)S(1)}, u32[]{:S(2)}, u32[]{:S(2)}) collective-permute-start(bf16[64,1280]{1,0:T(8,128)(2,1)S(1)} %add_convert_fusion), channel_id=1, source_target_pairs={{0,32},{32,0},{64,96},{96,64},{128,160},{160,128},{192,224},{224,1... | collective-permute-start | bytes 491528 | tf_op jit(solution)/shard_map/ppermute | solution.py:230
  444.3 8.4 %fusion.2 = bf16[1,128,2048]{2,1,0:T(8,128)(2,1)} fusion(bf16[2048,2560]{1,0:T(8,128)(2,1)} %all-gather.2.cloned.1.call-done, bf16[128,256]{0,1:T(8,128)(2,1)S(1)} %bitcast.133, bf16[128,256]{0,1:T(8,128)(2,1)S(1)} %bitcast.135, bf16[128,2048]{0,1:T(8,128)(2,1)S(1)} %bitcast.123), kind=kOutput, calls=%fused_computation.8 | convolution fusion | flops 1344405504 | bytes 11665408 | tf_op jit(solution)/shard_map/dot_general | solution.py:204
  453.0 1.0 copy.35
  (73 shorter events, 10.5 us)
Async XLA Ops:
  7.2 116.6 %copy-start = (bf16[1,128,2048]{2,1,0:T(8,128)(2,1)S(1)}, bf16[1,128,2048]{2,1,0:T(8,128)(2,1)}, u32[]{:S(2)}) copy-start(bf16[1,128,2048]{2,1,0:T(8,128)(2,1)} %param.7) | copy-start | bytes 1572868
  7.2 116.6 %all-gather.2.cloned.1.call-start = ((), (), s32[]{:S(2)}) async-start(), calls=%async_computation.2 | async-start | bytes 10813440 | tf_op jit(solution)/shard_map/all_gather | solution.py:160
  134.0 7.0 %copy-start.8 = (s32[32]{0:T(128)S(1)}, s32[32]{0:T(128)}, u32[]{:S(2)}) copy-start(s32[32]{0:T(128)} %param.12) | copy-start | bytes 388
  134.0 54.1 %all-to-all-start = ((bf16[32,128,256]{2,1,0:T(8,128)(2,1)}), bf16[32,128,256]{2,1,0:T(8,128)(2,1)S(1)}, u32[]{:S(2)}, u32[]{:S(2)}) async-start(bf16[32,128,256]{2,1,0:T(8,128)(2,1)} %pad_maximum_fusion), calls=%async_computation | async-start | bytes 4194304 | tf_op jit(solution)/shard_map/all_to_all | solution.py:173
  238.9 2.2 copy-start.5
  238.9 2.5 copy-start.6
  238.9 2.8 copy-start.7
  244.4 56.0 %all-to-all-start.1 = ((bf16[32,128,256]{2,1,0:T(8,128)(2,1)}), bf16[32,128,256]{2,1,0:T(8,128)(2,1)S(1)}, u32[]{:S(2)}, u32[]{:S(2)}) async-start(bf16[32,128,256]{2,1,0:T(8,128)(2,1)} %pad_maximum_fusion.1), calls=%async_computation.1 | async-start | bytes 4194304 | tf_op jit(solution)/shard_map/all_to_all | solution.py:191
  308.6 5.5 %copy-start.2 = (bf16[2560,2048]{0,1:T(8,128)(2,1)}, bf16[2560,2048]{0,1:T(8,128)(2,1)S(1)}, u32[]{:S(2)}) copy-start(bf16[2560,2048]{0,1:T(8,128)(2,1)S(1)} %multiply_convert_fusion) | copy-start | bytes 31457284
  314.1 11.1 %collective-permute-start = (bf16[2048,1280]{1,0:T(8,128)(2,1)}, bf16[2048,1280]{1,0:T(8,128)(2,1)}, u32[]{:S(2)}, u32[]{:S(2)}) collective-permute-start(bf16[2048,1280]{1,0:T(8,128)(2,1)} %dynamic-slice_bitcast_fusion), channel_id=1, source_target_pairs={{0,32},{32,0},{64,96},{96,64},{128,160},{160,128},{192,224},{224,1... | collective-permute-start | bytes 15728648 | tf_op jit(solution)/shard_map/ppermute | solution.py:218
  331.7 1.6 copy-start.3
  334.1 9.2 %collective-permute-start.11 = (bf16[4,64,640]{2,1,0:T(8,128)(2,1)}, bf16[4,64,640]{2,1,0:T(8,128)(2,1)}, u32[]{:S(2)}, u32[]{:S(2)}) collective-permute-start(bf16[4,64,640]{2,1,0:T(8,128)(2,1)} %dynamic-slice_bitcast_fusion.1), channel_id=1, source_target_pairs={{1,0},{2,1},{3,2},{4,3},{5,4},{6,5},{7,6},{0,7},{9,8},{10,9},{11,1... | collective-permute-start | bytes 983048 | tf_op jit(solution)/shard_map/ppermute | solution.py:140
  335.3 11.6 %collective-permute-start.1 = (bf16[4,64,640]{2,1,0:T(8,128)(2,1)}, bf16[4,64,640]{2,1,0:T(8,128)(2,1)}, u32[]{:S(2)}, u32[]{:S(2)}) collective-permute-start(bf16[4,64,640]{2,1,0:T(8,128)(2,1)} %dynamic-slice_bitcast_fusion.2), channel_id=1, source_target_pairs={{0,1},{1,2},{2,3},{3,4},{4,5},{5,6},{6,7},{7,0},{8,9},{9,10},{10,1... | collective-permute-start | bytes 983048 | tf_op jit(solution)/shard_map/ppermute | solution.py:140
  345.2 8.3 %collective-permute-start.12 = (bf16[4,64,640]{2,1,0:T(8,128)(2,1)}, bf16[4,64,640]{2,1,0:T(8,128)(2,1)}, u32[]{:S(2)}, u32[]{:S(2)}) collective-permute-start(bf16[4,64,640]{2,1,0:T(8,128)(2,1)} %fusion.9), channel_id=1, source_target_pairs={{1,0},{2,1},{3,2},{4,3},{5,4},{6,5},{7,6},{0,7},{9,8},{10,9},{11,1... | collective-permute-start | bytes 983048 | tf_op jit(solution)/shard_map/ppermute | solution.py:140
  348.6 9.6 %collective-permute-start.2 = (bf16[4,64,640]{2,1,0:T(8,128)(2,1)}, bf16[4,64,640]{2,1,0:T(8,128)(2,1)}, u32[]{:S(2)}, u32[]{:S(2)}) collective-permute-start(bf16[4,64,640]{2,1,0:T(8,128)(2,1)} %fusion.16), channel_id=1, source_target_pairs={{0,1},{1,2},{2,3},{3,4},{4,5},{5,6},{6,7},{7,0},{8,9},{9,10},{10,1... | collective-permute-start | bytes 983048 | tf_op jit(solution)/shard_map/ppermute | solution.py:140
  355.4 8.1 %collective-permute-start.13 = (bf16[4,64,640]{2,1,0:T(8,128)(2,1)}, bf16[4,64,640]{2,1,0:T(8,128)(2,1)}, u32[]{:S(2)}, u32[]{:S(2)}) collective-permute-start(bf16[4,64,640]{2,1,0:T(8,128)(2,1)} %fusion.8), channel_id=1, source_target_pairs={{1,0},{2,1},{3,2},{4,3},{5,4},{6,5},{7,6},{0,7},{9,8},{10,9},{11,1... | collective-permute-start | bytes 983048 | tf_op jit(solution)/shard_map/ppermute | solution.py:140
  360.0 8.9 %collective-permute-start.3 = (bf16[4,64,640]{2,1,0:T(8,128)(2,1)}, bf16[4,64,640]{2,1,0:T(8,128)(2,1)}, u32[]{:S(2)}, u32[]{:S(2)}) collective-permute-start(bf16[4,64,640]{2,1,0:T(8,128)(2,1)} %fusion.15), channel_id=1, source_target_pairs={{0,1},{1,2},{2,3},{3,4},{4,5},{5,6},{6,7},{7,0},{8,9},{9,10},{10,1... | collective-permute-start | bytes 983048 | tf_op jit(solution)/shard_map/ppermute | solution.py:140
  365.3 7.9 %collective-permute-start.14 = (bf16[4,64,640]{2,1,0:T(8,128)(2,1)}, bf16[4,64,640]{2,1,0:T(8,128)(2,1)}, u32[]{:S(2)}, u32[]{:S(2)}) collective-permute-start(bf16[4,64,640]{2,1,0:T(8,128)(2,1)} %fusion.7), channel_id=1, source_target_pairs={{1,0},{2,1},{3,2},{4,3},{5,4},{6,5},{7,6},{0,7},{9,8},{10,9},{11,1... | collective-permute-start | bytes 983048 | tf_op jit(solution)/shard_map/ppermute | solution.py:140
  370.7 7.5 %collective-permute-start.4 = (bf16[4,64,640]{2,1,0:T(8,128)(2,1)}, bf16[4,64,640]{2,1,0:T(8,128)(2,1)}, u32[]{:S(2)}, u32[]{:S(2)}) collective-permute-start(bf16[4,64,640]{2,1,0:T(8,128)(2,1)} %fusion.14), channel_id=1, source_target_pairs={{0,1},{1,2},{2,3},{3,4},{4,5},{5,6},{6,7},{7,0},{8,9},{9,10},{10,1... | collective-permute-start | bytes 983048 | tf_op jit(solution)/shard_map/ppermute | solution.py:140
  375.1 7.5 %collective-permute-start.15 = (bf16[4,64,640]{2,1,0:T(8,128)(2,1)}, bf16[4,64,640]{2,1,0:T(8,128)(2,1)}, u32[]{:S(2)}, u32[]{:S(2)}) collective-permute-start(bf16[4,64,640]{2,1,0:T(8,128)(2,1)} %fusion.6), channel_id=1, source_target_pairs={{1,0},{2,1},{3,2},{4,3},{5,4},{6,5},{7,6},{0,7},{9,8},{10,9},{11,1... | collective-permute-start | bytes 983048 | tf_op jit(solution)/shard_map/ppermute | solution.py:140
  380.0 7.5 %collective-permute-start.5 = (bf16[4,64,640]{2,1,0:T(8,128)(2,1)}, bf16[4,64,640]{2,1,0:T(8,128)(2,1)}, u32[]{:S(2)}, u32[]{:S(2)}) collective-permute-start(bf16[4,64,640]{2,1,0:T(8,128)(2,1)} %fusion.13), channel_id=1, source_target_pairs={{0,1},{1,2},{2,3},{3,4},{4,5},{5,6},{6,7},{7,0},{8,9},{9,10},{10,1... | collective-permute-start | bytes 983048 | tf_op jit(solution)/shard_map/ppermute | solution.py:140
  384.5 7.5 %collective-permute-start.16 = (bf16[4,64,640]{2,1,0:T(8,128)(2,1)}, bf16[4,64,640]{2,1,0:T(8,128)(2,1)}, u32[]{:S(2)}, u32[]{:S(2)}) collective-permute-start(bf16[4,64,640]{2,1,0:T(8,128)(2,1)} %fusion.5), channel_id=1, source_target_pairs={{1,0},{2,1},{3,2},{4,3},{5,4},{6,5},{7,6},{0,7},{9,8},{10,9},{11,1... | collective-permute-start | bytes 983048 | tf_op jit(solution)/shard_map/ppermute | solution.py:140
  389.4 7.5 %collective-permute-start.6 = (bf16[4,64,640]{2,1,0:T(8,128)(2,1)}, bf16[4,64,640]{2,1,0:T(8,128)(2,1)}, u32[]{:S(2)}, u32[]{:S(2)}) collective-permute-start(bf16[4,64,640]{2,1,0:T(8,128)(2,1)} %fusion.12), channel_id=1, source_target_pairs={{0,1},{1,2},{2,3},{3,4},{4,5},{5,6},{6,7},{7,0},{8,9},{9,10},{10,1... | collective-permute-start | bytes 983048 | tf_op jit(solution)/shard_map/ppermute | solution.py:140
  393.8 7.5 %collective-permute-start.17 = (bf16[4,64,640]{2,1,0:T(8,128)(2,1)}, bf16[4,64,640]{2,1,0:T(8,128)(2,1)}, u32[]{:S(2)}, u32[]{:S(2)}) collective-permute-start(bf16[4,64,640]{2,1,0:T(8,128)(2,1)} %fusion.4), channel_id=1, source_target_pairs={{1,0},{2,1},{3,2},{4,3},{5,4},{6,5},{7,6},{0,7},{9,8},{10,9},{11,1... | collective-permute-start | bytes 983048 | tf_op jit(solution)/shard_map/ppermute | solution.py:140
  398.0 8.3 %collective-permute-start.7 = (bf16[4,64,640]{2,1,0:T(8,128)(2,1)S(1)}, bf16[4,64,640]{2,1,0:T(8,128)(2,1)S(1)}, u32[]{:S(2)}, u32[]{:S(2)}) collective-permute-start(bf16[4,64,640]{2,1,0:T(8,128)(2,1)S(1)} %fusion.11), channel_id=1, source_target_pairs={{0,1},{1,2},{2,3},{3,4},{4,5},{5,6},{6,7},{7,0},{8,9},{9,10},{10,1... | collective-permute-start | bytes 983048 | tf_op jit(solution)/shard_map/ppermute | solution.py:140
  402.4 5.2 %collective-permute-start.18 = (bf16[64,640]{1,0:T(8,128)(2,1)S(1)}, bf16[64,640]{1,0:T(8,128)(2,1)S(1)}, u32[]{:S(2)}, u32[]{:S(2)}) collective-permute-start(bf16[64,640]{1,0:T(8,128)(2,1)S(1)} %dynamic-slice_bitcast_fusion.3), channel_id=1, source_target_pairs={{8,0},{9,1},{10,2},{11,3},{12,4},{13,5},{14,6},{15,7},{16,8},{17,9... | collective-permute-start | bytes 245768 | tf_op jit(solution)/shard_map/ppermute | solution.py:140
  406.4 4.9 %collective-permute-start.8 = (bf16[64,640]{1,0:T(8,128)(2,1)S(1)}, bf16[64,640]{1,0:T(8,128)(2,1)S(1)}, u32[]{:S(2)}, u32[]{:S(2)}) collective-permute-start(bf16[64,640]{1,0:T(8,128)(2,1)S(1)} %dynamic-slice_bitcast_fusion.4), channel_id=1, source_target_pairs={{0,8},{1,9},{2,10},{3,11},{4,12},{5,13},{6,14},{7,15},{8,16},{9,17... | collective-permute-start | bytes 245768 | tf_op jit(solution)/shard_map/ppermute | solution.py:140
  407.6 3.8 collective-permute-start.19
  411.3 4.6 collective-permute-start.9
  411.5 4.6 collective-permute-start.20
  416.0 4.6 collective-permute-start.10
  420.6 4.6 collective-permute-start.21
  425.2 6.0 %collective-permute-start.22 = (bf16[64,1280]{1,0:T(8,128)(2,1)S(1)}, bf16[64,1280]{1,0:T(8,128)(2,1)S(1)}, u32[]{:S(2)}, u32[]{:S(2)}) collective-permute-start(bf16[64,1280]{1,0:T(8,128)(2,1)S(1)} %add_convert_fusion.1), channel_id=1, source_target_pairs={{0,128},{32,160},{64,192},{96,224},{128,0},{160,32},{192,64},{224,... | collective-permute-start | bytes 491528 | tf_op jit(solution)/shard_map/ppermute | solution.py:227
  431.2 21.4 %copy-start.4 = (bf16[128,32,64]{2,0,1:T(8,128)(2,1)S(1)}, bf16[128,32,64]{2,0,1:T(8,128)(2,1)}, u32[]{:S(2)}) copy-start(bf16[128,32,64]{2,0,1:T(8,128)(2,1)} %get-tuple-element.26) | copy-start | bytes 1572868
  431.3 22.8 %collective-permute-start.23 = (bf16[64,1280]{1,0:T(8,128)(2,1)S(1)}, bf16[64,1280]{1,0:T(8,128)(2,1)S(1)}, u32[]{:S(2)}, u32[]{:S(2)}) collective-permute-start(bf16[64,1280]{1,0:T(8,128)(2,1)S(1)} %add_convert_fusion), channel_id=1, source_target_pairs={{0,32},{32,0},{64,96},{96,64},{128,160},{160,128},{192,224},{224,1... | collective-permute-start | bytes 491528 | tf_op jit(solution)/shard_map/ppermute | solution.py:230
  444.3 11.1 %copy-start.1 = (bf16[1,128,2048]{2,1,0:T(8,128)(2,1)S(1)}, bf16[1,128,2048]{2,1,0:T(8,128)(2,1)}, u32[]{:S(2)}) copy-start(bf16[1,128,2048]{2,1,0:T(8,128)(2,1)} %param.7) | copy-start | bytes 1572868
Sparse Core Ops, SparseCore 0:
  11.2 112.5 all-gather.1

commit v4 on v3

--- a/solution.py
+++ b/solution.py
@@ -157,24 +157,35 @@
     kv_cols = kv_heads * HD
     all_cols = query_cols + 2 * kv_cols
     w_local = jnp.concatenate([w_query, w_key, w_value], axis=1)
-    w_full = lax.all_gather(w_local, "seq", axis=0, tiled=True)
-    projected = jnp.dot(tokens, w_full, preferred_element_type=jnp.float32).astype(jnp.bfloat16)
+    half = all_cols // 2
+    core = dp_index % 2
+    pairs = [(i, i ^ 1) for i in range(dp_devices)]
+    grad_pieces = grad_rows.reshape(tok_count, heads, HD).transpose(1, 0, 2)
+    head_grad = lax.all_to_all(grad_pieces, "seq", split_axis=0, concat_axis=1, tiled=True)[0]
+    w_mine = lax.all_gather(
+        lax.dynamic_slice_in_dim(w_local, core * half, half, axis=1), "seq", axis=0, tiled=True
+    )
+    w_other = lax.ppermute(w_mine, "dp", pairs)
+    proj_mine = jnp.dot(tokens, w_mine, preferred_element_type=jnp.float32).astype(jnp.bfloat16)
+    proj_other = jnp.dot(tokens, w_other, preferred_element_type=jnp.float32).astype(jnp.bfloat16)
+    projected = jnp.concatenate(
+        [jnp.where(core == 0, proj_mine, proj_other), jnp.where(core == 0, proj_other, proj_mine)],
+        axis=1,
+    )
     queries = projected[:, :query_cols]
     key_proj = projected[:, query_cols : query_cols + kv_cols]
     value_proj = projected[:, query_cols + kv_cols :]
     query_pieces = queries.reshape(tok_count, heads, HD).transpose(1, 0, 2)
-    grad_pieces = grad_rows.reshape(tok_count, heads, HD).transpose(1, 0, 2)
     paired = jnp.concatenate(
         [key_proj.reshape(tok_count, kv_heads, HD), value_proj.reshape(tok_count, kv_heads, HD)],
         axis=2,
     )
     kv_pieces = jnp.repeat(paired.transpose(1, 0, 2), GROUP, axis=0)
-    sent = jnp.concatenate([query_pieces, grad_pieces, kv_pieces], axis=2)
+    sent = jnp.concatenate([query_pieces, kv_pieces], axis=2)
     landed = lax.all_to_all(sent, "seq", split_axis=0, concat_axis=1, tiled=True)[0]
     head_q = landed[:, :HD]
-    head_grad = landed[:, HD : 2 * HD]
-    head_k = landed[:, 2 * HD : 3 * HD]
-    head_v = landed[:, 3 * HD :]
+    head_k = landed[:, HD : 2 * HD]
+    head_v = landed[:, 2 * HD :]
     blocks_mine = lax.dynamic_index_in_dim(key_blocks, position, 0, keepdims=False)
     count_mine = lax.dynamic_index_in_dim(random_count, position, 0, keepdims=False)
     attended, grad_query, grad_kv = head_pass(
@@ -201,21 +212,22 @@
     grad_v_rows = kv_sum[:, :, HD:].transpose(1, 0, 2).reshape(tok_count, kv_heads * HD)
     combined = jnp.concatenate([grad_q_rows, grad_k_rows, grad_v_rows], axis=1)
     contract = (((1,), (1,)), ((), ()))
-    grad_x_rows = lax.dot_general(
-        combined, w_full, contract, preferred_element_type=jnp.float32
+    comb_mine = lax.dynamic_slice_in_dim(combined, core * half, half, axis=1)
+    comb_other = lax.dynamic_slice_in_dim(combined, (1 - core) * half, half, axis=1)
+    grad_x_rows = (
+        lax.dot_general(comb_mine, w_mine, contract, preferred_element_type=jnp.float32)
+        + lax.dot_general(comb_other, w_other, contract, preferred_element_type=jnp.float32)
     ).astype(jnp.bfloat16)
     factor = 1.0 / math.sqrt(tok_count * seq_devices * dp_devices)
     over_tokens = (((0,), (0,)), ((), ()))
-    term = (
-        lax.dot_general(tokens, combined, over_tokens, preferred_element_type=jnp.float32)
-        * factor
-    ).astype(jnp.bfloat16)
-    half = all_cols // 2
-    core = dp_index % 2
-    pairs = [(i, i ^ 1) for i in range(dp_devices)]
-    keep = lax.dynamic_slice_in_dim(term, core * half, half, axis=1)
-    give = lax.dynamic_slice_in_dim(term, (1 - core) * half, half, axis=1)
-    got = lax.ppermute(give, "dp", pairs)
+    def term_of(columns):
+        return (
+            lax.dot_general(tokens, columns, over_tokens, preferred_element_type=jnp.float32)
+            * factor
+        ).astype(jnp.bfloat16)
+
+    got = lax.ppermute(term_of(comb_other), "dp", pairs)
+    keep = term_of(comb_mine)
     chip_sum = (keep.astype(jnp.float32) + got.astype(jnp.float32)).astype(jnp.bfloat16)
     rows = chip_sum.shape[0] // seq_devices
     by_z = chip_sum.reshape(seq_devices // RING_Z, RING_Z, rows, half).transpose(1, 0, 2, 3)

time: 471 us -> 456 us (0.968)
  waiting for transfers between devices: 258 us -> 223 us
  starting transfers between devices: 60.1 us -> 70.1 us
  matrix products: 19.5 us -> 27.7 us
  local copies, waits for them, and re-layouts: 23.9 us -> 30.8 us
  other arithmetic: 37.9 us -> 32.4 us
    all_gather x1, waiting for transfers between devices: 113 us -> 88.8 us  [per_device(): lax.all_gather(lax.dynamic_slice_in_dim(w_local, core * half, half, axis=...]
    all_to_all x1, waiting for transfers between devices: 46.5 us -> 33.1 us  [per_device(): lax.all_to_all(sent, 'seq', split_axis=0, concat_axis=1, tiled=True)[0]]
    dot_general x3 -> x6, matrix products: 19.5 us -> 27.7 us  [the longest x2 10.1 us: term_of(): lax.dot_general(tokens, columns, over_tokens, preferred_element_type=jnp....]
    convert_element_type x0 -> x1, local copies, waits for them, and re-layouts: none -> 7.93 us  [per_device(): (keep.astype(jnp.float32) + got.astype(jnp.float32)).astype(jnp.bfloat16)]
    convert_element_type x1 -> x0, other arithmetic: 5.37 us -> none  [per_device(): (keep.astype(jnp.float32) + got.astype(jnp.float32)).astype(jnp.bfloat16)]
    all_to_all x0 -> x1, starting transfers between devices: none -> 5.32 us  [per_device(): lax.all_to_all(grad_pieces, 'seq', split_axis=0, concat_axis=1, tiled=True)]
    all_to_all x0 -> x1, waiting for transfers between devices: none -> 5.06 us  [per_device(): lax.all_to_all(grad_pieces, 'seq', split_axis=0, concat_axis=1, tiled=True)]
  transfers between devices with their start and end apart: 27 -> 29, of which waited for: 17 -> 18; matrix products, arithmetic and copies ran while one was open for 8% -> 11% of each run, Pallas kernels for 0% -> 0%
where the time goes in v4:
time: 456 us; the launch traced here: 447 us
  waiting for transfers between devices  223 us (49%)
  starting transfers between devices  70.1 us (15%)
  Pallas kernels  48.2 us (11%)
  other arithmetic  32.4 us (7%)
  local copies, waits for them, and re-layouts  30.8 us (7%)
  matrix products  27.7 us (6%)
  between operations  14.9 us (3%)
    all_gather x1, waiting for transfers between devices, per_device(): lax.all_gather(lax.dynamic_slice_in_dim(w_local, core * half, half, axis=...  88.8 us
    all_to_all x1, waiting for transfers between devices, per_device(): lax.all_to_all(back_sent, 'seq', split_axis=0, concat_axis=0, tiled=True)  48.7 us
    pallas_call x1, Pallas kernels, head_pass(): pl.pallas_call(head_kernel, grid_spec=grid_spec, out_shape=[jax.ShapeDtyp...  48.2 us
    ppermute x20, waiting for transfers between devices, ring_reduce_scatter(): got = lax.ppermute(buf, 'seq', perm)  35.4 us
    all_to_all x1, waiting for transfers between devices, per_device(): lax.all_to_all(sent, 'seq', split_axis=0, concat_axis=1, tiled=True)[0]  33.1 us
    ppermute x20, starting transfers between devices, ring_reduce_scatter(): got = lax.ppermute(buf, 'seq', perm)  27.4 us
    convert_element_type x20, other arithmetic, ring_reduce_scatter(): (got.astype(jnp.float32) + chunk(k + 1).astype(jnp.float32)).astype(jnp.b...  22.6 us
    ppermute x1, starting transfers between devices, per_device(): other_half = lax.ppermute(part, 'dp', pairs)  12.1 us
  transfers between devices with their start and end apart: 29, of which 18 were waited for; matrix products, arithmetic and copies ran while one was open for 11% of the time, Pallas kernels for 0%

profile of v4, /device:TPU:1, one launch (start us, length us, event | category | flops | bytes accessed | tf_op | source)
XLA Modules:
  0.0 447.1 jit_solution(1275348471587902800)
XLA Ops:
  7.2 1.7 fusion.28
  9.0 88.8 %all-gather.2.cloned.1.call-done = bf16[2048,1280]{1,0:T(8,128)(2,1)} async-done(((bf16[64,1280]{1,0:T(8,128)(2,1)}), bf16[2048,1280]{1,0:T(8,128)(2,1)}) %all-gather.2.cloned.1.call-update) | async-done | bytes 5242896 | tf_op jit(solution)/shard_map/all_gather | solution.py:165
  97.8 3.1 collective-permute-start
  100.9 2.0 copy.50
  103.0 5.3 %all-to-all-start.1 = ((bf16[32,128,64]{1,2,0:T(8,128)(2,1)}), bf16[32,128,64]{1,2,0:T(8,128)(2,1)S(1)}, u32[]{:S(2)}, u32[]{:S(2)}) async-start(bf16[32,128,64]{1,2,0:T(8,128)(2,1)} %bitcast.11), calls=%async_computation.1 | async-start | bytes 1048576 | tf_op jit(solution)/shard_map/all_to_all | solution.py:164
  108.3 4.1 convolution_convert_fusion.1
  112.4 4.1 select_bitcast_fusion.1
  118.1 5.1 %all-to-all-done.1 = bf16[32,128,64]{1,2,0:T(8,128)(2,1)S(1)} async-done(((bf16[32,128,64]{1,2,0:T(8,128)(2,1)}), bf16[32,128,64]{1,2,0:T(8,128)(2,1)S(1)}, u32[]{:S(2)}, u32[]{:S(2)}) %all-to-all-start.1) | async-done | bytes 524320 | tf_op jit(solution)/shard_map/all_to_all | solution.py:164
  123.1 7.4 %all-to-all-start = ((bf16[32,128,192]{1,2,0:T(8,128)(2,1)}), bf16[32,128,192]{1,2,0:T(8,128)(2,1)S(1)}, u32[]{:S(2)}, u32[]{:S(2)}) async-start(bf16[32,128,192]{1,2,0:T(8,128)(2,1)} %pad_maximum_fusion.1), calls=%async_computation | async-start | bytes 3145728 | tf_op jit(solution)/shard_map/all_to_all | solution.py:185
  132.6 1.4 copy.53.g_ref
  134.0 33.1 %all-to-all-done = bf16[32,128,192]{1,2,0:T(8,128)(2,1)S(1)} async-done(((bf16[32,128,192]{1,2,0:T(8,128)(2,1)}), bf16[32,128,192]{1,2,0:T(8,128)(2,1)S(1)}, u32[]{:S(2)}, u32[]{:S(2)}) %all-to-all-start) | async-done | bytes 1572896 | tf_op jit(solution)/shard_map/all_to_all | solution.py:185
  167.5 1.3 copy.49
  168.8 1.3 copy.51
  170.1 1.3 copy.52
  171.5 48.2 %shard_map.110 = (bf16[32,128,64]{2,1,0:T(8,128)(2,1)}, bf16[32,128,64]{2,1,0:T(8,128)(2,1)}, f32[32,128,64]{2,1,0:T(8,128)}, f32[32,128,64]{2,1,0:T(8,128)}) custom-call(s32[224]{0:T(256)} %reshape.101.table_ref, s32[1]{0:T(128)} %dynamic_slice.92.count_ref, bf16[32,128,64]{2,1,0:T(8,128)(2,1)} %bitcast.164, bf16[32,128,64]{2,1,0:T(8,128)(2,1)} %copy.53.g_ref, ...), custom_call_target="tpu_custom_call" | custom-call | flops 2818572288 | bytes 5242880 | tf_op jit(solution)/shard_map/pallas_call | solution.py:90
  219.7 1.9 convert.29
  222.5 2.7 pad_maximum_fusion
  225.2 8.0 %all-to-all-start.2 = ((bf16[32,128,256]{2,1,0:T(8,128)(2,1)}), bf16[32,128,256]{2,1,0:T(8,128)(2,1)S(1)}, u32[]{:S(2)}, u32[]{:S(2)}) async-start(bf16[32,128,256]{2,1,0:T(8,128)(2,1)} %pad_maximum_fusion), calls=%async_computation.2 | async-start | bytes 4194304 | tf_op jit(solution)/shard_map/all_to_all | solution.py:202
  233.2 48.7 %all-to-all-done.2 = bf16[32,128,256]{2,1,0:T(8,128)(2,1)S(1)} async-done(((bf16[32,128,256]{2,1,0:T(8,128)(2,1)}), bf16[32,128,256]{2,1,0:T(8,128)(2,1)S(1)}, u32[]{:S(2)}, u32[]{:S(2)}) %all-to-all-start.2) | async-done | bytes 2097184 | tf_op jit(solution)/shard_map/all_to_all | solution.py:202
  282.4 1.9 slice_bitcast_fusion
  284.3 1.6 copy.55
  286.0 3.8 fusion.1
  289.8 2.4 collective-permute-start.1
  292.2 8.6 %collective-permute-done.1 = bf16[2048,1280]{0,1:T(8,128)(2,1)} collective-permute-done((bf16[2048,1280]{0,1:T(8,128)(2,1)}, bf16[2048,1280]{0,1:T(8,128)(2,1)}, u32[]{:S(2)}, u32[]{:S(2)}) %collective-permute-start.1) | collective-permute-done | bytes 5242912 | tf_op jit(solution)/shard_map/ppermute | solution.py:229
  300.8 6.3 %fusion = bf16[2048,1280]{0,1:T(8,128)(2,1)} fusion(bf16[2048,1280]{0,1:T(8,128)(2,1)} %collective-permute-done.1, bf16[1,128,2048]{2,1,0:T(8,128)(2,1)S(1)} %copy-done, bf16[128,2560]{0,1:T(8,128)(2,1)S(1)} %pad_maximum_fusion.2, s32[]{:T(128)S(6)} %select_n.236), kind=kOutput, calls=%fused_computation.1 | convolution fusion | flops 686817280 | bytes 11337732 | tf_op jit(solution)/shard_map/dot_general | solution.py:225
  307.1 7.9 %copy.58 = bf16[2048,1280]{1,0:T(8,128)(2,1)} copy(bf16[2048,1280]{0,1:T(8,128)(2,1)} %fusion) | data formatting | bytes 10485760 | tf_op jit(solution)/shard_map/convert_element_type | solution.py:231
  315.0 3.1 fusion.39
  318.1 1.6 copy-done.2
  322.7 7.0 %collective-permute-done.12 = bf16[4,64,640]{2,1,0:T(8,128)(2,1)} collective-permute-done((bf16[4,64,640]{2,1,0:T(8,128)(2,1)}, bf16[4,64,640]{2,1,0:T(8,128)(2,1)}, u32[]{:S(2)}, u32[]{:S(2)}) %collective-permute-start.12) | collective-permute-done | bytes 327712 | tf_op jit(solution)/shard_map/ppermute | solution.py:140
  329.7 1.9 fusion.10
  331.6 1.7 collective-permute-start.13
  333.3 1.8 fusion.17
  335.0 4.9 %collective-permute-done.13 = bf16[4,64,640]{2,1,0:T(8,128)(2,1)} collective-permute-done((bf16[4,64,640]{2,1,0:T(8,128)(2,1)}, bf16[4,64,640]{2,1,0:T(8,128)(2,1)}, u32[]{:S(2)}, u32[]{:S(2)}) %collective-permute-start.13) | collective-permute-done | bytes 327712 | tf_op jit(solution)/shard_map/ppermute | solution.py:140
  339.9 1.9 fusion.9
  341.8 2.9 collective-permute-start.14
  344.7 1.8 fusion.16
  346.4 3.4 collective-permute-done.14
  349.9 1.9 fusion.8
  351.7 3.4 collective-permute-start.15
  355.1 1.8 fusion.15
  357.1 2.3 collective-permute-done.15
  359.5 1.9 fusion.7
  361.4 3.1 collective-permute-start.16
  364.6 1.8 fusion.14
  366.3 2.5 collective-permute-done.16
  368.8 1.9 fusion.6
  370.7 3.1 collective-permute-start.17
  373.8 1.8 fusion.13
  375.6 2.6 collective-permute-done.17
  378.1 1.9 fusion.5
  380.0 3.1 collective-permute-start.18
  384.3 3.2 collective-permute-done.18
  388.6 2.4 collective-permute-start.19
  391.0 1.5 collective-permute-done.8
  393.9 1.8 collective-permute-start.20
  395.6 1.9 collective-permute-done.9
  397.7 2.9 collective-permute-start.21
  400.6 1.6 collective-permute-done.10
  402.3 4.4 collective-permute-done.11
  408.1 3.3 collective-permute-done.22
  411.4 3.0 collective-permute-start.23
  414.4 4.3 fusion.25
  418.8 12.1 %collective-permute-start.24 = (bf16[64,1280]{1,0:T(8,128)(2,1)S(1)}, bf16[64,1280]{1,0:T(8,128)(2,1)}, u32[]{:S(2)}, u32[]{:S(2)}) collective-permute-start(bf16[64,1280]{1,0:T(8,128)(2,1)S(1)} %add_convert_fusion), channel_id=1, source_target_pairs={{0,32},{32,0},{64,96},{96,64},{128,160},{160,128},{192,224},{224,1... | collective-permute-start | bytes 491528 | tf_op jit(solution)/shard_map/ppermute | solution.py:242
  431.0 5.2 %fusion.3 = bf16[1,128,2048]{2,1,0:T(8,128)(2,1)} fusion(f32[128,2048]{1,0:T(8,128)S(1)} %fusion.25, bf16[2048,1280]{1,0:T(8,128)(2,1)} %collective-permute-done, bf16[128,2560]{0,1:T(8,128)(2,1)S(1)} %pad_maximum_fusion.2, s32[]{:T(128)S(6)} %select_n.241), kind=kOutput, calls=%fused_computation.9 | convolution fusion | flops 671612928 | bytes 7143428 | tf_op jit(solution)/shard_map/dot_general | solution.py:219
  (79 shorter events, 17.8 us)
Async XLA Ops:
  7.2 101.1 %copy-start = (bf16[1,128,2048]{2,1,0:T(8,128)(2,1)S(1)}, bf16[1,128,2048]{2,1,0:T(8,128)(2,1)}, u32[]{:S(2)}) copy-start(bf16[1,128,2048]{2,1,0:T(8,128)(2,1)} %param.7) | copy-start | bytes 1572868
  7.2 90.6 %all-gather.2.cloned.1.call-start = ((), (), s32[]{:S(2)}) async-start(), calls=%async_computation.3 | async-start | bytes 5406720 | tf_op jit(solution)/shard_map/all_gather | solution.py:165
  97.8 14.5 %collective-permute-start = (bf16[2048,1280]{1,0:T(8,128)(2,1)}, bf16[2048,1280]{1,0:T(8,128)(2,1)}, u32[]{:S(2)}, u32[]{:S(2)}) collective-permute-start(bf16[2048,1280]{1,0:T(8,128)(2,1)} %all-gather.2.cloned.1.call-done), channel_id=1, source_target_pairs={{0,32},{32,0},{64,96},{96,64},{128,160},{160,128},{192,224},{224,1... | collective-permute-start | bytes 15728648 | tf_op jit(solution)/shard_map/ppermute | solution.py:168
  103.0 20.2 %all-to-all-start.1 = ((bf16[32,128,64]{1,2,0:T(8,128)(2,1)}), bf16[32,128,64]{1,2,0:T(8,128)(2,1)S(1)}, u32[]{:S(2)}, u32[]{:S(2)}) async-start(bf16[32,128,64]{1,2,0:T(8,128)(2,1)} %bitcast.11), calls=%async_computation.1 | async-start | bytes 1048576 | tf_op jit(solution)/shard_map/all_to_all | solution.py:164
  116.8 15.3 %copy-start.7 = (s32[32]{0:T(128)S(1)}, s32[32]{0:T(128)}, u32[]{:S(2)}) copy-start(s32[32]{0:T(128)} %param.12) | copy-start | bytes 388
  123.1 44.0 %all-to-all-start = ((bf16[32,128,192]{1,2,0:T(8,128)(2,1)}), bf16[32,128,192]{1,2,0:T(8,128)(2,1)S(1)}, u32[]{:S(2)}, u32[]{:S(2)}) async-start(bf16[32,128,192]{1,2,0:T(8,128)(2,1)} %pad_maximum_fusion.1), calls=%async_computation | async-start | bytes 3145728 | tf_op jit(solution)/shard_map/all_to_all | solution.py:185
  219.6 2.2 copy-start.4
  219.7 2.5 copy-start.5
  219.7 2.8 copy-start.6
  225.2 56.7 %all-to-all-start.2 = ((bf16[32,128,256]{2,1,0:T(8,128)(2,1)}), bf16[32,128,256]{2,1,0:T(8,128)(2,1)S(1)}, u32[]{:S(2)}, u32[]{:S(2)}) async-start(bf16[32,128,256]{2,1,0:T(8,128)(2,1)} %pad_maximum_fusion), calls=%async_computation.2 | async-start | bytes 4194304 | tf_op jit(solution)/shard_map/all_to_all | solution.py:202
  289.8 11.1 %collective-permute-start.1 = (bf16[2048,1280]{0,1:T(8,128)(2,1)}, bf16[2048,1280]{0,1:T(8,128)(2,1)}, u32[]{:S(2)}, u32[]{:S(2)}) collective-permute-start(bf16[2048,1280]{0,1:T(8,128)(2,1)} %fusion.1), channel_id=1, source_target_pairs={{0,32},{32,0},{64,96},{96,64},{128,160},{160,128},{192,224},{224,1... | collective-permute-start | bytes 15728648 | tf_op jit(solution)/shard_map/ppermute | solution.py:229
  318.1 1.6 copy-start.2
  320.5 9.2 %collective-permute-start.12 = (bf16[4,64,640]{2,1,0:T(8,128)(2,1)}, bf16[4,64,640]{2,1,0:T(8,128)(2,1)}, u32[]{:S(2)}, u32[]{:S(2)}) collective-permute-start(bf16[4,64,640]{2,1,0:T(8,128)(2,1)} %dynamic-slice_bitcast_fusion), channel_id=1, source_target_pairs={{1,0},{2,1},{3,2},{4,3},{5,4},{6,5},{7,6},{0,7},{9,8},{10,9},{11,1... | collective-permute-start | bytes 983048 | tf_op jit(solution)/shard_map/ppermute | solution.py:140
  321.7 11.6 %collective-permute-start.2 = (bf16[4,64,640]{2,1,0:T(8,128)(2,1)}, bf16[4,64,640]{2,1,0:T(8,128)(2,1)}, u32[]{:S(2)}, u32[]{:S(2)}) collective-permute-start(bf16[4,64,640]{2,1,0:T(8,128)(2,1)} %dynamic-slice_bitcast_fusion.1), channel_id=1, source_target_pairs={{0,1},{1,2},{2,3},{3,4},{4,5},{5,6},{6,7},{7,0},{8,9},{9,10},{10,1... | collective-permute-start | bytes 983048 | tf_op jit(solution)/shard_map/ppermute | solution.py:140
  331.6 8.3 %collective-permute-start.13 = (bf16[4,64,640]{2,1,0:T(8,128)(2,1)}, bf16[4,64,640]{2,1,0:T(8,128)(2,1)}, u32[]{:S(2)}, u32[]{:S(2)}) collective-permute-start(bf16[4,64,640]{2,1,0:T(8,128)(2,1)} %fusion.10), channel_id=1, source_target_pairs={{1,0},{2,1},{3,2},{4,3},{5,4},{6,5},{7,6},{0,7},{9,8},{10,9},{11,1... | collective-permute-start | bytes 983048 | tf_op jit(solution)/shard_map/ppermute | solution.py:140
  335.0 9.6 %collective-permute-start.3 = (bf16[4,64,640]{2,1,0:T(8,128)(2,1)}, bf16[4,64,640]{2,1,0:T(8,128)(2,1)}, u32[]{:S(2)}, u32[]{:S(2)}) collective-permute-start(bf16[4,64,640]{2,1,0:T(8,128)(2,1)} %fusion.17), channel_id=1, source_target_pairs={{0,1},{1,2},{2,3},{3,4},{4,5},{5,6},{6,7},{7,0},{8,9},{9,10},{10,1... | collective-permute-start | bytes 983048 | tf_op jit(solution)/shard_map/ppermute | solution.py:140
  341.8 8.1 %collective-permute-start.14 = (bf16[4,64,640]{2,1,0:T(8,128)(2,1)}, bf16[4,64,640]{2,1,0:T(8,128)(2,1)}, u32[]{:S(2)}, u32[]{:S(2)}) collective-permute-start(bf16[4,64,640]{2,1,0:T(8,128)(2,1)} %fusion.9), channel_id=1, source_target_pairs={{1,0},{2,1},{3,2},{4,3},{5,4},{6,5},{7,6},{0,7},{9,8},{10,9},{11,1... | collective-permute-start | bytes 983048 | tf_op jit(solution)/shard_map/ppermute | solution.py:140
  346.4 8.7 %collective-permute-start.4 = (bf16[4,64,640]{2,1,0:T(8,128)(2,1)}, bf16[4,64,640]{2,1,0:T(8,128)(2,1)}, u32[]{:S(2)}, u32[]{:S(2)}) collective-permute-start(bf16[4,64,640]{2,1,0:T(8,128)(2,1)} %fusion.16), channel_id=1, source_target_pairs={{0,1},{1,2},{2,3},{3,4},{4,5},{5,6},{6,7},{7,0},{8,9},{9,10},{10,1... | collective-permute-start | bytes 983048 | tf_op jit(solution)/shard_map/ppermute | solution.py:140
  351.7 7.7 %collective-permute-start.15 = (bf16[4,64,640]{2,1,0:T(8,128)(2,1)}, bf16[4,64,640]{2,1,0:T(8,128)(2,1)}, u32[]{:S(2)}, u32[]{:S(2)}) collective-permute-start(bf16[4,64,640]{2,1,0:T(8,128)(2,1)} %fusion.8), channel_id=1, source_target_pairs={{1,0},{2,1},{3,2},{4,3},{5,4},{6,5},{7,6},{0,7},{9,8},{10,9},{11,1... | collective-permute-start | bytes 983048 | tf_op jit(solution)/shard_map/ppermute | solution.py:140
  356.9 7.6 %collective-permute-start.5 = (bf16[4,64,640]{2,1,0:T(8,128)(2,1)}, bf16[4,64,640]{2,1,0:T(8,128)(2,1)}, u32[]{:S(2)}, u32[]{:S(2)}) collective-permute-start(bf16[4,64,640]{2,1,0:T(8,128)(2,1)} %fusion.15), channel_id=1, source_target_pairs={{0,1},{1,2},{2,3},{3,4},{4,5},{5,6},{6,7},{7,0},{8,9},{9,10},{10,1... | collective-permute-start | bytes 983048 | tf_op jit(solution)/shard_map/ppermute | solution.py:140
  361.4 7.5 %collective-permute-start.16 = (bf16[4,64,640]{2,1,0:T(8,128)(2,1)}, bf16[4,64,640]{2,1,0:T(8,128)(2,1)}, u32[]{:S(2)}, u32[]{:S(2)}) collective-permute-start(bf16[4,64,640]{2,1,0:T(8,128)(2,1)} %fusion.7), channel_id=1, source_target_pairs={{1,0},{2,1},{3,2},{4,3},{5,4},{6,5},{7,6},{0,7},{9,8},{10,9},{11,1... | collective-permute-start | bytes 983048 | tf_op jit(solution)/shard_map/ppermute | solution.py:140
  366.3 7.5 %collective-permute-start.6 = (bf16[4,64,640]{2,1,0:T(8,128)(2,1)}, bf16[4,64,640]{2,1,0:T(8,128)(2,1)}, u32[]{:S(2)}, u32[]{:S(2)}) collective-permute-start(bf16[4,64,640]{2,1,0:T(8,128)(2,1)} %fusion.14), channel_id=1, source_target_pairs={{0,1},{1,2},{2,3},{3,4},{4,5},{5,6},{6,7},{7,0},{8,9},{9,10},{10,1... | collective-permute-start | bytes 983048 | tf_op jit(solution)/shard_map/ppermute | solution.py:140
  370.7 7.5 %collective-permute-start.17 = (bf16[4,64,640]{2,1,0:T(8,128)(2,1)}, bf16[4,64,640]{2,1,0:T(8,128)(2,1)}, u32[]{:S(2)}, u32[]{:S(2)}) collective-permute-start(bf16[4,64,640]{2,1,0:T(8,128)(2,1)} %fusion.6), channel_id=1, source_target_pairs={{1,0},{2,1},{3,2},{4,3},{5,4},{6,5},{7,6},{0,7},{9,8},{10,9},{11,1... | collective-permute-start | bytes 983048 | tf_op jit(solution)/shard_map/ppermute | solution.py:140
  375.6 7.6 %collective-permute-start.7 = (bf16[4,64,640]{2,1,0:T(8,128)(2,1)}, bf16[4,64,640]{2,1,0:T(8,128)(2,1)}, u32[]{:S(2)}, u32[]{:S(2)}) collective-permute-start(bf16[4,64,640]{2,1,0:T(8,128)(2,1)} %fusion.13), channel_id=1, source_target_pairs={{0,1},{1,2},{2,3},{3,4},{4,5},{5,6},{6,7},{7,0},{8,9},{9,10},{10,1... | collective-permute-start | bytes 983048 | tf_op jit(solution)/shard_map/ppermute | solution.py:140
  380.0 7.5 %collective-permute-start.18 = (bf16[4,64,640]{2,1,0:T(8,128)(2,1)}, bf16[4,64,640]{2,1,0:T(8,128)(2,1)}, u32[]{:S(2)}, u32[]{:S(2)}) collective-permute-start(bf16[4,64,640]{2,1,0:T(8,128)(2,1)} %fusion.5), channel_id=1, source_target_pairs={{1,0},{2,1},{3,2},{4,3},{5,4},{6,5},{7,6},{0,7},{9,8},{10,9},{11,1... | collective-permute-start | bytes 983048 | tf_op jit(solution)/shard_map/ppermute | solution.py:140
  384.2 8.3 %collective-permute-start.8 = (bf16[4,64,640]{2,1,0:T(8,128)(2,1)S(1)}, bf16[4,64,640]{2,1,0:T(8,128)(2,1)S(1)}, u32[]{:S(2)}, u32[]{:S(2)}) collective-permute-start(bf16[4,64,640]{2,1,0:T(8,128)(2,1)S(1)} %fusion.12), channel_id=1, source_target_pairs={{0,1},{1,2},{2,3},{3,4},{4,5},{5,6},{6,7},{7,0},{8,9},{9,10},{10,1... | collective-permute-start | bytes 983048 | tf_op jit(solution)/shard_map/ppermute | solution.py:140
  388.6 5.2 %collective-permute-start.19 = (bf16[64,640]{1,0:T(8,128)(2,1)S(1)}, bf16[64,640]{1,0:T(8,128)(2,1)S(1)}, u32[]{:S(2)}, u32[]{:S(2)}) collective-permute-start(bf16[64,640]{1,0:T(8,128)(2,1)S(1)} %dynamic-slice_bitcast_fusion.2), channel_id=1, source_target_pairs={{8,0},{9,1},{10,2},{11,3},{12,4},{13,5},{14,6},{15,7},{16,8},{17,9... | collective-permute-start | bytes 245768 | tf_op jit(solution)/shard_map/ppermute | solution.py:140
  392.7 4.9 %collective-permute-start.9 = (bf16[64,640]{1,0:T(8,128)(2,1)S(1)}, bf16[64,640]{1,0:T(8,128)(2,1)S(1)}, u32[]{:S(2)}, u32[]{:S(2)}) collective-permute-start(bf16[64,640]{1,0:T(8,128)(2,1)S(1)} %dynamic-slice_bitcast_fusion.3), channel_id=1, source_target_pairs={{0,8},{1,9},{2,10},{3,11},{4,12},{5,13},{6,14},{7,15},{8,16},{9,17... | collective-permute-start | bytes 245768 | tf_op jit(solution)/shard_map/ppermute | solution.py:140
  393.9 3.8 collective-permute-start.20
  397.6 4.6 %collective-permute-start.10 = (bf16[64,640]{1,0:T(8,128)(2,1)S(1)}, bf16[64,640]{1,0:T(8,128)(2,1)S(1)}, u32[]{:S(2)}, u32[]{:S(2)}) collective-permute-start(bf16[64,640]{1,0:T(8,128)(2,1)S(1)} %fusion.34), channel_id=1, source_target_pairs={{0,8},{1,9},{2,10},{3,11},{4,12},{5,13},{6,14},{7,15},{8,16},{9,17... | collective-permute-start | bytes 245768 | tf_op jit(solution)/shard_map/ppermute | solution.py:140
  397.7 4.6 %collective-permute-start.21 = (bf16[64,640]{1,0:T(8,128)(2,1)S(1)}, bf16[64,640]{1,0:T(8,128)(2,1)S(1)}, u32[]{:S(2)}, u32[]{:S(2)}) collective-permute-start(bf16[64,640]{1,0:T(8,128)(2,1)S(1)} %fusion.30), channel_id=1, source_target_pairs={{8,0},{9,1},{10,2},{11,3},{12,4},{13,5},{14,6},{15,7},{16,8},{17,9... | collective-permute-start | bytes 245768 | tf_op jit(solution)/shard_map/ppermute | solution.py:140
  402.2 4.6 %collective-permute-start.11 = (bf16[64,640]{1,0:T(8,128)(2,1)S(1)}, bf16[64,640]{1,0:T(8,128)(2,1)S(1)}, u32[]{:S(2)}, u32[]{:S(2)}) collective-permute-start(bf16[64,640]{1,0:T(8,128)(2,1)S(1)} %fusion.33), channel_id=1, source_target_pairs={{0,8},{1,9},{2,10},{3,11},{4,12},{5,13},{6,14},{7,15},{8,16},{9,17... | collective-permute-start | bytes 245768 | tf_op jit(solution)/shard_map/ppermute | solution.py:140
  406.8 4.6 %collective-permute-start.22 = (bf16[64,1280]{1,0:T(8,128)(2,1)S(1)}, bf16[64,1280]{1,0:T(8,128)(2,1)S(1)}, u32[]{:S(2)}, u32[]{:S(2)}) collective-permute-start(bf16[64,1280]{1,0:T(8,128)(2,1)S(1)} %pad_maximum_fusion.5), channel_id=1, source_target_pairs={{0,64},{32,96},{64,0},{96,32},{128,192},{160,224},{192,128},{224,1... | collective-permute-start | bytes 491528 | tf_op jit(solution)/shard_map/ppermute | solution.py:239
  411.4 7.4 %collective-permute-start.23 = (bf16[64,1280]{1,0:T(8,128)(2,1)S(1)}, bf16[64,1280]{1,0:T(8,128)(2,1)S(1)}, u32[]{:S(2)}, u32[]{:S(2)}) collective-permute-start(bf16[64,1280]{1,0:T(8,128)(2,1)S(1)} %add_convert_fusion.1), channel_id=1, source_target_pairs={{0,128},{32,160},{64,192},{96,224},{128,0},{160,32},{192,64},{224,... | collective-permute-start | bytes 491528 | tf_op jit(solution)/shard_map/ppermute | solution.py:239
  418.8 17.3 %copy-start.3 = (bf16[128,32,64]{2,0,1:T(8,128)(2,1)S(1)}, bf16[128,32,64]{2,0,1:T(8,128)(2,1)}, u32[]{:S(2)}) copy-start(bf16[128,32,64]{2,0,1:T(8,128)(2,1)} %get-tuple-element.31) | copy-start | bytes 1572868
  418.8 18.7 %collective-permute-start.24 = (bf16[64,1280]{1,0:T(8,128)(2,1)S(1)}, bf16[64,1280]{1,0:T(8,128)(2,1)}, u32[]{:S(2)}, u32[]{:S(2)}) collective-permute-start(bf16[64,1280]{1,0:T(8,128)(2,1)S(1)} %add_convert_fusion), channel_id=1, source_target_pairs={{0,32},{32,0},{64,96},{96,64},{128,160},{160,128},{192,224},{224,1... | collective-permute-start | bytes 491528 | tf_op jit(solution)/shard_map/ppermute | solution.py:242
  431.0 8.9 %copy-start.1 = (bf16[1,128,2048]{2,1,0:T(8,128)(2,1)S(1)}, bf16[1,128,2048]{2,1,0:T(8,128)(2,1)}, u32[]{:S(2)}) copy-start(bf16[1,128,2048]{2,1,0:T(8,128)(2,1)} %param.7) | copy-start | bytes 1572868
Sparse Core Ops, SparseCore 0:
  11.2 86.5 all-gather.1

commit v5 on v4

--- a/solution.py
+++ b/solution.py
@@ -118,11 +118,10 @@
     )
 
 
-def ring_reduce_scatter(parts, ring, stride, position):
+def ring_reduce_scatter(chunk, ring, stride, position):
     seq_devices = lax.axis_size("seq")
     group = ring * stride
     me = (position // stride) % ring
-    width = parts.shape[-1] // 2
     ahead = [
         (s, (s // group) * group + (((s // stride) % ring + 1) % ring) * stride + s % stride)
         for s in range(seq_devices)
@@ -130,17 +129,28 @@
     behind = [(b, a) for (a, b) in ahead]
     total = []
     for side, perm, sign in ((0, ahead, 1), (1, behind, -1)):
-        own = parts[..., side * width : (side + 1) * width]
-
-        def chunk(k):
-            return lax.dynamic_index_in_dim(own, (me - sign * (1 + k)) % ring, 0, keepdims=False)
-
-        buf = chunk(0)
+        buf = chunk((me - sign) % ring, side)
         for k in range(ring - 1):
             got = lax.ppermute(buf, "seq", perm)
-            buf = (got.astype(jnp.float32) + chunk(k + 1).astype(jnp.float32)).astype(jnp.bfloat16)
+            own = chunk((me - sign * (2 + k)) % ring, side)
+            buf = (got.astype(jnp.float32) + own.astype(jnp.float32)).astype(jnp.bfloat16)
         total.append(buf)
     return jnp.concatenate(total, axis=-1)
+
+
+def direct_sum(pieces, axis_name, size, stride, mine):
+    devices = lax.axis_size(axis_name)
+    group = size * stride
+    got = [lax.dynamic_index_in_dim(pieces, mine, 0, keepdims=False)]
+    for d in range(1, size):
+        perm = [
+            (i, (i // group) * group + (((i // stride) % size + d) % size) * stride + i % stride)
+            for i in range(devices)
+        ]
+        got.append(lax.ppermute(
+            lax.dynamic_index_in_dim(pieces, (mine + d) % size, 0, keepdims=False), axis_name, perm
+        ))
+    return got
 
 
 def per_device(activations, w_query, w_key, w_value, key_blocks, random_count, grad_out):
@@ -228,17 +238,29 @@
 
     got = lax.ppermute(term_of(comb_other), "dp", pairs)
     keep = term_of(comb_mine)
-    chip_sum = (keep.astype(jnp.float32) + got.astype(jnp.float32)).astype(jnp.bfloat16)
-    rows = chip_sum.shape[0] // seq_devices
-    by_z = chip_sum.reshape(seq_devices // RING_Z, RING_Z, rows, half).transpose(1, 0, 2, 3)
-    by_y = ring_reduce_scatter(by_z, RING_Z, 1, position)
-    part = ring_reduce_scatter(by_y, seq_devices // RING_Z, RING_Z, position)
-    step = 2
-    while step < dp_devices:
-        mates = [(i, i ^ step) for i in range(dp_devices)]
-        other = lax.ppermute(part, "dp", mates)
-        part = (part.astype(jnp.float32) + other.astype(jnp.float32)).astype(jnp.bfloat16)
-        step *= 2
+    rows = keep.shape[0] // seq_devices
+    y_count = seq_devices // RING_Z
+    keep4 = keep.reshape(y_count, RING_Z, rows, half)
+    got4 = got.reshape(y_count, RING_Z, rows, half)
+    quarter = half // 2
+
+    def chip_chunk(i, side):
+        a = lax.dynamic_index_in_dim(keep4, i, 1, keepdims=False)[..., side * quarter : (side + 1) * quarter]
+        b = lax.dynamic_index_in_dim(got4, i, 1, keepdims=False)[..., side * quarter : (side + 1) * quarter]
+        return (a.astype(jnp.float32) + b.astype(jnp.float32)).astype(jnp.bfloat16)
+
+    by_y = ring_reduce_scatter(chip_chunk, RING_Z, 1, position)
+    from_y = direct_sum(by_y, "seq", y_count, RING_Z, position // RING_Z)
+    total = from_y[0].astype(jnp.float32)
+    for piece in from_y[1:]:
+        total = total + piece.astype(jnp.float32)
+    part = total.astype(jnp.bfloat16)
+    chips = dp_devices // 2
+    chip = dp_index // 2
+    from_x = direct_sum(jnp.broadcast_to(part, (chips,) + part.shape), "dp", chips, 2, chip)
+    by_offset = jnp.stack(from_x)
+    in_order = jnp.take(by_offset, (chip - jnp.arange(chips)) % chips, axis=0)
+    part = jnp.sum(in_order.astype(jnp.float32), axis=0).astype(jnp.bfloat16)
     other_half = lax.ppermute(part, "dp", pairs)
     first = jnp.where(core == 0, part, other_half)
     second = jnp.where(core == 0, other_half, part)

time: 456 us -> 443 us (0.971)
  local copies, waits for them, and re-layouts: 30.8 us -> 45 us
  other arithmetic: 32.4 us -> 21.4 us
  waiting for transfers between devices: 223 us -> 216 us
  starting transfers between devices: 70.1 us -> 63.5 us
    convert_element_type x22 -> x17, other arithmetic: 22.7 us -> 10.2 us  [the longest x14 7.8 us: ring_reduce_scatter(): (got.astype(jnp.float32) + own.astype(jnp.float32)).astype(jnp.bfloat16)]
    squeeze x4 -> x1, local copies, waits for them, and re-layouts: 1.54 us -> 11.2 us  [chip_chunk(): lax.dynamic_index_in_dim(got4, i, 1, keepdims=False)]
    ppermute x1, waiting for transfers between devices: 8.63 us -> 0.01 us  [per_device(): got = lax.ppermute(term_of(comb_other), 'dp', pairs)]
    ppermute x0 -> x1, local copies, waits for them, and re-layouts: none -> 7.83 us  [per_device(): got = lax.ppermute(term_of(comb_other), 'dp', pairs)]
    ppermute x20 -> x14, starting transfers between devices: 27.4 us -> 22 us  [ring_reduce_scatter(): got = lax.ppermute(buf, 'seq', perm)]
    ppermute x2 -> x6, waiting for transfers between devices: 3.27 us -> 8.17 us  [direct_sum(): lax.ppermute(lax.dynamic_index_in_dim(pieces, (mine + d) % size, 0, keepd...]
    ppermute x20 -> x14, waiting for transfers between devices: 35.4 us -> 32.1 us  [ring_reduce_scatter(): got = lax.ppermute(buf, 'seq', perm)]
  transfers between devices with their start and end apart: 29 -> 27, of which waited for: 18 -> 17; matrix products, arithmetic and copies ran while one was open for 11% -> 11% of each run, Pallas kernels for 0% -> 0%
where the time goes in v5:
time: 443 us; the launch traced here: 434 us
  waiting for transfers between devices  216 us (49%)
  starting transfers between devices  63.5 us (14%)
  Pallas kernels  48.1 us (11%)
  local copies, waits for them, and re-layouts  45 us (10%)
  matrix products  25.3 us (6%)
  other arithmetic  21.4 us (5%)
  between operations  14.9 us (3%)
    all_gather x1, waiting for transfers between devices, per_device(): lax.all_gather(lax.dynamic_slice_in_dim(w_local, core * half, half, axis=...  88.8 us
    all_to_all x1, waiting for transfers between devices, per_device(): lax.all_to_all(back_sent, 'seq', split_axis=0, concat_axis=0, tiled=True)  48.7 us
    pallas_call x1, Pallas kernels, head_pass(): pl.pallas_call(head_kernel, grid_spec=grid_spec, out_shape=[jax.ShapeDtyp...  48.1 us
    all_to_all x1, waiting for transfers between devices, per_device(): lax.all_to_all(sent, 'seq', split_axis=0, concat_axis=1, tiled=True)[0]  33.1 us
    ppermute x14, waiting for transfers between devices, ring_reduce_scatter(): got = lax.ppermute(buf, 'seq', perm)  32.1 us
    ppermute x14, starting transfers between devices, ring_reduce_scatter(): got = lax.ppermute(buf, 'seq', perm)  22 us
    squeeze x1, local copies, waits for them, and re-layouts, chip_chunk(): lax.dynamic_index_in_dim(got4, i, 1, keepdims=False)  11.2 us
    ppermute x1, starting transfers between devices, per_device(): other_half = lax.ppermute(part, 'dp', pairs)  9.85 us
  transfers between devices with their start and end apart: 27, of which 17 were waited for; matrix products, arithmetic and copies ran while one was open for 11% of the time, Pallas kernels for 0%

profile of v5, /device:TPU:1, one launch (start us, length us, event | category | flops | bytes accessed | tf_op | source)
XLA Modules:
  0.0 434.3 jit_solution(12512736568094442570)
XLA Ops:
  7.2 1.7 fusion.17
  9.0 88.8 %all-gather.2.cloned.1.call-done = bf16[2048,1280]{1,0:T(8,128)(2,1)} async-done(((bf16[64,1280]{1,0:T(8,128)(2,1)}), bf16[2048,1280]{1,0:T(8,128)(2,1)}) %all-gather.2.cloned.1.call-update) | async-done | bytes 5242896 | tf_op jit(solution)/shard_map/all_gather | solution.py:175
  97.8 3.1 collective-permute-start
  100.9 2.0 copy.37
  103.0 5.3 %all-to-all-start.1 = ((bf16[32,128,64]{1,2,0:T(8,128)(2,1)}), bf16[32,128,64]{1,2,0:T(8,128)(2,1)S(1)}, u32[]{:S(2)}, u32[]{:S(2)}) async-start(bf16[32,128,64]{1,2,0:T(8,128)(2,1)} %bitcast.11), calls=%async_computation.1 | async-start | bytes 1048576 | tf_op jit(solution)/shard_map/all_to_all | solution.py:174
  108.3 4.1 convolution_convert_fusion.1
  112.4 4.1 select_bitcast_fusion.1
  116.8 1.3 pad_maximum_fusion.1
  118.0 5.1 %all-to-all-done.1 = bf16[32,128,64]{1,2,0:T(8,128)(2,1)S(1)} async-done(((bf16[32,128,64]{1,2,0:T(8,128)(2,1)}), bf16[32,128,64]{1,2,0:T(8,128)(2,1)S(1)}, u32[]{:S(2)}, u32[]{:S(2)}) %all-to-all-start.1) | async-done | bytes 524320 | tf_op jit(solution)/shard_map/all_to_all | solution.py:174
  123.1 7.4 %all-to-all-start = ((bf16[32,128,192]{1,2,0:T(8,128)(2,1)}), bf16[32,128,192]{1,2,0:T(8,128)(2,1)S(1)}, u32[]{:S(2)}, u32[]{:S(2)}) async-start(bf16[32,128,192]{1,2,0:T(8,128)(2,1)} %pad_maximum_fusion.1), calls=%async_computation | async-start | bytes 3145728 | tf_op jit(solution)/shard_map/all_to_all | solution.py:195
  132.6 1.4 copy.40.g_ref
  134.0 33.1 %all-to-all-done = bf16[32,128,192]{1,2,0:T(8,128)(2,1)S(1)} async-done(((bf16[32,128,192]{1,2,0:T(8,128)(2,1)}), bf16[32,128,192]{1,2,0:T(8,128)(2,1)S(1)}, u32[]{:S(2)}, u32[]{:S(2)}) %all-to-all-start) | async-done | bytes 1572896 | tf_op jit(solution)/shard_map/all_to_all | solution.py:195
  167.5 1.3 copy.36
  168.8 1.3 copy.38
  170.2 1.3 copy.39
  171.5 48.1 %shard_map.110 = (bf16[32,128,64]{2,1,0:T(8,128)(2,1)}, bf16[32,128,64]{2,1,0:T(8,128)(2,1)}, f32[32,128,64]{2,1,0:T(8,128)}, f32[32,128,64]{2,1,0:T(8,128)}) custom-call(s32[224]{0:T(256)} %reshape.121.table_ref, s32[1]{0:T(128)} %dynamic_slice.132.count_ref, bf16[32,128,64]{2,1,0:T(8,128)(2,1)} %bitcast.147, bf16[32,128,64]{2,1,0:T(8,128)(2,1)} %copy.40.g_ref, ...), custom_call_target="tpu_custom_call" | custom-call | flops 2818572288 | bytes 5242880 | tf_op jit(solution)/shard_map/pallas_call | solution.py:90
  219.7 1.9 convert.10
  222.4 2.7 pad_maximum_fusion
  225.1 8.0 %all-to-all-start.2 = ((bf16[32,128,256]{2,1,0:T(8,128)(2,1)}), bf16[32,128,256]{2,1,0:T(8,128)(2,1)S(1)}, u32[]{:S(2)}, u32[]{:S(2)}) async-start(bf16[32,128,256]{2,1,0:T(8,128)(2,1)} %pad_maximum_fusion), calls=%async_computation.2 | async-start | bytes 4194304 | tf_op jit(solution)/shard_map/all_to_all | solution.py:212
  233.2 48.7 %all-to-all-done.2 = bf16[32,128,256]{2,1,0:T(8,128)(2,1)S(1)} async-done(((bf16[32,128,256]{2,1,0:T(8,128)(2,1)}), bf16[32,128,256]{2,1,0:T(8,128)(2,1)S(1)}, u32[]{:S(2)}, u32[]{:S(2)}) %all-to-all-start.2) | async-done | bytes 2097184 | tf_op jit(solution)/shard_map/all_to_all | solution.py:212
  282.4 1.9 slice_bitcast_fusion
  284.2 1.6 copy.42
  285.9 3.8 fusion.1
  289.7 2.4 collective-permute-start.1
  292.1 3.9 fusion
  296.0 7.9 %copy.45 = bf16[2048,1280]{1,0:T(8,128)(2,1)} copy(bf16[2048,1280]{0,1:T(8,128)(2,1)} %fusion) | data formatting | bytes 10485760 | tf_op jit(solution)/shard_map/convert_element_type | solution.py:237
  303.9 7.8 %copy.46 = bf16[2048,1280]{1,0:T(8,128)(2,1)} copy(bf16[2048,1280]{0,1:T(8,128)(2,1)} %collective-permute-done.1) | data formatting | bytes 10485760 | tf_op jit(solution)/shard_map/ppermute | solution.py:239
  311.7 11.2 %dynamic-slice_bitcast_fusion = (bf16[4,64,1280]{2,1,0:T(8,128)(2,1)S(1)}, bf16[4,64,1280]{2,1,0:T(8,128)(2,1)}, bf16[4,64,1280]{2,1,0:T(8,128)(2,1)S(1)}, bf16[...) fusion(bf16[4,8,64,1280]{3,2,1,0:T(8,128)(2,1)} %bitcast.142, ...), kind=kLoop, calls=%fused_computation.29 | loop fusion | bytes 41943104 | tf_op jit(solution)/shard_map/jit(dynamic_index_in_dim)/squeeze | solution.py:249
  322.9 1.2 add_convert_fusion.29
  324.1 1.3 collective-permute-start.2
  325.4 1.2 add_convert_fusion.14
  326.5 1.5 collective-permute-start.9
  328.1 6.6 %collective-permute-done.2 = bf16[4,64,640]{2,1,0:T(8,128)(2,1)S(1)} collective-permute-done((bf16[4,64,640]{2,1,0:T(8,128)(2,1)S(1)}, bf16[4,64,640]{2,1,0:T(8,128)(2,1)S(1)}, u32[]{:S(2)}, u32[]{:S(2)}) %collective-permute-start.2) | collective-permute-done | bytes 327712 | tf_op jit(solution)/shard_map/ppermute | solution.py:134
  334.7 1.2 add_convert_fusion.27
  336.0 1.2 add_convert_fusion.12
  337.2 2.7 collective-permute-start.10
  339.9 5.7 %collective-permute-done.3 = bf16[4,64,640]{2,1,0:T(8,128)(2,1)S(1)} collective-permute-done((bf16[4,64,640]{2,1,0:T(8,128)(2,1)S(1)}, bf16[4,64,640]{2,1,0:T(8,128)(2,1)S(1)}, u32[]{:S(2)}, u32[]{:S(2)}) %collective-permute-start.3) | collective-permute-done | bytes 327712 | tf_op jit(solution)/shard_map/ppermute | solution.py:134
  346.0 3.7 collective-permute-start.11
  349.7 4.9 %collective-permute-done.4 = bf16[4,64,640]{2,1,0:T(8,128)(2,1)S(1)} collective-permute-done((bf16[4,64,640]{2,1,0:T(8,128)(2,1)S(1)}, bf16[4,64,640]{2,1,0:T(8,128)(2,1)S(1)}, u32[]{:S(2)}, u32[]{:S(2)}) %collective-permute-start.4) | collective-permute-done | bytes 327712 | tf_op jit(solution)/shard_map/ppermute | solution.py:134
  355.0 3.4 collective-permute-start.12
  358.4 4.3 collective-permute-done.5
  363.0 3.1 collective-permute-start.13
  366.1 3.9 collective-permute-done.6
  370.2 0.8 add_convert_fusion.4
  371.1 3.0 collective-permute-start.14
  374.1 3.4 collective-permute-done.7
  377.5 1.2 add_convert_fusion.17
  378.8 1.3 add_convert_fusion.2
  380.1 2.8 collective-permute-start.15
  382.9 3.1 collective-permute-done.8
  386.0 1.1 add_convert_fusion.15
  389.0 3.0 collective-permute-done.18
  392.0 1.9 collective-permute-done.17
  393.8 1.7 collective-permute-done.16
  395.5 2.5 collective-permute-start.21
  398.6 0.8 collective-permute-start.19
  399.4 4.3 fusion.14
  403.8 1.7 collective-permute-done.19
  405.5 1.4 gather_fusion
  407.0 1.4 select_reduce_fusion
  408.3 9.9 %collective-permute-start.22 = (bf16[64,1280]{1,0:T(8,128)(2,1)S(1)}, bf16[64,1280]{1,0:T(8,128)(2,1)}, u32[]{:S(2)}, u32[]{:S(2)}) collective-permute-start(bf16[64,1280]{1,0:T(8,128)(2,1)S(1)} %select_reduce_fusion), channel_id=1, source_target_pairs={{0,32},{32,0},{64,96},{96,64},{128,160},{160,128},{192,224},{224,1... | collective-permute-start | bytes 491528 | tf_op jit(solution)/shard_map/ppermute | solution.py:264
  418.2 5.1 %fusion.3 = bf16[1,128,2048]{2,1,0:T(8,128)(2,1)} fusion(f32[128,2048]{1,0:T(8,128)S(1)} %fusion.14, bf16[2048,1280]{1,0:T(8,128)(2,1)} %collective-permute-done, bf16[128,2560]{0,1:T(8,128)(2,1)S(1)} %pad_maximum_fusion.2, s32[]{:T(128)S(6)} %select_n.271), kind=kOutput, calls=%fused_computation.9 | convolution fusion | flops 671612928 | bytes 7143428 | tf_op jit(solution)/shard_map/dot_general | solution.py:229
  423.7 1.0 copy.47
  424.7 0.9 broadcast_select_fusion.1
  (71 shorter events, 10.0 us)
Async XLA Ops:
  7.2 101.1 %copy-start = (bf16[1,128,2048]{2,1,0:T(8,128)(2,1)S(1)}, bf16[1,128,2048]{2,1,0:T(8,128)(2,1)}, u32[]{:S(2)}) copy-start(bf16[1,128,2048]{2,1,0:T(8,128)(2,1)} %param.7) | copy-start | bytes 1572868
  7.2 90.6 %all-gather.2.cloned.1.call-start = ((), (), s32[]{:S(2)}) async-start(), calls=%async_computation.3 | async-start | bytes 5406720 | tf_op jit(solution)/shard_map/all_gather | solution.py:175
  97.8 14.5 %collective-permute-start = (bf16[2048,1280]{1,0:T(8,128)(2,1)}, bf16[2048,1280]{1,0:T(8,128)(2,1)}, u32[]{:S(2)}, u32[]{:S(2)}) collective-permute-start(bf16[2048,1280]{1,0:T(8,128)(2,1)} %all-gather.2.cloned.1.call-done), channel_id=1, source_target_pairs={{0,32},{32,0},{64,96},{96,64},{128,160},{160,128},{192,224},{224,1... | collective-permute-start | bytes 15728648 | tf_op jit(solution)/shard_map/ppermute | solution.py:178
  103.0 20.2 %all-to-all-start.1 = ((bf16[32,128,64]{1,2,0:T(8,128)(2,1)}), bf16[32,128,64]{1,2,0:T(8,128)(2,1)S(1)}, u32[]{:S(2)}, u32[]{:S(2)}) async-start(bf16[32,128,64]{1,2,0:T(8,128)(2,1)} %bitcast.11), calls=%async_computation.1 | async-start | bytes 1048576 | tf_op jit(solution)/shard_map/all_to_all | solution.py:174
  116.5 15.5 %copy-start.6 = (s32[32]{0:T(128)S(1)}, s32[32]{0:T(128)}, u32[]{:S(2)}) copy-start(s32[32]{0:T(128)} %param.12) | copy-start | bytes 388
  123.1 44.0 %all-to-all-start = ((bf16[32,128,192]{1,2,0:T(8,128)(2,1)}), bf16[32,128,192]{1,2,0:T(8,128)(2,1)S(1)}, u32[]{:S(2)}, u32[]{:S(2)}) async-start(bf16[32,128,192]{1,2,0:T(8,128)(2,1)} %pad_maximum_fusion.1), calls=%async_computation | async-start | bytes 3145728 | tf_op jit(solution)/shard_map/all_to_all | solution.py:195
  219.6 2.2 copy-start.3
  219.6 2.5 copy-start.4
  219.6 2.8 copy-start.5
  225.1 56.8 %all-to-all-start.2 = ((bf16[32,128,256]{2,1,0:T(8,128)(2,1)}), bf16[32,128,256]{2,1,0:T(8,128)(2,1)S(1)}, u32[]{:S(2)}, u32[]{:S(2)}) async-start(bf16[32,128,256]{2,1,0:T(8,128)(2,1)} %pad_maximum_fusion), calls=%async_computation.2 | async-start | bytes 4194304 | tf_op jit(solution)/shard_map/all_to_all | solution.py:212
  289.7 14.2 %collective-permute-start.1 = (bf16[2048,1280]{0,1:T(8,128)(2,1)}, bf16[2048,1280]{0,1:T(8,128)(2,1)}, u32[]{:S(2)}, u32[]{:S(2)}) collective-permute-start(bf16[2048,1280]{0,1:T(8,128)(2,1)} %fusion.1), channel_id=1, source_target_pairs={{0,32},{32,0},{64,96},{96,64},{128,160},{160,128},{192,224},{224,1... | collective-permute-start | bytes 15728648 | tf_op jit(solution)/shard_map/ppermute | solution.py:239
  324.1 10.6 %collective-permute-start.2 = (bf16[4,64,640]{2,1,0:T(8,128)(2,1)S(1)}, bf16[4,64,640]{2,1,0:T(8,128)(2,1)S(1)}, u32[]{:S(2)}, u32[]{:S(2)}) collective-permute-start(bf16[4,64,640]{2,1,0:T(8,128)(2,1)S(1)} %add_convert_fusion.29), channel_id=1, source_target_pairs={{0,1},{1,2},{2,3},{3,4},{4,5},{5,6},{6,7},{7,0},{8,9},{9,10},{10,1... | collective-permute-start | bytes 983048 | tf_op jit(solution)/shard_map/ppermute | solution.py:134
  326.5 9.5 %collective-permute-start.9 = (bf16[4,64,640]{2,1,0:T(8,128)(2,1)S(1)}, bf16[4,64,640]{2,1,0:T(8,128)(2,1)S(1)}, u32[]{:S(2)}, u32[]{:S(2)}) collective-permute-start(bf16[4,64,640]{2,1,0:T(8,128)(2,1)S(1)} %add_convert_fusion.14), channel_id=1, source_target_pairs={{1,0},{2,1},{3,2},{4,3},{5,4},{6,5},{7,6},{0,7},{9,8},{10,9},{11,1... | collective-permute-start | bytes 983048 | tf_op jit(solution)/shard_map/ppermute | solution.py:134
  335.9 9.7 %collective-permute-start.3 = (bf16[4,64,640]{2,1,0:T(8,128)(2,1)S(1)}, bf16[4,64,640]{2,1,0:T(8,128)(2,1)S(1)}, u32[]{:S(2)}, u32[]{:S(2)}) collective-permute-start(bf16[4,64,640]{2,1,0:T(8,128)(2,1)S(1)} %add_convert_fusion.27), channel_id=1, source_target_pairs={{0,1},{1,2},{2,3},{3,4},{4,5},{5,6},{6,7},{7,0},{8,9},{9,10},{10,1... | collective-permute-start | bytes 983048 | tf_op jit(solution)/shard_map/ppermute | solution.py:134
  337.2 8.7 %collective-permute-start.10 = (bf16[4,64,640]{2,1,0:T(8,128)(2,1)S(1)}, bf16[4,64,640]{2,1,0:T(8,128)(2,1)S(1)}, u32[]{:S(2)}, u32[]{:S(2)}) collective-permute-start(bf16[4,64,640]{2,1,0:T(8,128)(2,1)S(1)} %add_convert_fusion.12), channel_id=1, source_target_pairs={{1,0},{2,1},{3,2},{4,3},{5,4},{6,5},{7,6},{0,7},{9,8},{10,9},{11,1... | collective-permute-start | bytes 983048 | tf_op jit(solution)/shard_map/ppermute | solution.py:134
  345.8 8.8 %collective-permute-start.4 = (bf16[4,64,640]{2,1,0:T(8,128)(2,1)S(1)}, bf16[4,64,640]{2,1,0:T(8,128)(2,1)S(1)}, u32[]{:S(2)}, u32[]{:S(2)}) collective-permute-start(bf16[4,64,640]{2,1,0:T(8,128)(2,1)S(1)} %add_convert_fusion.25), channel_id=1, source_target_pairs={{0,1},{1,2},{2,3},{3,4},{4,5},{5,6},{6,7},{7,0},{8,9},{9,10},{10,1... | collective-permute-start | bytes 983048 | tf_op jit(solution)/shard_map/ppermute | solution.py:134
  346.0 8.8 %collective-permute-start.11 = (bf16[4,64,640]{2,1,0:T(8,128)(2,1)S(1)}, bf16[4,64,640]{2,1,0:T(8,128)(2,1)S(1)}, u32[]{:S(2)}, u32[]{:S(2)}) collective-permute-start(bf16[4,64,640]{2,1,0:T(8,128)(2,1)S(1)} %add_convert_fusion.10), channel_id=1, source_target_pairs={{1,0},{2,1},{3,2},{4,3},{5,4},{6,5},{7,6},{0,7},{9,8},{10,9},{11,1... | collective-permute-start | bytes 983048 | tf_op jit(solution)/shard_map/ppermute | solution.py:134
  354.7 7.9 %collective-permute-start.5 = (bf16[4,64,640]{2,1,0:T(8,128)(2,1)S(1)}, bf16[4,64,640]{2,1,0:T(8,128)(2,1)S(1)}, u32[]{:S(2)}, u32[]{:S(2)}) collective-permute-start(bf16[4,64,640]{2,1,0:T(8,128)(2,1)S(1)} %add_convert_fusion.23), channel_id=1, source_target_pairs={{0,1},{1,2},{2,3},{3,4},{4,5},{5,6},{6,7},{7,0},{8,9},{9,10},{10,1... | collective-permute-start | bytes 983048 | tf_op jit(solution)/shard_map/ppermute | solution.py:134
  355.0 7.9 %collective-permute-start.12 = (bf16[4,64,640]{2,1,0:T(8,128)(2,1)S(1)}, bf16[4,64,640]{2,1,0:T(8,128)(2,1)S(1)}, u32[]{:S(2)}, u32[]{:S(2)}) collective-permute-start(bf16[4,64,640]{2,1,0:T(8,128)(2,1)S(1)} %add_convert_fusion.8), channel_id=1, source_target_pairs={{1,0},{2,1},{3,2},{4,3},{5,4},{6,5},{7,6},{0,7},{9,8},{10,9},{11,1... | collective-permute-start | bytes 983048 | tf_op jit(solution)/shard_map/ppermute | solution.py:134
  362.8 7.2 %collective-permute-start.6 = (bf16[4,64,640]{2,1,0:T(8,128)(2,1)S(1)}, bf16[4,64,640]{2,1,0:T(8,128)(2,1)S(1)}, u32[]{:S(2)}, u32[]{:S(2)}) collective-permute-start(bf16[4,64,640]{2,1,0:T(8,128)(2,1)S(1)} %add_convert_fusion.21), channel_id=1, source_target_pairs={{0,1},{1,2},{2,3},{3,4},{4,5},{5,6},{6,7},{7,0},{8,9},{9,10},{10,1... | collective-permute-start | bytes 983048 | tf_op jit(solution)/shard_map/ppermute | solution.py:134
  363.0 7.2 %collective-permute-start.13 = (bf16[4,64,640]{2,1,0:T(8,128)(2,1)S(1)}, bf16[4,64,640]{2,1,0:T(8,128)(2,1)S(1)}, u32[]{:S(2)}, u32[]{:S(2)}) collective-permute-start(bf16[4,64,640]{2,1,0:T(8,128)(2,1)S(1)} %add_convert_fusion.6), channel_id=1, source_target_pairs={{1,0},{2,1},{3,2},{4,3},{5,4},{6,5},{7,6},{0,7},{9,8},{10,9},{11,1... | collective-permute-start | bytes 983048 | tf_op jit(solution)/shard_map/ppermute | solution.py:134
  370.1 7.4 %collective-permute-start.7 = (bf16[4,64,640]{2,1,0:T(8,128)(2,1)S(1)}, bf16[4,64,640]{2,1,0:T(8,128)(2,1)S(1)}, u32[]{:S(2)}, u32[]{:S(2)}) collective-permute-start(bf16[4,64,640]{2,1,0:T(8,128)(2,1)S(1)} %add_convert_fusion.19), channel_id=1, source_target_pairs={{0,1},{1,2},{2,3},{3,4},{4,5},{5,6},{6,7},{7,0},{8,9},{9,10},{10,1... | collective-permute-start | bytes 983048 | tf_op jit(solution)/shard_map/ppermute | solution.py:134
  371.1 7.7 %collective-permute-start.14 = (bf16[4,64,640]{2,1,0:T(8,128)(2,1)}, bf16[4,64,640]{2,1,0:T(8,128)(2,1)}, u32[]{:S(2)}, u32[]{:S(2)}) collective-permute-start(bf16[4,64,640]{2,1,0:T(8,128)(2,1)} %add_convert_fusion.4), channel_id=1, source_target_pairs={{1,0},{2,1},{3,2},{4,3},{5,4},{6,5},{7,6},{0,7},{9,8},{10,9},{11,1... | collective-permute-start | bytes 983048 | tf_op jit(solution)/shard_map/ppermute | solution.py:134
  378.7 7.4 %collective-permute-start.8 = (bf16[4,64,640]{2,1,0:T(8,128)(2,1)S(1)}, bf16[4,64,640]{2,1,0:T(8,128)(2,1)S(1)}, u32[]{:S(2)}, u32[]{:S(2)}) collective-permute-start(bf16[4,64,640]{2,1,0:T(8,128)(2,1)S(1)} %add_convert_fusion.17), channel_id=1, source_target_pairs={{0,1},{1,2},{2,3},{3,4},{4,5},{5,6},{6,7},{7,0},{8,9},{9,10},{10,1... | collective-permute-start | bytes 983048 | tf_op jit(solution)/shard_map/ppermute | solution.py:134
  380.1 7.2 %collective-permute-start.15 = (bf16[4,64,640]{2,1,0:T(8,128)(2,1)S(1)}, bf16[4,64,640]{2,1,0:T(8,128)(2,1)S(1)}, u32[]{:S(2)}, u32[]{:S(2)}) collective-permute-start(bf16[4,64,640]{2,1,0:T(8,128)(2,1)S(1)} %add_convert_fusion.2), channel_id=1, source_target_pairs={{1,0},{2,1},{3,2},{4,3},{5,4},{6,5},{7,6},{0,7},{9,8},{10,9},{11,1... | collective-permute-start | bytes 983048 | tf_op jit(solution)/shard_map/ppermute | solution.py:134
  387.4 4.5 %collective-permute-start.18 = (bf16[64,1280]{1,0:T(8,128)(2,1)S(1)}, bf16[64,1280]{1,0:T(8,128)(2,1)S(1)}, u32[]{:S(2)}, u32[]{:S(2)}) collective-permute-start(bf16[64,1280]{1,0:T(8,128)(2,1)S(1)} %get-tuple-element.67), channel_id=1, source_target_pairs={{0,24},{1,25},{2,26},{3,27},{4,28},{5,29},{6,30},{7,31},{8,0},{9,1... | collective-permute-start | bytes 491528 | tf_op jit(solution)/shard_map/ppermute | solution.py:150
  388.0 5.8 %collective-permute-start.17 = (bf16[64,1280]{1,0:T(8,128)(2,1)S(1)}, bf16[64,1280]{1,0:T(8,128)(2,1)S(1)}, u32[]{:S(2)}, u32[]{:S(2)}) collective-permute-start(bf16[64,1280]{1,0:T(8,128)(2,1)S(1)} %get-tuple-element.66), channel_id=1, source_target_pairs={{0,16},{1,17},{2,18},{3,19},{4,20},{5,21},{6,22},{7,23},{8,24},{9,... | collective-permute-start | bytes 491528 | tf_op jit(solution)/shard_map/ppermute | solution.py:150
  388.4 7.1 %collective-permute-start.16 = (bf16[64,1280]{1,0:T(8,128)(2,1)S(1)}, bf16[64,1280]{1,0:T(8,128)(2,1)S(1)}, u32[]{:S(2)}, u32[]{:S(2)}) collective-permute-start(bf16[64,1280]{1,0:T(8,128)(2,1)S(1)} %get-tuple-element.65), channel_id=1, source_target_pairs={{0,8},{1,9},{2,10},{3,11},{4,12},{5,13},{6,14},{7,15},{8,16},{9,17... | collective-permute-start | bytes 491528 | tf_op jit(solution)/shard_map/ppermute | solution.py:150
  395.5 8.2 %collective-permute-start.21 = (bf16[64,1280]{1,0:T(8,128)(2,1)S(1)}, bf16[64,1280]{1,0:T(8,128)(2,1)S(1)}, u32[]{:S(2)}, u32[]{:S(2)}) collective-permute-start(bf16[64,1280]{1,0:T(8,128)(2,1)S(1)} %fusion.10), channel_id=1, source_target_pairs={{0,192},{32,224},{64,0},{96,32},{128,64},{160,96},{192,128},{224,1... | collective-permute-start | bytes 491528 | tf_op jit(solution)/shard_map/ppermute | solution.py:150
  398.0 5.8 %collective-permute-start.20 = (bf16[64,1280]{1,0:T(8,128)(2,1)S(1)}, bf16[64,1280]{1,0:T(8,128)(2,1)S(1)}, u32[]{:S(2)}, u32[]{:S(2)}) collective-permute-start(bf16[64,1280]{1,0:T(8,128)(2,1)S(1)} %fusion.10), channel_id=1, source_target_pairs={{0,128},{32,160},{64,192},{96,224},{128,0},{160,32},{192,64},{224,... | collective-permute-start | bytes 491528 | tf_op jit(solution)/shard_map/ppermute | solution.py:150
  398.6 6.9 %collective-permute-start.19 = (bf16[64,1280]{1,0:T(8,128)(2,1)S(1)}, bf16[64,1280]{1,0:T(8,128)(2,1)S(1)}, u32[]{:S(2)}, u32[]{:S(2)}) collective-permute-start(bf16[64,1280]{1,0:T(8,128)(2,1)S(1)} %fusion.10), channel_id=1, source_target_pairs={{0,64},{32,96},{64,128},{96,160},{128,192},{160,224},{192,0},{224,... | collective-permute-start | bytes 491528 | tf_op jit(solution)/shard_map/ppermute | solution.py:150
  407.0 16.3 %copy-start.2 = (bf16[128,32,64]{2,0,1:T(8,128)(2,1)S(1)}, bf16[128,32,64]{2,0,1:T(8,128)(2,1)}, u32[]{:S(2)}) copy-start(bf16[128,32,64]{2,0,1:T(8,128)(2,1)} %get-tuple-element.61) | copy-start | bytes 1572868
  407.0 20.0 %copy-start.1 = (bf16[1,128,2048]{2,1,0:T(8,128)(2,1)S(1)}, bf16[1,128,2048]{2,1,0:T(8,128)(2,1)}, u32[]{:S(2)}) copy-start(bf16[1,128,2048]{2,1,0:T(8,128)(2,1)} %param.7) | copy-start | bytes 1572868
  408.3 16.4 %collective-permute-start.22 = (bf16[64,1280]{1,0:T(8,128)(2,1)S(1)}, bf16[64,1280]{1,0:T(8,128)(2,1)}, u32[]{:S(2)}, u32[]{:S(2)}) collective-permute-start(bf16[64,1280]{1,0:T(8,128)(2,1)S(1)} %select_reduce_fusion), channel_id=1, source_target_pairs={{0,32},{32,0},{64,96},{96,64},{128,160},{160,128},{192,224},{224,1... | collective-permute-start | bytes 491528 | tf_op jit(solution)/shard_map/ppermute | solution.py:264
Sparse Core Ops, SparseCore 0:
  11.2 86.5 all-gather.1

commit v6 on v5

--- a/solution.py
+++ b/solution.py
@@ -178,10 +178,9 @@
     w_other = lax.ppermute(w_mine, "dp", pairs)
     proj_mine = jnp.dot(tokens, w_mine, preferred_element_type=jnp.float32).astype(jnp.bfloat16)
     proj_other = jnp.dot(tokens, w_other, preferred_element_type=jnp.float32).astype(jnp.bfloat16)
-    projected = jnp.concatenate(
-        [jnp.where(core == 0, proj_mine, proj_other), jnp.where(core == 0, proj_other, proj_mine)],
-        axis=1,
-    )
+    projected = jnp.zeros((tok_count, all_cols), jnp.bfloat16)
+    projected = lax.dynamic_update_slice_in_dim(projected, proj_mine, core * half, axis=1)
+    projected = lax.dynamic_update_slice_in_dim(projected, proj_other, (1 - core) * half, axis=1)
     queries = projected[:, :query_cols]
     key_proj = projected[:, query_cols : query_cols + kv_cols]
     value_proj = projected[:, query_cols + kv_cols :]
@@ -230,23 +229,28 @@
     ).astype(jnp.bfloat16)
     factor = 1.0 / math.sqrt(tok_count * seq_devices * dp_devices)
     over_tokens = (((0,), (0,)), ((), ()))
+    y_count = seq_devices // RING_Z
+    rows = tokens.shape[1] // seq_devices
+    tokens_zy = (
+        tokens.reshape(tok_count, y_count, RING_Z, rows).transpose(0, 2, 1, 3).reshape(tok_count, -1)
+    )
+
     def term_of(columns):
         return (
-            lax.dot_general(tokens, columns, over_tokens, preferred_element_type=jnp.float32)
+            lax.dot_general(tokens_zy, columns, over_tokens, preferred_element_type=jnp.float32)
             * factor
         ).astype(jnp.bfloat16)
 
     got = lax.ppermute(term_of(comb_other), "dp", pairs)
     keep = term_of(comb_mine)
-    rows = keep.shape[0] // seq_devices
-    y_count = seq_devices // RING_Z
-    keep4 = keep.reshape(y_count, RING_Z, rows, half)
-    got4 = got.reshape(y_count, RING_Z, rows, half)
+    grad_x_rows, keep = lax.optimization_barrier((grad_x_rows, keep))
+    keep4 = keep.reshape(RING_Z, y_count, rows, half)
+    got4 = got.reshape(RING_Z, y_count, rows, half)
     quarter = half // 2
 
     def chip_chunk(i, side):
-        a = lax.dynamic_index_in_dim(keep4, i, 1, keepdims=False)[..., side * quarter : (side + 1) * quarter]
-        b = lax.dynamic_index_in_dim(got4, i, 1, keepdims=False)[..., side * quarter : (side + 1) * quarter]
+        a = lax.dynamic_index_in_dim(keep4, i, 0, keepdims=False)[..., side * quarter : (side + 1) * quarter]
+        b = lax.dynamic_index_in_dim(got4, i, 0, keepdims=False)[..., side * quarter : (side + 1) * quarter]
         return (a.astype(jnp.float32) + b.astype(jnp.float32)).astype(jnp.bfloat16)
 
     by_y = ring_reduce_scatter(chip_chunk, RING_Z, 1, position)

time: 443 us -> 444 us (level)
  waiting for transfers between devices: 216 us -> 223 us
    convert_element_type x1 -> x0, local copies, waits for them, and re-layouts: 7.92 us -> none  [term_of(): return (lax.dot_general(tokens, columns, over_tokens, preferred_element_t...]
    optimization_barrier x0 -> x1, local copies, waits for them, and re-layouts: none -> 7.9 us  [per_device(): grad_x_rows, keep = lax.optimization_barrier((grad_x_rows, keep))]
    ppermute x6, waiting for transfers between devices: 8.17 us -> 12.7 us  [direct_sum(): lax.ppermute(lax.dynamic_index_in_dim(pieces, (mine + d) % size, 0, keepd...]
  transfers between devices with their start and end apart: 27 -> 27, of which waited for: 17 -> 19; matrix products, arithmetic and copies ran while one was open for 11% -> 10% of each run, Pallas kernels for 0% -> 0%
where the time goes in v6:
time: 444 us; the launch traced here: 436 us
  waiting for transfers between devices  223 us (50%)
  starting transfers between devices  63.3 us (14%)
  Pallas kernels  48.1 us (11%)
  local copies, waits for them, and re-layouts  43.7 us (10%)
  matrix products  25.6 us (6%)
  other arithmetic  17.2 us (4%)
  between operations  15 us (3%)
    all_gather x1, waiting for transfers between devices, per_device(): lax.all_gather(lax.dynamic_slice_in_dim(w_local, core * half, half, axis=...  88.9 us
    all_to_all x1, waiting for transfers between devices, per_device(): lax.all_to_all(back_sent, 'seq', split_axis=0, concat_axis=0, tiled=True)  49 us
    pallas_call x1, Pallas kernels, head_pass(): pl.pallas_call(head_kernel, grid_spec=grid_spec, out_shape=[jax.ShapeDtyp...  48.1 us
    ppermute x14, waiting for transfers between devices, ring_reduce_scatter(): got = lax.ppermute(buf, 'seq', perm)  33.9 us
    all_to_all x1, waiting for transfers between devices, per_device(): lax.all_to_all(sent, 'seq', split_axis=0, concat_axis=1, tiled=True)[0]  33.8 us
    ppermute x14, starting transfers between devices, ring_reduce_scatter(): got = lax.ppermute(buf, 'seq', perm)  22.4 us
    ppermute x6, waiting for transfers between devices, direct_sum(): lax.ppermute(lax.dynamic_index_in_dim(pieces, (mine + d) % size, 0, keepd...  12.7 us
    squeeze x1, local copies, waits for them, and re-layouts, chip_chunk(): lax.dynamic_index_in_dim(got4, i, 0, keepdims=False)  11 us
  transfers between devices with their start and end apart: 27, of which 19 were waited for; matrix products, arithmetic and copies ran while one was open for 10% of the time, Pallas kernels for 0%

profile of v6, /device:TPU:1, one launch (start us, length us, event | category | flops | bytes accessed | tf_op | source)
XLA Modules:
  0.0 435.8 jit_solution(6282660087242981083)
XLA Ops:
  7.2 1.7 fusion.18
  8.9 88.9 %all-gather.2.cloned.1.call-done = bf16[2048,1280]{1,0:T(8,128)(2,1)} async-done(((bf16[64,1280]{1,0:T(8,128)(2,1)}), bf16[2048,1280]{1,0:T(8,128)(2,1)}) %all-gather.2.cloned.1.call-update) | async-done | bytes 5242896 | tf_op jit(solution)/shard_map/all_gather | solution.py:175
  97.8 3.1 collective-permute-start
  100.9 2.0 copy.39
  103.0 5.3 %all-to-all-start.1 = ((bf16[32,128,64]{1,2,0:T(8,128)(2,1)}), bf16[32,128,64]{1,2,0:T(8,128)(2,1)S(1)}, u32[]{:S(2)}, u32[]{:S(2)}) async-start(bf16[32,128,64]{1,2,0:T(8,128)(2,1)} %bitcast.11), calls=%async_computation.1 | async-start | bytes 1048576 | tf_op jit(solution)/shard_map/all_to_all | solution.py:174
  108.4 4.3 fusion.4
  112.8 4.2 fusion.6
  117.3 1.3 pad_maximum_fusion.1
  118.6 4.6 %all-to-all-done.1 = bf16[32,128,64]{1,2,0:T(8,128)(2,1)S(1)} async-done(((bf16[32,128,64]{1,2,0:T(8,128)(2,1)}), bf16[32,128,64]{1,2,0:T(8,128)(2,1)S(1)}, u32[]{:S(2)}, u32[]{:S(2)}) %all-to-all-start.1) | async-done | bytes 524320 | tf_op jit(solution)/shard_map/all_to_all | solution.py:174
  123.1 7.4 %all-to-all-start = ((bf16[32,128,192]{1,2,0:T(8,128)(2,1)}), bf16[32,128,192]{1,2,0:T(8,128)(2,1)S(1)}, u32[]{:S(2)}, u32[]{:S(2)}) async-start(bf16[32,128,192]{1,2,0:T(8,128)(2,1)} %pad_maximum_fusion.1), calls=%async_computation | async-start | bytes 3145728 | tf_op jit(solution)/shard_map/all_to_all | solution.py:194
  130.6 0.7 reshape.124.table_ref
  131.9 1.4 copy.42.g_ref
  133.3 33.8 %all-to-all-done = bf16[32,128,192]{1,2,0:T(8,128)(2,1)S(1)} async-done(((bf16[32,128,192]{1,2,0:T(8,128)(2,1)}), bf16[32,128,192]{1,2,0:T(8,128)(2,1)S(1)}, u32[]{:S(2)}, u32[]{:S(2)}) %all-to-all-start) | async-done | bytes 1572896 | tf_op jit(solution)/shard_map/all_to_all | solution.py:194
  167.5 1.3 copy.38
  168.8 1.3 copy.40
  170.1 1.3 copy.41
  171.5 48.1 %shard_map.110 = (bf16[32,128,64]{2,1,0:T(8,128)(2,1)}, bf16[32,128,64]{2,1,0:T(8,128)(2,1)}, f32[32,128,64]{2,1,0:T(8,128)}, f32[32,128,64]{2,1,0:T(8,128)}) custom-call(s32[224]{0:T(256)} %reshape.124.table_ref, s32[1]{0:T(128)} %dynamic_slice.132.count_ref, bf16[32,128,64]{2,1,0:T(8,128)(2,1)} %bitcast.153, bf16[32,128,64]{2,1,0:T(8,128)(2,1)} %copy.42.g_ref, ...), custom_call_target="tpu_custom_call" | custom-call | flops 2818572288 | bytes 5242880 | tf_op jit(solution)/shard_map/pallas_call | solution.py:90
  219.7 1.9 convert.10
  222.4 2.7 pad_maximum_fusion
  225.1 7.9 %all-to-all-start.2 = ((bf16[32,128,256]{2,1,0:T(8,128)(2,1)}), bf16[32,128,256]{2,1,0:T(8,128)(2,1)S(1)}, u32[]{:S(2)}, u32[]{:S(2)}) async-start(bf16[32,128,256]{2,1,0:T(8,128)(2,1)} %pad_maximum_fusion), calls=%async_computation.2 | async-start | bytes 4194304 | tf_op jit(solution)/shard_map/all_to_all | solution.py:211
  233.4 49.0 %all-to-all-done.2 = bf16[32,128,256]{2,1,0:T(8,128)(2,1)S(1)} async-done(((bf16[32,128,256]{2,1,0:T(8,128)(2,1)}), bf16[32,128,256]{2,1,0:T(8,128)(2,1)S(1)}, u32[]{:S(2)}, u32[]{:S(2)}) %all-to-all-start.2) | async-done | bytes 2097184 | tf_op jit(solution)/shard_map/all_to_all | solution.py:211
  282.8 1.9 slice_bitcast_fusion
  284.7 1.6 copy.44
  286.3 3.8 fusion.1
  290.2 1.9 collective-permute-start.1
  292.1 3.8 fusion
  295.9 4.3 fusion.15
  300.2 5.1 %fusion.2 = bf16[128,2048]{1,0:T(8,128)(2,1)} fusion(f32[128,2048]{1,0:T(8,128)S(1)} %fusion.15, bf16[2048,1280]{1,0:T(8,128)(2,1)} %collective-permute-done, bf16[128,2560]{0,1:T(8,128)(2,1)S(1)} %pad_maximum_fusion.2, s32[]{:T(128)S(6)} %select_n.250), kind=kOutput, calls=%fused_computation.6 | convolution fusion | flops 671612928 | bytes 7143428 | tf_op jit(solution)/shard_map/dot_general | solution.py:228
  305.3 7.9 %copy.49 = bf16[2048,1280]{1,0:T(8,128)(2,1)} copy(bf16[2048,1280]{0,1:T(8,128)(2,1)} %fusion) | data formatting | bytes 10485760 | tf_op jit(solution)/shard_map/optimization_barrier | solution.py:246
  313.3 7.9 %copy.50 = bf16[2048,1280]{1,0:T(8,128)(2,1)} copy(bf16[2048,1280]{0,1:T(8,128)(2,1)} %collective-permute-done.1) | data formatting | bytes 10485760 | tf_op jit(solution)/shard_map/ppermute | solution.py:244
  321.1 11.0 %dynamic-slice_bitcast_fusion = (bf16[4,64,1280]{2,1,0:T(8,128)(2,1)S(1)}, bf16[4,64,1280]{2,1,0:T(8,128)(2,1)S(1)}, bf16[4,64,1280]{2,1,0:T(8,128)(2,1)S(1)}, b...) fusion(bf16[8,4,64,1280]{3,2,1,0:T(8,128)(2,1)} %bitcast.145, ...), kind=kLoop, calls=%fused_computation.32 | loop fusion | bytes 41943104 | tf_op jit(solution)/shard_map/jit(dynamic_index_in_dim)/squeeze | solution.py:253
  332.2 1.2 add_convert_fusion.29
  333.4 1.3 collective-permute-start.2
  334.7 1.2 add_convert_fusion.14
  335.9 1.5 collective-permute-start.9
  337.4 6.6 %collective-permute-done.2 = bf16[4,64,640]{2,1,0:T(8,128)(2,1)S(1)} collective-permute-done((bf16[4,64,640]{2,1,0:T(8,128)(2,1)S(1)}, bf16[4,64,640]{2,1,0:T(8,128)(2,1)S(1)}, u32[]{:S(2)}, u32[]{:S(2)}) %collective-permute-start.2) | collective-permute-done | bytes 327712 | tf_op jit(solution)/shard_map/ppermute | solution.py:134
  344.0 1.2 add_convert_fusion.27
  345.4 1.2 add_convert_fusion.12
  346.6 2.9 collective-permute-start.10
  349.5 5.5 %collective-permute-done.3 = bf16[4,64,640]{2,1,0:T(8,128)(2,1)S(1)} collective-permute-done((bf16[4,64,640]{2,1,0:T(8,128)(2,1)S(1)}, bf16[4,64,640]{2,1,0:T(8,128)(2,1)S(1)}, u32[]{:S(2)}, u32[]{:S(2)}) %collective-permute-start.3) | collective-permute-done | bytes 327712 | tf_op jit(solution)/shard_map/ppermute | solution.py:134
  355.5 3.5 collective-permute-start.11
  359.0 4.9 %collective-permute-done.4 = bf16[4,64,640]{2,1,0:T(8,128)(2,1)S(1)} collective-permute-done((bf16[4,64,640]{2,1,0:T(8,128)(2,1)S(1)}, bf16[4,64,640]{2,1,0:T(8,128)(2,1)S(1)}, u32[]{:S(2)}, u32[]{:S(2)}) %collective-permute-start.4) | collective-permute-done | bytes 327712 | tf_op jit(solution)/shard_map/ppermute | solution.py:134
  364.3 3.4 collective-permute-start.12
  367.7 4.3 collective-permute-done.5
  372.3 3.1 collective-permute-start.13
  375.4 3.9 collective-permute-done.6
  379.6 3.1 collective-permute-start.14
  382.7 4.1 collective-permute-done.7
  387.2 0.8 add_convert_fusion.2
  388.0 3.1 collective-permute-start.15
  391.1 4.2 collective-permute-done.8
  395.3 1.3 add_convert_fusion.15
  397.7 0.7 collective-permute-start.16
  398.4 3.0 collective-permute-done.18
  401.4 1.9 collective-permute-done.17
  403.2 1.7 collective-permute-done.16
  405.0 2.8 collective-permute-start.21
  408.2 0.7 collective-permute-start.19
  408.9 2.8 collective-permute-done.21
  411.7 1.8 collective-permute-done.20
  413.5 1.7 collective-permute-done.19
  416.0 9.8 %collective-permute-start.22 = (bf16[64,1280]{1,0:T(8,128)(2,1)S(1)}, bf16[64,1280]{1,0:T(8,128)(2,1)S(1)}, u32[]{:S(2)}, u32[]{:S(2)}) collective-permute-start(bf16[64,1280]{1,0:T(8,128)(2,1)S(1)} %select_reduce_fusion), channel_id=1, source_target_pairs={{0,32},{32,0},{64,96},{96,64},{128,160},{160,128},{192,224},{224,1... | collective-permute-start | bytes 491528 | tf_op jit(solution)/shard_map/ppermute | solution.py:268
  426.1 1.0 copy.51
  427.8 0.7 pad_maximum_fusion.4
  (78 shorter events, 8.8 us)
Async XLA Ops:
  7.2 123.3 %copy-start = (s32[32,32,7]{1,0,2:T(8,128)S(1)}, s32[32,32,7]{1,0,2:T(8,128)}, u32[]{:S(2)}) copy-start(s32[32,32,7]{1,0,2:T(8,128)} %param.11) | copy-start | bytes 86020
  7.2 90.6 %all-gather.2.cloned.1.call-start = ((), (), s32[]{:S(2)}) async-start(), calls=%async_computation.3 | async-start | bytes 5406720 | tf_op jit(solution)/shard_map/all_gather | solution.py:175
  97.8 14.9 %collective-permute-start = (bf16[2048,1280]{1,0:T(8,128)(2,1)}, bf16[2048,1280]{1,0:T(8,128)(2,1)}, u32[]{:S(2)}, u32[]{:S(2)}) collective-permute-start(bf16[2048,1280]{1,0:T(8,128)(2,1)} %all-gather.2.cloned.1.call-done), channel_id=1, source_target_pairs={{0,32},{32,0},{64,96},{96,64},{128,160},{160,128},{192,224},{224,1... | collective-permute-start | bytes 15728648 | tf_op jit(solution)/shard_map/ppermute | solution.py:178
  103.0 20.2 %all-to-all-start.1 = ((bf16[32,128,64]{1,2,0:T(8,128)(2,1)}), bf16[32,128,64]{1,2,0:T(8,128)(2,1)S(1)}, u32[]{:S(2)}, u32[]{:S(2)}) async-start(bf16[32,128,64]{1,2,0:T(8,128)(2,1)} %bitcast.11), calls=%async_computation.1 | async-start | bytes 1048576 | tf_op jit(solution)/shard_map/all_to_all | solution.py:174
  108.3 4.5 %copy-start.7 = (bf16[1,128,2048]{2,1,0:T(8,128)(2,1)S(1)}, bf16[1,128,2048]{2,1,0:T(8,128)(2,1)}, u32[]{:S(2)}) copy-start(bf16[1,128,2048]{2,1,0:T(8,128)(2,1)} %param.7) | copy-start | bytes 1572868
  117.0 14.3 %copy-start.8 = (s32[32]{0:T(128)S(1)}, s32[32]{0:T(128)}, u32[]{:S(2)}) copy-start(s32[32]{0:T(128)} %param.12) | copy-start | bytes 388
  123.1 44.0 %all-to-all-start = ((bf16[32,128,192]{1,2,0:T(8,128)(2,1)}), bf16[32,128,192]{1,2,0:T(8,128)(2,1)S(1)}, u32[]{:S(2)}, u32[]{:S(2)}) async-start(bf16[32,128,192]{1,2,0:T(8,128)(2,1)} %pad_maximum_fusion.1), calls=%async_computation | async-start | bytes 3145728 | tf_op jit(solution)/shard_map/all_to_all | solution.py:194
  219.6 2.2 copy-start.3
  219.6 2.5 copy-start.5
  219.6 2.8 copy-start.6
  225.1 57.2 %all-to-all-start.2 = ((bf16[32,128,256]{2,1,0:T(8,128)(2,1)}), bf16[32,128,256]{2,1,0:T(8,128)(2,1)S(1)}, u32[]{:S(2)}, u32[]{:S(2)}) async-start(bf16[32,128,256]{2,1,0:T(8,128)(2,1)} %pad_maximum_fusion), calls=%async_computation.2 | async-start | bytes 4194304 | tf_op jit(solution)/shard_map/all_to_all | solution.py:211
  290.2 23.1 %collective-permute-start.1 = (bf16[2048,1280]{0,1:T(8,128)(2,1)}, bf16[2048,1280]{0,1:T(8,128)(2,1)}, u32[]{:S(2)}, u32[]{:S(2)}) collective-permute-start(bf16[2048,1280]{0,1:T(8,128)(2,1)} %fusion.1), channel_id=1, source_target_pairs={{0,32},{32,0},{64,96},{96,64},{128,160},{160,128},{192,224},{224,1... | collective-permute-start | bytes 15728648 | tf_op jit(solution)/shard_map/ppermute | solution.py:244
  332.2 22.8 %copy-start.4 = (bf16[4,64,1280]{2,1,0:T(8,128)(2,1)S(1)}, bf16[4,64,1280]{2,1,0:T(8,128)(2,1)}, u32[]{:S(2)}) copy-start(bf16[4,64,1280]{2,1,0:T(8,128)(2,1)} %get-tuple-element.82) | copy-start | bytes 1966084
  333.4 10.6 %collective-permute-start.2 = (bf16[4,64,640]{2,1,0:T(8,128)(2,1)S(1)}, bf16[4,64,640]{2,1,0:T(8,128)(2,1)S(1)}, u32[]{:S(2)}, u32[]{:S(2)}) collective-permute-start(bf16[4,64,640]{2,1,0:T(8,128)(2,1)S(1)} %add_convert_fusion.29), channel_id=1, source_target_pairs={{0,1},{1,2},{2,3},{3,4},{4,5},{5,6},{6,7},{7,0},{8,9},{9,10},{10,1... | collective-permute-start | bytes 983048 | tf_op jit(solution)/shard_map/ppermute | solution.py:134
  335.9 9.5 %collective-permute-start.9 = (bf16[4,64,640]{2,1,0:T(8,128)(2,1)S(1)}, bf16[4,64,640]{2,1,0:T(8,128)(2,1)S(1)}, u32[]{:S(2)}, u32[]{:S(2)}) collective-permute-start(bf16[4,64,640]{2,1,0:T(8,128)(2,1)S(1)} %add_convert_fusion.14), channel_id=1, source_target_pairs={{1,0},{2,1},{3,2},{4,3},{5,4},{6,5},{7,6},{0,7},{9,8},{10,9},{11,1... | collective-permute-start | bytes 983048 | tf_op jit(solution)/shard_map/ppermute | solution.py:134
  345.2 9.7 %collective-permute-start.3 = (bf16[4,64,640]{2,1,0:T(8,128)(2,1)S(1)}, bf16[4,64,640]{2,1,0:T(8,128)(2,1)S(1)}, u32[]{:S(2)}, u32[]{:S(2)}) collective-permute-start(bf16[4,64,640]{2,1,0:T(8,128)(2,1)S(1)} %add_convert_fusion.27), channel_id=1, source_target_pairs={{0,1},{1,2},{2,3},{3,4},{4,5},{5,6},{6,7},{7,0},{8,9},{9,10},{10,1... | collective-permute-start | bytes 983048 | tf_op jit(solution)/shard_map/ppermute | solution.py:134
  346.6 8.8 %collective-permute-start.10 = (bf16[4,64,640]{2,1,0:T(8,128)(2,1)S(1)}, bf16[4,64,640]{2,1,0:T(8,128)(2,1)S(1)}, u32[]{:S(2)}, u32[]{:S(2)}) collective-permute-start(bf16[4,64,640]{2,1,0:T(8,128)(2,1)S(1)} %add_convert_fusion.12), channel_id=1, source_target_pairs={{1,0},{2,1},{3,2},{4,3},{5,4},{6,5},{7,6},{0,7},{9,8},{10,9},{11,1... | collective-permute-start | bytes 983048 | tf_op jit(solution)/shard_map/ppermute | solution.py:134
  355.1 8.8 %collective-permute-start.4 = (bf16[4,64,640]{2,1,0:T(8,128)(2,1)S(1)}, bf16[4,64,640]{2,1,0:T(8,128)(2,1)S(1)}, u32[]{:S(2)}, u32[]{:S(2)}) collective-permute-start(bf16[4,64,640]{2,1,0:T(8,128)(2,1)S(1)} %add_convert_fusion.25), channel_id=1, source_target_pairs={{0,1},{1,2},{2,3},{3,4},{4,5},{5,6},{6,7},{7,0},{8,9},{9,10},{10,1... | collective-permute-start | bytes 983048 | tf_op jit(solution)/shard_map/ppermute | solution.py:134
  355.5 8.6 %collective-permute-start.11 = (bf16[4,64,640]{2,1,0:T(8,128)(2,1)S(1)}, bf16[4,64,640]{2,1,0:T(8,128)(2,1)S(1)}, u32[]{:S(2)}, u32[]{:S(2)}) collective-permute-start(bf16[4,64,640]{2,1,0:T(8,128)(2,1)S(1)} %add_convert_fusion.10), channel_id=1, source_target_pairs={{1,0},{2,1},{3,2},{4,3},{5,4},{6,5},{7,6},{0,7},{9,8},{10,9},{11,1... | collective-permute-start | bytes 983048 | tf_op jit(solution)/shard_map/ppermute | solution.py:134
  364.0 7.9 %collective-permute-start.5 = (bf16[4,64,640]{2,1,0:T(8,128)(2,1)S(1)}, bf16[4,64,640]{2,1,0:T(8,128)(2,1)S(1)}, u32[]{:S(2)}, u32[]{:S(2)}) collective-permute-start(bf16[4,64,640]{2,1,0:T(8,128)(2,1)S(1)} %add_convert_fusion.23), channel_id=1, source_target_pairs={{0,1},{1,2},{2,3},{3,4},{4,5},{5,6},{6,7},{7,0},{8,9},{9,10},{10,1... | collective-permute-start | bytes 983048 | tf_op jit(solution)/shard_map/ppermute | solution.py:134
  364.3 7.9 %collective-permute-start.12 = (bf16[4,64,640]{2,1,0:T(8,128)(2,1)S(1)}, bf16[4,64,640]{2,1,0:T(8,128)(2,1)S(1)}, u32[]{:S(2)}, u32[]{:S(2)}) collective-permute-start(bf16[4,64,640]{2,1,0:T(8,128)(2,1)S(1)} %add_convert_fusion.8), channel_id=1, source_target_pairs={{1,0},{2,1},{3,2},{4,3},{5,4},{6,5},{7,6},{0,7},{9,8},{10,9},{11,1... | collective-permute-start | bytes 983048 | tf_op jit(solution)/shard_map/ppermute | solution.py:134
  372.1 7.2 %collective-permute-start.6 = (bf16[4,64,640]{2,1,0:T(8,128)(2,1)S(1)}, bf16[4,64,640]{2,1,0:T(8,128)(2,1)S(1)}, u32[]{:S(2)}, u32[]{:S(2)}) collective-permute-start(bf16[4,64,640]{2,1,0:T(8,128)(2,1)S(1)} %add_convert_fusion.21), channel_id=1, source_target_pairs={{0,1},{1,2},{2,3},{3,4},{4,5},{5,6},{6,7},{7,0},{8,9},{9,10},{10,1... | collective-permute-start | bytes 983048 | tf_op jit(solution)/shard_map/ppermute | solution.py:134
  372.3 7.2 %collective-permute-start.13 = (bf16[4,64,640]{2,1,0:T(8,128)(2,1)S(1)}, bf16[4,64,640]{2,1,0:T(8,128)(2,1)S(1)}, u32[]{:S(2)}, u32[]{:S(2)}) collective-permute-start(bf16[4,64,640]{2,1,0:T(8,128)(2,1)S(1)} %add_convert_fusion.6), channel_id=1, source_target_pairs={{1,0},{2,1},{3,2},{4,3},{5,4},{6,5},{7,6},{0,7},{9,8},{10,9},{11,1... | collective-permute-start | bytes 983048 | tf_op jit(solution)/shard_map/ppermute | solution.py:134
  379.4 7.4 %collective-permute-start.7 = (bf16[4,64,640]{2,1,0:T(8,128)(2,1)S(1)}, bf16[4,64,640]{2,1,0:T(8,128)(2,1)S(1)}, u32[]{:S(2)}, u32[]{:S(2)}) collective-permute-start(bf16[4,64,640]{2,1,0:T(8,128)(2,1)S(1)} %add_convert_fusion.19), channel_id=1, source_target_pairs={{0,1},{1,2},{2,3},{3,4},{4,5},{5,6},{6,7},{7,0},{8,9},{9,10},{10,1... | collective-permute-start | bytes 983048 | tf_op jit(solution)/shard_map/ppermute | solution.py:134
  379.6 7.5 %collective-permute-start.14 = (bf16[4,64,640]{2,1,0:T(8,128)(2,1)S(1)}, bf16[4,64,640]{2,1,0:T(8,128)(2,1)S(1)}, u32[]{:S(2)}, u32[]{:S(2)}) collective-permute-start(bf16[4,64,640]{2,1,0:T(8,128)(2,1)S(1)} %add_convert_fusion.4), channel_id=1, source_target_pairs={{1,0},{2,1},{3,2},{4,3},{5,4},{6,5},{7,6},{0,7},{9,8},{10,9},{11,1... | collective-permute-start | bytes 983048 | tf_op jit(solution)/shard_map/ppermute | solution.py:134
  386.9 8.4 %collective-permute-start.8 = (bf16[4,64,640]{2,1,0:T(8,128)(2,1)S(1)}, bf16[4,64,640]{2,1,0:T(8,128)(2,1)S(1)}, u32[]{:S(2)}, u32[]{:S(2)}) collective-permute-start(bf16[4,64,640]{2,1,0:T(8,128)(2,1)S(1)} %add_convert_fusion.17), channel_id=1, source_target_pairs={{0,1},{1,2},{2,3},{3,4},{4,5},{5,6},{6,7},{7,0},{8,9},{9,10},{10,1... | collective-permute-start | bytes 983048 | tf_op jit(solution)/shard_map/ppermute | solution.py:134
  388.0 8.6 %collective-permute-start.15 = (bf16[4,64,640]{2,1,0:T(8,128)(2,1)}, bf16[4,64,640]{2,1,0:T(8,128)(2,1)S(1)}, u32[]{:S(2)}, u32[]{:S(2)}) collective-permute-start(bf16[4,64,640]{2,1,0:T(8,128)(2,1)} %add_convert_fusion.2), channel_id=1, source_target_pairs={{1,0},{2,1},{3,2},{4,3},{5,4},{6,5},{7,6},{0,7},{9,8},{10,9},{11,1... | collective-permute-start | bytes 983048 | tf_op jit(solution)/shard_map/ppermute | solution.py:134
  395.3 30.4 %copy-start.2 = (bf16[128,32,64]{2,0,1:T(8,128)(2,1)S(1)}, bf16[128,32,64]{2,0,1:T(8,128)(2,1)}, u32[]{:S(2)}) copy-start(bf16[128,32,64]{2,0,1:T(8,128)(2,1)} %get-tuple-element.65) | copy-start | bytes 1572868
  396.8 4.5 %collective-permute-start.18 = (bf16[64,1280]{1,0:T(8,128)(2,1)S(1)}, bf16[64,1280]{1,0:T(8,128)(2,1)S(1)}, u32[]{:S(2)}, u32[]{:S(2)}) collective-permute-start(bf16[64,1280]{1,0:T(8,128)(2,1)S(1)} %get-tuple-element.71), channel_id=1, source_target_pairs={{0,24},{1,25},{2,26},{3,27},{4,28},{5,29},{6,30},{7,31},{8,0},{9,1... | collective-permute-start | bytes 491528 | tf_op jit(solution)/shard_map/ppermute | solution.py:150
  397.4 5.8 %collective-permute-start.17 = (bf16[64,1280]{1,0:T(8,128)(2,1)S(1)}, bf16[64,1280]{1,0:T(8,128)(2,1)S(1)}, u32[]{:S(2)}, u32[]{:S(2)}) collective-permute-start(bf16[64,1280]{1,0:T(8,128)(2,1)S(1)} %get-tuple-element.70), channel_id=1, source_target_pairs={{0,16},{1,17},{2,18},{3,19},{4,20},{5,21},{6,22},{7,23},{8,24},{9,... | collective-permute-start | bytes 491528 | tf_op jit(solution)/shard_map/ppermute | solution.py:150
  397.7 7.2 %collective-permute-start.16 = (bf16[64,1280]{1,0:T(8,128)(2,1)S(1)}, bf16[64,1280]{1,0:T(8,128)(2,1)S(1)}, u32[]{:S(2)}, u32[]{:S(2)}) collective-permute-start(bf16[64,1280]{1,0:T(8,128)(2,1)S(1)} %get-tuple-element.69), channel_id=1, source_target_pairs={{0,8},{1,9},{2,10},{3,11},{4,12},{5,13},{6,14},{7,15},{8,16},{9,17... | collective-permute-start | bytes 491528 | tf_op jit(solution)/shard_map/ppermute | solution.py:150
  398.4 30.2 %copy-start.1 = (s32[32,32,7]{1,0,2:T(8,128)S(1)}, s32[32,32,7]{1,0,2:T(8,128)}, u32[]{:S(2)}) copy-start(s32[32,32,7]{1,0,2:T(8,128)} %param.11) | copy-start | bytes 86020
  405.0 6.8 %collective-permute-start.21 = (bf16[64,1280]{1,0:T(8,128)(2,1)S(1)}, bf16[64,1280]{1,0:T(8,128)(2,1)S(1)}, u32[]{:S(2)}, u32[]{:S(2)}) collective-permute-start(bf16[64,1280]{1,0:T(8,128)(2,1)S(1)} %fusion.11), channel_id=1, source_target_pairs={{0,192},{32,224},{64,0},{96,32},{128,64},{160,96},{192,128},{224,1... | collective-permute-start | bytes 491528 | tf_op jit(solution)/shard_map/ppermute | solution.py:150
  407.7 5.8 %collective-permute-start.20 = (bf16[64,1280]{1,0:T(8,128)(2,1)S(1)}, bf16[64,1280]{1,0:T(8,128)(2,1)S(1)}, u32[]{:S(2)}, u32[]{:S(2)}) collective-permute-start(bf16[64,1280]{1,0:T(8,128)(2,1)S(1)} %fusion.11), channel_id=1, source_target_pairs={{0,128},{32,160},{64,192},{96,224},{128,0},{160,32},{192,64},{224,... | collective-permute-start | bytes 491528 | tf_op jit(solution)/shard_map/ppermute | solution.py:150
  408.2 7.0 %collective-permute-start.19 = (bf16[64,1280]{1,0:T(8,128)(2,1)S(1)}, bf16[64,1280]{1,0:T(8,128)(2,1)S(1)}, u32[]{:S(2)}, u32[]{:S(2)}) collective-permute-start(bf16[64,1280]{1,0:T(8,128)(2,1)S(1)} %fusion.11), channel_id=1, source_target_pairs={{0,64},{32,96},{64,128},{96,160},{128,192},{160,224},{192,0},{224,... | collective-permute-start | bytes 491528 | tf_op jit(solution)/shard_map/ppermute | solution.py:150
  416.0 11.2 %collective-permute-start.22 = (bf16[64,1280]{1,0:T(8,128)(2,1)S(1)}, bf16[64,1280]{1,0:T(8,128)(2,1)S(1)}, u32[]{:S(2)}, u32[]{:S(2)}) collective-permute-start(bf16[64,1280]{1,0:T(8,128)(2,1)S(1)} %select_reduce_fusion), channel_id=1, source_target_pairs={{0,32},{32,0},{64,96},{96,64},{128,160},{160,128},{192,224},{224,1... | collective-permute-start | bytes 491528 | tf_op jit(solution)/shard_map/ppermute | solution.py:268
Sparse Core Ops, SparseCore 0:
  11.2 86.5 all-gather.1

commit v7 on v6

--- a/solution.py
+++ b/solution.py
@@ -231,29 +231,46 @@
     over_tokens = (((0,), (0,)), ((), ()))
     y_count = seq_devices // RING_Z
     rows = tokens.shape[1] // seq_devices
-    tokens_zy = (
-        tokens.reshape(tok_count, y_count, RING_Z, rows).transpose(0, 2, 1, 3).reshape(tok_count, -1)
-    )
-
-    def term_of(columns):
+    span = y_count * rows
+    quarter = half // 2
+    tok4 = tokens.reshape(tok_count, y_count, RING_Z, rows)
+    z_me = position % RING_Z
+
+    def ring_tokens(sign):
+        order = (z_me - sign * (1 + jnp.arange(RING_Z))) % RING_Z
+        return jnp.take(tok4, order, axis=2).transpose(0, 2, 1, 3).reshape(tok_count, -1)
+
+    def term_t(columns, toks):
         return (
-            lax.dot_general(tokens_zy, columns, over_tokens, preferred_element_type=jnp.float32)
+            lax.dot_general(columns, toks, over_tokens, preferred_element_type=jnp.float32)
             * factor
         ).astype(jnp.bfloat16)
 
-    got = lax.ppermute(term_of(comb_other), "dp", pairs)
-    keep = term_of(comb_mine)
+    signs = (1, -1)
+    toks = [ring_tokens(sign) for sign in signs]
+    give = jnp.stack(
+        [term_t(comb_other[:, i * quarter : (i + 1) * quarter], toks[i]) for i in range(2)]
+    )
+    got = lax.ppermute(give, "dp", pairs)
+    keep = [term_t(comb_mine[:, i * quarter : (i + 1) * quarter], toks[i]) for i in range(2)]
     grad_x_rows, keep = lax.optimization_barrier((grad_x_rows, keep))
-    keep4 = keep.reshape(RING_Z, y_count, rows, half)
-    got4 = got.reshape(RING_Z, y_count, rows, half)
-    quarter = half // 2
-
-    def chip_chunk(i, side):
-        a = lax.dynamic_index_in_dim(keep4, i, 0, keepdims=False)[..., side * quarter : (side + 1) * quarter]
-        b = lax.dynamic_index_in_dim(got4, i, 0, keepdims=False)[..., side * quarter : (side + 1) * quarter]
-        return (a.astype(jnp.float32) + b.astype(jnp.float32)).astype(jnp.bfloat16)
-
-    by_y = ring_reduce_scatter(chip_chunk, RING_Z, 1, position)
+    ahead = [(s, (s // RING_Z) * RING_Z + (s % RING_Z + 1) % RING_Z) for s in range(seq_devices)]
+    behind = [(b, a) for (a, b) in ahead]
+    ends = []
+    for i, perm in enumerate((ahead, behind)):
+
+        def chunk(k):
+            piece = slice(k * span, (k + 1) * span)
+            return (
+                keep[i][:, piece].astype(jnp.float32) + got[i][:, piece].astype(jnp.float32)
+            ).astype(jnp.bfloat16)
+
+        buf = chunk(0)
+        for k in range(RING_Z - 1):
+            arrived = lax.ppermute(buf, "seq", perm)
+            buf = (arrived.astype(jnp.float32) + chunk(k + 1).astype(jnp.float32)).astype(jnp.bfloat16)
+        ends.append(buf)
+    by_y = jnp.concatenate(ends, axis=0).reshape(half, y_count, rows).transpose(1, 2, 0)
     from_y = direct_sum(by_y, "seq", y_count, RING_Z, position // RING_Z)
     total = from_y[0].astype(jnp.float32)
     for piece in from_y[1:]:

time: 444 us -> 422 us (0.950)
  local copies, waits for them, and re-layouts: 43.7 us -> 22.4 us
    optimization_barrier x1 -> x0, local copies, waits for them, and re-layouts: 7.9 us -> none  [per_device(): grad_x_rows, keep = lax.optimization_barrier((grad_x_rows, keep))]
    ppermute x1 -> x0, local copies, waits for them, and re-layouts: 7.9 us -> none  [per_device(): got = lax.ppermute(term_of(comb_other), 'dp', pairs)]
    squeeze x1 -> x2, local copies, waits for them, and re-layouts: 11 us -> 3.15 us  [the longest x1 3.11 us: chunk(): got[i][:, piece].astype(jnp.float32)]
  transfers between devices with their start and end apart: 27 -> 27, of which waited for: 19 -> 19; matrix products, arithmetic and copies ran while one was open for 10% -> 9% of each run, Pallas kernels for 0% -> 0%
where the time goes in v7:
time: 422 us; the launch traced here: 413 us
  waiting for transfers between devices  223 us (53%)
  starting transfers between devices  64.3 us (15%)
  Pallas kernels  48.2 us (11%)
  local copies, waits for them, and re-layouts  22.4 us (5%)
  matrix products  22.2 us (5%)
  other arithmetic  19 us (5%)
  between operations  15 us (4%)
    all_gather x1, waiting for transfers between devices, per_device(): lax.all_gather(lax.dynamic_slice_in_dim(w_local, core * half, half, axis=...  88.8 us
    pallas_call x1, Pallas kernels, head_pass(): pl.pallas_call(head_kernel, grid_spec=grid_spec, out_shape=[jax.ShapeDtyp...  48.2 us
    all_to_all x1, waiting for transfers between devices, per_device(): lax.all_to_all(back_sent, 'seq', split_axis=0, concat_axis=0, tiled=True)  45 us
    ppermute x14, waiting for transfers between devices, per_device(): arrived = lax.ppermute(buf, 'seq', perm)  37.7 us
    all_to_all x1, waiting for transfers between devices, per_device(): lax.all_to_all(sent, 'seq', split_axis=0, concat_axis=1, tiled=True)[0]  33.9 us
    ppermute x14, starting transfers between devices, per_device(): arrived = lax.ppermute(buf, 'seq', perm)  20.4 us
    ppermute x6, waiting for transfers between devices, direct_sum(): lax.ppermute(lax.dynamic_index_in_dim(pieces, (mine + d) % size, 0, keepd...  12.4 us
    ppermute x1, starting transfers between devices, per_device(): other_half = lax.ppermute(part, 'dp', pairs)  10.4 us
  transfers between devices with their start and end apart: 27, of which 19 were waited for; matrix products, arithmetic and copies ran while one was open for 9% of the time, Pallas kernels for 0%

profile of v7, /device:TPU:1, one launch (start us, length us, event | category | flops | bytes accessed | tf_op | source)
XLA Modules:
  0.0 413.5 jit_solution(9658337060908270607)
XLA Ops:
  7.3 1.7 fusion.16
  9.0 88.8 %all-gather.2.cloned.1.call-done = bf16[2048,1280]{1,0:T(8,128)(2,1)} async-done(((bf16[64,1280]{1,0:T(8,128)(2,1)}), bf16[2048,1280]{1,0:T(8,128)(2,1)}) %all-gather.2.cloned.1.call-update) | async-done | bytes 5242896 | tf_op jit(solution)/shard_map/all_gather | solution.py:175
  97.8 3.1 collective-permute-start
  100.9 2.0 copy.38
  103.0 5.3 %all-to-all-start.1 = ((bf16[32,128,64]{1,2,0:T(8,128)(2,1)}), bf16[32,128,64]{1,2,0:T(8,128)(2,1)S(1)}, u32[]{:S(2)}, u32[]{:S(2)}) async-start(bf16[32,128,64]{1,2,0:T(8,128)(2,1)} %bitcast.11), calls=%async_computation.1 | async-start | bytes 1048576 | tf_op jit(solution)/shard_map/all_to_all | solution.py:174
  108.4 4.2 %fusion.4 = bf16[128,2560]{0,1:T(8,128)(2,1)S(1)} fusion(bf16[128,2560]{0,1:T(8,128)(2,1)S(1)} %broadcast_in_dim.31, s32[]{:T(128)S(6)} %select_n.136, bf16[2048,1280]{1,0:T(8,128)(2,1)} %all-gather.2.cloned.1.call-done, bf16[1,128,2048]{2,1,0:T(8,128)(2,1)S(1)} %copy-done.9), kind=kOutput, calls=%fused_computation.17 | convolution fusion | flops 671252480 | bytes 6094852 | tf_op jit(solution)/shard_map/dot_general | solution.py:179
  112.6 4.2 %fusion.6 = bf16[128,2560]{0,1:T(8,128)(2,1)S(1)} fusion(bf16[128,2560]{0,1:T(8,128)(2,1)S(1)} %fusion.4, s32[]{:T(128)S(6)} %select_n.137, bf16[2048,1280]{1,0:T(8,128)(2,1)} %collective-permute-done, bf16[1,128,2048]{2,1,0:T(8,128)(2,1)S(1)} %copy-done.9), kind=kOutput, calls=%fused_computation.19 | convolution fusion | flops 671252480 | bytes 6094852 | tf_op jit(solution)/shard_map/dot_general | solution.py:180
  117.1 1.3 pad_maximum_fusion.2
  118.4 4.7 %all-to-all-done.1 = bf16[32,128,64]{1,2,0:T(8,128)(2,1)S(1)} async-done(((bf16[32,128,64]{1,2,0:T(8,128)(2,1)}), bf16[32,128,64]{1,2,0:T(8,128)(2,1)S(1)}, u32[]{:S(2)}, u32[]{:S(2)}) %all-to-all-start.1) | async-done | bytes 524320 | tf_op jit(solution)/shard_map/all_to_all | solution.py:174
  123.1 7.4 %all-to-all-start = ((bf16[32,128,192]{1,2,0:T(8,128)(2,1)}), bf16[32,128,192]{1,2,0:T(8,128)(2,1)S(1)}, u32[]{:S(2)}, u32[]{:S(2)}) async-start(bf16[32,128,192]{1,2,0:T(8,128)(2,1)} %pad_maximum_fusion.2), calls=%async_computation | async-start | bytes 3145728 | tf_op jit(solution)/shard_map/all_to_all | solution.py:194
  130.6 0.7 reshape.129.table_ref
  131.9 1.4 copy.41.g_ref
  133.3 33.9 %all-to-all-done = bf16[32,128,192]{1,2,0:T(8,128)(2,1)S(1)} async-done(((bf16[32,128,192]{1,2,0:T(8,128)(2,1)}), bf16[32,128,192]{1,2,0:T(8,128)(2,1)S(1)}, u32[]{:S(2)}, u32[]{:S(2)}) %all-to-all-start) | async-done | bytes 1572896 | tf_op jit(solution)/shard_map/all_to_all | solution.py:194
  167.5 1.3 copy.37
  168.8 1.3 copy.39
  170.2 1.3 copy.40
  171.5 48.2 %shard_map.110 = (bf16[32,128,64]{2,1,0:T(8,128)(2,1)}, bf16[32,128,64]{2,1,0:T(8,128)(2,1)}, f32[32,128,64]{2,1,0:T(8,128)}, f32[32,128,64]{2,1,0:T(8,128)}) custom-call(s32[224]{0:T(256)} %reshape.129.table_ref, s32[1]{0:T(128)} %dynamic_slice.35.count_ref, bf16[32,128,64]{2,1,0:T(8,128)(2,1)} %bitcast.115, bf16[32,128,64]{2,1,0:T(8,128)(2,1)} %copy.41.g_ref, ...), custom_call_target="tpu_custom_call" | custom-call | flops 2818572288 | bytes 5242880 | tf_op jit(solution)/shard_map/pallas_call | solution.py:90
  219.7 1.9 convert.11
  222.5 2.7 pad_maximum_fusion.1
  225.2 8.0 %all-to-all-start.2 = ((bf16[32,128,256]{2,1,0:T(8,128)(2,1)}), bf16[32,128,256]{2,1,0:T(8,128)(2,1)S(1)}, u32[]{:S(2)}, u32[]{:S(2)}) async-start(bf16[32,128,256]{2,1,0:T(8,128)(2,1)} %pad_maximum_fusion.1), calls=%async_computation.2 | async-start | bytes 4194304 | tf_op jit(solution)/shard_map/all_to_all | solution.py:211
  234.3 1.4 gather_fusion.2
  235.8 1.2 broadcast_select_fusion
  237.0 45.0 %all-to-all-done.2 = bf16[32,128,256]{2,1,0:T(8,128)(2,1)S(1)} async-done(((bf16[32,128,256]{2,1,0:T(8,128)(2,1)}), bf16[32,128,256]{2,1,0:T(8,128)(2,1)S(1)}, u32[]{:S(2)}, u32[]{:S(2)}) %all-to-all-start.2) | async-done | bytes 2097184 | tf_op jit(solution)/shard_map/all_to_all | solution.py:211
  282.5 1.8 slice_bitcast_fusion.2
  284.3 1.6 copy.43
  286.0 0.8 fusion
  286.8 0.8 fusion.1
  287.7 2.7 pad_maximum_fusion
  290.4 2.4 collective-permute-start.1
  292.8 0.8 multiply_convert_fusion.3
  293.6 0.8 multiply_convert_fusion.2
  294.5 5.3 %fusion.13 = f32[128,2048]{1,0:T(8,128)S(1)} fusion(bf16[2048,1280]{1,0:T(8,128)(2,1)} %all-gather.2.cloned.1.call-done, bf16[128,2560]{0,1:T(8,128)(2,1)S(1)} %pad_maximum_fusion.3, s32[]{:T(128)S(6)} %select_n.136), kind=kOutput, calls=%fused_computation.72 | convolution fusion | flops 671088640 | bytes 6619140 | tf_op jit(solution)/shard_map/dot_general | solution.py:227
  299.8 5.1 %fusion.2 = bf16[128,2048]{1,0:T(8,128)(2,1)} fusion(f32[128,2048]{1,0:T(8,128)S(1)} %fusion.13, bf16[2048,1280]{1,0:T(8,128)(2,1)} %collective-permute-done, bf16[128,2560]{0,1:T(8,128)(2,1)S(1)} %pad_maximum_fusion.3, s32[]{:T(128)S(6)} %select_n.137), kind=kOutput, calls=%fused_computation.13 | convolution fusion | flops 671612928 | bytes 7143428 | tf_op jit(solution)/shard_map/dot_general | solution.py:228
  304.9 3.1 slice_bitcast_fusion.1
  308.9 1.1 collective-permute-start.2
  310.0 7.6 %collective-permute-done.9 = bf16[640,256]{1,0:T(8,128)(2,1)S(1)} collective-permute-done((bf16[640,256]{1,0:T(8,128)(2,1)S(1)}, bf16[640,256]{1,0:T(8,128)(2,1)S(1)}, u32[]{:S(2)}, u32[]{:S(2)}) %collective-permute-start.9) | collective-permute-done | bytes 327712 | tf_op jit(solution)/shard_map/ppermute | solution.py:270
  317.8 1.8 collective-permute-start.10
  320.1 6.2 %collective-permute-done.10 = bf16[640,256]{1,0:T(8,128)(2,1)S(1)} collective-permute-done((bf16[640,256]{1,0:T(8,128)(2,1)S(1)}, bf16[640,256]{1,0:T(8,128)(2,1)S(1)}, u32[]{:S(2)}, u32[]{:S(2)}) %collective-permute-start.10) | collective-permute-done | bytes 327712 | tf_op jit(solution)/shard_map/ppermute | solution.py:270
  326.5 3.0 collective-permute-start.11
  329.8 5.0 %collective-permute-done.11 = bf16[640,256]{1,0:T(8,128)(2,1)S(1)} collective-permute-done((bf16[640,256]{1,0:T(8,128)(2,1)S(1)}, bf16[640,256]{1,0:T(8,128)(2,1)S(1)}, u32[]{:S(2)}, u32[]{:S(2)}) %collective-permute-start.11) | collective-permute-done | bytes 327712 | tf_op jit(solution)/shard_map/ppermute | solution.py:270
  335.1 3.5 collective-permute-start.12
  338.8 4.1 collective-permute-done.12
  343.2 3.5 collective-permute-start.13
  346.9 3.7 collective-permute-done.13
  350.9 3.2 collective-permute-start.14
  354.4 3.8 collective-permute-done.14
  358.4 3.2 collective-permute-start.15
  361.8 0.9 add_convert_fusion.17
  362.8 4.0 collective-permute-done.15
  366.7 1.2 add_convert_fusion
  367.9 2.9 collective-permute-done.8
  370.8 1.2 add_convert_fusion.15
  372.3 2.4 collective-permute-start.18
  375.4 0.8 collective-permute-start.16
  376.2 2.6 collective-permute-done.18
  378.8 1.8 collective-permute-done.17
  380.6 1.7 collective-permute-done.16
  382.3 2.5 collective-permute-start.21
  385.8 3.0 collective-permute-done.21
  388.8 1.8 collective-permute-done.20
  390.5 1.7 collective-permute-done.19
  393.0 10.4 %collective-permute-start.22 = (bf16[64,1280]{1,0:T(8,128)(2,1)S(1)}, bf16[64,1280]{1,0:T(8,128)(2,1)S(1)}, u32[]{:S(2)}, u32[]{:S(2)}) collective-permute-start(bf16[64,1280]{1,0:T(8,128)(2,1)S(1)} %select_reduce_fusion), channel_id=1, source_target_pairs={{0,32},{32,0},{64,96},{96,64},{128,160},{160,128},{192,224},{224,1... | collective-permute-start | bytes 491528 | tf_op jit(solution)/shard_map/ppermute | solution.py:285
  403.8 1.0 copy.48
  405.5 0.7 pad_maximum_fusion.6
  (92 shorter events, 11.8 us)
Async XLA Ops:
  7.2 123.4 %copy-start = (s32[32,32,7]{1,0,2:T(8,128)S(1)}, s32[32,32,7]{1,0,2:T(8,128)}, u32[]{:S(2)}) copy-start(s32[32,32,7]{1,0,2:T(8,128)} %param.13) | copy-start | bytes 86020
  7.2 101.2 %copy-start.9 = (bf16[1,128,2048]{2,1,0:T(8,128)(2,1)S(1)}, bf16[1,128,2048]{2,1,0:T(8,128)(2,1)}, u32[]{:S(2)}) copy-start(bf16[1,128,2048]{2,1,0:T(8,128)(2,1)} %param.9) | copy-start | bytes 1572868
  7.2 90.6 %all-gather.2.cloned.1.call-start = ((), (), s32[]{:S(2)}) async-start(), calls=%async_computation.3 | async-start | bytes 5406720 | tf_op jit(solution)/shard_map/all_gather | solution.py:175
  97.8 14.8 %collective-permute-start = (bf16[2048,1280]{1,0:T(8,128)(2,1)}, bf16[2048,1280]{1,0:T(8,128)(2,1)}, u32[]{:S(2)}, u32[]{:S(2)}) collective-permute-start(bf16[2048,1280]{1,0:T(8,128)(2,1)} %all-gather.2.cloned.1.call-done), channel_id=1, source_target_pairs={{0,32},{32,0},{64,96},{96,64},{128,160},{160,128},{192,224},{224,1... | collective-permute-start | bytes 15728648 | tf_op jit(solution)/shard_map/ppermute | solution.py:178
  103.0 20.2 %all-to-all-start.1 = ((bf16[32,128,64]{1,2,0:T(8,128)(2,1)}), bf16[32,128,64]{1,2,0:T(8,128)(2,1)S(1)}, u32[]{:S(2)}, u32[]{:S(2)}) async-start(bf16[32,128,64]{1,2,0:T(8,128)(2,1)} %bitcast.11), calls=%async_computation.1 | async-start | bytes 1048576 | tf_op jit(solution)/shard_map/all_to_all | solution.py:174
  117.1 14.2 %copy-start.10 = (s32[32]{0:T(128)S(1)}, s32[32]{0:T(128)}, u32[]{:S(2)}) copy-start(s32[32]{0:T(128)} %param.14) | copy-start | bytes 388
  123.1 44.0 %all-to-all-start = ((bf16[32,128,192]{1,2,0:T(8,128)(2,1)}), bf16[32,128,192]{1,2,0:T(8,128)(2,1)S(1)}, u32[]{:S(2)}, u32[]{:S(2)}) async-start(bf16[32,128,192]{1,2,0:T(8,128)(2,1)} %pad_maximum_fusion.2), calls=%async_computation | async-start | bytes 3145728 | tf_op jit(solution)/shard_map/all_to_all | solution.py:194
  219.7 2.2 copy-start.6
  219.7 2.5 copy-start.7
  219.7 2.8 copy-start.8
  225.2 56.7 %all-to-all-start.2 = ((bf16[32,128,256]{2,1,0:T(8,128)(2,1)}), bf16[32,128,256]{2,1,0:T(8,128)(2,1)S(1)}, u32[]{:S(2)}, u32[]{:S(2)}) async-start(bf16[32,128,256]{2,1,0:T(8,128)(2,1)} %pad_maximum_fusion.1), calls=%async_computation.2 | async-start | bytes 4194304 | tf_op jit(solution)/shard_map/all_to_all | solution.py:211
  290.4 14.5 %collective-permute-start.1 = (bf16[2,640,2048]{2,1,0:T(8,128)(2,1)}, bf16[2,640,2048]{2,1,0:T(8,128)(2,1)}, u32[]{:S(2)}, u32[]{:S(2)}) collective-permute-start(bf16[2,640,2048]{2,1,0:T(8,128)(2,1)} %pad_maximum_fusion), channel_id=1, source_target_pairs={{0,32},{32,0},{64,96},{96,64},{128,160},{160,128},{192,224},{224,1... | collective-permute-start | bytes 15728648 | tf_op jit(solution)/shard_map/ppermute | solution.py:254
  293.6 68.2 %copy-start.3 = (bf16[640,2048]{1,0:T(8,128)(2,1)}, bf16[640,2048]{1,0:T(8,128)(2,1)S(1)}, u32[]{:S(2)}) copy-start(bf16[640,2048]{1,0:T(8,128)(2,1)S(1)} %multiply_convert_fusion.3) | copy-start | bytes 7864324
  294.5 63.7 %copy-start.4 = (bf16[640,2048]{1,0:T(8,128)(2,1)}, bf16[640,2048]{1,0:T(8,128)(2,1)S(1)}, u32[]{:S(2)}) copy-start(bf16[640,2048]{1,0:T(8,128)(2,1)S(1)} %multiply_convert_fusion.2) | copy-start | bytes 7864324
  308.0 50.1 %copy-start.2 = (bf16[640,2048]{1,0:T(8,128)(2,1)}, bf16[640,2048]{1,0:T(8,128)(2,1)S(1)}, u32[]{:S(2)}) copy-start(bf16[640,2048]{1,0:T(8,128)(2,1)S(1)} %get-tuple-element.36) | copy-start | bytes 7864324
  308.2 9.4 %collective-permute-start.9 = (bf16[640,256]{1,0:T(8,128)(2,1)S(1)}, bf16[640,256]{1,0:T(8,128)(2,1)S(1)}, u32[]{:S(2)}, u32[]{:S(2)}) collective-permute-start(bf16[640,256]{1,0:T(8,128)(2,1)S(1)} %add_convert_fusion.14), channel_id=1, source_target_pairs={{1,0},{2,1},{3,2},{4,3},{5,4},{6,5},{7,6},{0,7},{9,8},{10,9},{11,1... | collective-permute-start | bytes 983048 | tf_op jit(solution)/shard_map/ppermute | solution.py:270
  308.9 10.7 %collective-permute-start.2 = (bf16[640,256]{1,0:T(8,128)(2,1)S(1)}, bf16[640,256]{1,0:T(8,128)(2,1)S(1)}, u32[]{:S(2)}, u32[]{:S(2)}) collective-permute-start(bf16[640,256]{1,0:T(8,128)(2,1)S(1)} %add_convert_fusion.29), channel_id=1, source_target_pairs={{0,1},{1,2},{2,3},{3,4},{4,5},{5,6},{6,7},{7,0},{8,9},{9,10},{10,1... | collective-permute-start | bytes 983048 | tf_op jit(solution)/shard_map/ppermute | solution.py:270
  317.8 8.5 %collective-permute-start.10 = (bf16[640,256]{1,0:T(8,128)(2,1)S(1)}, bf16[640,256]{1,0:T(8,128)(2,1)S(1)}, u32[]{:S(2)}, u32[]{:S(2)}) collective-permute-start(bf16[640,256]{1,0:T(8,128)(2,1)S(1)} %add_convert_fusion.12), channel_id=1, source_target_pairs={{1,0},{2,1},{3,2},{4,3},{5,4},{6,5},{7,6},{0,7},{9,8},{10,9},{11,1... | collective-permute-start | bytes 983048 | tf_op jit(solution)/shard_map/ppermute | solution.py:270
  319.8 9.7 %collective-permute-start.3 = (bf16[640,256]{1,0:T(8,128)(2,1)S(1)}, bf16[640,256]{1,0:T(8,128)(2,1)S(1)}, u32[]{:S(2)}, u32[]{:S(2)}) collective-permute-start(bf16[640,256]{1,0:T(8,128)(2,1)S(1)} %add_convert_fusion.27), channel_id=1, source_target_pairs={{0,1},{1,2},{2,3},{3,4},{4,5},{5,6},{6,7},{7,0},{8,9},{9,10},{10,1... | collective-permute-start | bytes 983048 | tf_op jit(solution)/shard_map/ppermute | solution.py:270
  326.5 8.3 %collective-permute-start.11 = (bf16[640,256]{1,0:T(8,128)(2,1)S(1)}, bf16[640,256]{1,0:T(8,128)(2,1)S(1)}, u32[]{:S(2)}, u32[]{:S(2)}) collective-permute-start(bf16[640,256]{1,0:T(8,128)(2,1)S(1)} %add_convert_fusion.10), channel_id=1, source_target_pairs={{1,0},{2,1},{3,2},{4,3},{5,4},{6,5},{7,6},{0,7},{9,8},{10,9},{11,1... | collective-permute-start | bytes 983048 | tf_op jit(solution)/shard_map/ppermute | solution.py:270
  329.7 8.8 %collective-permute-start.4 = (bf16[640,256]{1,0:T(8,128)(2,1)S(1)}, bf16[640,256]{1,0:T(8,128)(2,1)S(1)}, u32[]{:S(2)}, u32[]{:S(2)}) collective-permute-start(bf16[640,256]{1,0:T(8,128)(2,1)S(1)} %add_convert_fusion.25), channel_id=1, source_target_pairs={{0,1},{1,2},{2,3},{3,4},{4,5},{5,6},{6,7},{7,0},{8,9},{9,10},{10,1... | collective-permute-start | bytes 983048 | tf_op jit(solution)/shard_map/ppermute | solution.py:270
  335.1 7.9 %collective-permute-start.12 = (bf16[640,256]{1,0:T(8,128)(2,1)S(1)}, bf16[640,256]{1,0:T(8,128)(2,1)S(1)}, u32[]{:S(2)}, u32[]{:S(2)}) collective-permute-start(bf16[640,256]{1,0:T(8,128)(2,1)S(1)} %add_convert_fusion.8), channel_id=1, source_target_pairs={{1,0},{2,1},{3,2},{4,3},{5,4},{6,5},{7,6},{0,7},{9,8},{10,9},{11,1... | collective-permute-start | bytes 983048 | tf_op jit(solution)/shard_map/ppermute | solution.py:270
  338.8 7.9 %collective-permute-start.5 = (bf16[640,256]{1,0:T(8,128)(2,1)S(1)}, bf16[640,256]{1,0:T(8,128)(2,1)S(1)}, u32[]{:S(2)}, u32[]{:S(2)}) collective-permute-start(bf16[640,256]{1,0:T(8,128)(2,1)S(1)} %add_convert_fusion.23), channel_id=1, source_target_pairs={{0,1},{1,2},{2,3},{3,4},{4,5},{5,6},{6,7},{7,0},{8,9},{9,10},{10,1... | collective-permute-start | bytes 983048 | tf_op jit(solution)/shard_map/ppermute | solution.py:270
  343.2 7.5 %collective-permute-start.13 = (bf16[640,256]{1,0:T(8,128)(2,1)S(1)}, bf16[640,256]{1,0:T(8,128)(2,1)S(1)}, u32[]{:S(2)}, u32[]{:S(2)}) collective-permute-start(bf16[640,256]{1,0:T(8,128)(2,1)S(1)} %add_convert_fusion.6), channel_id=1, source_target_pairs={{1,0},{2,1},{3,2},{4,3},{5,4},{6,5},{7,6},{0,7},{9,8},{10,9},{11,1... | collective-permute-start | bytes 983048 | tf_op jit(solution)/shard_map/ppermute | solution.py:270
  346.9 7.2 %collective-permute-start.6 = (bf16[640,256]{1,0:T(8,128)(2,1)S(1)}, bf16[640,256]{1,0:T(8,128)(2,1)S(1)}, u32[]{:S(2)}, u32[]{:S(2)}) collective-permute-start(bf16[640,256]{1,0:T(8,128)(2,1)S(1)} %add_convert_fusion.21), channel_id=1, source_target_pairs={{0,1},{1,2},{2,3},{3,4},{4,5},{5,6},{6,7},{7,0},{8,9},{9,10},{10,1... | collective-permute-start | bytes 983048 | tf_op jit(solution)/shard_map/ppermute | solution.py:270
  350.9 7.3 %collective-permute-start.14 = (bf16[640,256]{1,0:T(8,128)(2,1)S(1)}, bf16[640,256]{1,0:T(8,128)(2,1)S(1)}, u32[]{:S(2)}, u32[]{:S(2)}) collective-permute-start(bf16[640,256]{1,0:T(8,128)(2,1)S(1)} %add_convert_fusion.4), channel_id=1, source_target_pairs={{1,0},{2,1},{3,2},{4,3},{5,4},{6,5},{7,6},{0,7},{9,8},{10,9},{11,1... | collective-permute-start | bytes 983048 | tf_op jit(solution)/shard_map/ppermute | solution.py:270
  354.3 7.6 %collective-permute-start.7 = (bf16[640,256]{1,0:T(8,128)(2,1)S(1)}, bf16[640,256]{1,0:T(8,128)(2,1)S(1)}, u32[]{:S(2)}, u32[]{:S(2)}) collective-permute-start(bf16[640,256]{1,0:T(8,128)(2,1)S(1)} %add_convert_fusion.19), channel_id=1, source_target_pairs={{0,1},{1,2},{2,3},{3,4},{4,5},{5,6},{6,7},{7,0},{8,9},{9,10},{10,1... | collective-permute-start | bytes 983048 | tf_op jit(solution)/shard_map/ppermute | solution.py:270
  358.4 8.4 %collective-permute-start.15 = (bf16[640,256]{1,0:T(8,128)(2,1)S(1)}, bf16[640,256]{1,0:T(8,128)(2,1)S(1)}, u32[]{:S(2)}, u32[]{:S(2)}) collective-permute-start(bf16[640,256]{1,0:T(8,128)(2,1)S(1)} %add_convert_fusion.2), channel_id=1, source_target_pairs={{1,0},{2,1},{3,2},{4,3},{5,4},{6,5},{7,6},{0,7},{9,8},{10,9},{11,1... | collective-permute-start | bytes 983048 | tf_op jit(solution)/shard_map/ppermute | solution.py:270
  362.8 8.0 %collective-permute-start.8 = (bf16[640,256]{1,0:T(8,128)(2,1)}, bf16[640,256]{1,0:T(8,128)(2,1)}, u32[]{:S(2)}, u32[]{:S(2)}) collective-permute-start(bf16[640,256]{1,0:T(8,128)(2,1)} %add_convert_fusion.17), channel_id=1, source_target_pairs={{0,1},{1,2},{2,3},{3,4},{4,5},{5,6},{6,7},{7,0},{8,9},{9,10},{10,1... | collective-permute-start | bytes 983048 | tf_op jit(solution)/shard_map/ppermute | solution.py:270
  372.3 31.1 %copy-start.5 = (bf16[128,32,64]{2,0,1:T(8,128)(2,1)S(1)}, bf16[128,32,64]{2,0,1:T(8,128)(2,1)}, u32[]{:S(2)}) copy-start(bf16[128,32,64]{2,0,1:T(8,128)(2,1)} %get-tuple-element.38) | copy-start | bytes 1572868
  372.3 6.4 %collective-permute-start.18 = (bf16[64,1280]{1,0:T(8,128)(2,1)S(1)}, bf16[64,1280]{1,0:T(8,128)(2,1)S(1)}, u32[]{:S(2)}, u32[]{:S(2)}) collective-permute-start(bf16[64,1280]{1,0:T(8,128)(2,1)S(1)} %get-tuple-element.43), channel_id=1, source_target_pairs={{0,24},{1,25},{2,26},{3,27},{4,28},{5,29},{6,30},{7,31},{8,0},{9,1... | collective-permute-start | bytes 491528 | tf_op jit(solution)/shard_map/ppermute | solution.py:150
  374.8 5.8 %collective-permute-start.17 = (bf16[64,1280]{1,0:T(8,128)(2,1)S(1)}, bf16[64,1280]{1,0:T(8,128)(2,1)S(1)}, u32[]{:S(2)}, u32[]{:S(2)}) collective-permute-start(bf16[64,1280]{1,0:T(8,128)(2,1)S(1)} %get-tuple-element.44), channel_id=1, source_target_pairs={{0,16},{1,17},{2,18},{3,19},{4,20},{5,21},{6,22},{7,23},{8,24},{9,... | collective-permute-start | bytes 491528 | tf_op jit(solution)/shard_map/ppermute | solution.py:150
  375.4 6.8 %collective-permute-start.16 = (bf16[64,1280]{1,0:T(8,128)(2,1)S(1)}, bf16[64,1280]{1,0:T(8,128)(2,1)S(1)}, u32[]{:S(2)}, u32[]{:S(2)}) collective-permute-start(bf16[64,1280]{1,0:T(8,128)(2,1)S(1)} %get-tuple-element.42), channel_id=1, source_target_pairs={{0,8},{1,9},{2,10},{3,11},{4,12},{5,13},{6,14},{7,15},{8,16},{9,17... | collective-permute-start | bytes 491528 | tf_op jit(solution)/shard_map/ppermute | solution.py:150
  382.3 6.5 %collective-permute-start.21 = (bf16[64,1280]{1,0:T(8,128)(2,1)S(1)}, bf16[64,1280]{1,0:T(8,128)(2,1)S(1)}, u32[]{:S(2)}, u32[]{:S(2)}) collective-permute-start(bf16[64,1280]{1,0:T(8,128)(2,1)S(1)} %fusion.11), channel_id=1, source_target_pairs={{0,192},{32,224},{64,0},{96,32},{128,64},{160,96},{192,128},{224,1... | collective-permute-start | bytes 491528 | tf_op jit(solution)/shard_map/ppermute | solution.py:150
  384.8 5.8 %collective-permute-start.20 = (bf16[64,1280]{1,0:T(8,128)(2,1)S(1)}, bf16[64,1280]{1,0:T(8,128)(2,1)S(1)}, u32[]{:S(2)}, u32[]{:S(2)}) collective-permute-start(bf16[64,1280]{1,0:T(8,128)(2,1)S(1)} %fusion.11), channel_id=1, source_target_pairs={{0,128},{32,160},{64,192},{96,224},{128,0},{160,32},{192,64},{224,... | collective-permute-start | bytes 491528 | tf_op jit(solution)/shard_map/ppermute | solution.py:150
  385.2 7.0 %collective-permute-start.19 = (bf16[64,1280]{1,0:T(8,128)(2,1)S(1)}, bf16[64,1280]{1,0:T(8,128)(2,1)S(1)}, u32[]{:S(2)}, u32[]{:S(2)}) collective-permute-start(bf16[64,1280]{1,0:T(8,128)(2,1)S(1)} %fusion.11), channel_id=1, source_target_pairs={{0,64},{32,96},{64,128},{96,160},{128,192},{160,224},{192,0},{224,... | collective-permute-start | bytes 491528 | tf_op jit(solution)/shard_map/ppermute | solution.py:150
  392.3 13.9 %copy-start.1 = (s32[32,32,7]{1,0,2:T(8,128)S(1)}, s32[32,32,7]{1,0,2:T(8,128)}, u32[]{:S(2)}) copy-start(s32[32,32,7]{1,0,2:T(8,128)} %param.13) | copy-start | bytes 86020
  393.0 11.8 %collective-permute-start.22 = (bf16[64,1280]{1,0:T(8,128)(2,1)S(1)}, bf16[64,1280]{1,0:T(8,128)(2,1)S(1)}, u32[]{:S(2)}, u32[]{:S(2)}) collective-permute-start(bf16[64,1280]{1,0:T(8,128)(2,1)S(1)} %select_reduce_fusion), channel_id=1, source_target_pairs={{0,32},{32,0},{64,96},{96,64},{128,160},{160,128},{192,224},{224,1... | collective-permute-start | bytes 491528 | tf_op jit(solution)/shard_map/ppermute | solution.py:285
Sparse Core Ops, SparseCore 0:
  11.2 86.5 all-gather.1

commit v8 on v7

--- a/solution.py
+++ b/solution.py
@@ -17,9 +17,10 @@
 
 
 def head_kernel(table_ref, count_ref, q_ref, g_ref, k_ref, v_ref,
-                out_ref, gq_ref, dk_ref, dv_ref):
+                out_ref, gq_ref, dk_ref, dv_ref, k_cat, v_cat):
     b = pl.program_id(0)
     slot_count = table_ref.shape[0] // pl.num_programs(0)
+    block_len = q_ref.shape[1]
     head_width = q_ref.shape[-1]
     score_scale = head_width ** (-0.5)
 
@@ -32,45 +33,32 @@
     g = g_ref[0]
     used = 4 + count_ref[0]
     chosen = [table_ref[b * slot_count + j] for j in range(slot_count)]
-    keys = [k_ref[c] for c in chosen]
-    vals = [v_ref[c] for c in chosen]
+    for j in range(slot_count):
+        k_cat[j * block_len : (j + 1) * block_len, :] = k_ref[chosen[j]]
+        v_cat[j * block_len : (j + 1) * block_len, :] = v_ref[chosen[j]]
+    keys = k_cat[...]
+    vals = v_cat[...]
     nt = (((1,), (1,)), ((), ()))
     tn = (((0,), (0,)), ((), ()))
-    scores = []
+    scores = lax.dot_general(q, keys, nt, preferred_element_type=jnp.float32) * score_scale
+    slot_of = lax.broadcasted_iota(jnp.int32, (1, slot_count * block_len), 1) // block_len
+    scores = jnp.where(slot_of < used, scores, masked_score)
+    highest = scores.max(axis=-1, keepdims=True)
+    exps = jnp.exp(scores - highest)
+    shares = exps / exps.sum(axis=-1, keepdims=True)
+    shares_low = shares.astype(jnp.bfloat16)
+    attended = jnp.dot(shares_low, vals, preferred_element_type=jnp.float32)
+    out_ref[0] = attended.astype(out_ref.dtype)
+    grad_shares = lax.dot_general(g, vals, nt, preferred_element_type=jnp.float32)
+    weighted = (grad_shares * shares).sum(axis=-1, keepdims=True)
+    grad_scores = (shares * (grad_shares - weighted)).astype(jnp.bfloat16)
+    grad_query = jnp.dot(grad_scores, keys, preferred_element_type=jnp.float32)
+    gq_ref[0] = (grad_query * score_scale).astype(gq_ref.dtype)
+    dk = lax.dot_general(grad_scores, q, tn, preferred_element_type=jnp.float32) * score_scale
+    dv = lax.dot_general(shares_low, g, tn, preferred_element_type=jnp.float32)
     for j in range(slot_count):
-        s = lax.dot_general(q, keys[j], nt, preferred_element_type=jnp.float32) * score_scale
-        if j >= 4:
-            s = jnp.where(j < used, s, masked_score)
-        scores.append(s)
-    highest = scores[0].max(axis=-1, keepdims=True)
-    for s in scores[1:]:
-        highest = jnp.maximum(highest, s.max(axis=-1, keepdims=True))
-    exps = [jnp.exp(s - highest) for s in scores]
-    denom = exps[0].sum(axis=-1, keepdims=True)
-    for e in exps[1:]:
-        denom = denom + e.sum(axis=-1, keepdims=True)
-    shares = [e / denom for e in exps]
-    shares_low = [p.astype(jnp.bfloat16) for p in shares]
-    attended = jnp.dot(shares_low[0], vals[0], preferred_element_type=jnp.float32)
-    for j in range(1, slot_count):
-        attended = attended + jnp.dot(shares_low[j], vals[j], preferred_element_type=jnp.float32)
-    out_ref[0] = attended.astype(out_ref.dtype)
-    grad_shares = [lax.dot_general(g, vals[j], nt, preferred_element_type=jnp.float32)
-                   for j in range(slot_count)]
-    weighted = (grad_shares[0] * shares[0]).sum(axis=-1, keepdims=True)
-    for j in range(1, slot_count):
-        weighted = weighted + (grad_shares[j] * shares[j]).sum(axis=-1, keepdims=True)
-    grad_scores = [(shares[j] * (grad_shares[j] - weighted)).astype(jnp.bfloat16)
-                   for j in range(slot_count)]
-    grad_query = jnp.dot(grad_scores[0], keys[0], preferred_element_type=jnp.float32)
-    for j in range(1, slot_count):
-        grad_query = grad_query + jnp.dot(grad_scores[j], keys[j], preferred_element_type=jnp.float32)
-    gq_ref[0] = (grad_query * score_scale).astype(gq_ref.dtype)
-    for j in range(slot_count):
-        dk = lax.dot_general(grad_scores[j], q, tn, preferred_element_type=jnp.float32) * score_scale
-        dv = lax.dot_general(shares_low[j], g, tn, preferred_element_type=jnp.float32)
-        dk_ref[chosen[j]] += dk
-        dv_ref[chosen[j]] += dv
+        dk_ref[chosen[j]] += dk[j * block_len : (j + 1) * block_len]
+        dv_ref[chosen[j]] += dv[j * block_len : (j + 1) * block_len]
 
 
 def head_pass(queries, key_rows, value_rows, grad_head, blocks, extra_count):
@@ -85,6 +73,10 @@
         grid=(block_count,),
         in_specs=[one_block, one_block, whole, whole],
         out_specs=[one_block, one_block, whole, whole],
+        scratch_shapes=[
+            pltpu.VMEM((slot_count * block_len, head_width), jnp.bfloat16),
+            pltpu.VMEM((slot_count * block_len, head_width), jnp.bfloat16),
+        ],
     )
     flops = 2 * seq_len * slot_count * block_len * head_width * 6
     attended, grad_query, grad_k, grad_v = pl.pallas_call(

time: 422 us -> 416 us (0.986)
  Pallas kernels: 48.2 us -> 42 us
    pallas_call x1, Pallas kernels: 48.2 us -> 42 us  [head_pass(): pl.pallas_call(head_kernel, grid_spec=grid_spec, out_shape=[jax.ShapeDtyp...]
where the time goes in v8:
time: 416 us; the launch traced here: 407 us
  waiting for transfers between devices  222 us (53%)
  starting transfers between devices  64.4 us (15%)
  Pallas kernels  42 us (10%)
  local copies, waits for them, and re-layouts  22.4 us (5%)
  matrix products  22.2 us (5%)
  other arithmetic  19 us (5%)
  between operations  15 us (4%)
    all_gather x1, waiting for transfers between devices, per_device(): lax.all_gather(lax.dynamic_slice_in_dim(w_local, core * half, half, axis=...  88.8 us
    all_to_all x1, waiting for transfers between devices, per_device(): lax.all_to_all(back_sent, 'seq', split_axis=0, concat_axis=0, tiled=True)  45 us
    pallas_call x1, Pallas kernels, head_pass(): pl.pallas_call(head_kernel, grid_spec=grid_spec, out_shape=[jax.ShapeDtyp...  42 us
    ppermute x14, waiting for transfers between devices, per_device(): arrived = lax.ppermute(buf, 'seq', perm)  37.7 us
    all_to_all x1, waiting for transfers between devices, per_device(): lax.all_to_all(sent, 'seq', split_axis=0, concat_axis=1, tiled=True)[0]  33.9 us
    ppermute x14, starting transfers between devices, per_device(): arrived = lax.ppermute(buf, 'seq', perm)  20.3 us
    ppermute x6, waiting for transfers between devices, direct_sum(): lax.ppermute(lax.dynamic_index_in_dim(pieces, (mine + d) % size, 0, keepd...  12.3 us
    ppermute x1, starting transfers between devices, per_device(): other_half = lax.ppermute(part, 'dp', pairs)  10.4 us
  transfers between devices with their start and end apart: 27, of which 19 were waited for; matrix products, arithmetic and copies ran while one was open for 9% of the time, Pallas kernels for 0%

profile of v8, /device:TPU:1, one launch (start us, length us, event | category | flops | bytes accessed | tf_op | source)
XLA Modules:
  0.0 407.3 jit_solution(10321983093835598029)
XLA Ops:
  7.3 1.7 fusion.16
  9.0 88.8 %all-gather.2.cloned.1.call-done = bf16[2048,1280]{1,0:T(8,128)(2,1)} async-done(((bf16[64,1280]{1,0:T(8,128)(2,1)}), bf16[2048,1280]{1,0:T(8,128)(2,1)}) %all-gather.2.cloned.1.call-update) | async-done | bytes 5242896 | tf_op jit(solution)/shard_map/all_gather | solution.py:167
  97.8 3.1 collective-permute-start
  100.9 2.0 copy.38
  103.0 5.3 %all-to-all-start.1 = ((bf16[32,128,64]{1,2,0:T(8,128)(2,1)}), bf16[32,128,64]{1,2,0:T(8,128)(2,1)S(1)}, u32[]{:S(2)}, u32[]{:S(2)}) async-start(bf16[32,128,64]{1,2,0:T(8,128)(2,1)} %bitcast.11), calls=%async_computation.1 | async-start | bytes 1048576 | tf_op jit(solution)/shard_map/all_to_all | solution.py:166
  108.4 4.2 %fusion.4 = bf16[128,2560]{0,1:T(8,128)(2,1)S(1)} fusion(bf16[128,2560]{0,1:T(8,128)(2,1)S(1)} %broadcast_in_dim.31, s32[]{:T(128)S(6)} %select_n.136, bf16[2048,1280]{1,0:T(8,128)(2,1)} %all-gather.2.cloned.1.call-done, bf16[1,128,2048]{2,1,0:T(8,128)(2,1)S(1)} %copy-done.9), kind=kOutput, calls=%fused_computation.17 | convolution fusion | flops 671252480 | bytes 6094852 | tf_op jit(solution)/shard_map/dot_general | solution.py:171
  112.6 4.2 %fusion.6 = bf16[128,2560]{0,1:T(8,128)(2,1)S(1)} fusion(bf16[128,2560]{0,1:T(8,128)(2,1)S(1)} %fusion.4, s32[]{:T(128)S(6)} %select_n.137, bf16[2048,1280]{1,0:T(8,128)(2,1)} %collective-permute-done, bf16[1,128,2048]{2,1,0:T(8,128)(2,1)S(1)} %copy-done.9), kind=kOutput, calls=%fused_computation.19 | convolution fusion | flops 671252480 | bytes 6094852 | tf_op jit(solution)/shard_map/dot_general | solution.py:172
  117.1 1.3 pad_maximum_fusion.2
  118.4 4.7 %all-to-all-done.1 = bf16[32,128,64]{1,2,0:T(8,128)(2,1)S(1)} async-done(((bf16[32,128,64]{1,2,0:T(8,128)(2,1)}), bf16[32,128,64]{1,2,0:T(8,128)(2,1)S(1)}, u32[]{:S(2)}, u32[]{:S(2)}) %all-to-all-start.1) | async-done | bytes 524320 | tf_op jit(solution)/shard_map/all_to_all | solution.py:166
  123.1 7.4 %all-to-all-start = ((bf16[32,128,192]{1,2,0:T(8,128)(2,1)}), bf16[32,128,192]{1,2,0:T(8,128)(2,1)S(1)}, u32[]{:S(2)}, u32[]{:S(2)}) async-start(bf16[32,128,192]{1,2,0:T(8,128)(2,1)} %pad_maximum_fusion.2), calls=%async_computation | async-start | bytes 3145728 | tf_op jit(solution)/shard_map/all_to_all | solution.py:186
  130.6 0.7 reshape.129.table_ref
  131.9 1.4 copy.41.g_ref
  133.3 33.9 %all-to-all-done = bf16[32,128,192]{1,2,0:T(8,128)(2,1)S(1)} async-done(((bf16[32,128,192]{1,2,0:T(8,128)(2,1)}), bf16[32,128,192]{1,2,0:T(8,128)(2,1)S(1)}, u32[]{:S(2)}, u32[]{:S(2)}) %all-to-all-start) | async-done | bytes 1572896 | tf_op jit(solution)/shard_map/all_to_all | solution.py:186
  167.5 1.3 copy.37
  168.8 1.3 copy.39
  170.2 1.3 copy.40
  171.5 42.0 %shard_map.110 = (bf16[32,128,64]{2,1,0:T(8,128)(2,1)}, bf16[32,128,64]{2,1,0:T(8,128)(2,1)}, f32[32,128,64]{2,1,0:T(8,128)}, f32[32,128,64]{2,1,0:T(8,128)}) custom-call(s32[224]{0:T(256)} %reshape.129.table_ref, s32[1]{0:T(128)} %dynamic_slice.35.count_ref, bf16[32,128,64]{2,1,0:T(8,128)(2,1)} %bitcast.115, bf16[32,128,64]{2,1,0:T(8,128)(2,1)} %copy.41.g_ref, ...), custom_call_target="tpu_custom_call" | custom-call | flops 2818572288 | bytes 5242880 | tf_op jit(solution)/shard_map/pallas_call | solution.py:82
  213.6 1.9 convert.11
  216.3 2.7 pad_maximum_fusion.1
  219.1 8.0 %all-to-all-start.2 = ((bf16[32,128,256]{2,1,0:T(8,128)(2,1)}), bf16[32,128,256]{2,1,0:T(8,128)(2,1)S(1)}, u32[]{:S(2)}, u32[]{:S(2)}) async-start(bf16[32,128,256]{2,1,0:T(8,128)(2,1)} %pad_maximum_fusion.1), calls=%async_computation.2 | async-start | bytes 4194304 | tf_op jit(solution)/shard_map/all_to_all | solution.py:203
  228.1 1.4 gather_fusion.2
  229.7 1.2 broadcast_select_fusion
  230.8 45.0 %all-to-all-done.2 = bf16[32,128,256]{2,1,0:T(8,128)(2,1)S(1)} async-done(((bf16[32,128,256]{2,1,0:T(8,128)(2,1)}), bf16[32,128,256]{2,1,0:T(8,128)(2,1)S(1)}, u32[]{:S(2)}, u32[]{:S(2)}) %all-to-all-start.2) | async-done | bytes 2097184 | tf_op jit(solution)/shard_map/all_to_all | solution.py:203
  276.3 1.8 slice_bitcast_fusion.2
  278.1 1.6 copy.43
  279.8 0.8 fusion
  280.7 0.8 fusion.1
  281.5 2.7 pad_maximum_fusion
  284.2 2.4 collective-permute-start.1
  286.6 0.8 multiply_convert_fusion.3
  287.5 0.8 multiply_convert_fusion.2
  288.4 5.3 %fusion.13 = f32[128,2048]{1,0:T(8,128)S(1)} fusion(bf16[2048,1280]{1,0:T(8,128)(2,1)} %all-gather.2.cloned.1.call-done, bf16[128,2560]{0,1:T(8,128)(2,1)S(1)} %pad_maximum_fusion.3, s32[]{:T(128)S(6)} %select_n.136), kind=kOutput, calls=%fused_computation.72 | convolution fusion | flops 671088640 | bytes 6619140 | tf_op jit(solution)/shard_map/dot_general | solution.py:219
  293.6 5.1 %fusion.2 = bf16[128,2048]{1,0:T(8,128)(2,1)} fusion(f32[128,2048]{1,0:T(8,128)S(1)} %fusion.13, bf16[2048,1280]{1,0:T(8,128)(2,1)} %collective-permute-done, bf16[128,2560]{0,1:T(8,128)(2,1)S(1)} %pad_maximum_fusion.3, s32[]{:T(128)S(6)} %select_n.137), kind=kOutput, calls=%fused_computation.13 | convolution fusion | flops 671612928 | bytes 7143428 | tf_op jit(solution)/shard_map/dot_general | solution.py:220
  298.8 3.1 slice_bitcast_fusion.1
  302.8 1.1 collective-permute-start.2
  303.8 7.6 %collective-permute-done.9 = bf16[640,256]{1,0:T(8,128)(2,1)S(1)} collective-permute-done((bf16[640,256]{1,0:T(8,128)(2,1)S(1)}, bf16[640,256]{1,0:T(8,128)(2,1)S(1)}, u32[]{:S(2)}, u32[]{:S(2)}) %collective-permute-start.9) | collective-permute-done | bytes 327712 | tf_op jit(solution)/shard_map/ppermute | solution.py:262
  311.7 1.8 collective-permute-start.10
  313.9 6.3 %collective-permute-done.10 = bf16[640,256]{1,0:T(8,128)(2,1)S(1)} collective-permute-done((bf16[640,256]{1,0:T(8,128)(2,1)S(1)}, bf16[640,256]{1,0:T(8,128)(2,1)S(1)}, u32[]{:S(2)}, u32[]{:S(2)}) %collective-permute-start.10) | collective-permute-done | bytes 327712 | tf_op jit(solution)/shard_map/ppermute | solution.py:262
  320.4 3.0 collective-permute-start.11
  323.7 5.0 %collective-permute-done.11 = bf16[640,256]{1,0:T(8,128)(2,1)S(1)} collective-permute-done((bf16[640,256]{1,0:T(8,128)(2,1)S(1)}, bf16[640,256]{1,0:T(8,128)(2,1)S(1)}, u32[]{:S(2)}, u32[]{:S(2)}) %collective-permute-start.11) | collective-permute-done | bytes 327712 | tf_op jit(solution)/shard_map/ppermute | solution.py:262
  328.9 3.5 collective-permute-start.12
  332.7 4.1 %collective-permute-done.12 = bf16[640,256]{1,0:T(8,128)(2,1)S(1)} collective-permute-done((bf16[640,256]{1,0:T(8,128)(2,1)S(1)}, bf16[640,256]{1,0:T(8,128)(2,1)S(1)}, u32[]{:S(2)}, u32[]{:S(2)}) %collective-permute-start.12) | collective-permute-done | bytes 327712 | tf_op jit(solution)/shard_map/ppermute | solution.py:262
  337.0 3.5 collective-permute-start.13
  340.8 3.7 collective-permute-done.13
  344.7 3.2 collective-permute-start.14
  348.2 3.8 collective-permute-done.14
  352.2 3.2 collective-permute-start.15
  355.6 0.9 add_convert_fusion.17
  356.6 4.0 collective-permute-done.15
  360.5 1.2 add_convert_fusion
  361.7 2.9 collective-permute-done.8
  364.6 1.2 add_convert_fusion.15
  366.2 2.5 collective-permute-start.18
  369.2 0.8 collective-permute-start.16
  370.0 2.6 collective-permute-done.18
  372.6 1.8 collective-permute-done.17
  374.4 1.7 collective-permute-done.16
  376.1 2.5 collective-permute-start.21
  379.8 2.8 collective-permute-done.21
  382.6 1.8 collective-permute-done.20
  384.4 1.7 collective-permute-done.19
  386.9 10.4 %collective-permute-start.22 = (bf16[64,1280]{1,0:T(8,128)(2,1)S(1)}, bf16[64,1280]{1,0:T(8,128)(2,1)S(1)}, u32[]{:S(2)}, u32[]{:S(2)}) collective-permute-start(bf16[64,1280]{1,0:T(8,128)(2,1)S(1)} %select_reduce_fusion), channel_id=1, source_target_pairs={{0,32},{32,0},{64,96},{96,64},{128,160},{160,128},{192,224},{224,1... | collective-permute-start | bytes 491528 | tf_op jit(solution)/shard_map/ppermute | solution.py:277
  397.6 1.0 copy.48
  399.3 0.7 pad_maximum_fusion.6
  (92 shorter events, 11.9 us)
Async XLA Ops:
  7.2 123.4 %copy-start = (s32[32,32,7]{1,0,2:T(8,128)S(1)}, s32[32,32,7]{1,0,2:T(8,128)}, u32[]{:S(2)}) copy-start(s32[32,32,7]{1,0,2:T(8,128)} %param.13) | copy-start | bytes 86020
  7.2 101.2 %copy-start.9 = (bf16[1,128,2048]{2,1,0:T(8,128)(2,1)S(1)}, bf16[1,128,2048]{2,1,0:T(8,128)(2,1)}, u32[]{:S(2)}) copy-start(bf16[1,128,2048]{2,1,0:T(8,128)(2,1)} %param.9) | copy-start | bytes 1572868
  7.2 90.6 %all-gather.2.cloned.1.call-start = ((), (), s32[]{:S(2)}) async-start(), calls=%async_computation.3 | async-start | bytes 5406720 | tf_op jit(solution)/shard_map/all_gather | solution.py:167
  97.8 14.8 %collective-permute-start = (bf16[2048,1280]{1,0:T(8,128)(2,1)}, bf16[2048,1280]{1,0:T(8,128)(2,1)}, u32[]{:S(2)}, u32[]{:S(2)}) collective-permute-start(bf16[2048,1280]{1,0:T(8,128)(2,1)} %all-gather.2.cloned.1.call-done), channel_id=1, source_target_pairs={{0,32},{32,0},{64,96},{96,64},{128,160},{160,128},{192,224},{224,1... | collective-permute-start | bytes 15728648 | tf_op jit(solution)/shard_map/ppermute | solution.py:170
  103.0 20.2 %all-to-all-start.1 = ((bf16[32,128,64]{1,2,0:T(8,128)(2,1)}), bf16[32,128,64]{1,2,0:T(8,128)(2,1)S(1)}, u32[]{:S(2)}, u32[]{:S(2)}) async-start(bf16[32,128,64]{1,2,0:T(8,128)(2,1)} %bitcast.11), calls=%async_computation.1 | async-start | bytes 1048576 | tf_op jit(solution)/shard_map/all_to_all | solution.py:166
  117.1 14.2 %copy-start.10 = (s32[32]{0:T(128)S(1)}, s32[32]{0:T(128)}, u32[]{:S(2)}) copy-start(s32[32]{0:T(128)} %param.14) | copy-start | bytes 388
  123.1 44.0 %all-to-all-start = ((bf16[32,128,192]{1,2,0:T(8,128)(2,1)}), bf16[32,128,192]{1,2,0:T(8,128)(2,1)S(1)}, u32[]{:S(2)}, u32[]{:S(2)}) async-start(bf16[32,128,192]{1,2,0:T(8,128)(2,1)} %pad_maximum_fusion.2), calls=%async_computation | async-start | bytes 3145728 | tf_op jit(solution)/shard_map/all_to_all | solution.py:186
  213.5 2.2 copy-start.6
  213.6 2.5 copy-start.7
  213.6 2.8 copy-start.8
  219.1 56.7 %all-to-all-start.2 = ((bf16[32,128,256]{2,1,0:T(8,128)(2,1)}), bf16[32,128,256]{2,1,0:T(8,128)(2,1)S(1)}, u32[]{:S(2)}, u32[]{:S(2)}) async-start(bf16[32,128,256]{2,1,0:T(8,128)(2,1)} %pad_maximum_fusion.1), calls=%async_computation.2 | async-start | bytes 4194304 | tf_op jit(solution)/shard_map/all_to_all | solution.py:203
  284.2 14.5 %collective-permute-start.1 = (bf16[2,640,2048]{2,1,0:T(8,128)(2,1)}, bf16[2,640,2048]{2,1,0:T(8,128)(2,1)}, u32[]{:S(2)}, u32[]{:S(2)}) collective-permute-start(bf16[2,640,2048]{2,1,0:T(8,128)(2,1)} %pad_maximum_fusion), channel_id=1, source_target_pairs={{0,32},{32,0},{64,96},{96,64},{128,160},{160,128},{192,224},{224,1... | collective-permute-start | bytes 15728648 | tf_op jit(solution)/shard_map/ppermute | solution.py:246
  287.5 68.2 %copy-start.3 = (bf16[640,2048]{1,0:T(8,128)(2,1)}, bf16[640,2048]{1,0:T(8,128)(2,1)S(1)}, u32[]{:S(2)}) copy-start(bf16[640,2048]{1,0:T(8,128)(2,1)S(1)} %multiply_convert_fusion.3) | copy-start | bytes 7864324
  288.4 63.6 %copy-start.4 = (bf16[640,2048]{1,0:T(8,128)(2,1)}, bf16[640,2048]{1,0:T(8,128)(2,1)S(1)}, u32[]{:S(2)}) copy-start(bf16[640,2048]{1,0:T(8,128)(2,1)S(1)} %multiply_convert_fusion.2) | copy-start | bytes 7864324
  301.9 50.1 %copy-start.2 = (bf16[640,2048]{1,0:T(8,128)(2,1)}, bf16[640,2048]{1,0:T(8,128)(2,1)S(1)}, u32[]{:S(2)}) copy-start(bf16[640,2048]{1,0:T(8,128)(2,1)S(1)} %get-tuple-element.36) | copy-start | bytes 7864324
  302.1 9.4 %collective-permute-start.9 = (bf16[640,256]{1,0:T(8,128)(2,1)S(1)}, bf16[640,256]{1,0:T(8,128)(2,1)S(1)}, u32[]{:S(2)}, u32[]{:S(2)}) collective-permute-start(bf16[640,256]{1,0:T(8,128)(2,1)S(1)} %add_convert_fusion.14), channel_id=1, source_target_pairs={{1,0},{2,1},{3,2},{4,3},{5,4},{6,5},{7,6},{0,7},{9,8},{10,9},{11,1... | collective-permute-start | bytes 983048 | tf_op jit(solution)/shard_map/ppermute | solution.py:262
  302.8 10.7 %collective-permute-start.2 = (bf16[640,256]{1,0:T(8,128)(2,1)S(1)}, bf16[640,256]{1,0:T(8,128)(2,1)S(1)}, u32[]{:S(2)}, u32[]{:S(2)}) collective-permute-start(bf16[640,256]{1,0:T(8,128)(2,1)S(1)} %add_convert_fusion.29), channel_id=1, source_target_pairs={{0,1},{1,2},{2,3},{3,4},{4,5},{5,6},{6,7},{7,0},{8,9},{9,10},{10,1... | collective-permute-start | bytes 983048 | tf_op jit(solution)/shard_map/ppermute | solution.py:262
  311.7 8.5 %collective-permute-start.10 = (bf16[640,256]{1,0:T(8,128)(2,1)S(1)}, bf16[640,256]{1,0:T(8,128)(2,1)S(1)}, u32[]{:S(2)}, u32[]{:S(2)}) collective-permute-start(bf16[640,256]{1,0:T(8,128)(2,1)S(1)} %add_convert_fusion.12), channel_id=1, source_target_pairs={{1,0},{2,1},{3,2},{4,3},{5,4},{6,5},{7,6},{0,7},{9,8},{10,9},{11,1... | collective-permute-start | bytes 983048 | tf_op jit(solution)/shard_map/ppermute | solution.py:262
  313.6 9.7 %collective-permute-start.3 = (bf16[640,256]{1,0:T(8,128)(2,1)S(1)}, bf16[640,256]{1,0:T(8,128)(2,1)S(1)}, u32[]{:S(2)}, u32[]{:S(2)}) collective-permute-start(bf16[640,256]{1,0:T(8,128)(2,1)S(1)} %add_convert_fusion.27), channel_id=1, source_target_pairs={{0,1},{1,2},{2,3},{3,4},{4,5},{5,6},{6,7},{7,0},{8,9},{9,10},{10,1... | collective-permute-start | bytes 983048 | tf_op jit(solution)/shard_map/ppermute | solution.py:262
  320.4 8.3 %collective-permute-start.11 = (bf16[640,256]{1,0:T(8,128)(2,1)S(1)}, bf16[640,256]{1,0:T(8,128)(2,1)S(1)}, u32[]{:S(2)}, u32[]{:S(2)}) collective-permute-start(bf16[640,256]{1,0:T(8,128)(2,1)S(1)} %add_convert_fusion.10), channel_id=1, source_target_pairs={{1,0},{2,1},{3,2},{4,3},{5,4},{6,5},{7,6},{0,7},{9,8},{10,9},{11,1... | collective-permute-start | bytes 983048 | tf_op jit(solution)/shard_map/ppermute | solution.py:262
  323.6 8.8 %collective-permute-start.4 = (bf16[640,256]{1,0:T(8,128)(2,1)S(1)}, bf16[640,256]{1,0:T(8,128)(2,1)S(1)}, u32[]{:S(2)}, u32[]{:S(2)}) collective-permute-start(bf16[640,256]{1,0:T(8,128)(2,1)S(1)} %add_convert_fusion.25), channel_id=1, source_target_pairs={{0,1},{1,2},{2,3},{3,4},{4,5},{5,6},{6,7},{7,0},{8,9},{9,10},{10,1... | collective-permute-start | bytes 983048 | tf_op jit(solution)/shard_map/ppermute | solution.py:262
  328.9 7.9 %collective-permute-start.12 = (bf16[640,256]{1,0:T(8,128)(2,1)S(1)}, bf16[640,256]{1,0:T(8,128)(2,1)S(1)}, u32[]{:S(2)}, u32[]{:S(2)}) collective-permute-start(bf16[640,256]{1,0:T(8,128)(2,1)S(1)} %add_convert_fusion.8), channel_id=1, source_target_pairs={{1,0},{2,1},{3,2},{4,3},{5,4},{6,5},{7,6},{0,7},{9,8},{10,9},{11,1... | collective-permute-start | bytes 983048 | tf_op jit(solution)/shard_map/ppermute | solution.py:262
  332.6 7.9 %collective-permute-start.5 = (bf16[640,256]{1,0:T(8,128)(2,1)S(1)}, bf16[640,256]{1,0:T(8,128)(2,1)S(1)}, u32[]{:S(2)}, u32[]{:S(2)}) collective-permute-start(bf16[640,256]{1,0:T(8,128)(2,1)S(1)} %add_convert_fusion.23), channel_id=1, source_target_pairs={{0,1},{1,2},{2,3},{3,4},{4,5},{5,6},{6,7},{7,0},{8,9},{9,10},{10,1... | collective-permute-start | bytes 983048 | tf_op jit(solution)/shard_map/ppermute | solution.py:262
  337.0 7.5 %collective-permute-start.13 = (bf16[640,256]{1,0:T(8,128)(2,1)S(1)}, bf16[640,256]{1,0:T(8,128)(2,1)S(1)}, u32[]{:S(2)}, u32[]{:S(2)}) collective-permute-start(bf16[640,256]{1,0:T(8,128)(2,1)S(1)} %add_convert_fusion.6), channel_id=1, source_target_pairs={{1,0},{2,1},{3,2},{4,3},{5,4},{6,5},{7,6},{0,7},{9,8},{10,9},{11,1... | collective-permute-start | bytes 983048 | tf_op jit(solution)/shard_map/ppermute | solution.py:262
  340.7 7.2 %collective-permute-start.6 = (bf16[640,256]{1,0:T(8,128)(2,1)S(1)}, bf16[640,256]{1,0:T(8,128)(2,1)S(1)}, u32[]{:S(2)}, u32[]{:S(2)}) collective-permute-start(bf16[640,256]{1,0:T(8,128)(2,1)S(1)} %add_convert_fusion.21), channel_id=1, source_target_pairs={{0,1},{1,2},{2,3},{3,4},{4,5},{5,6},{6,7},{7,0},{8,9},{9,10},{10,1... | collective-permute-start | bytes 983048 | tf_op jit(solution)/shard_map/ppermute | solution.py:262
  344.7 7.3 %collective-permute-start.14 = (bf16[640,256]{1,0:T(8,128)(2,1)S(1)}, bf16[640,256]{1,0:T(8,128)(2,1)S(1)}, u32[]{:S(2)}, u32[]{:S(2)}) collective-permute-start(bf16[640,256]{1,0:T(8,128)(2,1)S(1)} %add_convert_fusion.4), channel_id=1, source_target_pairs={{1,0},{2,1},{3,2},{4,3},{5,4},{6,5},{7,6},{0,7},{9,8},{10,9},{11,1... | collective-permute-start | bytes 983048 | tf_op jit(solution)/shard_map/ppermute | solution.py:262
  348.1 7.6 %collective-permute-start.7 = (bf16[640,256]{1,0:T(8,128)(2,1)S(1)}, bf16[640,256]{1,0:T(8,128)(2,1)S(1)}, u32[]{:S(2)}, u32[]{:S(2)}) collective-permute-start(bf16[640,256]{1,0:T(8,128)(2,1)S(1)} %add_convert_fusion.19), channel_id=1, source_target_pairs={{0,1},{1,2},{2,3},{3,4},{4,5},{5,6},{6,7},{7,0},{8,9},{9,10},{10,1... | collective-permute-start | bytes 983048 | tf_op jit(solution)/shard_map/ppermute | solution.py:262
  352.2 8.4 %collective-permute-start.15 = (bf16[640,256]{1,0:T(8,128)(2,1)S(1)}, bf16[640,256]{1,0:T(8,128)(2,1)S(1)}, u32[]{:S(2)}, u32[]{:S(2)}) collective-permute-start(bf16[640,256]{1,0:T(8,128)(2,1)S(1)} %add_convert_fusion.2), channel_id=1, source_target_pairs={{1,0},{2,1},{3,2},{4,3},{5,4},{6,5},{7,6},{0,7},{9,8},{10,9},{11,1... | collective-permute-start | bytes 983048 | tf_op jit(solution)/shard_map/ppermute | solution.py:262
  356.6 8.0 %collective-permute-start.8 = (bf16[640,256]{1,0:T(8,128)(2,1)}, bf16[640,256]{1,0:T(8,128)(2,1)}, u32[]{:S(2)}, u32[]{:S(2)}) collective-permute-start(bf16[640,256]{1,0:T(8,128)(2,1)} %add_convert_fusion.17), channel_id=1, source_target_pairs={{0,1},{1,2},{2,3},{3,4},{4,5},{5,6},{6,7},{7,0},{8,9},{9,10},{10,1... | collective-permute-start | bytes 983048 | tf_op jit(solution)/shard_map/ppermute | solution.py:262
  366.1 31.1 %copy-start.5 = (bf16[128,32,64]{2,0,1:T(8,128)(2,1)S(1)}, bf16[128,32,64]{2,0,1:T(8,128)(2,1)}, u32[]{:S(2)}) copy-start(bf16[128,32,64]{2,0,1:T(8,128)(2,1)} %get-tuple-element.38) | copy-start | bytes 1572868
  366.2 6.5 %collective-permute-start.18 = (bf16[64,1280]{1,0:T(8,128)(2,1)S(1)}, bf16[64,1280]{1,0:T(8,128)(2,1)S(1)}, u32[]{:S(2)}, u32[]{:S(2)}) collective-permute-start(bf16[64,1280]{1,0:T(8,128)(2,1)S(1)} %get-tuple-element.43), channel_id=1, source_target_pairs={{0,24},{1,25},{2,26},{3,27},{4,28},{5,29},{6,30},{7,31},{8,0},{9,1... | collective-permute-start | bytes 491528 | tf_op jit(solution)/shard_map/ppermute | solution.py:142
  368.6 5.8 %collective-permute-start.17 = (bf16[64,1280]{1,0:T(8,128)(2,1)S(1)}, bf16[64,1280]{1,0:T(8,128)(2,1)S(1)}, u32[]{:S(2)}, u32[]{:S(2)}) collective-permute-start(bf16[64,1280]{1,0:T(8,128)(2,1)S(1)} %get-tuple-element.44), channel_id=1, source_target_pairs={{0,16},{1,17},{2,18},{3,19},{4,20},{5,21},{6,22},{7,23},{8,24},{9,... | collective-permute-start | bytes 491528 | tf_op jit(solution)/shard_map/ppermute | solution.py:142
  369.2 6.9 %collective-permute-start.16 = (bf16[64,1280]{1,0:T(8,128)(2,1)S(1)}, bf16[64,1280]{1,0:T(8,128)(2,1)S(1)}, u32[]{:S(2)}, u32[]{:S(2)}) collective-permute-start(bf16[64,1280]{1,0:T(8,128)(2,1)S(1)} %get-tuple-element.42), channel_id=1, source_target_pairs={{0,8},{1,9},{2,10},{3,11},{4,12},{5,13},{6,14},{7,15},{8,16},{9,17... | collective-permute-start | bytes 491528 | tf_op jit(solution)/shard_map/ppermute | solution.py:142
  376.1 6.5 %collective-permute-start.21 = (bf16[64,1280]{1,0:T(8,128)(2,1)S(1)}, bf16[64,1280]{1,0:T(8,128)(2,1)S(1)}, u32[]{:S(2)}, u32[]{:S(2)}) collective-permute-start(bf16[64,1280]{1,0:T(8,128)(2,1)S(1)} %fusion.11), channel_id=1, source_target_pairs={{0,192},{32,224},{64,0},{96,32},{128,64},{160,96},{192,128},{224,1... | collective-permute-start | bytes 491528 | tf_op jit(solution)/shard_map/ppermute | solution.py:142
  378.6 5.8 %collective-permute-start.20 = (bf16[64,1280]{1,0:T(8,128)(2,1)S(1)}, bf16[64,1280]{1,0:T(8,128)(2,1)S(1)}, u32[]{:S(2)}, u32[]{:S(2)}) collective-permute-start(bf16[64,1280]{1,0:T(8,128)(2,1)S(1)} %fusion.11), channel_id=1, source_target_pairs={{0,128},{32,160},{64,192},{96,224},{128,0},{160,32},{192,64},{224,... | collective-permute-start | bytes 491528 | tf_op jit(solution)/shard_map/ppermute | solution.py:142
  379.2 6.8 %collective-permute-start.19 = (bf16[64,1280]{1,0:T(8,128)(2,1)S(1)}, bf16[64,1280]{1,0:T(8,128)(2,1)S(1)}, u32[]{:S(2)}, u32[]{:S(2)}) collective-permute-start(bf16[64,1280]{1,0:T(8,128)(2,1)S(1)} %fusion.11), channel_id=1, source_target_pairs={{0,64},{32,96},{64,128},{96,160},{128,192},{160,224},{192,0},{224,... | collective-permute-start | bytes 491528 | tf_op jit(solution)/shard_map/ppermute | solution.py:142
  386.1 13.9 %copy-start.1 = (s32[32,32,7]{1,0,2:T(8,128)S(1)}, s32[32,32,7]{1,0,2:T(8,128)}, u32[]{:S(2)}) copy-start(s32[32,32,7]{1,0,2:T(8,128)} %param.13) | copy-start | bytes 86020
  386.9 11.8 %collective-permute-start.22 = (bf16[64,1280]{1,0:T(8,128)(2,1)S(1)}, bf16[64,1280]{1,0:T(8,128)(2,1)S(1)}, u32[]{:S(2)}, u32[]{:S(2)}) collective-permute-start(bf16[64,1280]{1,0:T(8,128)(2,1)S(1)} %select_reduce_fusion), channel_id=1, source_target_pairs={{0,32},{32,0},{64,96},{96,64},{128,160},{160,128},{192,224},{224,1... | collective-permute-start | bytes 491528 | tf_op jit(solution)/shard_map/ppermute | solution.py:277
Sparse Core Ops, SparseCore 0:
  11.2 86.5 all-gather.1

commit v9 on v8

--- a/solution.py
+++ b/solution.py
@@ -145,6 +145,53 @@
     return got
 
 
+def ring_gather_weights(piece, position, dp_index):
+    dp_devices = lax.axis_size("dp")
+    seq_devices = lax.axis_size("seq")
+    y_count = seq_devices // RING_Z
+    sizes = {"z": RING_Z, "y": y_count}
+
+    def step_to(s, dim, shift):
+        y, z = s // RING_Z, s % RING_Z
+        if dim == "z":
+            return y * RING_Z + (z + shift) % RING_Z
+        return ((y + shift) % y_count) * RING_Z + z
+
+    def ring(x, which, dim):
+        n = sizes[dim]
+        got = [x]
+        for shift, steps in ((1, n // 2), (-1, n - 1 - n // 2)):
+            perm = [
+                (d * seq_devices + s, d * seq_devices + step_to(s, dim, shift))
+                for d in range(dp_devices) if d % 2 == which
+                for s in range(seq_devices)
+            ]
+            cur = x
+            for _ in range(steps):
+                cur = lax.ppermute(cur, ("dp", "seq"), perm)
+                got.append(cur)
+        ahead = got[1 : 1 + n // 2]
+        behind = got[1 + n // 2 :]
+        return jnp.stack([x] + ahead + behind[::-1])
+
+    first = ring(ring(piece, 0, "z"), 0, "y")
+    second = ring(ring(piece, 1, "y"), 1, "z")
+    return first.reshape(-1, piece.shape[-1]), second.reshape(-1, piece.shape[-1])
+
+
+def ring_blocks(position, z_first):
+    seq_devices = lax.axis_size("seq")
+    y_count = seq_devices // RING_Z
+    y, z = position // RING_Z, position % RING_Z
+    dy = jnp.arange(y_count)
+    dz = jnp.arange(RING_Z)
+    if z_first:
+        origin = ((y - dy) % y_count)[:, None] * RING_Z + ((z - dz) % RING_Z)[None, :]
+    else:
+        origin = ((y - dy) % y_count)[None, :] * RING_Z + ((z - dz) % RING_Z)[:, None]
+    return origin.reshape(-1)
+
+
 def per_device(activations, w_query, w_key, w_value, key_blocks, random_count, grad_out):
     seq_devices = lax.axis_size("seq")
     dp_devices = lax.axis_size("dp")
@@ -164,12 +211,20 @@
     pairs = [(i, i ^ 1) for i in range(dp_devices)]
     grad_pieces = grad_rows.reshape(tok_count, heads, HD).transpose(1, 0, 2)
     head_grad = lax.all_to_all(grad_pieces, "seq", split_axis=0, concat_axis=1, tiled=True)[0]
-    w_mine = lax.all_gather(
-        lax.dynamic_slice_in_dim(w_local, core * half, half, axis=1), "seq", axis=0, tiled=True
-    )
+    by_z, by_y = ring_gather_weights(
+        lax.dynamic_slice_in_dim(w_local, core * half, half, axis=1), position, dp_index
+    )
+    w_mine = jnp.where(core == 0, by_z, by_y)
     w_other = lax.ppermute(w_mine, "dp", pairs)
-    proj_mine = jnp.dot(tokens, w_mine, preferred_element_type=jnp.float32).astype(jnp.bfloat16)
-    proj_other = jnp.dot(tokens, w_other, preferred_element_type=jnp.float32).astype(jnp.bfloat16)
+    order_z, order_y = ring_blocks(position, True), ring_blocks(position, False)
+    order_mine = jnp.where(core == 0, order_z, order_y)
+    order_other = jnp.where(core == 0, order_y, order_z)
+    feat = w_local.shape[0]
+    token_blocks = tokens.reshape(tok_count, seq_devices, feat)
+    tokens_mine = jnp.take(token_blocks, order_mine, axis=1).reshape(tok_count, -1)
+    tokens_other = jnp.take(token_blocks, order_other, axis=1).reshape(tok_count, -1)
+    proj_mine = jnp.dot(tokens_mine, w_mine, preferred_element_type=jnp.float32).astype(jnp.bfloat16)
+    proj_other = jnp.dot(tokens_other, w_other, preferred_element_type=jnp.float32).astype(jnp.bfloat16)
     projected = jnp.zeros((tok_count, all_cols), jnp.bfloat16)
     projected = lax.dynamic_update_slice_in_dim(projected, proj_mine, core * half, axis=1)
     projected = lax.dynamic_update_slice_in_dim(projected, proj_other, (1 - core) * half, axis=1)
@@ -215,9 +270,13 @@
     contract = (((1,), (1,)), ((), ()))
     comb_mine = lax.dynamic_slice_in_dim(combined, core * half, half, axis=1)
     comb_other = lax.dynamic_slice_in_dim(combined, (1 - core) * half, half, axis=1)
+    def natural(part, order):
+        back = jnp.zeros_like(order).at[order].set(jnp.arange(seq_devices, dtype=order.dtype))
+        return jnp.take(part.reshape(tok_count, seq_devices, feat), back, axis=1).reshape(tok_count, -1)
+
     grad_x_rows = (
-        lax.dot_general(comb_mine, w_mine, contract, preferred_element_type=jnp.float32)
-        + lax.dot_general(comb_other, w_other, contract, preferred_element_type=jnp.float32)
+        natural(lax.dot_general(comb_mine, w_mine, contract, preferred_element_type=jnp.float32), order_mine)
+        + natural(lax.dot_general(comb_other, w_other, contract, preferred_element_type=jnp.float32), order_other)
     ).astype(jnp.bfloat16)
     factor = 1.0 / math.sqrt(tok_count * seq_devices * dp_devices)
     over_tokens = (((0,), (0,)), ((), ()))

time: 416 us -> 412 us (level)
  waiting for transfers between devices: 222 us -> 160 us
  starting transfers between devices: 64.4 us -> 115 us
  other arithmetic: 19 us -> 34.1 us
  between operations: 15 us -> 2.31 us
  local copies, waits for them, and re-layouts: 22.4 us -> 34.5 us
  matrix products: 22.2 us -> 15.9 us
    all_gather x1 -> x0, waiting for transfers between devices: 88.8 us -> none  [per_device(): lax.all_gather(lax.dynamic_slice_in_dim(w_local, core * half, half, axis=...]
    ppermute x0 -> x20, starting transfers between devices: none -> 40.6 us  [ring(): cur = lax.ppermute(cur, ('dp', 'seq'), perm)]
    ppermute x0 -> x20, waiting for transfers between devices: none -> 29.1 us  [ring(): cur = lax.ppermute(cur, ('dp', 'seq'), perm)]
    ppermute x1, starting transfers between devices: 3.1 us -> 15.5 us  [per_device(): w_other = lax.ppermute(w_mine, 'dp', pairs)]
    select_n x0 -> x8, other arithmetic: none -> 8.92 us  [the longest x2 8.66 us: per_device(): w_mine = jnp.where(core == 0, by_z, by_y)]
    another operation x2 -> x4, other arithmetic: 2.06 us -> 6.89 us  [the longest x2 4.83 us: ring(): return jnp.stack([x] + ahead + behind[::-1])]
  transfers between devices with their start and end apart: 27 -> 46, of which waited for: 19 -> 22; matrix products, arithmetic and copies ran while one was open for 9% -> 12% of each run, Pallas kernels for 0% -> 0%
where the time goes in v9:
time: 412 us; the launch traced here: 404 us
  waiting for transfers between devices  160 us (39%)
  starting transfers between devices  115 us (28%)
  Pallas kernels  41.9 us (10%)
  local copies, waits for them, and re-layouts  34.5 us (8%)
  other arithmetic  34.1 us (8%)
  matrix products  15.9 us (4%)
    all_to_all x1, waiting for transfers between devices, per_device(): lax.all_to_all(back_sent, 'seq', split_axis=0, concat_axis=0, tiled=True)  44.5 us
    pallas_call x1, Pallas kernels, head_pass(): pl.pallas_call(head_kernel, grid_spec=grid_spec, out_shape=[jax.ShapeDtyp...  41.9 us
    ppermute x20, starting transfers between devices, ring(): cur = lax.ppermute(cur, ('dp', 'seq'), perm)  40.6 us
    ppermute x14, waiting for transfers between devices, per_device(): arrived = lax.ppermute(buf, 'seq', perm)  37.2 us
    all_to_all x1, waiting for transfers between devices, per_device(): lax.all_to_all(sent, 'seq', split_axis=0, concat_axis=1, tiled=True)[0]  33.9 us
    ppermute x20, waiting for transfers between devices, ring(): cur = lax.ppermute(cur, ('dp', 'seq'), perm)  29.1 us
    ppermute x14, starting transfers between devices, per_device(): arrived = lax.ppermute(buf, 'seq', perm)  20.3 us
    ppermute x1, starting transfers between devices, per_device(): w_other = lax.ppermute(w_mine, 'dp', pairs)  15.5 us
  transfers between devices with their start and end apart: 46, of which 22 were waited for; matrix products, arithmetic and copies ran while one was open for 12% of the time, Pallas kernels for 0%

profile of v9, /device:TPU:1, one launch (start us, length us, event | category | flops | bytes accessed | tf_op | source)
XLA Modules:
  0.0 403.9 jit_solution(8036173338875177301)
XLA Ops:
  1.7 4.0 collective-permute-start.10
  7.1 3.4 collective-permute-start.12
  10.5 1.9 collective-permute-start.11
  13.9 4.2 %collective-permute-done.11 = bf16[64,1280]{1,0:T(8,128)(2,1)S(1)} collective-permute-done((bf16[64,1280]{1,0:T(8,128)(2,1)S(1)}, bf16[64,1280]{1,0:T(8,128)(2,1)S(1)}, u32[]{:S(2)}, u32[]{:S(2)}) %collective-permute-start.11) | collective-permute-done | bytes 163872 | tf_op jit(solution)/shard_map/ppermute | solution.py:171
  19.0 3.2 collective-permute-start.13
  22.2 5.9 %collective-permute-start.17 = (bf16[4,64,1280]{2,1,0:T(8,128)(2,1)}, bf16[4,64,1280]{2,1,0:T(8,128)(2,1)}, u32[]{:S(2)}, u32[]{:S(2)}) collective-permute-start(bf16[4,64,1280]{2,1,0:T(8,128)(2,1)} %pad_maximum_fusion.4), channel_id=1, source_target_pairs={{32,39},{33,32},{34,33},{35,34},{36,35},{37,36},{38,37},{39,38},{4... | collective-permute-start | bytes 1966088 | tf_op jit(solution)/shard_map/ppermute | solution.py:171
  30.3 4.7 %collective-permute-done.13 = bf16[4,64,1280]{2,1,0:T(8,128)(2,1)} collective-permute-done((bf16[4,64,1280]{2,1,0:T(8,128)(2,1)}, bf16[4,64,1280]{2,1,0:T(8,128)(2,1)}, u32[]{:S(2)}, u32[]{:S(2)}) %collective-permute-start.13) | collective-permute-done | bytes 655392 | tf_op jit(solution)/shard_map/ppermute | solution.py:171
  35.0 1.9 collective-permute-start.14
  37.7 5.0 %collective-permute-start.18 = (bf16[4,64,1280]{2,1,0:T(8,128)(2,1)}, bf16[4,64,1280]{2,1,0:T(8,128)(2,1)S(1)}, u32[]{:S(2)}, u32[]{:S(2)}) collective-permute-start(bf16[4,64,1280]{2,1,0:T(8,128)(2,1)} %collective-permute-done.17), channel_id=1, source_target_pairs={{32,39},{33,32},{34,33},{35,34},{36,35},{37,36},{38,37},{39,38},{4... | collective-permute-start | bytes 1966088 | tf_op jit(solution)/shard_map/ppermute | solution.py:171
  42.7 6.9 %collective-permute-done.14 = bf16[4,64,1280]{2,1,0:T(8,128)(2,1)} collective-permute-done((bf16[4,64,1280]{2,1,0:T(8,128)(2,1)}, bf16[4,64,1280]{2,1,0:T(8,128)(2,1)}, u32[]{:S(2)}, u32[]{:S(2)}) %collective-permute-start.14) | collective-permute-done | bytes 655392 | tf_op jit(solution)/shard_map/ppermute | solution.py:171
  49.6 1.9 collective-permute-start.15
  53.5 4.6 %collective-permute-start.19 = (bf16[4,64,1280]{2,1,0:T(8,128)(2,1)S(1)}, bf16[4,64,1280]{2,1,0:T(8,128)(2,1)S(1)}, u32[]{:S(2)}, u32[]{:S(2)}) collective-permute-start(bf16[4,64,1280]{2,1,0:T(8,128)(2,1)S(1)} %collective-permute-done.18), channel_id=1, source_target_pairs={{32,39},{33,32},{34,33},{35,34},{36,35},{37,36},{38,37},{39,38},{4... | collective-permute-start | bytes 1966088 | tf_op jit(solution)/shard_map/ppermute | solution.py:171
  58.1 4.6 %collective-permute-done.15 = bf16[4,64,1280]{2,1,0:T(8,128)(2,1)S(1)} collective-permute-done((bf16[4,64,1280]{2,1,0:T(8,128)(2,1)}, bf16[4,64,1280]{2,1,0:T(8,128)(2,1)S(1)}, u32[]{:S(2)}, u32[]{:S(2)}) %collective-permute-start.15) | collective-permute-done | bytes 655392 | tf_op jit(solution)/shard_map/ppermute | solution.py:171
  62.6 1.9 collective-permute-start.16
  66.5 8.7 %collective-permute-done.16 = bf16[4,64,1280]{2,1,0:T(8,128)(2,1)S(1)} collective-permute-done((bf16[4,64,1280]{2,1,0:T(8,128)(2,1)S(1)}, bf16[4,64,1280]{2,1,0:T(8,128)(2,1)S(1)}, u32[]{:S(2)}, u32[]{:S(2)}) %collective-permute-start.16) | collective-permute-done | bytes 655392 | tf_op jit(solution)/shard_map/ppermute | solution.py:171
  76.5 3.9 pad_maximum_fusion
  80.4 4.1 %bitcast_select_fusion.1 = bf16[2048,1280]{1,0:T(8,128)(2,1)} fusion(bf16[8,4,64,1280]{3,2,1,0:T(8,128)(2,1)S(1)} %bitcast_dynamic-update-slice_fusion, bf16[4,8,64,1280]{3,2,1,0:T(8,128)(2,1)S(1)} %get-tuple-element.45, pred[]{:T(512)S(6)} %eq.27), kind=kLoop, calls=%fused_computation.12 | loop fusion | flops 2621440 | bytes 15728641 | tf_op jit(solution)/shard_map/jit(_where)/select_n | solution.py:217
  84.5 15.5 %collective-permute-start.20 = (bf16[2048,1280]{1,0:T(8,128)(2,1)}, bf16[2048,1280]{1,0:T(8,128)(2,1)}, u32[]{:S(2)}, u32[]{:S(2)}) collective-permute-start(bf16[2048,1280]{1,0:T(8,128)(2,1)} %bitcast_select_fusion.1), channel_id=1, source_target_pairs={{0,32},{32,0},{64,96},{96,64},{128,160},{160,128},{192,224},{224,1... | collective-permute-start | bytes 15728648 | tf_op jit(solution)/shard_map/ppermute | solution.py:218
  101.0 3.9 all-to-all-start.1
  107.1 3.4 convolution_convert_fusion.1
  110.9 3.4 convolution_convert_fusion
  116.2 5.2 %all-to-all-done.1 = bf16[32,128,64]{1,2,0:T(8,128)(2,1)S(1)} async-done(((bf16[32,128,64]{1,2,0:T(8,128)(2,1)}), bf16[32,128,64]{1,2,0:T(8,128)(2,1)S(1)}, u32[]{:S(2)}, u32[]{:S(2)}) %all-to-all-start.1) | async-done | bytes 524320 | tf_op jit(solution)/shard_map/all_to_all | solution.py:213
  121.3 6.0 %all-to-all-start = ((bf16[32,128,192]{1,2,0:T(8,128)(2,1)}), bf16[32,128,192]{1,2,0:T(8,128)(2,1)S(1)}, u32[]{:S(2)}, u32[]{:S(2)}) async-start(bf16[32,128,192]{1,2,0:T(8,128)(2,1)} %pad_maximum_fusion.3), calls=%async_computation | async-start | bytes 3145728 | tf_op jit(solution)/shard_map/all_to_all | solution.py:241
  128.6 1.3 copy.61.g_ref
  130.0 33.9 %all-to-all-done = bf16[32,128,192]{1,2,0:T(8,128)(2,1)S(1)} async-done(((bf16[32,128,192]{1,2,0:T(8,128)(2,1)}), bf16[32,128,192]{1,2,0:T(8,128)(2,1)S(1)}, u32[]{:S(2)}, u32[]{:S(2)}) %all-to-all-start) | async-done | bytes 1572896 | tf_op jit(solution)/shard_map/all_to_all | solution.py:241
  164.3 1.4 copy.60
  165.6 1.4 copy.59
  167.0 1.4 copy.57
  168.3 41.9 %shard_map.110 = (bf16[32,128,64]{2,1,0:T(8,128)(2,1)}, bf16[32,128,64]{2,1,0:T(8,128)(2,1)}, f32[32,128,64]{2,1,0:T(8,128)}, f32[32,128,64]{2,1,0:T(8,128)}) custom-call(s32[224]{0:T(256)} %reshape.330.table_ref, s32[1]{0:T(128)} %dynamic_slice.35.count_ref, bf16[32,128,64]{2,1,0:T(8,128)(2,1)} %bitcast.194, bf16[32,128,64]{2,1,0:T(8,128)(2,1)} %copy.61.g_ref, ...), custom_call_target="tpu_custom_call" | custom-call | flops 2818572288 | bytes 5242880 | tf_op jit(solution)/shard_map/pallas_call | solution.py:82
  210.3 1.9 convert.10
  213.0 2.7 pad_maximum_fusion.2
  215.7 7.8 %all-to-all-start.2 = ((bf16[32,128,256]{2,1,0:T(8,128)(2,1)}), bf16[32,128,256]{2,1,0:T(8,128)(2,1)S(1)}, u32[]{:S(2)}, u32[]{:S(2)}) async-start(bf16[32,128,256]{2,1,0:T(8,128)(2,1)} %pad_maximum_fusion.2), calls=%async_computation.2 | async-start | bytes 4194304 | tf_op jit(solution)/shard_map/all_to_all | solution.py:258
  224.2 1.4 gather_fusion.5
  227.8 44.5 %all-to-all-done.2 = bf16[32,128,256]{2,1,0:T(8,128)(2,1)S(1)} async-done(((bf16[32,128,256]{2,1,0:T(8,128)(2,1)}), bf16[32,128,256]{2,1,0:T(8,128)(2,1)S(1)}, u32[]{:S(2)}, u32[]{:S(2)}) %all-to-all-start.2) | async-done | bytes 2097184 | tf_op jit(solution)/shard_map/all_to_all | solution.py:258
  272.3 1.9 slice_bitcast_fusion.2
  274.1 1.6 copy.63
  279.7 2.8 pad_maximum_fusion.1
  282.4 2.4 collective-permute-start.21
  286.6 4.6 %bitcast_select_fusion = bf16[32,64,1280]{2,1,0:T(8,128)(2,1)S(1)} fusion(bf16[8,4,64,1280]{3,2,1,0:T(8,128)(2,1)} %copy-done.2, bf16[4,8,64,1280]{3,2,1,0:T(8,128)(2,1)} %copy-done.3, pred[]{:T(512)S(6)} %eq.27), kind=kLoop, calls=%fused_computation.11 | loop fusion | flops 2621440 | bytes 15728641 | tf_op jit(solution)/shard_map/jit(_where)/select_n | solution.py:217
  291.3 1.5 fusion.6
  293.4 4.1 %fusion.8 = f32[128,2048]{0,1:T(8,128)S(1)} fusion(bf16[2048,1280]{1,0:T(8,128)(2,1)} %collective-permute-done.20, bf16[128,2560]{1,0:T(8,128)(2,1)} %copy-done.7, s32[]{:T(128)S(6)} %select_n.274), kind=kOutput, calls=%fused_computation.88 | convolution fusion | flops 671088640 | bytes 6619140 | tf_op jit(solution)/shard_map/dot_general | solution.py:279
  301.2 4.0 %slice_bitcast_fusion.1 = (bf16[640,2048]{1,0:T(8,128)(2,1)S(1)}, bf16[640,2048]{1,0:T(8,128)(2,1)S(1)}) fusion(bf16[2,640,2048]{2,1,0:T(8,128)(2,1)} %collective-permute-done.21), kind=kLoop, calls=%fused_computation.21 | loop fusion | bytes 10485760 | tf_op jit(solution)/shard_map/squeeze | solution.py:316
  307.2 7.7 %collective-permute-done.29 = bf16[640,256]{1,0:T(8,128)(2,1)S(1)} collective-permute-done((bf16[640,256]{1,0:T(8,128)(2,1)S(1)}, bf16[640,256]{1,0:T(8,128)(2,1)S(1)}, u32[]{:S(2)}, u32[]{:S(2)}) %collective-permute-start.29) | collective-permute-done | bytes 327712 | tf_op jit(solution)/shard_map/ppermute | solution.py:321
  315.1 1.8 collective-permute-start.30
  317.1 6.5 %collective-permute-done.30 = bf16[640,256]{1,0:T(8,128)(2,1)S(1)} collective-permute-done((bf16[640,256]{1,0:T(8,128)(2,1)S(1)}, bf16[640,256]{1,0:T(8,128)(2,1)S(1)}, u32[]{:S(2)}, u32[]{:S(2)}) %collective-permute-start.30) | collective-permute-done | bytes 327712 | tf_op jit(solution)/shard_map/ppermute | solution.py:321
  323.8 3.0 collective-permute-start.31
  327.1 5.0 %collective-permute-done.31 = bf16[640,256]{1,0:T(8,128)(2,1)S(1)} collective-permute-done((bf16[640,256]{1,0:T(8,128)(2,1)S(1)}, bf16[640,256]{1,0:T(8,128)(2,1)S(1)}, u32[]{:S(2)}, u32[]{:S(2)}) %collective-permute-start.31) | collective-permute-done | bytes 327712 | tf_op jit(solution)/shard_map/ppermute | solution.py:321
  332.3 3.7 collective-permute-start.32
  336.4 4.1 %collective-permute-done.32 = bf16[640,256]{1,0:T(8,128)(2,1)S(1)} collective-permute-done((bf16[640,256]{1,0:T(8,128)(2,1)S(1)}, bf16[640,256]{1,0:T(8,128)(2,1)S(1)}, u32[]{:S(2)}, u32[]{:S(2)}) %collective-permute-start.32) | collective-permute-done | bytes 327712 | tf_op jit(solution)/shard_map/ppermute | solution.py:321
  340.7 3.5 collective-permute-start.33
  344.5 3.7 collective-permute-done.33
  348.4 3.2 collective-permute-start.34
  351.9 3.8 collective-permute-done.34
  356.6 3.1 collective-permute-start.35
  360.6 3.7 collective-permute-done.35
  365.6 2.7 collective-permute-done.28
  371.1 1.5 collective-permute-start.38
  372.6 1.4 collective-permute-start.37
  376.6 1.7 collective-permute-done.37
  378.4 2.6 collective-permute-start.41
  382.1 2.9 collective-permute-done.41
  385.0 1.8 collective-permute-done.40
  386.8 1.6 collective-permute-done.39
  389.2 10.4 %collective-permute-start.42 = (bf16[64,1280]{1,0:T(8,128)(2,1)S(1)}, bf16[64,1280]{1,0:T(8,128)(2,1)S(1)}, u32[]{:S(2)}, u32[]{:S(2)}) collective-permute-start(bf16[64,1280]{1,0:T(8,128)(2,1)S(1)} %select_reduce_fusion), channel_id=1, source_target_pairs={{0,32},{32,0},{64,96},{96,64},{128,160},{160,128},{192,224},{224,1... | collective-permute-start | bytes 491528 | tf_op jit(solution)/shard_map/ppermute | solution.py:336
  (202 shorter events, 51.9 us)
Async XLA Ops:
  0.6 127.2 %copy-start = (s32[32,32,7]{1,0,2:T(8,128)S(1)}, s32[32,32,7]{1,0,2:T(8,128)}, u32[]{:S(2)}) copy-start(s32[32,32,7]{1,0,2:T(8,128)} %param.17) | copy-start | bytes 86020
  1.7 8.8 %collective-permute-start.10 = (bf16[64,1280]{1,0:T(8,128)(2,1)S(1)}, bf16[64,1280]{1,0:T(8,128)(2,1)S(1)}, u32[]{:S(2)}, u32[]{:S(2)}) collective-permute-start(bf16[64,1280]{1,0:T(8,128)(2,1)S(1)} %get-tuple-element.40), channel_id=1, source_target_pairs={{32,40},{33,41},{34,42},{35,43},{36,44},{37,45},{38,46},{39,47},{4... | collective-permute-start | bytes 491528 | tf_op jit(solution)/shard_map/ppermute | solution.py:171
  5.8 6.7 %collective-permute-start.4 = (bf16[64,1280]{1,0:T(8,128)(2,1)S(1)}, bf16[64,1280]{1,0:T(8,128)(2,1)S(1)}, u32[]{:S(2)}, u32[]{:S(2)}) collective-permute-start(bf16[64,1280]{1,0:T(8,128)(2,1)S(1)} %get-tuple-element.40), channel_id=1, source_target_pairs={{0,7},{1,0},{2,1},{3,2},{4,3},{5,4},{6,5},{7,6},{8,15},{9,8},{10,9... | collective-permute-start | bytes 491528 | tf_op jit(solution)/shard_map/ppermute | solution.py:171
  6.5 6.7 %collective-permute-start = (bf16[64,1280]{1,0:T(8,128)(2,1)S(1)}, bf16[64,1280]{1,0:T(8,128)(2,1)S(1)}, u32[]{:S(2)}, u32[]{:S(2)}) collective-permute-start(bf16[64,1280]{1,0:T(8,128)(2,1)S(1)} %get-tuple-element.40), channel_id=1, source_target_pairs={{0,1},{1,2},{2,3},{3,4},{4,5},{5,6},{6,7},{7,0},{8,9},{9,10},{10,1... | collective-permute-start | bytes 491528 | tf_op jit(solution)/shard_map/ppermute | solution.py:171
  7.1 6.7 %collective-permute-start.12 = (bf16[64,1280]{1,0:T(8,128)(2,1)S(1)}, bf16[64,1280]{1,0:T(8,128)(2,1)S(1)}, u32[]{:S(2)}, u32[]{:S(2)}) collective-permute-start(bf16[64,1280]{1,0:T(8,128)(2,1)S(1)} %get-tuple-element.40), channel_id=1, source_target_pairs={{32,56},{33,57},{34,58},{35,59},{36,60},{37,61},{38,62},{39,63},{4... | collective-permute-start | bytes 491528 | tf_op jit(solution)/shard_map/ppermute | solution.py:171
  10.5 7.6 %collective-permute-start.11 = (bf16[64,1280]{1,0:T(8,128)(2,1)S(1)}, bf16[64,1280]{1,0:T(8,128)(2,1)S(1)}, u32[]{:S(2)}, u32[]{:S(2)}) collective-permute-start(bf16[64,1280]{1,0:T(8,128)(2,1)S(1)} %collective-permute-done.10), channel_id=1, source_target_pairs={{32,40},{33,41},{34,42},{35,43},{36,44},{37,45},{38,46},{39,47},{4... | collective-permute-start | bytes 491528 | tf_op jit(solution)/shard_map/ppermute | solution.py:171
  12.5 15.7 %collective-permute-start.5 = (bf16[64,1280]{1,0:T(8,128)(2,1)S(1)}, bf16[64,1280]{1,0:T(8,128)(2,1)S(1)}, u32[]{:S(2)}, u32[]{:S(2)}) collective-permute-start(bf16[64,1280]{1,0:T(8,128)(2,1)S(1)} %collective-permute-done.4), channel_id=1, source_target_pairs={{0,7},{1,0},{2,1},{3,2},{4,3},{5,4},{6,5},{7,6},{8,15},{9,8},{10,9... | collective-permute-start | bytes 491528 | tf_op jit(solution)/shard_map/ppermute | solution.py:171
  13.1 15.7 %collective-permute-start.1 = (bf16[64,1280]{1,0:T(8,128)(2,1)S(1)}, bf16[64,1280]{1,0:T(8,128)(2,1)S(1)}, u32[]{:S(2)}, u32[]{:S(2)}) collective-permute-start(bf16[64,1280]{1,0:T(8,128)(2,1)S(1)} %collective-permute-done), channel_id=1, source_target_pairs={{0,1},{1,2},{2,3},{3,4},{4,5},{5,6},{6,7},{7,0},{8,9},{9,10},{10,1... | collective-permute-start | bytes 491528 | tf_op jit(solution)/shard_map/ppermute | solution.py:171
  19.0 16.0 %collective-permute-start.13 = (bf16[4,64,1280]{2,1,0:T(8,128)(2,1)}, bf16[4,64,1280]{2,1,0:T(8,128)(2,1)}, u32[]{:S(2)}, u32[]{:S(2)}) collective-permute-start(bf16[4,64,1280]{2,1,0:T(8,128)(2,1)} %pad_maximum_fusion.4), channel_id=1, source_target_pairs={{32,33},{33,34},{34,35},{35,36},{36,37},{37,38},{38,39},{39,32},{4... | collective-permute-start | bytes 1966088 | tf_op jit(solution)/shard_map/ppermute | solution.py:171
  22.2 15.5 %collective-permute-start.17 = (bf16[4,64,1280]{2,1,0:T(8,128)(2,1)}, bf16[4,64,1280]{2,1,0:T(8,128)(2,1)}, u32[]{:S(2)}, u32[]{:S(2)}) collective-permute-start(bf16[4,64,1280]{2,1,0:T(8,128)(2,1)} %pad_maximum_fusion.4), channel_id=1, source_target_pairs={{32,39},{33,32},{34,33},{35,34},{36,35},{37,36},{38,37},{39,38},{4... | collective-permute-start | bytes 1966088 | tf_op jit(solution)/shard_map/ppermute | solution.py:171
  28.1 2.1 collective-permute-start.6
  28.8 0.7 collective-permute-start.2
  29.5 0.7 collective-permute-start.3
  35.0 14.6 %collective-permute-start.14 = (bf16[4,64,1280]{2,1,0:T(8,128)(2,1)}, bf16[4,64,1280]{2,1,0:T(8,128)(2,1)}, u32[]{:S(2)}, u32[]{:S(2)}) collective-permute-start(bf16[4,64,1280]{2,1,0:T(8,128)(2,1)} %collective-permute-done.13), channel_id=1, source_target_pairs={{32,33},{33,34},{34,35},{35,36},{36,37},{37,38},{38,39},{39,32},{4... | collective-permute-start | bytes 1966088 | tf_op jit(solution)/shard_map/ppermute | solution.py:171
  37.0 28.7 %collective-permute-start.7 = (bf16[8,64,1280]{2,1,0:T(8,128)(2,1)S(1)}, bf16[8,64,1280]{2,1,0:T(8,128)(2,1)S(1)}, u32[]{:S(2)}, u32[]{:S(2)}) collective-permute-start(bf16[8,64,1280]{2,1,0:T(8,128)(2,1)S(1)} %bitcast_dynamic-update-slice_fusion.8), channel_id=1, source_target_pairs={{0,8},{1,9},{2,10},{3,11},{4,12},{5,13},{6,14},{7,15},{8,16},{9,17... | collective-permute-start | bytes 3932168 | tf_op jit(solution)/shard_map/ppermute | solution.py:171
  37.7 15.7 %collective-permute-start.18 = (bf16[4,64,1280]{2,1,0:T(8,128)(2,1)}, bf16[4,64,1280]{2,1,0:T(8,128)(2,1)S(1)}, u32[]{:S(2)}, u32[]{:S(2)}) collective-permute-start(bf16[4,64,1280]{2,1,0:T(8,128)(2,1)} %collective-permute-done.17), channel_id=1, source_target_pairs={{32,39},{33,32},{34,33},{35,34},{36,35},{37,36},{38,37},{39,38},{4... | collective-permute-start | bytes 1966088 | tf_op jit(solution)/shard_map/ppermute | solution.py:171
  49.6 13.0 %collective-permute-start.15 = (bf16[4,64,1280]{2,1,0:T(8,128)(2,1)}, bf16[4,64,1280]{2,1,0:T(8,128)(2,1)S(1)}, u32[]{:S(2)}, u32[]{:S(2)}) collective-permute-start(bf16[4,64,1280]{2,1,0:T(8,128)(2,1)} %collective-permute-done.14), channel_id=1, source_target_pairs={{32,33},{33,34},{34,35},{35,36},{36,37},{37,38},{38,39},{39,32},{4... | collective-permute-start | bytes 1966088 | tf_op jit(solution)/shard_map/ppermute | solution.py:171
  51.6 24.9 %collective-permute-start.9 = (bf16[8,64,1280]{2,1,0:T(8,128)(2,1)S(1)}, bf16[8,64,1280]{2,1,0:T(8,128)(2,1)S(1)}, u32[]{:S(2)}, u32[]{:S(2)}) collective-permute-start(bf16[8,64,1280]{2,1,0:T(8,128)(2,1)S(1)} %bitcast_dynamic-update-slice_fusion.8), channel_id=1, source_target_pairs={{0,24},{1,25},{2,26},{3,27},{4,28},{5,29},{6,30},{7,31},{8,0},{9,1... | collective-permute-start | bytes 3932168 | tf_op jit(solution)/shard_map/ppermute | solution.py:171
  53.5 21.7 %collective-permute-start.19 = (bf16[4,64,1280]{2,1,0:T(8,128)(2,1)S(1)}, bf16[4,64,1280]{2,1,0:T(8,128)(2,1)S(1)}, u32[]{:S(2)}, u32[]{:S(2)}) collective-permute-start(bf16[4,64,1280]{2,1,0:T(8,128)(2,1)S(1)} %collective-permute-done.18), channel_id=1, source_target_pairs={{32,39},{33,32},{34,33},{35,34},{36,35},{37,36},{38,37},{39,38},{4... | collective-permute-start | bytes 1966088 | tf_op jit(solution)/shard_map/ppermute | solution.py:171
  62.6 12.5 %collective-permute-start.16 = (bf16[4,64,1280]{2,1,0:T(8,128)(2,1)S(1)}, bf16[4,64,1280]{2,1,0:T(8,128)(2,1)S(1)}, u32[]{:S(2)}, u32[]{:S(2)}) collective-permute-start(bf16[4,64,1280]{2,1,0:T(8,128)(2,1)S(1)} %collective-permute-done.15), channel_id=1, source_target_pairs={{32,33},{33,34},{34,35},{35,36},{36,37},{37,38},{38,39},{39,32},{4... | collective-permute-start | bytes 1966088 | tf_op jit(solution)/shard_map/ppermute | solution.py:171
  65.7 10.8 %collective-permute-start.8 = (bf16[8,64,1280]{2,1,0:T(8,128)(2,1)S(1)}, bf16[8,64,1280]{2,1,0:T(8,128)(2,1)S(1)}, u32[]{:S(2)}, u32[]{:S(2)}) collective-permute-start(bf16[8,64,1280]{2,1,0:T(8,128)(2,1)S(1)} %collective-permute-done.7), channel_id=1, source_target_pairs={{0,8},{1,9},{2,10},{3,11},{4,12},{5,13},{6,14},{7,15},{8,16},{9,17... | collective-permute-start | bytes 3932168 | tf_op jit(solution)/shard_map/ppermute | solution.py:171
  76.5 3.9 copy-start.2
  80.4 4.1 %copy-start.3 = (bf16[4,8,64,1280]{3,2,1,0:T(8,128)(2,1)}, bf16[4,8,64,1280]{3,2,1,0:T(8,128)(2,1)S(1)}, u32[]{:S(2)}) copy-start(bf16[4,8,64,1280]{3,2,1,0:T(8,128)(2,1)S(1)} %get-tuple-element.45) | copy-start | bytes 15728644
  80.4 19.6 %copy-start.18 = (bf16[1,128,2048]{2,1,0:T(8,128)(2,1)S(1)}, bf16[1,128,2048]{2,1,0:T(8,128)(2,1)}, u32[]{:S(2)}) copy-start(bf16[1,128,2048]{2,1,0:T(8,128)(2,1)} %param.19) | copy-start | bytes 1572868
  80.4 24.8 %copy-start.19 = (bf16[1,128,2048]{2,1,0:T(8,128)(2,1)S(1)}, bf16[1,128,2048]{2,1,0:T(8,128)(2,1)}, u32[]{:S(2)}) copy-start(bf16[1,128,2048]{2,1,0:T(8,128)(2,1)} %param.13) | copy-start | bytes 1572868
  84.5 26.4 %collective-permute-start.20 = (bf16[2048,1280]{1,0:T(8,128)(2,1)}, bf16[2048,1280]{1,0:T(8,128)(2,1)}, u32[]{:S(2)}, u32[]{:S(2)}) collective-permute-start(bf16[2048,1280]{1,0:T(8,128)(2,1)} %bitcast_select_fusion.1), channel_id=1, source_target_pairs={{0,32},{32,0},{64,96},{96,64},{128,160},{160,128},{192,224},{224,1... | collective-permute-start | bytes 15728648 | tf_op jit(solution)/shard_map/ppermute | solution.py:218
  101.0 20.3 %all-to-all-start.1 = ((bf16[32,128,64]{1,2,0:T(8,128)(2,1)}), bf16[32,128,64]{1,2,0:T(8,128)(2,1)S(1)}, u32[]{:S(2)}, u32[]{:S(2)}) async-start(bf16[32,128,64]{1,2,0:T(8,128)(2,1)} %bitcast.40), calls=%async_computation.1 | async-start | bytes 1048576 | tf_op jit(solution)/shard_map/all_to_all | solution.py:213
  114.9 12.4 %copy-start.20 = (s32[32]{0:T(128)S(1)}, s32[32]{0:T(128)}, u32[]{:S(2)}) copy-start(s32[32]{0:T(128)} %param.18) | copy-start | bytes 388
  121.3 42.5 %all-to-all-start = ((bf16[32,128,192]{1,2,0:T(8,128)(2,1)}), bf16[32,128,192]{1,2,0:T(8,128)(2,1)S(1)}, u32[]{:S(2)}, u32[]{:S(2)}) async-start(bf16[32,128,192]{1,2,0:T(8,128)(2,1)} %pad_maximum_fusion.3), calls=%async_computation | async-start | bytes 3145728 | tf_op jit(solution)/shard_map/all_to_all | solution.py:241
  210.2 2.2 copy-start.14
  210.2 2.5 copy-start.16
  210.2 2.8 copy-start.17
  215.7 56.6 %all-to-all-start.2 = ((bf16[32,128,256]{2,1,0:T(8,128)(2,1)}), bf16[32,128,256]{2,1,0:T(8,128)(2,1)S(1)}, u32[]{:S(2)}, u32[]{:S(2)}) async-start(bf16[32,128,256]{2,1,0:T(8,128)(2,1)} %pad_maximum_fusion.2), calls=%async_computation.2 | async-start | bytes 4194304 | tf_op jit(solution)/shard_map/all_to_all | solution.py:258
  226.8 51.0 %copy-start.9 = (bf16[8,128,4,64]{1,3,2,0:T(8,128)(2,1)}, bf16[8,128,4,64]{1,3,2,0:T(8,128)(2,1)S(1)}, u32[]{:S(2)}) copy-start(bf16[8,128,4,64]{1,3,2,0:T(8,128)(2,1)S(1)} %broadcast_select_fusion.1) | copy-start | bytes 1572868
  277.0 1.7 copy-start.11
  277.9 13.4 %copy-start.7 = (bf16[128,2560]{1,0:T(8,128)(2,1)}, bf16[128,2560]{1,0:T(8,128)(2,1)S(1)}, u32[]{:S(2)}) copy-start(bf16[128,2560]{1,0:T(8,128)(2,1)S(1)} %pad_maximum_fusion.5) | copy-start | bytes 1966084
  282.4 18.8 %collective-permute-start.21 = (bf16[2,640,2048]{2,1,0:T(8,128)(2,1)}, bf16[2,640,2048]{2,1,0:T(8,128)(2,1)}, u32[]{:S(2)}, u32[]{:S(2)}) collective-permute-start(bf16[2,640,2048]{2,1,0:T(8,128)(2,1)} %pad_maximum_fusion.1), channel_id=1, source_target_pairs={{0,32},{32,0},{64,96},{96,64},{128,160},{160,128},{192,224},{224,1... | collective-permute-start | bytes 15728648 | tf_op jit(solution)/shard_map/ppermute | solution.py:305
  298.2 2.1 copy-start.12
  300.3 59.4 %copy-start.5 = (bf16[640,2048]{1,0:T(8,128)(2,1)}, bf16[640,2048]{1,0:T(8,128)(2,1)S(1)}, u32[]{:S(2)}) copy-start(bf16[640,2048]{1,0:T(8,128)(2,1)S(1)} %multiply_convert_fusion.3) | copy-start | bytes 7864324
  301.2 54.5 %copy-start.6 = (bf16[640,2048]{1,0:T(8,128)(2,1)}, bf16[640,2048]{1,0:T(8,128)(2,1)S(1)}, u32[]{:S(2)}) copy-start(bf16[640,2048]{1,0:T(8,128)(2,1)S(1)} %multiply_convert_fusion.2) | copy-start | bytes 7864324
  305.3 50.4 %copy-start.4 = (bf16[640,2048]{1,0:T(8,128)(2,1)}, bf16[640,2048]{1,0:T(8,128)(2,1)S(1)}, u32[]{:S(2)}) copy-start(bf16[640,2048]{1,0:T(8,128)(2,1)S(1)} %get-tuple-element.44) | copy-start | bytes 7864324
  305.5 9.4 %collective-permute-start.29 = (bf16[640,256]{1,0:T(8,128)(2,1)S(1)}, bf16[640,256]{1,0:T(8,128)(2,1)S(1)}, u32[]{:S(2)}, u32[]{:S(2)}) collective-permute-start(bf16[640,256]{1,0:T(8,128)(2,1)S(1)} %add_convert_fusion.14), channel_id=1, source_target_pairs={{1,0},{2,1},{3,2},{4,3},{5,4},{6,5},{7,6},{0,7},{9,8},{10,9},{11,1... | collective-permute-start | bytes 983048 | tf_op jit(solution)/shard_map/ppermute | solution.py:321
  306.2 10.7 %collective-permute-start.22 = (bf16[640,256]{1,0:T(8,128)(2,1)S(1)}, bf16[640,256]{1,0:T(8,128)(2,1)S(1)}, u32[]{:S(2)}, u32[]{:S(2)}) collective-permute-start(bf16[640,256]{1,0:T(8,128)(2,1)S(1)} %add_convert_fusion.29), channel_id=1, source_target_pairs={{0,1},{1,2},{2,3},{3,4},{4,5},{5,6},{6,7},{7,0},{8,9},{9,10},{10,1... | collective-permute-start | bytes 983048 | tf_op jit(solution)/shard_map/ppermute | solution.py:321
  315.1 8.5 %collective-permute-start.30 = (bf16[640,256]{1,0:T(8,128)(2,1)S(1)}, bf16[640,256]{1,0:T(8,128)(2,1)S(1)}, u32[]{:S(2)}, u32[]{:S(2)}) collective-permute-start(bf16[640,256]{1,0:T(8,128)(2,1)S(1)} %add_convert_fusion.12), channel_id=1, source_target_pairs={{1,0},{2,1},{3,2},{4,3},{5,4},{6,5},{7,6},{0,7},{9,8},{10,9},{11,1... | collective-permute-start | bytes 983048 | tf_op jit(solution)/shard_map/ppermute | solution.py:321
  317.0 9.8 %collective-permute-start.23 = (bf16[640,256]{1,0:T(8,128)(2,1)S(1)}, bf16[640,256]{1,0:T(8,128)(2,1)S(1)}, u32[]{:S(2)}, u32[]{:S(2)}) collective-permute-start(bf16[640,256]{1,0:T(8,128)(2,1)S(1)} %add_convert_fusion.27), channel_id=1, source_target_pairs={{0,1},{1,2},{2,3},{3,4},{4,5},{5,6},{6,7},{7,0},{8,9},{9,10},{10,1... | collective-permute-start | bytes 983048 | tf_op jit(solution)/shard_map/ppermute | solution.py:321
  323.8 8.3 %collective-permute-start.31 = (bf16[640,256]{1,0:T(8,128)(2,1)S(1)}, bf16[640,256]{1,0:T(8,128)(2,1)S(1)}, u32[]{:S(2)}, u32[]{:S(2)}) collective-permute-start(bf16[640,256]{1,0:T(8,128)(2,1)S(1)} %add_convert_fusion.10), channel_id=1, source_target_pairs={{1,0},{2,1},{3,2},{4,3},{5,4},{6,5},{7,6},{0,7},{9,8},{10,9},{11,1... | collective-permute-start | bytes 983048 | tf_op jit(solution)/shard_map/ppermute | solution.py:321
  327.0 9.1 %collective-permute-start.24 = (bf16[640,256]{1,0:T(8,128)(2,1)S(1)}, bf16[640,256]{1,0:T(8,128)(2,1)S(1)}, u32[]{:S(2)}, u32[]{:S(2)}) collective-permute-start(bf16[640,256]{1,0:T(8,128)(2,1)S(1)} %add_convert_fusion.25), channel_id=1, source_target_pairs={{0,1},{1,2},{2,3},{3,4},{4,5},{5,6},{6,7},{7,0},{8,9},{9,10},{10,1... | collective-permute-start | bytes 983048 | tf_op jit(solution)/shard_map/ppermute | solution.py:321
  332.3 8.2 %collective-permute-start.32 = (bf16[640,256]{1,0:T(8,128)(2,1)S(1)}, bf16[640,256]{1,0:T(8,128)(2,1)S(1)}, u32[]{:S(2)}, u32[]{:S(2)}) collective-permute-start(bf16[640,256]{1,0:T(8,128)(2,1)S(1)} %add_convert_fusion.8), channel_id=1, source_target_pairs={{1,0},{2,1},{3,2},{4,3},{5,4},{6,5},{7,6},{0,7},{9,8},{10,9},{11,1... | collective-permute-start | bytes 983048 | tf_op jit(solution)/shard_map/ppermute | solution.py:321
  336.3 7.9 %collective-permute-start.25 = (bf16[640,256]{1,0:T(8,128)(2,1)S(1)}, bf16[640,256]{1,0:T(8,128)(2,1)S(1)}, u32[]{:S(2)}, u32[]{:S(2)}) collective-permute-start(bf16[640,256]{1,0:T(8,128)(2,1)S(1)} %add_convert_fusion.23), channel_id=1, source_target_pairs={{0,1},{1,2},{2,3},{3,4},{4,5},{5,6},{6,7},{7,0},{8,9},{9,10},{10,1... | collective-permute-start | bytes 983048 | tf_op jit(solution)/shard_map/ppermute | solution.py:321
  340.7 7.5 %collective-permute-start.33 = (bf16[640,256]{1,0:T(8,128)(2,1)S(1)}, bf16[640,256]{1,0:T(8,128)(2,1)S(1)}, u32[]{:S(2)}, u32[]{:S(2)}) collective-permute-start(bf16[640,256]{1,0:T(8,128)(2,1)S(1)} %add_convert_fusion.6), channel_id=1, source_target_pairs={{1,0},{2,1},{3,2},{4,3},{5,4},{6,5},{7,6},{0,7},{9,8},{10,9},{11,1... | collective-permute-start | bytes 983048 | tf_op jit(solution)/shard_map/ppermute | solution.py:321
  344.4 7.2 %collective-permute-start.26 = (bf16[640,256]{1,0:T(8,128)(2,1)S(1)}, bf16[640,256]{1,0:T(8,128)(2,1)S(1)}, u32[]{:S(2)}, u32[]{:S(2)}) collective-permute-start(bf16[640,256]{1,0:T(8,128)(2,1)S(1)} %add_convert_fusion.21), channel_id=1, source_target_pairs={{0,1},{1,2},{2,3},{3,4},{4,5},{5,6},{6,7},{7,0},{8,9},{9,10},{10,1... | collective-permute-start | bytes 983048 | tf_op jit(solution)/shard_map/ppermute | solution.py:321
  348.4 7.3 %collective-permute-start.34 = (bf16[640,256]{1,0:T(8,128)(2,1)S(1)}, bf16[640,256]{1,0:T(8,128)(2,1)S(1)}, u32[]{:S(2)}, u32[]{:S(2)}) collective-permute-start(bf16[640,256]{1,0:T(8,128)(2,1)S(1)} %add_convert_fusion.4), channel_id=1, source_target_pairs={{1,0},{2,1},{3,2},{4,3},{5,4},{6,5},{7,6},{0,7},{9,8},{10,9},{11,1... | collective-permute-start | bytes 983048 | tf_op jit(solution)/shard_map/ppermute | solution.py:321
  351.8 7.9 %collective-permute-start.27 = (bf16[640,256]{1,0:T(8,128)(2,1)S(1)}, bf16[640,256]{1,0:T(8,128)(2,1)S(1)}, u32[]{:S(2)}, u32[]{:S(2)}) collective-permute-start(bf16[640,256]{1,0:T(8,128)(2,1)S(1)} %add_convert_fusion.19), channel_id=1, source_target_pairs={{0,1},{1,2},{2,3},{3,4},{4,5},{5,6},{6,7},{7,0},{8,9},{9,10},{10,1... | collective-permute-start | bytes 983048 | tf_op jit(solution)/shard_map/ppermute | solution.py:321
  356.6 7.7 %collective-permute-start.35 = (bf16[640,256]{1,0:T(8,128)(2,1)}, bf16[640,256]{1,0:T(8,128)(2,1)}, u32[]{:S(2)}, u32[]{:S(2)}) collective-permute-start(bf16[640,256]{1,0:T(8,128)(2,1)} %add_convert_fusion.2), channel_id=1, source_target_pairs={{1,0},{2,1},{3,2},{4,3},{5,4},{6,5},{7,6},{0,7},{9,8},{10,9},{11,1... | collective-permute-start | bytes 983048 | tf_op jit(solution)/shard_map/ppermute | solution.py:321
  360.6 7.7 %collective-permute-start.28 = (bf16[640,256]{1,0:T(8,128)(2,1)}, bf16[640,256]{1,0:T(8,128)(2,1)}, u32[]{:S(2)}, u32[]{:S(2)}) collective-permute-start(bf16[640,256]{1,0:T(8,128)(2,1)} %add_convert_fusion.17), channel_id=1, source_target_pairs={{0,1},{1,2},{2,3},{3,4},{4,5},{5,6},{6,7},{7,0},{8,9},{9,10},{10,1... | collective-permute-start | bytes 983048 | tf_op jit(solution)/shard_map/ppermute | solution.py:321
  369.8 29.8 %copy-start.13 = (bf16[128,32,64]{2,0,1:T(8,128)(2,1)S(1)}, bf16[128,32,64]{2,0,1:T(8,128)(2,1)}, u32[]{:S(2)}) copy-start(bf16[128,32,64]{2,0,1:T(8,128)(2,1)} %get-tuple-element.48) | copy-start | bytes 1572868
  369.9 5.5 %collective-permute-start.36 = (bf16[64,1280]{1,0:T(8,128)(2,1)S(1)}, bf16[64,1280]{1,0:T(8,128)(2,1)S(1)}, u32[]{:S(2)}, u32[]{:S(2)}) collective-permute-start(bf16[64,1280]{1,0:T(8,128)(2,1)S(1)} %get-tuple-element.52), channel_id=1, source_target_pairs={{0,8},{1,9},{2,10},{3,11},{4,12},{5,13},{6,14},{7,15},{8,16},{9,17... | collective-permute-start | bytes 491528 | tf_op jit(solution)/shard_map/ppermute | solution.py:142
  371.1 5.6 %collective-permute-start.38 = (bf16[64,1280]{1,0:T(8,128)(2,1)S(1)}, bf16[64,1280]{1,0:T(8,128)(2,1)S(1)}, u32[]{:S(2)}, u32[]{:S(2)}) collective-permute-start(bf16[64,1280]{1,0:T(8,128)(2,1)S(1)} %get-tuple-element.53), channel_id=1, source_target_pairs={{0,24},{1,25},{2,26},{3,27},{4,28},{5,29},{6,30},{7,31},{8,0},{9,1... | collective-permute-start | bytes 491528 | tf_op jit(solution)/shard_map/ppermute | solution.py:142
  372.6 5.7 %collective-permute-start.37 = (bf16[64,1280]{1,0:T(8,128)(2,1)S(1)}, bf16[64,1280]{1,0:T(8,128)(2,1)S(1)}, u32[]{:S(2)}, u32[]{:S(2)}) collective-permute-start(bf16[64,1280]{1,0:T(8,128)(2,1)S(1)} %get-tuple-element.54), channel_id=1, source_target_pairs={{0,16},{1,17},{2,18},{3,19},{4,20},{5,21},{6,22},{7,23},{8,24},{9,... | collective-permute-start | bytes 491528 | tf_op jit(solution)/shard_map/ppermute | solution.py:142
  378.4 6.6 %collective-permute-start.41 = (bf16[64,1280]{1,0:T(8,128)(2,1)S(1)}, bf16[64,1280]{1,0:T(8,128)(2,1)S(1)}, u32[]{:S(2)}, u32[]{:S(2)}) collective-permute-start(bf16[64,1280]{1,0:T(8,128)(2,1)S(1)} %fusion.5), channel_id=1, source_target_pairs={{0,192},{32,224},{64,0},{96,32},{128,64},{160,96},{192,128},{224,1... | collective-permute-start | bytes 491528 | tf_op jit(solution)/shard_map/ppermute | solution.py:142
  380.9 5.9 %collective-permute-start.40 = (bf16[64,1280]{1,0:T(8,128)(2,1)S(1)}, bf16[64,1280]{1,0:T(8,128)(2,1)S(1)}, u32[]{:S(2)}, u32[]{:S(2)}) collective-permute-start(bf16[64,1280]{1,0:T(8,128)(2,1)S(1)} %fusion.5), channel_id=1, source_target_pairs={{0,128},{32,160},{64,192},{96,224},{128,0},{160,32},{192,64},{224,... | collective-permute-start | bytes 491528 | tf_op jit(solution)/shard_map/ppermute | solution.py:142
  381.4 6.9 %collective-permute-start.39 = (bf16[64,1280]{1,0:T(8,128)(2,1)S(1)}, bf16[64,1280]{1,0:T(8,128)(2,1)S(1)}, u32[]{:S(2)}, u32[]{:S(2)}) collective-permute-start(bf16[64,1280]{1,0:T(8,128)(2,1)S(1)} %fusion.5), channel_id=1, source_target_pairs={{0,64},{32,96},{64,128},{96,160},{128,192},{160,224},{192,0},{224,... | collective-permute-start | bytes 491528 | tf_op jit(solution)/shard_map/ppermute | solution.py:142
  389.1 14.4 %copy-start.1 = (s32[32,32,7]{1,0,2:T(8,128)S(1)}, s32[32,32,7]{1,0,2:T(8,128)}, u32[]{:S(2)}) copy-start(s32[32,32,7]{1,0,2:T(8,128)} %param.17) | copy-start | bytes 86020
  389.2 12.8 %collective-permute-start.42 = (bf16[64,1280]{1,0:T(8,128)(2,1)S(1)}, bf16[64,1280]{1,0:T(8,128)(2,1)S(1)}, u32[]{:S(2)}, u32[]{:S(2)}) collective-permute-start(bf16[64,1280]{1,0:T(8,128)(2,1)S(1)} %select_reduce_fusion), channel_id=1, source_target_pairs={{0,32},{32,0},{64,96},{96,64},{128,160},{160,128},{192,224},{224,1... | collective-permute-start | bytes 491528 | tf_op jit(solution)/shard_map/ppermute | solution.py:336
  (3 other events, 3.4 us)

commit v10 on v9

--- a/solution.py
+++ b/solution.py
@@ -18,47 +18,50 @@
 
 def head_kernel(table_ref, count_ref, q_ref, g_ref, k_ref, v_ref,
                 out_ref, gq_ref, dk_ref, dv_ref, k_cat, v_cat):
-    b = pl.program_id(0)
-    slot_count = table_ref.shape[0] // pl.num_programs(0)
+    step = pl.program_id(0)
+    per_step = q_ref.shape[0]
+    slot_count = table_ref.shape[0] // (pl.num_programs(0) * per_step)
     block_len = q_ref.shape[1]
     head_width = q_ref.shape[-1]
     score_scale = head_width ** (-0.5)
 
-    @pl.when(b == 0)
+    @pl.when(step == 0)
     def _():
         dk_ref[...] = jnp.zeros_like(dk_ref)
         dv_ref[...] = jnp.zeros_like(dv_ref)
 
-    q = q_ref[0]
-    g = g_ref[0]
     used = 4 + count_ref[0]
-    chosen = [table_ref[b * slot_count + j] for j in range(slot_count)]
-    for j in range(slot_count):
-        k_cat[j * block_len : (j + 1) * block_len, :] = k_ref[chosen[j]]
-        v_cat[j * block_len : (j + 1) * block_len, :] = v_ref[chosen[j]]
-    keys = k_cat[...]
-    vals = v_cat[...]
     nt = (((1,), (1,)), ((), ()))
     tn = (((0,), (0,)), ((), ()))
-    scores = lax.dot_general(q, keys, nt, preferred_element_type=jnp.float32) * score_scale
-    slot_of = lax.broadcasted_iota(jnp.int32, (1, slot_count * block_len), 1) // block_len
-    scores = jnp.where(slot_of < used, scores, masked_score)
-    highest = scores.max(axis=-1, keepdims=True)
-    exps = jnp.exp(scores - highest)
-    shares = exps / exps.sum(axis=-1, keepdims=True)
-    shares_low = shares.astype(jnp.bfloat16)
-    attended = jnp.dot(shares_low, vals, preferred_element_type=jnp.float32)
-    out_ref[0] = attended.astype(out_ref.dtype)
-    grad_shares = lax.dot_general(g, vals, nt, preferred_element_type=jnp.float32)
-    weighted = (grad_shares * shares).sum(axis=-1, keepdims=True)
-    grad_scores = (shares * (grad_shares - weighted)).astype(jnp.bfloat16)
-    grad_query = jnp.dot(grad_scores, keys, preferred_element_type=jnp.float32)
-    gq_ref[0] = (grad_query * score_scale).astype(gq_ref.dtype)
-    dk = lax.dot_general(grad_scores, q, tn, preferred_element_type=jnp.float32) * score_scale
-    dv = lax.dot_general(shares_low, g, tn, preferred_element_type=jnp.float32)
-    for j in range(slot_count):
-        dk_ref[chosen[j]] += dk[j * block_len : (j + 1) * block_len]
-        dv_ref[chosen[j]] += dv[j * block_len : (j + 1) * block_len]
+    for sub in range(per_step):
+        b = step * per_step + sub
+        q = q_ref[sub]
+        g = g_ref[sub]
+        chosen = [table_ref[b * slot_count + j] for j in range(slot_count)]
+        for j in range(slot_count):
+            k_cat[j * block_len : (j + 1) * block_len, :] = k_ref[chosen[j]]
+            v_cat[j * block_len : (j + 1) * block_len, :] = v_ref[chosen[j]]
+        keys = k_cat[...]
+        vals = v_cat[...]
+        scores = lax.dot_general(q, keys, nt, preferred_element_type=jnp.float32) * score_scale
+        slot_of = lax.broadcasted_iota(jnp.int32, (1, slot_count * block_len), 1) // block_len
+        scores = jnp.where(slot_of < used, scores, masked_score)
+        highest = scores.max(axis=-1, keepdims=True)
+        exps = jnp.exp(scores - highest)
+        shares = exps / exps.sum(axis=-1, keepdims=True)
+        shares_low = shares.astype(jnp.bfloat16)
+        attended = jnp.dot(shares_low, vals, preferred_element_type=jnp.float32)
+        out_ref[sub] = attended.astype(out_ref.dtype)
+        grad_shares = lax.dot_general(g, vals, nt, preferred_element_type=jnp.float32)
+        weighted = (grad_shares * shares).sum(axis=-1, keepdims=True)
+        grad_scores = (shares * (grad_shares - weighted)).astype(jnp.bfloat16)
+        grad_query = jnp.dot(grad_scores, keys, preferred_element_type=jnp.float32)
+        gq_ref[sub] = (grad_query * score_scale).astype(gq_ref.dtype)
+        dk = lax.dot_general(grad_scores, q, tn, preferred_element_type=jnp.float32) * score_scale
+        dv = lax.dot_general(shares_low, g, tn, preferred_element_type=jnp.float32)
+        for j in range(slot_count):
+            dk_ref[chosen[j]] += dk[j * block_len : (j + 1) * block_len]
+            dv_ref[chosen[j]] += dv[j * block_len : (j + 1) * block_len]
 
 
 def head_pass(queries, key_rows, value_rows, grad_head, blocks, extra_count):
@@ -66,11 +69,12 @@
     block_count, slot_count = blocks.shape
     block_len = seq_len // block_count
     tiles = (block_count, block_len, head_width)
-    one_block = pl.BlockSpec((1, block_len, head_width), lambda b, t, c: (b, 0, 0))
+    per_step = 2
+    one_block = pl.BlockSpec((per_step, block_len, head_width), lambda b, t, c: (b, 0, 0))
     whole = pl.BlockSpec(tiles, lambda b, t, c: (0, 0, 0))
     grid_spec = pltpu.PrefetchScalarGridSpec(
         num_scalar_prefetch=2,
-        grid=(block_count,),
+        grid=(block_count // per_step,),
         in_specs=[one_block, one_block, whole, whole],
         out_specs=[one_block, one_block, whole, whole],
         scratch_shapes=[

time: 412 us -> 409 us (level)
  transfers between devices with their start and end apart: 46 -> 46, of which waited for: 22 -> 21; matrix products, arithmetic and copies ran while one was open for 12% -> 12% of each run, Pallas kernels for 0% -> 0%
where the time goes in v10:
time: 409 us; the launch traced here: 401 us
  waiting for transfers between devices  160 us (39%)
  starting transfers between devices  115 us (28%)
  Pallas kernels  39.3 us (10%)
  local copies, waits for them, and re-layouts  34.7 us (8%)
  other arithmetic  34.1 us (8%)
  matrix products  15.9 us (4%)
    all_to_all x1, waiting for transfers between devices, per_device(): lax.all_to_all(back_sent, 'seq', split_axis=0, concat_axis=0, tiled=True)  44.4 us
    ppermute x20, starting transfers between devices, ring(): cur = lax.ppermute(cur, ('dp', 'seq'), perm)  40.6 us
    pallas_call x1, Pallas kernels, head_pass(): pl.pallas_call(head_kernel, grid_spec=grid_spec, out_shape=[jax.ShapeDtyp...  39.3 us
    ppermute x14, waiting for transfers between devices, per_device(): arrived = lax.ppermute(buf, 'seq', perm)  37.2 us
    all_to_all x1, waiting for transfers between devices, per_device(): lax.all_to_all(sent, 'seq', split_axis=0, concat_axis=1, tiled=True)[0]  33.9 us
    ppermute x20, waiting for transfers between devices, ring(): cur = lax.ppermute(cur, ('dp', 'seq'), perm)  29.1 us
    ppermute x14, starting transfers between devices, per_device(): arrived = lax.ppermute(buf, 'seq', perm)  20.2 us
    ppermute x1, starting transfers between devices, per_device(): w_other = lax.ppermute(w_mine, 'dp', pairs)  15.5 us
  transfers between devices with their start and end apart: 46, of which 21 were waited for; matrix products, arithmetic and copies ran while one was open for 12% of the time, Pallas kernels for 0%

profile of v10, /device:TPU:1, one launch (start us, length us, event | category | flops | bytes accessed | tf_op | source)
XLA Modules:
  0.0 401.1 jit_solution(14324293600330511630)
XLA Ops:
  1.7 4.0 %collective-permute-start.10 = (bf16[64,1280]{1,0:T(8,128)(2,1)S(1)}, bf16[64,1280]{1,0:T(8,128)(2,1)S(1)}, u32[]{:S(2)}, u32[]{:S(2)}) collective-permute-start(bf16[64,1280]{1,0:T(8,128)(2,1)S(1)} %get-tuple-element.40), channel_id=1, source_target_pairs={{32,40},{33,41},{34,42},{35,43},{36,44},{37,45},{38,46},{39,47},{4... | collective-permute-start | bytes 491528 | tf_op jit(solution)/shard_map/ppermute | solution.py:175
  7.1 3.4 collective-permute-start.12
  10.5 1.9 collective-permute-start.11
  13.9 4.2 %collective-permute-done.11 = bf16[64,1280]{1,0:T(8,128)(2,1)S(1)} collective-permute-done((bf16[64,1280]{1,0:T(8,128)(2,1)S(1)}, bf16[64,1280]{1,0:T(8,128)(2,1)S(1)}, u32[]{:S(2)}, u32[]{:S(2)}) %collective-permute-start.11) | collective-permute-done | bytes 163872 | tf_op jit(solution)/shard_map/ppermute | solution.py:175
  19.0 3.2 collective-permute-start.13
  22.2 5.9 %collective-permute-start.17 = (bf16[4,64,1280]{2,1,0:T(8,128)(2,1)}, bf16[4,64,1280]{2,1,0:T(8,128)(2,1)}, u32[]{:S(2)}, u32[]{:S(2)}) collective-permute-start(bf16[4,64,1280]{2,1,0:T(8,128)(2,1)} %pad_maximum_fusion.4), channel_id=1, source_target_pairs={{32,39},{33,32},{34,33},{35,34},{36,35},{37,36},{38,37},{39,38},{4... | collective-permute-start | bytes 1966088 | tf_op jit(solution)/shard_map/ppermute | solution.py:175
  30.3 4.7 %collective-permute-done.13 = bf16[4,64,1280]{2,1,0:T(8,128)(2,1)} collective-permute-done((bf16[4,64,1280]{2,1,0:T(8,128)(2,1)}, bf16[4,64,1280]{2,1,0:T(8,128)(2,1)}, u32[]{:S(2)}, u32[]{:S(2)}) %collective-permute-start.13) | collective-permute-done | bytes 655392 | tf_op jit(solution)/shard_map/ppermute | solution.py:175
  35.0 1.9 collective-permute-start.14
  37.7 5.0 %collective-permute-start.18 = (bf16[4,64,1280]{2,1,0:T(8,128)(2,1)}, bf16[4,64,1280]{2,1,0:T(8,128)(2,1)S(1)}, u32[]{:S(2)}, u32[]{:S(2)}) collective-permute-start(bf16[4,64,1280]{2,1,0:T(8,128)(2,1)} %collective-permute-done.17), channel_id=1, source_target_pairs={{32,39},{33,32},{34,33},{35,34},{36,35},{37,36},{38,37},{39,38},{4... | collective-permute-start | bytes 1966088 | tf_op jit(solution)/shard_map/ppermute | solution.py:175
  42.7 6.9 %collective-permute-done.14 = bf16[4,64,1280]{2,1,0:T(8,128)(2,1)} collective-permute-done((bf16[4,64,1280]{2,1,0:T(8,128)(2,1)}, bf16[4,64,1280]{2,1,0:T(8,128)(2,1)}, u32[]{:S(2)}, u32[]{:S(2)}) %collective-permute-start.14) | collective-permute-done | bytes 655392 | tf_op jit(solution)/shard_map/ppermute | solution.py:175
  49.6 1.9 collective-permute-start.15
  53.5 4.6 %collective-permute-start.19 = (bf16[4,64,1280]{2,1,0:T(8,128)(2,1)S(1)}, bf16[4,64,1280]{2,1,0:T(8,128)(2,1)S(1)}, u32[]{:S(2)}, u32[]{:S(2)}) collective-permute-start(bf16[4,64,1280]{2,1,0:T(8,128)(2,1)S(1)} %collective-permute-done.18), channel_id=1, source_target_pairs={{32,39},{33,32},{34,33},{35,34},{36,35},{37,36},{38,37},{39,38},{4... | collective-permute-start | bytes 1966088 | tf_op jit(solution)/shard_map/ppermute | solution.py:175
  58.1 4.6 %collective-permute-done.15 = bf16[4,64,1280]{2,1,0:T(8,128)(2,1)S(1)} collective-permute-done((bf16[4,64,1280]{2,1,0:T(8,128)(2,1)}, bf16[4,64,1280]{2,1,0:T(8,128)(2,1)S(1)}, u32[]{:S(2)}, u32[]{:S(2)}) %collective-permute-start.15) | collective-permute-done | bytes 655392 | tf_op jit(solution)/shard_map/ppermute | solution.py:175
  62.6 1.9 collective-permute-start.16
  66.5 8.7 %collective-permute-done.16 = bf16[4,64,1280]{2,1,0:T(8,128)(2,1)S(1)} collective-permute-done((bf16[4,64,1280]{2,1,0:T(8,128)(2,1)S(1)}, bf16[4,64,1280]{2,1,0:T(8,128)(2,1)S(1)}, u32[]{:S(2)}, u32[]{:S(2)}) %collective-permute-start.16) | collective-permute-done | bytes 655392 | tf_op jit(solution)/shard_map/ppermute | solution.py:175
  76.5 3.9 pad_maximum_fusion
  80.4 4.1 %bitcast_select_fusion.1 = bf16[2048,1280]{1,0:T(8,128)(2,1)} fusion(bf16[8,4,64,1280]{3,2,1,0:T(8,128)(2,1)S(1)} %bitcast_dynamic-update-slice_fusion, bf16[4,8,64,1280]{3,2,1,0:T(8,128)(2,1)S(1)} %get-tuple-element.45, pred[]{:T(512)S(6)} %eq.27), kind=kLoop, calls=%fused_computation.12 | loop fusion | flops 2621440 | bytes 15728641 | tf_op jit(solution)/shard_map/jit(_where)/select_n | solution.py:221
  84.5 15.5 %collective-permute-start.20 = (bf16[2048,1280]{1,0:T(8,128)(2,1)}, bf16[2048,1280]{1,0:T(8,128)(2,1)}, u32[]{:S(2)}, u32[]{:S(2)}) collective-permute-start(bf16[2048,1280]{1,0:T(8,128)(2,1)} %bitcast_select_fusion.1), channel_id=1, source_target_pairs={{0,32},{32,0},{64,96},{96,64},{128,160},{160,128},{192,224},{224,1... | collective-permute-start | bytes 15728648 | tf_op jit(solution)/shard_map/ppermute | solution.py:222
  101.0 3.9 all-to-all-start.1
  107.1 3.4 convolution_convert_fusion.1
  110.9 3.4 convolution_convert_fusion
  116.2 5.2 %all-to-all-done.1 = bf16[32,128,64]{1,2,0:T(8,128)(2,1)S(1)} async-done(((bf16[32,128,64]{1,2,0:T(8,128)(2,1)}), bf16[32,128,64]{1,2,0:T(8,128)(2,1)S(1)}, u32[]{:S(2)}, u32[]{:S(2)}) %all-to-all-start.1) | async-done | bytes 524320 | tf_op jit(solution)/shard_map/all_to_all | solution.py:217
  121.3 6.0 %all-to-all-start = ((bf16[32,128,192]{1,2,0:T(8,128)(2,1)}), bf16[32,128,192]{1,2,0:T(8,128)(2,1)S(1)}, u32[]{:S(2)}, u32[]{:S(2)}) async-start(bf16[32,128,192]{1,2,0:T(8,128)(2,1)} %pad_maximum_fusion.3), calls=%async_computation | async-start | bytes 3145728 | tf_op jit(solution)/shard_map/all_to_all | solution.py:245
  128.6 1.3 copy.61.g_ref
  130.0 33.9 %all-to-all-done = bf16[32,128,192]{1,2,0:T(8,128)(2,1)S(1)} async-done(((bf16[32,128,192]{1,2,0:T(8,128)(2,1)}), bf16[32,128,192]{1,2,0:T(8,128)(2,1)S(1)}, u32[]{:S(2)}, u32[]{:S(2)}) %all-to-all-start) | async-done | bytes 1572896 | tf_op jit(solution)/shard_map/all_to_all | solution.py:245
  164.3 1.4 copy.60
  165.6 1.4 copy.59
  167.0 1.4 copy.57
  168.3 39.3 %shard_map.110 = (bf16[32,128,64]{2,1,0:T(8,128)(2,1)}, bf16[32,128,64]{2,1,0:T(8,128)(2,1)}, f32[32,128,64]{2,1,0:T(8,128)}, f32[32,128,64]{2,1,0:T(8,128)}) custom-call(s32[224]{0:T(256)} %reshape.330.table_ref, s32[1]{0:T(128)} %dynamic_slice.35.count_ref, bf16[32,128,64]{2,1,0:T(8,128)(2,1)} %bitcast.194, bf16[32,128,64]{2,1,0:T(8,128)(2,1)} %copy.61.g_ref, ...), custom_call_target="tpu_custom_call" | custom-call | flops 2818572288 | bytes 5242880 | tf_op jit(solution)/shard_map/pallas_call | solution.py:86
  207.6 1.9 convert.10
  210.4 2.7 pad_maximum_fusion.2
  213.1 7.9 %all-to-all-start.2 = ((bf16[32,128,256]{2,1,0:T(8,128)(2,1)}), bf16[32,128,256]{2,1,0:T(8,128)(2,1)S(1)}, u32[]{:S(2)}, u32[]{:S(2)}) async-start(bf16[32,128,256]{2,1,0:T(8,128)(2,1)} %pad_maximum_fusion.2), calls=%async_computation.2 | async-start | bytes 4194304 | tf_op jit(solution)/shard_map/all_to_all | solution.py:262
  221.6 1.4 gather_fusion.5
  225.2 44.4 %all-to-all-done.2 = bf16[32,128,256]{2,1,0:T(8,128)(2,1)S(1)} async-done(((bf16[32,128,256]{2,1,0:T(8,128)(2,1)}), bf16[32,128,256]{2,1,0:T(8,128)(2,1)S(1)}, u32[]{:S(2)}, u32[]{:S(2)}) %all-to-all-start.2) | async-done | bytes 2097184 | tf_op jit(solution)/shard_map/all_to_all | solution.py:262
  269.6 1.9 slice_bitcast_fusion.2
  271.5 1.6 copy.63
  277.0 2.8 pad_maximum_fusion.1
  279.8 2.4 collective-permute-start.21
  284.2 4.6 %bitcast_select_fusion = bf16[32,64,1280]{2,1,0:T(8,128)(2,1)S(1)} fusion(bf16[8,4,64,1280]{3,2,1,0:T(8,128)(2,1)} %copy-done.2, bf16[4,8,64,1280]{3,2,1,0:T(8,128)(2,1)} %copy-done.3, pred[]{:T(512)S(6)} %eq.27), kind=kLoop, calls=%fused_computation.11 | loop fusion | flops 2621440 | bytes 15728641 | tf_op jit(solution)/shard_map/jit(_where)/select_n | solution.py:221
  288.8 1.5 fusion.6
  291.0 4.1 %fusion.8 = f32[128,2048]{0,1:T(8,128)S(1)} fusion(bf16[2048,1280]{1,0:T(8,128)(2,1)} %collective-permute-done.20, bf16[128,2560]{1,0:T(8,128)(2,1)} %copy-done.7, s32[]{:T(128)S(6)} %select_n.274), kind=kOutput, calls=%fused_computation.88 | convolution fusion | flops 671088640 | bytes 6619140 | tf_op jit(solution)/shard_map/dot_general | solution.py:283
  298.8 4.0 %slice_bitcast_fusion.1 = (bf16[640,2048]{1,0:T(8,128)(2,1)S(1)}, bf16[640,2048]{1,0:T(8,128)(2,1)S(1)}) fusion(bf16[2,640,2048]{2,1,0:T(8,128)(2,1)} %collective-permute-done.21), kind=kLoop, calls=%fused_computation.21 | loop fusion | bytes 10485760 | tf_op jit(solution)/shard_map/squeeze | solution.py:320
  304.8 7.7 %collective-permute-done.29 = bf16[640,256]{1,0:T(8,128)(2,1)S(1)} collective-permute-done((bf16[640,256]{1,0:T(8,128)(2,1)S(1)}, bf16[640,256]{1,0:T(8,128)(2,1)S(1)}, u32[]{:S(2)}, u32[]{:S(2)}) %collective-permute-start.29) | collective-permute-done | bytes 327712 | tf_op jit(solution)/shard_map/ppermute | solution.py:325
  312.7 1.8 collective-permute-start.30
  314.7 6.5 %collective-permute-done.30 = bf16[640,256]{1,0:T(8,128)(2,1)S(1)} collective-permute-done((bf16[640,256]{1,0:T(8,128)(2,1)S(1)}, bf16[640,256]{1,0:T(8,128)(2,1)S(1)}, u32[]{:S(2)}, u32[]{:S(2)}) %collective-permute-start.30) | collective-permute-done | bytes 327712 | tf_op jit(solution)/shard_map/ppermute | solution.py:325
  321.4 3.0 collective-permute-start.31
  324.7 5.0 %collective-permute-done.31 = bf16[640,256]{1,0:T(8,128)(2,1)S(1)} collective-permute-done((bf16[640,256]{1,0:T(8,128)(2,1)S(1)}, bf16[640,256]{1,0:T(8,128)(2,1)S(1)}, u32[]{:S(2)}, u32[]{:S(2)}) %collective-permute-start.31) | collective-permute-done | bytes 327712 | tf_op jit(solution)/shard_map/ppermute | solution.py:325
  329.9 3.7 collective-permute-start.32
  333.8 4.1 %collective-permute-done.32 = bf16[640,256]{1,0:T(8,128)(2,1)S(1)} collective-permute-done((bf16[640,256]{1,0:T(8,128)(2,1)S(1)}, bf16[640,256]{1,0:T(8,128)(2,1)S(1)}, u32[]{:S(2)}, u32[]{:S(2)}) %collective-permute-start.32) | collective-permute-done | bytes 327712 | tf_op jit(solution)/shard_map/ppermute | solution.py:325
  338.2 3.5 collective-permute-start.33
  342.0 3.7 collective-permute-done.33
  345.9 3.2 collective-permute-start.34
  349.4 3.8 collective-permute-done.34
  354.1 3.1 collective-permute-start.35
  358.1 3.7 collective-permute-done.35
  363.1 2.7 collective-permute-done.28
  368.6 1.5 collective-permute-start.38
  370.1 1.4 collective-permute-start.37
  372.8 3.0 collective-permute-done.37
  375.9 2.5 collective-permute-start.41
  379.6 2.9 collective-permute-done.41
  382.4 1.8 collective-permute-done.40
  384.3 1.6 collective-permute-done.39
  386.7 10.4 %collective-permute-start.42 = (bf16[64,1280]{1,0:T(8,128)(2,1)S(1)}, bf16[64,1280]{1,0:T(8,128)(2,1)S(1)}, u32[]{:S(2)}, u32[]{:S(2)}) collective-permute-start(bf16[64,1280]{1,0:T(8,128)(2,1)S(1)} %select_reduce_fusion), channel_id=1, source_target_pairs={{0,32},{32,0},{64,96},{96,64},{128,160},{160,128},{192,224},{224,1... | collective-permute-start | bytes 491528 | tf_op jit(solution)/shard_map/ppermute | solution.py:340
  (202 shorter events, 50.7 us)
Async XLA Ops:
  0.6 127.2 %copy-start = (s32[32,32,7]{1,0,2:T(8,128)S(1)}, s32[32,32,7]{1,0,2:T(8,128)}, u32[]{:S(2)}) copy-start(s32[32,32,7]{1,0,2:T(8,128)} %param.17) | copy-start | bytes 86020
  1.7 8.8 %collective-permute-start.10 = (bf16[64,1280]{1,0:T(8,128)(2,1)S(1)}, bf16[64,1280]{1,0:T(8,128)(2,1)S(1)}, u32[]{:S(2)}, u32[]{:S(2)}) collective-permute-start(bf16[64,1280]{1,0:T(8,128)(2,1)S(1)} %get-tuple-element.40), channel_id=1, source_target_pairs={{32,40},{33,41},{34,42},{35,43},{36,44},{37,45},{38,46},{39,47},{4... | collective-permute-start | bytes 491528 | tf_op jit(solution)/shard_map/ppermute | solution.py:175
  5.8 6.7 %collective-permute-start.4 = (bf16[64,1280]{1,0:T(8,128)(2,1)S(1)}, bf16[64,1280]{1,0:T(8,128)(2,1)S(1)}, u32[]{:S(2)}, u32[]{:S(2)}) collective-permute-start(bf16[64,1280]{1,0:T(8,128)(2,1)S(1)} %get-tuple-element.40), channel_id=1, source_target_pairs={{0,7},{1,0},{2,1},{3,2},{4,3},{5,4},{6,5},{7,6},{8,15},{9,8},{10,9... | collective-permute-start | bytes 491528 | tf_op jit(solution)/shard_map/ppermute | solution.py:175
  6.5 6.7 %collective-permute-start = (bf16[64,1280]{1,0:T(8,128)(2,1)S(1)}, bf16[64,1280]{1,0:T(8,128)(2,1)S(1)}, u32[]{:S(2)}, u32[]{:S(2)}) collective-permute-start(bf16[64,1280]{1,0:T(8,128)(2,1)S(1)} %get-tuple-element.40), channel_id=1, source_target_pairs={{0,1},{1,2},{2,3},{3,4},{4,5},{5,6},{6,7},{7,0},{8,9},{9,10},{10,1... | collective-permute-start | bytes 491528 | tf_op jit(solution)/shard_map/ppermute | solution.py:175
  7.1 6.7 %collective-permute-start.12 = (bf16[64,1280]{1,0:T(8,128)(2,1)S(1)}, bf16[64,1280]{1,0:T(8,128)(2,1)S(1)}, u32[]{:S(2)}, u32[]{:S(2)}) collective-permute-start(bf16[64,1280]{1,0:T(8,128)(2,1)S(1)} %get-tuple-element.40), channel_id=1, source_target_pairs={{32,56},{33,57},{34,58},{35,59},{36,60},{37,61},{38,62},{39,63},{4... | collective-permute-start | bytes 491528 | tf_op jit(solution)/shard_map/ppermute | solution.py:175
  10.5 7.6 %collective-permute-start.11 = (bf16[64,1280]{1,0:T(8,128)(2,1)S(1)}, bf16[64,1280]{1,0:T(8,128)(2,1)S(1)}, u32[]{:S(2)}, u32[]{:S(2)}) collective-permute-start(bf16[64,1280]{1,0:T(8,128)(2,1)S(1)} %collective-permute-done.10), channel_id=1, source_target_pairs={{32,40},{33,41},{34,42},{35,43},{36,44},{37,45},{38,46},{39,47},{4... | collective-permute-start | bytes 491528 | tf_op jit(solution)/shard_map/ppermute | solution.py:175
  12.5 15.7 %collective-permute-start.5 = (bf16[64,1280]{1,0:T(8,128)(2,1)S(1)}, bf16[64,1280]{1,0:T(8,128)(2,1)S(1)}, u32[]{:S(2)}, u32[]{:S(2)}) collective-permute-start(bf16[64,1280]{1,0:T(8,128)(2,1)S(1)} %collective-permute-done.4), channel_id=1, source_target_pairs={{0,7},{1,0},{2,1},{3,2},{4,3},{5,4},{6,5},{7,6},{8,15},{9,8},{10,9... | collective-permute-start | bytes 491528 | tf_op jit(solution)/shard_map/ppermute | solution.py:175
  13.1 15.7 %collective-permute-start.1 = (bf16[64,1280]{1,0:T(8,128)(2,1)S(1)}, bf16[64,1280]{1,0:T(8,128)(2,1)S(1)}, u32[]{:S(2)}, u32[]{:S(2)}) collective-permute-start(bf16[64,1280]{1,0:T(8,128)(2,1)S(1)} %collective-permute-done), channel_id=1, source_target_pairs={{0,1},{1,2},{2,3},{3,4},{4,5},{5,6},{6,7},{7,0},{8,9},{9,10},{10,1... | collective-permute-start | bytes 491528 | tf_op jit(solution)/shard_map/ppermute | solution.py:175
  19.0 16.0 %collective-permute-start.13 = (bf16[4,64,1280]{2,1,0:T(8,128)(2,1)}, bf16[4,64,1280]{2,1,0:T(8,128)(2,1)}, u32[]{:S(2)}, u32[]{:S(2)}) collective-permute-start(bf16[4,64,1280]{2,1,0:T(8,128)(2,1)} %pad_maximum_fusion.4), channel_id=1, source_target_pairs={{32,33},{33,34},{34,35},{35,36},{36,37},{37,38},{38,39},{39,32},{4... | collective-permute-start | bytes 1966088 | tf_op jit(solution)/shard_map/ppermute | solution.py:175
  22.2 15.5 %collective-permute-start.17 = (bf16[4,64,1280]{2,1,0:T(8,128)(2,1)}, bf16[4,64,1280]{2,1,0:T(8,128)(2,1)}, u32[]{:S(2)}, u32[]{:S(2)}) collective-permute-start(bf16[4,64,1280]{2,1,0:T(8,128)(2,1)} %pad_maximum_fusion.4), channel_id=1, source_target_pairs={{32,39},{33,32},{34,33},{35,34},{36,35},{37,36},{38,37},{39,38},{4... | collective-permute-start | bytes 1966088 | tf_op jit(solution)/shard_map/ppermute | solution.py:175
  28.1 2.1 collective-permute-start.6
  28.8 0.7 collective-permute-start.2
  29.5 0.7 collective-permute-start.3
  35.0 14.6 %collective-permute-start.14 = (bf16[4,64,1280]{2,1,0:T(8,128)(2,1)}, bf16[4,64,1280]{2,1,0:T(8,128)(2,1)}, u32[]{:S(2)}, u32[]{:S(2)}) collective-permute-start(bf16[4,64,1280]{2,1,0:T(8,128)(2,1)} %collective-permute-done.13), channel_id=1, source_target_pairs={{32,33},{33,34},{34,35},{35,36},{36,37},{37,38},{38,39},{39,32},{4... | collective-permute-start | bytes 1966088 | tf_op jit(solution)/shard_map/ppermute | solution.py:175
  37.0 28.7 %collective-permute-start.7 = (bf16[8,64,1280]{2,1,0:T(8,128)(2,1)S(1)}, bf16[8,64,1280]{2,1,0:T(8,128)(2,1)S(1)}, u32[]{:S(2)}, u32[]{:S(2)}) collective-permute-start(bf16[8,64,1280]{2,1,0:T(8,128)(2,1)S(1)} %bitcast_dynamic-update-slice_fusion.8), channel_id=1, source_target_pairs={{0,8},{1,9},{2,10},{3,11},{4,12},{5,13},{6,14},{7,15},{8,16},{9,17... | collective-permute-start | bytes 3932168 | tf_op jit(solution)/shard_map/ppermute | solution.py:175
  37.7 15.7 %collective-permute-start.18 = (bf16[4,64,1280]{2,1,0:T(8,128)(2,1)}, bf16[4,64,1280]{2,1,0:T(8,128)(2,1)S(1)}, u32[]{:S(2)}, u32[]{:S(2)}) collective-permute-start(bf16[4,64,1280]{2,1,0:T(8,128)(2,1)} %collective-permute-done.17), channel_id=1, source_target_pairs={{32,39},{33,32},{34,33},{35,34},{36,35},{37,36},{38,37},{39,38},{4... | collective-permute-start | bytes 1966088 | tf_op jit(solution)/shard_map/ppermute | solution.py:175
  49.6 13.0 %collective-permute-start.15 = (bf16[4,64,1280]{2,1,0:T(8,128)(2,1)}, bf16[4,64,1280]{2,1,0:T(8,128)(2,1)S(1)}, u32[]{:S(2)}, u32[]{:S(2)}) collective-permute-start(bf16[4,64,1280]{2,1,0:T(8,128)(2,1)} %collective-permute-done.14), channel_id=1, source_target_pairs={{32,33},{33,34},{34,35},{35,36},{36,37},{37,38},{38,39},{39,32},{4... | collective-permute-start | bytes 1966088 | tf_op jit(solution)/shard_map/ppermute | solution.py:175
  51.6 24.9 %collective-permute-start.9 = (bf16[8,64,1280]{2,1,0:T(8,128)(2,1)S(1)}, bf16[8,64,1280]{2,1,0:T(8,128)(2,1)S(1)}, u32[]{:S(2)}, u32[]{:S(2)}) collective-permute-start(bf16[8,64,1280]{2,1,0:T(8,128)(2,1)S(1)} %bitcast_dynamic-update-slice_fusion.8), channel_id=1, source_target_pairs={{0,24},{1,25},{2,26},{3,27},{4,28},{5,29},{6,30},{7,31},{8,0},{9,1... | collective-permute-start | bytes 3932168 | tf_op jit(solution)/shard_map/ppermute | solution.py:175
  53.5 21.7 %collective-permute-start.19 = (bf16[4,64,1280]{2,1,0:T(8,128)(2,1)S(1)}, bf16[4,64,1280]{2,1,0:T(8,128)(2,1)S(1)}, u32[]{:S(2)}, u32[]{:S(2)}) collective-permute-start(bf16[4,64,1280]{2,1,0:T(8,128)(2,1)S(1)} %collective-permute-done.18), channel_id=1, source_target_pairs={{32,39},{33,32},{34,33},{35,34},{36,35},{37,36},{38,37},{39,38},{4... | collective-permute-start | bytes 1966088 | tf_op jit(solution)/shard_map/ppermute | solution.py:175
  62.6 12.5 %collective-permute-start.16 = (bf16[4,64,1280]{2,1,0:T(8,128)(2,1)S(1)}, bf16[4,64,1280]{2,1,0:T(8,128)(2,1)S(1)}, u32[]{:S(2)}, u32[]{:S(2)}) collective-permute-start(bf16[4,64,1280]{2,1,0:T(8,128)(2,1)S(1)} %collective-permute-done.15), channel_id=1, source_target_pairs={{32,33},{33,34},{34,35},{35,36},{36,37},{37,38},{38,39},{39,32},{4... | collective-permute-start | bytes 1966088 | tf_op jit(solution)/shard_map/ppermute | solution.py:175
  65.7 10.8 %collective-permute-start.8 = (bf16[8,64,1280]{2,1,0:T(8,128)(2,1)S(1)}, bf16[8,64,1280]{2,1,0:T(8,128)(2,1)S(1)}, u32[]{:S(2)}, u32[]{:S(2)}) collective-permute-start(bf16[8,64,1280]{2,1,0:T(8,128)(2,1)S(1)} %collective-permute-done.7), channel_id=1, source_target_pairs={{0,8},{1,9},{2,10},{3,11},{4,12},{5,13},{6,14},{7,15},{8,16},{9,17... | collective-permute-start | bytes 3932168 | tf_op jit(solution)/shard_map/ppermute | solution.py:175
  76.5 3.9 copy-start.2
  80.4 4.1 %copy-start.3 = (bf16[4,8,64,1280]{3,2,1,0:T(8,128)(2,1)}, bf16[4,8,64,1280]{3,2,1,0:T(8,128)(2,1)S(1)}, u32[]{:S(2)}) copy-start(bf16[4,8,64,1280]{3,2,1,0:T(8,128)(2,1)S(1)} %get-tuple-element.45) | copy-start | bytes 15728644
  80.4 19.6 %copy-start.18 = (bf16[1,128,2048]{2,1,0:T(8,128)(2,1)S(1)}, bf16[1,128,2048]{2,1,0:T(8,128)(2,1)}, u32[]{:S(2)}) copy-start(bf16[1,128,2048]{2,1,0:T(8,128)(2,1)} %param.19) | copy-start | bytes 1572868
  80.4 24.8 %copy-start.19 = (bf16[1,128,2048]{2,1,0:T(8,128)(2,1)S(1)}, bf16[1,128,2048]{2,1,0:T(8,128)(2,1)}, u32[]{:S(2)}) copy-start(bf16[1,128,2048]{2,1,0:T(8,128)(2,1)} %param.13) | copy-start | bytes 1572868
  84.5 26.4 %collective-permute-start.20 = (bf16[2048,1280]{1,0:T(8,128)(2,1)}, bf16[2048,1280]{1,0:T(8,128)(2,1)}, u32[]{:S(2)}, u32[]{:S(2)}) collective-permute-start(bf16[2048,1280]{1,0:T(8,128)(2,1)} %bitcast_select_fusion.1), channel_id=1, source_target_pairs={{0,32},{32,0},{64,96},{96,64},{128,160},{160,128},{192,224},{224,1... | collective-permute-start | bytes 15728648 | tf_op jit(solution)/shard_map/ppermute | solution.py:222
  101.0 20.3 %all-to-all-start.1 = ((bf16[32,128,64]{1,2,0:T(8,128)(2,1)}), bf16[32,128,64]{1,2,0:T(8,128)(2,1)S(1)}, u32[]{:S(2)}, u32[]{:S(2)}) async-start(bf16[32,128,64]{1,2,0:T(8,128)(2,1)} %bitcast.40), calls=%async_computation.1 | async-start | bytes 1048576 | tf_op jit(solution)/shard_map/all_to_all | solution.py:217
  114.9 12.4 %copy-start.20 = (s32[32]{0:T(128)S(1)}, s32[32]{0:T(128)}, u32[]{:S(2)}) copy-start(s32[32]{0:T(128)} %param.18) | copy-start | bytes 388
  121.3 42.6 %all-to-all-start = ((bf16[32,128,192]{1,2,0:T(8,128)(2,1)}), bf16[32,128,192]{1,2,0:T(8,128)(2,1)S(1)}, u32[]{:S(2)}, u32[]{:S(2)}) async-start(bf16[32,128,192]{1,2,0:T(8,128)(2,1)} %pad_maximum_fusion.3), calls=%async_computation | async-start | bytes 3145728 | tf_op jit(solution)/shard_map/all_to_all | solution.py:245
  207.6 2.2 copy-start.14
  207.6 2.5 copy-start.16
  207.6 2.8 copy-start.17
  213.1 56.6 %all-to-all-start.2 = ((bf16[32,128,256]{2,1,0:T(8,128)(2,1)}), bf16[32,128,256]{2,1,0:T(8,128)(2,1)S(1)}, u32[]{:S(2)}, u32[]{:S(2)}) async-start(bf16[32,128,256]{2,1,0:T(8,128)(2,1)} %pad_maximum_fusion.2), calls=%async_computation.2 | async-start | bytes 4194304 | tf_op jit(solution)/shard_map/all_to_all | solution.py:262
  224.2 51.0 %copy-start.9 = (bf16[8,128,4,64]{1,3,2,0:T(8,128)(2,1)}, bf16[8,128,4,64]{1,3,2,0:T(8,128)(2,1)S(1)}, u32[]{:S(2)}) copy-start(bf16[8,128,4,64]{1,3,2,0:T(8,128)(2,1)S(1)} %broadcast_select_fusion.1) | copy-start | bytes 1572868
  274.4 1.7 copy-start.11
  275.2 13.6 %copy-start.7 = (bf16[128,2560]{1,0:T(8,128)(2,1)}, bf16[128,2560]{1,0:T(8,128)(2,1)S(1)}, u32[]{:S(2)}) copy-start(bf16[128,2560]{1,0:T(8,128)(2,1)S(1)} %pad_maximum_fusion.5) | copy-start | bytes 1966084
  279.8 19.0 %collective-permute-start.21 = (bf16[2,640,2048]{2,1,0:T(8,128)(2,1)}, bf16[2,640,2048]{2,1,0:T(8,128)(2,1)}, u32[]{:S(2)}, u32[]{:S(2)}) collective-permute-start(bf16[2,640,2048]{2,1,0:T(8,128)(2,1)} %pad_maximum_fusion.1), channel_id=1, source_target_pairs={{0,32},{32,0},{64,96},{96,64},{128,160},{160,128},{192,224},{224,1... | collective-permute-start | bytes 15728648 | tf_op jit(solution)/shard_map/ppermute | solution.py:309
  295.8 2.1 copy-start.12
  297.9 59.3 %copy-start.5 = (bf16[640,2048]{1,0:T(8,128)(2,1)}, bf16[640,2048]{1,0:T(8,128)(2,1)S(1)}, u32[]{:S(2)}) copy-start(bf16[640,2048]{1,0:T(8,128)(2,1)S(1)} %multiply_convert_fusion.3) | copy-start | bytes 7864324
  298.8 54.4 %copy-start.6 = (bf16[640,2048]{1,0:T(8,128)(2,1)}, bf16[640,2048]{1,0:T(8,128)(2,1)S(1)}, u32[]{:S(2)}) copy-start(bf16[640,2048]{1,0:T(8,128)(2,1)S(1)} %multiply_convert_fusion.2) | copy-start | bytes 7864324
  302.9 50.3 %copy-start.4 = (bf16[640,2048]{1,0:T(8,128)(2,1)}, bf16[640,2048]{1,0:T(8,128)(2,1)S(1)}, u32[]{:S(2)}) copy-start(bf16[640,2048]{1,0:T(8,128)(2,1)S(1)} %get-tuple-element.44) | copy-start | bytes 7864324
  303.0 9.4 %collective-permute-start.29 = (bf16[640,256]{1,0:T(8,128)(2,1)S(1)}, bf16[640,256]{1,0:T(8,128)(2,1)S(1)}, u32[]{:S(2)}, u32[]{:S(2)}) collective-permute-start(bf16[640,256]{1,0:T(8,128)(2,1)S(1)} %add_convert_fusion.14), channel_id=1, source_target_pairs={{1,0},{2,1},{3,2},{4,3},{5,4},{6,5},{7,6},{0,7},{9,8},{10,9},{11,1... | collective-permute-start | bytes 983048 | tf_op jit(solution)/shard_map/ppermute | solution.py:325
  303.7 10.7 %collective-permute-start.22 = (bf16[640,256]{1,0:T(8,128)(2,1)S(1)}, bf16[640,256]{1,0:T(8,128)(2,1)S(1)}, u32[]{:S(2)}, u32[]{:S(2)}) collective-permute-start(bf16[640,256]{1,0:T(8,128)(2,1)S(1)} %add_convert_fusion.29), channel_id=1, source_target_pairs={{0,1},{1,2},{2,3},{3,4},{4,5},{5,6},{6,7},{7,0},{8,9},{9,10},{10,1... | collective-permute-start | bytes 983048 | tf_op jit(solution)/shard_map/ppermute | solution.py:325
  312.7 8.5 %collective-permute-start.30 = (bf16[640,256]{1,0:T(8,128)(2,1)S(1)}, bf16[640,256]{1,0:T(8,128)(2,1)S(1)}, u32[]{:S(2)}, u32[]{:S(2)}) collective-permute-start(bf16[640,256]{1,0:T(8,128)(2,1)S(1)} %add_convert_fusion.12), channel_id=1, source_target_pairs={{1,0},{2,1},{3,2},{4,3},{5,4},{6,5},{7,6},{0,7},{9,8},{10,9},{11,1... | collective-permute-start | bytes 983048 | tf_op jit(solution)/shard_map/ppermute | solution.py:325
  314.6 9.8 %collective-permute-start.23 = (bf16[640,256]{1,0:T(8,128)(2,1)S(1)}, bf16[640,256]{1,0:T(8,128)(2,1)S(1)}, u32[]{:S(2)}, u32[]{:S(2)}) collective-permute-start(bf16[640,256]{1,0:T(8,128)(2,1)S(1)} %add_convert_fusion.27), channel_id=1, source_target_pairs={{0,1},{1,2},{2,3},{3,4},{4,5},{5,6},{6,7},{7,0},{8,9},{9,10},{10,1... | collective-permute-start | bytes 983048 | tf_op jit(solution)/shard_map/ppermute | solution.py:325
  321.4 8.3 %collective-permute-start.31 = (bf16[640,256]{1,0:T(8,128)(2,1)S(1)}, bf16[640,256]{1,0:T(8,128)(2,1)S(1)}, u32[]{:S(2)}, u32[]{:S(2)}) collective-permute-start(bf16[640,256]{1,0:T(8,128)(2,1)S(1)} %add_convert_fusion.10), channel_id=1, source_target_pairs={{1,0},{2,1},{3,2},{4,3},{5,4},{6,5},{7,6},{0,7},{9,8},{10,9},{11,1... | collective-permute-start | bytes 983048 | tf_op jit(solution)/shard_map/ppermute | solution.py:325
  324.6 9.0 %collective-permute-start.24 = (bf16[640,256]{1,0:T(8,128)(2,1)S(1)}, bf16[640,256]{1,0:T(8,128)(2,1)S(1)}, u32[]{:S(2)}, u32[]{:S(2)}) collective-permute-start(bf16[640,256]{1,0:T(8,128)(2,1)S(1)} %add_convert_fusion.25), channel_id=1, source_target_pairs={{0,1},{1,2},{2,3},{3,4},{4,5},{5,6},{6,7},{7,0},{8,9},{9,10},{10,1... | collective-permute-start | bytes 983048 | tf_op jit(solution)/shard_map/ppermute | solution.py:325
  329.9 8.1 %collective-permute-start.32 = (bf16[640,256]{1,0:T(8,128)(2,1)S(1)}, bf16[640,256]{1,0:T(8,128)(2,1)S(1)}, u32[]{:S(2)}, u32[]{:S(2)}) collective-permute-start(bf16[640,256]{1,0:T(8,128)(2,1)S(1)} %add_convert_fusion.8), channel_id=1, source_target_pairs={{1,0},{2,1},{3,2},{4,3},{5,4},{6,5},{7,6},{0,7},{9,8},{10,9},{11,1... | collective-permute-start | bytes 983048 | tf_op jit(solution)/shard_map/ppermute | solution.py:325
  333.8 7.9 %collective-permute-start.25 = (bf16[640,256]{1,0:T(8,128)(2,1)S(1)}, bf16[640,256]{1,0:T(8,128)(2,1)S(1)}, u32[]{:S(2)}, u32[]{:S(2)}) collective-permute-start(bf16[640,256]{1,0:T(8,128)(2,1)S(1)} %add_convert_fusion.23), channel_id=1, source_target_pairs={{0,1},{1,2},{2,3},{3,4},{4,5},{5,6},{6,7},{7,0},{8,9},{9,10},{10,1... | collective-permute-start | bytes 983048 | tf_op jit(solution)/shard_map/ppermute | solution.py:325
  338.2 7.5 %collective-permute-start.33 = (bf16[640,256]{1,0:T(8,128)(2,1)S(1)}, bf16[640,256]{1,0:T(8,128)(2,1)S(1)}, u32[]{:S(2)}, u32[]{:S(2)}) collective-permute-start(bf16[640,256]{1,0:T(8,128)(2,1)S(1)} %add_convert_fusion.6), channel_id=1, source_target_pairs={{1,0},{2,1},{3,2},{4,3},{5,4},{6,5},{7,6},{0,7},{9,8},{10,9},{11,1... | collective-permute-start | bytes 983048 | tf_op jit(solution)/shard_map/ppermute | solution.py:325
  341.9 7.2 %collective-permute-start.26 = (bf16[640,256]{1,0:T(8,128)(2,1)S(1)}, bf16[640,256]{1,0:T(8,128)(2,1)S(1)}, u32[]{:S(2)}, u32[]{:S(2)}) collective-permute-start(bf16[640,256]{1,0:T(8,128)(2,1)S(1)} %add_convert_fusion.21), channel_id=1, source_target_pairs={{0,1},{1,2},{2,3},{3,4},{4,5},{5,6},{6,7},{7,0},{8,9},{9,10},{10,1... | collective-permute-start | bytes 983048 | tf_op jit(solution)/shard_map/ppermute | solution.py:325
  345.9 7.3 %collective-permute-start.34 = (bf16[640,256]{1,0:T(8,128)(2,1)S(1)}, bf16[640,256]{1,0:T(8,128)(2,1)S(1)}, u32[]{:S(2)}, u32[]{:S(2)}) collective-permute-start(bf16[640,256]{1,0:T(8,128)(2,1)S(1)} %add_convert_fusion.4), channel_id=1, source_target_pairs={{1,0},{2,1},{3,2},{4,3},{5,4},{6,5},{7,6},{0,7},{9,8},{10,9},{11,1... | collective-permute-start | bytes 983048 | tf_op jit(solution)/shard_map/ppermute | solution.py:325
  349.3 7.9 %collective-permute-start.27 = (bf16[640,256]{1,0:T(8,128)(2,1)S(1)}, bf16[640,256]{1,0:T(8,128)(2,1)S(1)}, u32[]{:S(2)}, u32[]{:S(2)}) collective-permute-start(bf16[640,256]{1,0:T(8,128)(2,1)S(1)} %add_convert_fusion.19), channel_id=1, source_target_pairs={{0,1},{1,2},{2,3},{3,4},{4,5},{5,6},{6,7},{7,0},{8,9},{9,10},{10,1... | collective-permute-start | bytes 983048 | tf_op jit(solution)/shard_map/ppermute | solution.py:325
  354.1 7.7 %collective-permute-start.35 = (bf16[640,256]{1,0:T(8,128)(2,1)}, bf16[640,256]{1,0:T(8,128)(2,1)}, u32[]{:S(2)}, u32[]{:S(2)}) collective-permute-start(bf16[640,256]{1,0:T(8,128)(2,1)} %add_convert_fusion.2), channel_id=1, source_target_pairs={{1,0},{2,1},{3,2},{4,3},{5,4},{6,5},{7,6},{0,7},{9,8},{10,9},{11,1... | collective-permute-start | bytes 983048 | tf_op jit(solution)/shard_map/ppermute | solution.py:325
  358.1 7.7 %collective-permute-start.28 = (bf16[640,256]{1,0:T(8,128)(2,1)}, bf16[640,256]{1,0:T(8,128)(2,1)}, u32[]{:S(2)}, u32[]{:S(2)}) collective-permute-start(bf16[640,256]{1,0:T(8,128)(2,1)} %add_convert_fusion.17), channel_id=1, source_target_pairs={{0,1},{1,2},{2,3},{3,4},{4,5},{5,6},{6,7},{7,0},{8,9},{9,10},{10,1... | collective-permute-start | bytes 983048 | tf_op jit(solution)/shard_map/ppermute | solution.py:325
  367.3 29.8 %copy-start.13 = (bf16[128,32,64]{2,0,1:T(8,128)(2,1)S(1)}, bf16[128,32,64]{2,0,1:T(8,128)(2,1)}, u32[]{:S(2)}) copy-start(bf16[128,32,64]{2,0,1:T(8,128)(2,1)} %get-tuple-element.48) | copy-start | bytes 1572868
  367.3 5.5 %collective-permute-start.36 = (bf16[64,1280]{1,0:T(8,128)(2,1)S(1)}, bf16[64,1280]{1,0:T(8,128)(2,1)S(1)}, u32[]{:S(2)}, u32[]{:S(2)}) collective-permute-start(bf16[64,1280]{1,0:T(8,128)(2,1)S(1)} %get-tuple-element.52), channel_id=1, source_target_pairs={{0,8},{1,9},{2,10},{3,11},{4,12},{5,13},{6,14},{7,15},{8,16},{9,17... | collective-permute-start | bytes 491528 | tf_op jit(solution)/shard_map/ppermute | solution.py:146
  368.6 4.2 %collective-permute-start.38 = (bf16[64,1280]{1,0:T(8,128)(2,1)S(1)}, bf16[64,1280]{1,0:T(8,128)(2,1)S(1)}, u32[]{:S(2)}, u32[]{:S(2)}) collective-permute-start(bf16[64,1280]{1,0:T(8,128)(2,1)S(1)} %get-tuple-element.53), channel_id=1, source_target_pairs={{0,24},{1,25},{2,26},{3,27},{4,28},{5,29},{6,30},{7,31},{8,0},{9,1... | collective-permute-start | bytes 491528 | tf_op jit(solution)/shard_map/ppermute | solution.py:146
  370.1 5.7 %collective-permute-start.37 = (bf16[64,1280]{1,0:T(8,128)(2,1)S(1)}, bf16[64,1280]{1,0:T(8,128)(2,1)S(1)}, u32[]{:S(2)}, u32[]{:S(2)}) collective-permute-start(bf16[64,1280]{1,0:T(8,128)(2,1)S(1)} %get-tuple-element.54), channel_id=1, source_target_pairs={{0,16},{1,17},{2,18},{3,19},{4,20},{5,21},{6,22},{7,23},{8,24},{9,... | collective-permute-start | bytes 491528 | tf_op jit(solution)/shard_map/ppermute | solution.py:146
  375.9 6.6 %collective-permute-start.41 = (bf16[64,1280]{1,0:T(8,128)(2,1)S(1)}, bf16[64,1280]{1,0:T(8,128)(2,1)S(1)}, u32[]{:S(2)}, u32[]{:S(2)}) collective-permute-start(bf16[64,1280]{1,0:T(8,128)(2,1)S(1)} %fusion.5), channel_id=1, source_target_pairs={{0,192},{32,224},{64,0},{96,32},{128,64},{160,96},{192,128},{224,1... | collective-permute-start | bytes 491528 | tf_op jit(solution)/shard_map/ppermute | solution.py:146
  378.4 5.9 %collective-permute-start.40 = (bf16[64,1280]{1,0:T(8,128)(2,1)S(1)}, bf16[64,1280]{1,0:T(8,128)(2,1)S(1)}, u32[]{:S(2)}, u32[]{:S(2)}) collective-permute-start(bf16[64,1280]{1,0:T(8,128)(2,1)S(1)} %fusion.5), channel_id=1, source_target_pairs={{0,128},{32,160},{64,192},{96,224},{128,0},{160,32},{192,64},{224,... | collective-permute-start | bytes 491528 | tf_op jit(solution)/shard_map/ppermute | solution.py:146
  378.9 6.9 %collective-permute-start.39 = (bf16[64,1280]{1,0:T(8,128)(2,1)S(1)}, bf16[64,1280]{1,0:T(8,128)(2,1)S(1)}, u32[]{:S(2)}, u32[]{:S(2)}) collective-permute-start(bf16[64,1280]{1,0:T(8,128)(2,1)S(1)} %fusion.5), channel_id=1, source_target_pairs={{0,64},{32,96},{64,128},{96,160},{128,192},{160,224},{192,0},{224,... | collective-permute-start | bytes 491528 | tf_op jit(solution)/shard_map/ppermute | solution.py:146
  386.5 14.4 %copy-start.1 = (s32[32,32,7]{1,0,2:T(8,128)S(1)}, s32[32,32,7]{1,0,2:T(8,128)}, u32[]{:S(2)}) copy-start(s32[32,32,7]{1,0,2:T(8,128)} %param.17) | copy-start | bytes 86020
  386.7 12.8 %collective-permute-start.42 = (bf16[64,1280]{1,0:T(8,128)(2,1)S(1)}, bf16[64,1280]{1,0:T(8,128)(2,1)S(1)}, u32[]{:S(2)}, u32[]{:S(2)}) collective-permute-start(bf16[64,1280]{1,0:T(8,128)(2,1)S(1)} %select_reduce_fusion), channel_id=1, source_target_pairs={{0,32},{32,0},{64,96},{96,64},{128,160},{160,128},{192,224},{224,1... | collective-permute-start | bytes 491528 | tf_op jit(solution)/shard_map/ppermute | solution.py:340
  (3 other events, 3.4 us)

commit v11 on v10

--- a/solution.py
+++ b/solution.py
@@ -69,7 +69,7 @@
     block_count, slot_count = blocks.shape
     block_len = seq_len // block_count
     tiles = (block_count, block_len, head_width)
-    per_step = 2
+    per_step = 4
     one_block = pl.BlockSpec((per_step, block_len, head_width), lambda b, t, c: (b, 0, 0))
     whole = pl.BlockSpec(tiles, lambda b, t, c: (0, 0, 0))
     grid_spec = pltpu.PrefetchScalarGridSpec(

time: 409 us -> 407 us (level)
  transfers between devices with their start and end apart: 46 -> 46, of which waited for: 21 -> 22; matrix products, arithmetic and copies ran while one was open for 12% -> 12% of each run, Pallas kernels for 0% -> 0%
where the time goes in v11:
time: 407 us; the launch traced here: 399 us
  waiting for transfers between devices  160 us (39%)
  starting transfers between devices  115 us (28%)
  Pallas kernels  37.1 us (9%)
  local copies, waits for them, and re-layouts  34.3 us (8%)
  other arithmetic  34.1 us (8%)
  matrix products  15.9 us (4%)
    all_to_all x1, waiting for transfers between devices, per_device(): lax.all_to_all(back_sent, 'seq', split_axis=0, concat_axis=0, tiled=True)  44.4 us
    ppermute x20, starting transfers between devices, ring(): cur = lax.ppermute(cur, ('dp', 'seq'), perm)  40.6 us
    ppermute x14, waiting for transfers between devices, per_device(): arrived = lax.ppermute(buf, 'seq', perm)  37.2 us
    pallas_call x1, Pallas kernels, head_pass(): pl.pallas_call(head_kernel, grid_spec=grid_spec, out_shape=[jax.ShapeDtyp...  37.1 us
    all_to_all x1, waiting for transfers between devices, per_device(): lax.all_to_all(sent, 'seq', split_axis=0, concat_axis=1, tiled=True)[0]  33.9 us
    ppermute x20, waiting for transfers between devices, ring(): cur = lax.ppermute(cur, ('dp', 'seq'), perm)  29.1 us
    ppermute x14, starting transfers between devices, per_device(): arrived = lax.ppermute(buf, 'seq', perm)  20.2 us
    ppermute x1, starting transfers between devices, per_device(): w_other = lax.ppermute(w_mine, 'dp', pairs)  15.5 us
  transfers between devices with their start and end apart: 46, of which 22 were waited for; matrix products, arithmetic and copies ran while one was open for 12% of the time, Pallas kernels for 0%

profile of v11, /device:TPU:1, one launch (start us, length us, event | category | flops | bytes accessed | tf_op | source)
XLA Modules:
  0.0 398.9 jit_solution(3999861520141821592)
XLA Ops:
  1.7 4.0 %collective-permute-start.10 = (bf16[64,1280]{1,0:T(8,128)(2,1)S(1)}, bf16[64,1280]{1,0:T(8,128)(2,1)S(1)}, u32[]{:S(2)}, u32[]{:S(2)}) collective-permute-start(bf16[64,1280]{1,0:T(8,128)(2,1)S(1)} %get-tuple-element.40), channel_id=1, source_target_pairs={{32,40},{33,41},{34,42},{35,43},{36,44},{37,45},{38,46},{39,47},{4... | collective-permute-start | bytes 491528 | tf_op jit(solution)/shard_map/ppermute | solution.py:175
  7.1 3.4 collective-permute-start.12
  10.5 1.9 collective-permute-start.11
  13.9 4.2 %collective-permute-done.11 = bf16[64,1280]{1,0:T(8,128)(2,1)S(1)} collective-permute-done((bf16[64,1280]{1,0:T(8,128)(2,1)S(1)}, bf16[64,1280]{1,0:T(8,128)(2,1)S(1)}, u32[]{:S(2)}, u32[]{:S(2)}) %collective-permute-start.11) | collective-permute-done | bytes 163872 | tf_op jit(solution)/shard_map/ppermute | solution.py:175
  19.0 3.2 collective-permute-start.13
  22.2 5.9 %collective-permute-start.17 = (bf16[4,64,1280]{2,1,0:T(8,128)(2,1)}, bf16[4,64,1280]{2,1,0:T(8,128)(2,1)}, u32[]{:S(2)}, u32[]{:S(2)}) collective-permute-start(bf16[4,64,1280]{2,1,0:T(8,128)(2,1)} %pad_maximum_fusion.4), channel_id=1, source_target_pairs={{32,39},{33,32},{34,33},{35,34},{36,35},{37,36},{38,37},{39,38},{4... | collective-permute-start | bytes 1966088 | tf_op jit(solution)/shard_map/ppermute | solution.py:175
  30.3 4.7 %collective-permute-done.13 = bf16[4,64,1280]{2,1,0:T(8,128)(2,1)} collective-permute-done((bf16[4,64,1280]{2,1,0:T(8,128)(2,1)}, bf16[4,64,1280]{2,1,0:T(8,128)(2,1)}, u32[]{:S(2)}, u32[]{:S(2)}) %collective-permute-start.13) | collective-permute-done | bytes 655392 | tf_op jit(solution)/shard_map/ppermute | solution.py:175
  35.0 1.9 collective-permute-start.14
  37.7 5.0 %collective-permute-start.18 = (bf16[4,64,1280]{2,1,0:T(8,128)(2,1)}, bf16[4,64,1280]{2,1,0:T(8,128)(2,1)S(1)}, u32[]{:S(2)}, u32[]{:S(2)}) collective-permute-start(bf16[4,64,1280]{2,1,0:T(8,128)(2,1)} %collective-permute-done.17), channel_id=1, source_target_pairs={{32,39},{33,32},{34,33},{35,34},{36,35},{37,36},{38,37},{39,38},{4... | collective-permute-start | bytes 1966088 | tf_op jit(solution)/shard_map/ppermute | solution.py:175
  42.7 6.9 %collective-permute-done.14 = bf16[4,64,1280]{2,1,0:T(8,128)(2,1)} collective-permute-done((bf16[4,64,1280]{2,1,0:T(8,128)(2,1)}, bf16[4,64,1280]{2,1,0:T(8,128)(2,1)}, u32[]{:S(2)}, u32[]{:S(2)}) %collective-permute-start.14) | collective-permute-done | bytes 655392 | tf_op jit(solution)/shard_map/ppermute | solution.py:175
  49.6 1.9 collective-permute-start.15
  53.5 4.6 %collective-permute-start.19 = (bf16[4,64,1280]{2,1,0:T(8,128)(2,1)S(1)}, bf16[4,64,1280]{2,1,0:T(8,128)(2,1)S(1)}, u32[]{:S(2)}, u32[]{:S(2)}) collective-permute-start(bf16[4,64,1280]{2,1,0:T(8,128)(2,1)S(1)} %collective-permute-done.18), channel_id=1, source_target_pairs={{32,39},{33,32},{34,33},{35,34},{36,35},{37,36},{38,37},{39,38},{4... | collective-permute-start | bytes 1966088 | tf_op jit(solution)/shard_map/ppermute | solution.py:175
  58.1 4.6 %collective-permute-done.15 = bf16[4,64,1280]{2,1,0:T(8,128)(2,1)S(1)} collective-permute-done((bf16[4,64,1280]{2,1,0:T(8,128)(2,1)}, bf16[4,64,1280]{2,1,0:T(8,128)(2,1)S(1)}, u32[]{:S(2)}, u32[]{:S(2)}) %collective-permute-start.15) | collective-permute-done | bytes 655392 | tf_op jit(solution)/shard_map/ppermute | solution.py:175
  62.6 1.9 collective-permute-start.16
  66.5 8.7 %collective-permute-done.16 = bf16[4,64,1280]{2,1,0:T(8,128)(2,1)S(1)} collective-permute-done((bf16[4,64,1280]{2,1,0:T(8,128)(2,1)S(1)}, bf16[4,64,1280]{2,1,0:T(8,128)(2,1)S(1)}, u32[]{:S(2)}, u32[]{:S(2)}) %collective-permute-start.16) | collective-permute-done | bytes 655392 | tf_op jit(solution)/shard_map/ppermute | solution.py:175
  76.5 3.9 pad_maximum_fusion
  80.4 4.1 %bitcast_select_fusion.1 = bf16[2048,1280]{1,0:T(8,128)(2,1)} fusion(bf16[8,4,64,1280]{3,2,1,0:T(8,128)(2,1)S(1)} %bitcast_dynamic-update-slice_fusion, bf16[4,8,64,1280]{3,2,1,0:T(8,128)(2,1)S(1)} %get-tuple-element.45, pred[]{:T(512)S(6)} %eq.27), kind=kLoop, calls=%fused_computation.12 | loop fusion | flops 2621440 | bytes 15728641 | tf_op jit(solution)/shard_map/jit(_where)/select_n | solution.py:221
  84.5 15.5 %collective-permute-start.20 = (bf16[2048,1280]{1,0:T(8,128)(2,1)}, bf16[2048,1280]{1,0:T(8,128)(2,1)}, u32[]{:S(2)}, u32[]{:S(2)}) collective-permute-start(bf16[2048,1280]{1,0:T(8,128)(2,1)} %bitcast_select_fusion.1), channel_id=1, source_target_pairs={{0,32},{32,0},{64,96},{96,64},{128,160},{160,128},{192,224},{224,1... | collective-permute-start | bytes 15728648 | tf_op jit(solution)/shard_map/ppermute | solution.py:222
  101.0 3.9 all-to-all-start.1
  107.1 3.4 convolution_convert_fusion.1
  110.9 3.4 convolution_convert_fusion
  116.2 5.2 %all-to-all-done.1 = bf16[32,128,64]{1,2,0:T(8,128)(2,1)S(1)} async-done(((bf16[32,128,64]{1,2,0:T(8,128)(2,1)}), bf16[32,128,64]{1,2,0:T(8,128)(2,1)S(1)}, u32[]{:S(2)}, u32[]{:S(2)}) %all-to-all-start.1) | async-done | bytes 524320 | tf_op jit(solution)/shard_map/all_to_all | solution.py:217
  121.3 6.0 %all-to-all-start = ((bf16[32,128,192]{1,2,0:T(8,128)(2,1)}), bf16[32,128,192]{1,2,0:T(8,128)(2,1)S(1)}, u32[]{:S(2)}, u32[]{:S(2)}) async-start(bf16[32,128,192]{1,2,0:T(8,128)(2,1)} %pad_maximum_fusion.3), calls=%async_computation | async-start | bytes 3145728 | tf_op jit(solution)/shard_map/all_to_all | solution.py:245
  128.6 1.3 copy.61.g_ref
  130.0 33.9 %all-to-all-done = bf16[32,128,192]{1,2,0:T(8,128)(2,1)S(1)} async-done(((bf16[32,128,192]{1,2,0:T(8,128)(2,1)}), bf16[32,128,192]{1,2,0:T(8,128)(2,1)S(1)}, u32[]{:S(2)}, u32[]{:S(2)}) %all-to-all-start) | async-done | bytes 1572896 | tf_op jit(solution)/shard_map/all_to_all | solution.py:245
  164.3 1.4 copy.60
  165.6 1.4 copy.59
  167.0 1.4 copy.57
  168.3 37.1 %shard_map.110 = (bf16[32,128,64]{2,1,0:T(8,128)(2,1)}, bf16[32,128,64]{2,1,0:T(8,128)(2,1)}, f32[32,128,64]{2,1,0:T(8,128)}, f32[32,128,64]{2,1,0:T(8,128)}) custom-call(s32[224]{0:T(256)} %reshape.330.table_ref, s32[1]{0:T(128)} %dynamic_slice.35.count_ref, bf16[32,128,64]{2,1,0:T(8,128)(2,1)} %bitcast.194, bf16[32,128,64]{2,1,0:T(8,128)(2,1)} %copy.61.g_ref, ...), custom_call_target="tpu_custom_call" | custom-call | flops 2818572288 | bytes 5242880 | tf_op jit(solution)/shard_map/pallas_call | solution.py:86
  205.4 1.9 convert.10
  208.2 2.7 pad_maximum_fusion.2
  210.9 7.9 %all-to-all-start.2 = ((bf16[32,128,256]{2,1,0:T(8,128)(2,1)}), bf16[32,128,256]{2,1,0:T(8,128)(2,1)S(1)}, u32[]{:S(2)}, u32[]{:S(2)}) async-start(bf16[32,128,256]{2,1,0:T(8,128)(2,1)} %pad_maximum_fusion.2), calls=%async_computation.2 | async-start | bytes 4194304 | tf_op jit(solution)/shard_map/all_to_all | solution.py:262
  219.4 1.4 gather_fusion.5
  223.0 44.4 %all-to-all-done.2 = bf16[32,128,256]{2,1,0:T(8,128)(2,1)S(1)} async-done(((bf16[32,128,256]{2,1,0:T(8,128)(2,1)}), bf16[32,128,256]{2,1,0:T(8,128)(2,1)S(1)}, u32[]{:S(2)}, u32[]{:S(2)}) %all-to-all-start.2) | async-done | bytes 2097184 | tf_op jit(solution)/shard_map/all_to_all | solution.py:262
  267.4 1.9 slice_bitcast_fusion.2
  269.3 1.6 copy.63
  274.8 2.8 pad_maximum_fusion.1
  277.6 2.8 collective-permute-start.21
  282.0 4.6 %bitcast_select_fusion = bf16[32,64,1280]{2,1,0:T(8,128)(2,1)S(1)} fusion(bf16[8,4,64,1280]{3,2,1,0:T(8,128)(2,1)} %copy-done.2, bf16[4,8,64,1280]{3,2,1,0:T(8,128)(2,1)} %copy-done.3, pred[]{:T(512)S(6)} %eq.27), kind=kLoop, calls=%fused_computation.11 | loop fusion | flops 2621440 | bytes 15728641 | tf_op jit(solution)/shard_map/jit(_where)/select_n | solution.py:221
  286.6 1.5 fusion.6
  288.8 4.1 %fusion.8 = f32[128,2048]{0,1:T(8,128)S(1)} fusion(bf16[2048,1280]{1,0:T(8,128)(2,1)} %collective-permute-done.20, bf16[128,2560]{1,0:T(8,128)(2,1)} %copy-done.7, s32[]{:T(128)S(6)} %select_n.274), kind=kOutput, calls=%fused_computation.88 | convolution fusion | flops 671088640 | bytes 6619140 | tf_op jit(solution)/shard_map/dot_general | solution.py:283
  296.6 4.0 %slice_bitcast_fusion.1 = (bf16[640,2048]{1,0:T(8,128)(2,1)S(1)}, bf16[640,2048]{1,0:T(8,128)(2,1)S(1)}) fusion(bf16[2,640,2048]{2,1,0:T(8,128)(2,1)} %collective-permute-done.21), kind=kLoop, calls=%fused_computation.21 | loop fusion | bytes 10485760 | tf_op jit(solution)/shard_map/squeeze | solution.py:320
  302.6 7.6 %collective-permute-done.29 = bf16[640,256]{1,0:T(8,128)(2,1)S(1)} collective-permute-done((bf16[640,256]{1,0:T(8,128)(2,1)S(1)}, bf16[640,256]{1,0:T(8,128)(2,1)S(1)}, u32[]{:S(2)}, u32[]{:S(2)}) %collective-permute-start.29) | collective-permute-done | bytes 327712 | tf_op jit(solution)/shard_map/ppermute | solution.py:325
  310.4 1.8 collective-permute-start.30
  312.5 6.5 %collective-permute-done.30 = bf16[640,256]{1,0:T(8,128)(2,1)S(1)} collective-permute-done((bf16[640,256]{1,0:T(8,128)(2,1)S(1)}, bf16[640,256]{1,0:T(8,128)(2,1)S(1)}, u32[]{:S(2)}, u32[]{:S(2)}) %collective-permute-start.30) | collective-permute-done | bytes 327712 | tf_op jit(solution)/shard_map/ppermute | solution.py:325
  319.2 3.0 collective-permute-start.31
  322.4 5.0 %collective-permute-done.31 = bf16[640,256]{1,0:T(8,128)(2,1)S(1)} collective-permute-done((bf16[640,256]{1,0:T(8,128)(2,1)S(1)}, bf16[640,256]{1,0:T(8,128)(2,1)S(1)}, u32[]{:S(2)}, u32[]{:S(2)}) %collective-permute-start.31) | collective-permute-done | bytes 327712 | tf_op jit(solution)/shard_map/ppermute | solution.py:325
  327.6 3.7 collective-permute-start.32
  331.6 4.1 %collective-permute-done.32 = bf16[640,256]{1,0:T(8,128)(2,1)S(1)} collective-permute-done((bf16[640,256]{1,0:T(8,128)(2,1)S(1)}, bf16[640,256]{1,0:T(8,128)(2,1)S(1)}, u32[]{:S(2)}, u32[]{:S(2)}) %collective-permute-start.32) | collective-permute-done | bytes 327712 | tf_op jit(solution)/shard_map/ppermute | solution.py:325
  335.9 3.5 collective-permute-start.33
  339.7 3.7 collective-permute-done.33
  343.6 3.2 collective-permute-start.34
  347.1 3.8 collective-permute-done.34
  351.8 3.1 collective-permute-start.35
  355.9 3.7 collective-permute-done.35
  360.9 2.7 collective-permute-done.28
  366.3 1.5 collective-permute-start.38
  367.9 1.4 collective-permute-start.37
  371.9 1.7 collective-permute-done.37
  373.6 2.6 collective-permute-start.41
  377.3 2.9 collective-permute-done.41
  380.2 1.9 collective-permute-done.40
  382.1 1.6 collective-permute-done.39
  384.4 10.4 %collective-permute-start.42 = (bf16[64,1280]{1,0:T(8,128)(2,1)S(1)}, bf16[64,1280]{1,0:T(8,128)(2,1)S(1)}, u32[]{:S(2)}, u32[]{:S(2)}) collective-permute-start(bf16[64,1280]{1,0:T(8,128)(2,1)S(1)} %select_reduce_fusion), channel_id=1, source_target_pairs={{0,32},{32,0},{64,96},{96,64},{128,160},{160,128},{192,224},{224,1... | collective-permute-start | bytes 491528 | tf_op jit(solution)/shard_map/ppermute | solution.py:340
  (202 shorter events, 51.6 us)
Async XLA Ops:
  0.6 127.2 %copy-start = (s32[32,32,7]{1,0,2:T(8,128)S(1)}, s32[32,32,7]{1,0,2:T(8,128)}, u32[]{:S(2)}) copy-start(s32[32,32,7]{1,0,2:T(8,128)} %param.17) | copy-start | bytes 86020
  1.7 8.8 %collective-permute-start.10 = (bf16[64,1280]{1,0:T(8,128)(2,1)S(1)}, bf16[64,1280]{1,0:T(8,128)(2,1)S(1)}, u32[]{:S(2)}, u32[]{:S(2)}) collective-permute-start(bf16[64,1280]{1,0:T(8,128)(2,1)S(1)} %get-tuple-element.40), channel_id=1, source_target_pairs={{32,40},{33,41},{34,42},{35,43},{36,44},{37,45},{38,46},{39,47},{4... | collective-permute-start | bytes 491528 | tf_op jit(solution)/shard_map/ppermute | solution.py:175
  5.8 6.7 %collective-permute-start.4 = (bf16[64,1280]{1,0:T(8,128)(2,1)S(1)}, bf16[64,1280]{1,0:T(8,128)(2,1)S(1)}, u32[]{:S(2)}, u32[]{:S(2)}) collective-permute-start(bf16[64,1280]{1,0:T(8,128)(2,1)S(1)} %get-tuple-element.40), channel_id=1, source_target_pairs={{0,7},{1,0},{2,1},{3,2},{4,3},{5,4},{6,5},{7,6},{8,15},{9,8},{10,9... | collective-permute-start | bytes 491528 | tf_op jit(solution)/shard_map/ppermute | solution.py:175
  6.5 6.7 %collective-permute-start = (bf16[64,1280]{1,0:T(8,128)(2,1)S(1)}, bf16[64,1280]{1,0:T(8,128)(2,1)S(1)}, u32[]{:S(2)}, u32[]{:S(2)}) collective-permute-start(bf16[64,1280]{1,0:T(8,128)(2,1)S(1)} %get-tuple-element.40), channel_id=1, source_target_pairs={{0,1},{1,2},{2,3},{3,4},{4,5},{5,6},{6,7},{7,0},{8,9},{9,10},{10,1... | collective-permute-start | bytes 491528 | tf_op jit(solution)/shard_map/ppermute | solution.py:175
  7.1 6.7 %collective-permute-start.12 = (bf16[64,1280]{1,0:T(8,128)(2,1)S(1)}, bf16[64,1280]{1,0:T(8,128)(2,1)S(1)}, u32[]{:S(2)}, u32[]{:S(2)}) collective-permute-start(bf16[64,1280]{1,0:T(8,128)(2,1)S(1)} %get-tuple-element.40), channel_id=1, source_target_pairs={{32,56},{33,57},{34,58},{35,59},{36,60},{37,61},{38,62},{39,63},{4... | collective-permute-start | bytes 491528 | tf_op jit(solution)/shard_map/ppermute | solution.py:175
  10.5 7.6 %collective-permute-start.11 = (bf16[64,1280]{1,0:T(8,128)(2,1)S(1)}, bf16[64,1280]{1,0:T(8,128)(2,1)S(1)}, u32[]{:S(2)}, u32[]{:S(2)}) collective-permute-start(bf16[64,1280]{1,0:T(8,128)(2,1)S(1)} %collective-permute-done.10), channel_id=1, source_target_pairs={{32,40},{33,41},{34,42},{35,43},{36,44},{37,45},{38,46},{39,47},{4... | collective-permute-start | bytes 491528 | tf_op jit(solution)/shard_map/ppermute | solution.py:175
  12.5 15.7 %collective-permute-start.5 = (bf16[64,1280]{1,0:T(8,128)(2,1)S(1)}, bf16[64,1280]{1,0:T(8,128)(2,1)S(1)}, u32[]{:S(2)}, u32[]{:S(2)}) collective-permute-start(bf16[64,1280]{1,0:T(8,128)(2,1)S(1)} %collective-permute-done.4), channel_id=1, source_target_pairs={{0,7},{1,0},{2,1},{3,2},{4,3},{5,4},{6,5},{7,6},{8,15},{9,8},{10,9... | collective-permute-start | bytes 491528 | tf_op jit(solution)/shard_map/ppermute | solution.py:175
  13.1 15.7 %collective-permute-start.1 = (bf16[64,1280]{1,0:T(8,128)(2,1)S(1)}, bf16[64,1280]{1,0:T(8,128)(2,1)S(1)}, u32[]{:S(2)}, u32[]{:S(2)}) collective-permute-start(bf16[64,1280]{1,0:T(8,128)(2,1)S(1)} %collective-permute-done), channel_id=1, source_target_pairs={{0,1},{1,2},{2,3},{3,4},{4,5},{5,6},{6,7},{7,0},{8,9},{9,10},{10,1... | collective-permute-start | bytes 491528 | tf_op jit(solution)/shard_map/ppermute | solution.py:175
  19.0 16.0 %collective-permute-start.13 = (bf16[4,64,1280]{2,1,0:T(8,128)(2,1)}, bf16[4,64,1280]{2,1,0:T(8,128)(2,1)}, u32[]{:S(2)}, u32[]{:S(2)}) collective-permute-start(bf16[4,64,1280]{2,1,0:T(8,128)(2,1)} %pad_maximum_fusion.4), channel_id=1, source_target_pairs={{32,33},{33,34},{34,35},{35,36},{36,37},{37,38},{38,39},{39,32},{4... | collective-permute-start | bytes 1966088 | tf_op jit(solution)/shard_map/ppermute | solution.py:175
  22.2 15.5 %collective-permute-start.17 = (bf16[4,64,1280]{2,1,0:T(8,128)(2,1)}, bf16[4,64,1280]{2,1,0:T(8,128)(2,1)}, u32[]{:S(2)}, u32[]{:S(2)}) collective-permute-start(bf16[4,64,1280]{2,1,0:T(8,128)(2,1)} %pad_maximum_fusion.4), channel_id=1, source_target_pairs={{32,39},{33,32},{34,33},{35,34},{36,35},{37,36},{38,37},{39,38},{4... | collective-permute-start | bytes 1966088 | tf_op jit(solution)/shard_map/ppermute | solution.py:175
  28.1 2.1 collective-permute-start.6
  28.8 0.7 collective-permute-start.2
  29.5 0.7 collective-permute-start.3
  35.0 14.6 %collective-permute-start.14 = (bf16[4,64,1280]{2,1,0:T(8,128)(2,1)}, bf16[4,64,1280]{2,1,0:T(8,128)(2,1)}, u32[]{:S(2)}, u32[]{:S(2)}) collective-permute-start(bf16[4,64,1280]{2,1,0:T(8,128)(2,1)} %collective-permute-done.13), channel_id=1, source_target_pairs={{32,33},{33,34},{34,35},{35,36},{36,37},{37,38},{38,39},{39,32},{4... | collective-permute-start | bytes 1966088 | tf_op jit(solution)/shard_map/ppermute | solution.py:175
  37.0 28.7 %collective-permute-start.7 = (bf16[8,64,1280]{2,1,0:T(8,128)(2,1)S(1)}, bf16[8,64,1280]{2,1,0:T(8,128)(2,1)S(1)}, u32[]{:S(2)}, u32[]{:S(2)}) collective-permute-start(bf16[8,64,1280]{2,1,0:T(8,128)(2,1)S(1)} %bitcast_dynamic-update-slice_fusion.8), channel_id=1, source_target_pairs={{0,8},{1,9},{2,10},{3,11},{4,12},{5,13},{6,14},{7,15},{8,16},{9,17... | collective-permute-start | bytes 3932168 | tf_op jit(solution)/shard_map/ppermute | solution.py:175
  37.7 15.7 %collective-permute-start.18 = (bf16[4,64,1280]{2,1,0:T(8,128)(2,1)}, bf16[4,64,1280]{2,1,0:T(8,128)(2,1)S(1)}, u32[]{:S(2)}, u32[]{:S(2)}) collective-permute-start(bf16[4,64,1280]{2,1,0:T(8,128)(2,1)} %collective-permute-done.17), channel_id=1, source_target_pairs={{32,39},{33,32},{34,33},{35,34},{36,35},{37,36},{38,37},{39,38},{4... | collective-permute-start | bytes 1966088 | tf_op jit(solution)/shard_map/ppermute | solution.py:175
  49.6 13.0 %collective-permute-start.15 = (bf16[4,64,1280]{2,1,0:T(8,128)(2,1)}, bf16[4,64,1280]{2,1,0:T(8,128)(2,1)S(1)}, u32[]{:S(2)}, u32[]{:S(2)}) collective-permute-start(bf16[4,64,1280]{2,1,0:T(8,128)(2,1)} %collective-permute-done.14), channel_id=1, source_target_pairs={{32,33},{33,34},{34,35},{35,36},{36,37},{37,38},{38,39},{39,32},{4... | collective-permute-start | bytes 1966088 | tf_op jit(solution)/shard_map/ppermute | solution.py:175
  51.6 24.9 %collective-permute-start.9 = (bf16[8,64,1280]{2,1,0:T(8,128)(2,1)S(1)}, bf16[8,64,1280]{2,1,0:T(8,128)(2,1)S(1)}, u32[]{:S(2)}, u32[]{:S(2)}) collective-permute-start(bf16[8,64,1280]{2,1,0:T(8,128)(2,1)S(1)} %bitcast_dynamic-update-slice_fusion.8), channel_id=1, source_target_pairs={{0,24},{1,25},{2,26},{3,27},{4,28},{5,29},{6,30},{7,31},{8,0},{9,1... | collective-permute-start | bytes 3932168 | tf_op jit(solution)/shard_map/ppermute | solution.py:175
  53.5 21.7 %collective-permute-start.19 = (bf16[4,64,1280]{2,1,0:T(8,128)(2,1)S(1)}, bf16[4,64,1280]{2,1,0:T(8,128)(2,1)S(1)}, u32[]{:S(2)}, u32[]{:S(2)}) collective-permute-start(bf16[4,64,1280]{2,1,0:T(8,128)(2,1)S(1)} %collective-permute-done.18), channel_id=1, source_target_pairs={{32,39},{33,32},{34,33},{35,34},{36,35},{37,36},{38,37},{39,38},{4... | collective-permute-start | bytes 1966088 | tf_op jit(solution)/shard_map/ppermute | solution.py:175
  62.6 12.5 %collective-permute-start.16 = (bf16[4,64,1280]{2,1,0:T(8,128)(2,1)S(1)}, bf16[4,64,1280]{2,1,0:T(8,128)(2,1)S(1)}, u32[]{:S(2)}, u32[]{:S(2)}) collective-permute-start(bf16[4,64,1280]{2,1,0:T(8,128)(2,1)S(1)} %collective-permute-done.15), channel_id=1, source_target_pairs={{32,33},{33,34},{34,35},{35,36},{36,37},{37,38},{38,39},{39,32},{4... | collective-permute-start | bytes 1966088 | tf_op jit(solution)/shard_map/ppermute | solution.py:175
  65.7 10.8 %collective-permute-start.8 = (bf16[8,64,1280]{2,1,0:T(8,128)(2,1)S(1)}, bf16[8,64,1280]{2,1,0:T(8,128)(2,1)S(1)}, u32[]{:S(2)}, u32[]{:S(2)}) collective-permute-start(bf16[8,64,1280]{2,1,0:T(8,128)(2,1)S(1)} %collective-permute-done.7), channel_id=1, source_target_pairs={{0,8},{1,9},{2,10},{3,11},{4,12},{5,13},{6,14},{7,15},{8,16},{9,17... | collective-permute-start | bytes 3932168 | tf_op jit(solution)/shard_map/ppermute | solution.py:175
  76.5 3.9 copy-start.2
  80.4 4.1 %copy-start.3 = (bf16[4,8,64,1280]{3,2,1,0:T(8,128)(2,1)}, bf16[4,8,64,1280]{3,2,1,0:T(8,128)(2,1)S(1)}, u32[]{:S(2)}) copy-start(bf16[4,8,64,1280]{3,2,1,0:T(8,128)(2,1)S(1)} %get-tuple-element.45) | copy-start | bytes 15728644
  80.4 19.6 %copy-start.18 = (bf16[1,128,2048]{2,1,0:T(8,128)(2,1)S(1)}, bf16[1,128,2048]{2,1,0:T(8,128)(2,1)}, u32[]{:S(2)}) copy-start(bf16[1,128,2048]{2,1,0:T(8,128)(2,1)} %param.19) | copy-start | bytes 1572868
  80.4 24.8 %copy-start.19 = (bf16[1,128,2048]{2,1,0:T(8,128)(2,1)S(1)}, bf16[1,128,2048]{2,1,0:T(8,128)(2,1)}, u32[]{:S(2)}) copy-start(bf16[1,128,2048]{2,1,0:T(8,128)(2,1)} %param.13) | copy-start | bytes 1572868
  84.5 26.4 %collective-permute-start.20 = (bf16[2048,1280]{1,0:T(8,128)(2,1)}, bf16[2048,1280]{1,0:T(8,128)(2,1)}, u32[]{:S(2)}, u32[]{:S(2)}) collective-permute-start(bf16[2048,1280]{1,0:T(8,128)(2,1)} %bitcast_select_fusion.1), channel_id=1, source_target_pairs={{0,32},{32,0},{64,96},{96,64},{128,160},{160,128},{192,224},{224,1... | collective-permute-start | bytes 15728648 | tf_op jit(solution)/shard_map/ppermute | solution.py:222
  101.0 20.3 %all-to-all-start.1 = ((bf16[32,128,64]{1,2,0:T(8,128)(2,1)}), bf16[32,128,64]{1,2,0:T(8,128)(2,1)S(1)}, u32[]{:S(2)}, u32[]{:S(2)}) async-start(bf16[32,128,64]{1,2,0:T(8,128)(2,1)} %bitcast.40), calls=%async_computation.1 | async-start | bytes 1048576 | tf_op jit(solution)/shard_map/all_to_all | solution.py:217
  114.9 12.4 %copy-start.20 = (s32[32]{0:T(128)S(1)}, s32[32]{0:T(128)}, u32[]{:S(2)}) copy-start(s32[32]{0:T(128)} %param.18) | copy-start | bytes 388
  121.3 42.6 %all-to-all-start = ((bf16[32,128,192]{1,2,0:T(8,128)(2,1)}), bf16[32,128,192]{1,2,0:T(8,128)(2,1)S(1)}, u32[]{:S(2)}, u32[]{:S(2)}) async-start(bf16[32,128,192]{1,2,0:T(8,128)(2,1)} %pad_maximum_fusion.3), calls=%async_computation | async-start | bytes 3145728 | tf_op jit(solution)/shard_map/all_to_all | solution.py:245
  205.4 2.2 copy-start.14
  205.4 2.5 copy-start.16
  205.4 2.8 copy-start.17
  210.9 56.6 %all-to-all-start.2 = ((bf16[32,128,256]{2,1,0:T(8,128)(2,1)}), bf16[32,128,256]{2,1,0:T(8,128)(2,1)S(1)}, u32[]{:S(2)}, u32[]{:S(2)}) async-start(bf16[32,128,256]{2,1,0:T(8,128)(2,1)} %pad_maximum_fusion.2), calls=%async_computation.2 | async-start | bytes 4194304 | tf_op jit(solution)/shard_map/all_to_all | solution.py:262
  222.0 51.0 %copy-start.9 = (bf16[8,128,4,64]{1,3,2,0:T(8,128)(2,1)}, bf16[8,128,4,64]{1,3,2,0:T(8,128)(2,1)S(1)}, u32[]{:S(2)}) copy-start(bf16[8,128,4,64]{1,3,2,0:T(8,128)(2,1)S(1)} %broadcast_select_fusion.1) | copy-start | bytes 1572868
  272.2 1.7 copy-start.11
  273.0 13.6 %copy-start.7 = (bf16[128,2560]{1,0:T(8,128)(2,1)}, bf16[128,2560]{1,0:T(8,128)(2,1)S(1)}, u32[]{:S(2)}) copy-start(bf16[128,2560]{1,0:T(8,128)(2,1)S(1)} %pad_maximum_fusion.5) | copy-start | bytes 1966084
  277.6 19.0 %collective-permute-start.21 = (bf16[2,640,2048]{2,1,0:T(8,128)(2,1)}, bf16[2,640,2048]{2,1,0:T(8,128)(2,1)}, u32[]{:S(2)}, u32[]{:S(2)}) collective-permute-start(bf16[2,640,2048]{2,1,0:T(8,128)(2,1)} %pad_maximum_fusion.1), channel_id=1, source_target_pairs={{0,32},{32,0},{64,96},{96,64},{128,160},{160,128},{192,224},{224,1... | collective-permute-start | bytes 15728648 | tf_op jit(solution)/shard_map/ppermute | solution.py:309
  293.5 2.1 copy-start.12
  295.7 59.3 %copy-start.5 = (bf16[640,2048]{1,0:T(8,128)(2,1)}, bf16[640,2048]{1,0:T(8,128)(2,1)S(1)}, u32[]{:S(2)}) copy-start(bf16[640,2048]{1,0:T(8,128)(2,1)S(1)} %multiply_convert_fusion.3) | copy-start | bytes 7864324
  296.6 54.3 %copy-start.6 = (bf16[640,2048]{1,0:T(8,128)(2,1)}, bf16[640,2048]{1,0:T(8,128)(2,1)S(1)}, u32[]{:S(2)}) copy-start(bf16[640,2048]{1,0:T(8,128)(2,1)S(1)} %multiply_convert_fusion.2) | copy-start | bytes 7864324
  300.6 50.3 %copy-start.4 = (bf16[640,2048]{1,0:T(8,128)(2,1)}, bf16[640,2048]{1,0:T(8,128)(2,1)S(1)}, u32[]{:S(2)}) copy-start(bf16[640,2048]{1,0:T(8,128)(2,1)S(1)} %get-tuple-element.44) | copy-start | bytes 7864324
  300.8 9.4 %collective-permute-start.29 = (bf16[640,256]{1,0:T(8,128)(2,1)S(1)}, bf16[640,256]{1,0:T(8,128)(2,1)S(1)}, u32[]{:S(2)}, u32[]{:S(2)}) collective-permute-start(bf16[640,256]{1,0:T(8,128)(2,1)S(1)} %add_convert_fusion.14), channel_id=1, source_target_pairs={{1,0},{2,1},{3,2},{4,3},{5,4},{6,5},{7,6},{0,7},{9,8},{10,9},{11,1... | collective-permute-start | bytes 983048 | tf_op jit(solution)/shard_map/ppermute | solution.py:325
  301.5 10.7 %collective-permute-start.22 = (bf16[640,256]{1,0:T(8,128)(2,1)S(1)}, bf16[640,256]{1,0:T(8,128)(2,1)S(1)}, u32[]{:S(2)}, u32[]{:S(2)}) collective-permute-start(bf16[640,256]{1,0:T(8,128)(2,1)S(1)} %add_convert_fusion.29), channel_id=1, source_target_pairs={{0,1},{1,2},{2,3},{3,4},{4,5},{5,6},{6,7},{7,0},{8,9},{9,10},{10,1... | collective-permute-start | bytes 983048 | tf_op jit(solution)/shard_map/ppermute | solution.py:325
  310.4 8.5 %collective-permute-start.30 = (bf16[640,256]{1,0:T(8,128)(2,1)S(1)}, bf16[640,256]{1,0:T(8,128)(2,1)S(1)}, u32[]{:S(2)}, u32[]{:S(2)}) collective-permute-start(bf16[640,256]{1,0:T(8,128)(2,1)S(1)} %add_convert_fusion.12), channel_id=1, source_target_pairs={{1,0},{2,1},{3,2},{4,3},{5,4},{6,5},{7,6},{0,7},{9,8},{10,9},{11,1... | collective-permute-start | bytes 983048 | tf_op jit(solution)/shard_map/ppermute | solution.py:325
  312.4 9.7 %collective-permute-start.23 = (bf16[640,256]{1,0:T(8,128)(2,1)S(1)}, bf16[640,256]{1,0:T(8,128)(2,1)S(1)}, u32[]{:S(2)}, u32[]{:S(2)}) collective-permute-start(bf16[640,256]{1,0:T(8,128)(2,1)S(1)} %add_convert_fusion.27), channel_id=1, source_target_pairs={{0,1},{1,2},{2,3},{3,4},{4,5},{5,6},{6,7},{7,0},{8,9},{9,10},{10,1... | collective-permute-start | bytes 983048 | tf_op jit(solution)/shard_map/ppermute | solution.py:325
  319.2 8.3 %collective-permute-start.31 = (bf16[640,256]{1,0:T(8,128)(2,1)S(1)}, bf16[640,256]{1,0:T(8,128)(2,1)S(1)}, u32[]{:S(2)}, u32[]{:S(2)}) collective-permute-start(bf16[640,256]{1,0:T(8,128)(2,1)S(1)} %add_convert_fusion.10), channel_id=1, source_target_pairs={{1,0},{2,1},{3,2},{4,3},{5,4},{6,5},{7,6},{0,7},{9,8},{10,9},{11,1... | collective-permute-start | bytes 983048 | tf_op jit(solution)/shard_map/ppermute | solution.py:325
  322.3 9.0 %collective-permute-start.24 = (bf16[640,256]{1,0:T(8,128)(2,1)S(1)}, bf16[640,256]{1,0:T(8,128)(2,1)S(1)}, u32[]{:S(2)}, u32[]{:S(2)}) collective-permute-start(bf16[640,256]{1,0:T(8,128)(2,1)S(1)} %add_convert_fusion.25), channel_id=1, source_target_pairs={{0,1},{1,2},{2,3},{3,4},{4,5},{5,6},{6,7},{7,0},{8,9},{9,10},{10,1... | collective-permute-start | bytes 983048 | tf_op jit(solution)/shard_map/ppermute | solution.py:325
  327.6 8.1 %collective-permute-start.32 = (bf16[640,256]{1,0:T(8,128)(2,1)S(1)}, bf16[640,256]{1,0:T(8,128)(2,1)S(1)}, u32[]{:S(2)}, u32[]{:S(2)}) collective-permute-start(bf16[640,256]{1,0:T(8,128)(2,1)S(1)} %add_convert_fusion.8), channel_id=1, source_target_pairs={{1,0},{2,1},{3,2},{4,3},{5,4},{6,5},{7,6},{0,7},{9,8},{10,9},{11,1... | collective-permute-start | bytes 983048 | tf_op jit(solution)/shard_map/ppermute | solution.py:325
  331.5 7.9 %collective-permute-start.25 = (bf16[640,256]{1,0:T(8,128)(2,1)S(1)}, bf16[640,256]{1,0:T(8,128)(2,1)S(1)}, u32[]{:S(2)}, u32[]{:S(2)}) collective-permute-start(bf16[640,256]{1,0:T(8,128)(2,1)S(1)} %add_convert_fusion.23), channel_id=1, source_target_pairs={{0,1},{1,2},{2,3},{3,4},{4,5},{5,6},{6,7},{7,0},{8,9},{9,10},{10,1... | collective-permute-start | bytes 983048 | tf_op jit(solution)/shard_map/ppermute | solution.py:325
  335.9 7.5 %collective-permute-start.33 = (bf16[640,256]{1,0:T(8,128)(2,1)S(1)}, bf16[640,256]{1,0:T(8,128)(2,1)S(1)}, u32[]{:S(2)}, u32[]{:S(2)}) collective-permute-start(bf16[640,256]{1,0:T(8,128)(2,1)S(1)} %add_convert_fusion.6), channel_id=1, source_target_pairs={{1,0},{2,1},{3,2},{4,3},{5,4},{6,5},{7,6},{0,7},{9,8},{10,9},{11,1... | collective-permute-start | bytes 983048 | tf_op jit(solution)/shard_map/ppermute | solution.py:325
  339.6 7.2 %collective-permute-start.26 = (bf16[640,256]{1,0:T(8,128)(2,1)S(1)}, bf16[640,256]{1,0:T(8,128)(2,1)S(1)}, u32[]{:S(2)}, u32[]{:S(2)}) collective-permute-start(bf16[640,256]{1,0:T(8,128)(2,1)S(1)} %add_convert_fusion.21), channel_id=1, source_target_pairs={{0,1},{1,2},{2,3},{3,4},{4,5},{5,6},{6,7},{7,0},{8,9},{9,10},{10,1... | collective-permute-start | bytes 983048 | tf_op jit(solution)/shard_map/ppermute | solution.py:325
  343.6 7.3 %collective-permute-start.34 = (bf16[640,256]{1,0:T(8,128)(2,1)S(1)}, bf16[640,256]{1,0:T(8,128)(2,1)S(1)}, u32[]{:S(2)}, u32[]{:S(2)}) collective-permute-start(bf16[640,256]{1,0:T(8,128)(2,1)S(1)} %add_convert_fusion.4), channel_id=1, source_target_pairs={{1,0},{2,1},{3,2},{4,3},{5,4},{6,5},{7,6},{0,7},{9,8},{10,9},{11,1... | collective-permute-start | bytes 983048 | tf_op jit(solution)/shard_map/ppermute | solution.py:325
  347.0 7.9 %collective-permute-start.27 = (bf16[640,256]{1,0:T(8,128)(2,1)S(1)}, bf16[640,256]{1,0:T(8,128)(2,1)S(1)}, u32[]{:S(2)}, u32[]{:S(2)}) collective-permute-start(bf16[640,256]{1,0:T(8,128)(2,1)S(1)} %add_convert_fusion.19), channel_id=1, source_target_pairs={{0,1},{1,2},{2,3},{3,4},{4,5},{5,6},{6,7},{7,0},{8,9},{9,10},{10,1... | collective-permute-start | bytes 983048 | tf_op jit(solution)/shard_map/ppermute | solution.py:325
  351.8 7.8 %collective-permute-start.35 = (bf16[640,256]{1,0:T(8,128)(2,1)}, bf16[640,256]{1,0:T(8,128)(2,1)}, u32[]{:S(2)}, u32[]{:S(2)}) collective-permute-start(bf16[640,256]{1,0:T(8,128)(2,1)} %add_convert_fusion.2), channel_id=1, source_target_pairs={{1,0},{2,1},{3,2},{4,3},{5,4},{6,5},{7,6},{0,7},{9,8},{10,9},{11,1... | collective-permute-start | bytes 983048 | tf_op jit(solution)/shard_map/ppermute | solution.py:325
  355.9 7.7 %collective-permute-start.28 = (bf16[640,256]{1,0:T(8,128)(2,1)}, bf16[640,256]{1,0:T(8,128)(2,1)}, u32[]{:S(2)}, u32[]{:S(2)}) collective-permute-start(bf16[640,256]{1,0:T(8,128)(2,1)} %add_convert_fusion.17), channel_id=1, source_target_pairs={{0,1},{1,2},{2,3},{3,4},{4,5},{5,6},{6,7},{7,0},{8,9},{9,10},{10,1... | collective-permute-start | bytes 983048 | tf_op jit(solution)/shard_map/ppermute | solution.py:325
  365.0 29.8 %copy-start.13 = (bf16[128,32,64]{2,0,1:T(8,128)(2,1)S(1)}, bf16[128,32,64]{2,0,1:T(8,128)(2,1)}, u32[]{:S(2)}) copy-start(bf16[128,32,64]{2,0,1:T(8,128)(2,1)} %get-tuple-element.48) | copy-start | bytes 1572868
  365.1 5.5 %collective-permute-start.36 = (bf16[64,1280]{1,0:T(8,128)(2,1)S(1)}, bf16[64,1280]{1,0:T(8,128)(2,1)S(1)}, u32[]{:S(2)}, u32[]{:S(2)}) collective-permute-start(bf16[64,1280]{1,0:T(8,128)(2,1)S(1)} %get-tuple-element.52), channel_id=1, source_target_pairs={{0,8},{1,9},{2,10},{3,11},{4,12},{5,13},{6,14},{7,15},{8,16},{9,17... | collective-permute-start | bytes 491528 | tf_op jit(solution)/shard_map/ppermute | solution.py:146
  366.3 5.6 %collective-permute-start.38 = (bf16[64,1280]{1,0:T(8,128)(2,1)S(1)}, bf16[64,1280]{1,0:T(8,128)(2,1)S(1)}, u32[]{:S(2)}, u32[]{:S(2)}) collective-permute-start(bf16[64,1280]{1,0:T(8,128)(2,1)S(1)} %get-tuple-element.53), channel_id=1, source_target_pairs={{0,24},{1,25},{2,26},{3,27},{4,28},{5,29},{6,30},{7,31},{8,0},{9,1... | collective-permute-start | bytes 491528 | tf_op jit(solution)/shard_map/ppermute | solution.py:146
  367.9 5.7 %collective-permute-start.37 = (bf16[64,1280]{1,0:T(8,128)(2,1)S(1)}, bf16[64,1280]{1,0:T(8,128)(2,1)S(1)}, u32[]{:S(2)}, u32[]{:S(2)}) collective-permute-start(bf16[64,1280]{1,0:T(8,128)(2,1)S(1)} %get-tuple-element.54), channel_id=1, source_target_pairs={{0,16},{1,17},{2,18},{3,19},{4,20},{5,21},{6,22},{7,23},{8,24},{9,... | collective-permute-start | bytes 491528 | tf_op jit(solution)/shard_map/ppermute | solution.py:146
  373.6 6.6 %collective-permute-start.41 = (bf16[64,1280]{1,0:T(8,128)(2,1)S(1)}, bf16[64,1280]{1,0:T(8,128)(2,1)S(1)}, u32[]{:S(2)}, u32[]{:S(2)}) collective-permute-start(bf16[64,1280]{1,0:T(8,128)(2,1)S(1)} %fusion.5), channel_id=1, source_target_pairs={{0,192},{32,224},{64,0},{96,32},{128,64},{160,96},{192,128},{224,1... | collective-permute-start | bytes 491528 | tf_op jit(solution)/shard_map/ppermute | solution.py:146
  376.2 5.9 %collective-permute-start.40 = (bf16[64,1280]{1,0:T(8,128)(2,1)S(1)}, bf16[64,1280]{1,0:T(8,128)(2,1)S(1)}, u32[]{:S(2)}, u32[]{:S(2)}) collective-permute-start(bf16[64,1280]{1,0:T(8,128)(2,1)S(1)} %fusion.5), channel_id=1, source_target_pairs={{0,128},{32,160},{64,192},{96,224},{128,0},{160,32},{192,64},{224,... | collective-permute-start | bytes 491528 | tf_op jit(solution)/shard_map/ppermute | solution.py:146
  376.7 6.9 %collective-permute-start.39 = (bf16[64,1280]{1,0:T(8,128)(2,1)S(1)}, bf16[64,1280]{1,0:T(8,128)(2,1)S(1)}, u32[]{:S(2)}, u32[]{:S(2)}) collective-permute-start(bf16[64,1280]{1,0:T(8,128)(2,1)S(1)} %fusion.5), channel_id=1, source_target_pairs={{0,64},{32,96},{64,128},{96,160},{128,192},{160,224},{192,0},{224,... | collective-permute-start | bytes 491528 | tf_op jit(solution)/shard_map/ppermute | solution.py:146
  384.3 14.4 %copy-start.1 = (s32[32,32,7]{1,0,2:T(8,128)S(1)}, s32[32,32,7]{1,0,2:T(8,128)}, u32[]{:S(2)}) copy-start(s32[32,32,7]{1,0,2:T(8,128)} %param.17) | copy-start | bytes 86020
  384.4 12.8 %collective-permute-start.42 = (bf16[64,1280]{1,0:T(8,128)(2,1)S(1)}, bf16[64,1280]{1,0:T(8,128)(2,1)S(1)}, u32[]{:S(2)}, u32[]{:S(2)}) collective-permute-start(bf16[64,1280]{1,0:T(8,128)(2,1)S(1)} %select_reduce_fusion), channel_id=1, source_target_pairs={{0,32},{32,0},{64,96},{96,64},{128,160},{160,128},{192,224},{224,1... | collective-permute-start | bytes 491528 | tf_op jit(solution)/shard_map/ppermute | solution.py:340
  (3 other events, 3.4 us)

commit v12 on v11

--- a/solution.py
+++ b/solution.py
@@ -17,7 +17,7 @@
 
 
 def head_kernel(table_ref, count_ref, q_ref, g_ref, k_ref, v_ref,
-                out_ref, gq_ref, dk_ref, dv_ref, k_cat, v_cat):
+                out_ref, gq_ref, dk_out, dv_out, k_cat, v_cat, dk_ref, dv_ref):
     step = pl.program_id(0)
     per_step = q_ref.shape[0]
     slot_count = table_ref.shape[0] // (pl.num_programs(0) * per_step)
@@ -63,6 +63,11 @@
             dk_ref[chosen[j]] += dk[j * block_len : (j + 1) * block_len]
             dv_ref[chosen[j]] += dv[j * block_len : (j + 1) * block_len]
 
+    @pl.when(step == pl.num_programs(0) - 1)
+    def _():
+        dk_out[...] = dk_ref[...].astype(dk_out.dtype)
+        dv_out[...] = dv_ref[...].astype(dv_out.dtype)
+
 
 def head_pass(queries, key_rows, value_rows, grad_head, blocks, extra_count):
     seq_len, head_width = queries.shape
@@ -80,6 +85,8 @@
         scratch_shapes=[
             pltpu.VMEM((slot_count * block_len, head_width), jnp.bfloat16),
             pltpu.VMEM((slot_count * block_len, head_width), jnp.bfloat16),
+            pltpu.VMEM(tiles, jnp.float32),
+            pltpu.VMEM(tiles, jnp.float32),
         ],
     )
     flops = 2 * seq_len * slot_count * block_len * head_width * 6
@@ -89,8 +96,8 @@
         out_shape=[
             jax.ShapeDtypeStruct(tiles, jnp.bfloat16),
             jax.ShapeDtypeStruct(tiles, jnp.bfloat16),
-            jax.ShapeDtypeStruct(tiles, jnp.float32),
-            jax.ShapeDtypeStruct(tiles, jnp.float32),
+            jax.ShapeDtypeStruct(tiles, jnp.bfloat16),
+            jax.ShapeDtypeStruct(tiles, jnp.bfloat16),
         ],
         compiler_params=pltpu.CompilerParams(dimension_semantics=("arbitrary",)),
         cost_estimate=pl.CostEstimate(

time: 407 us -> 411 us (level)
  waiting for transfers between devices: 160 us -> 166 us
  starting transfers between devices: 115 us -> 110 us
    ppermute x1, starting transfers between devices: 15.5 us -> 7.72 us  [per_device(): w_other = lax.ppermute(w_mine, 'dp', pairs)]
    ppermute x20, waiting for transfers between devices: 29.1 us -> 33.3 us  [ring(): cur = lax.ppermute(cur, ('dp', 'seq'), perm)]
  transfers between devices with their start and end apart: 46 -> 46, of which waited for: 22 -> 24; matrix products, arithmetic and copies ran while one was open for 12% -> 13% of each run, Pallas kernels for 0% -> 0%
where the time goes in v12:
time: 411 us; the launch traced here: 403 us
  waiting for transfers between devices  166 us (40%)
  starting transfers between devices  110 us (27%)
  Pallas kernels  36.9 us (9%)
  other arithmetic  35.8 us (9%)
  local copies, waits for them, and re-layouts  33.8 us (8%)
  matrix products  18.3 us (4%)
    all_to_all x1, waiting for transfers between devices, per_device(): lax.all_to_all(back_sent, 'seq', split_axis=0, concat_axis=0, tiled=True)  45.1 us
    ppermute x20, starting transfers between devices, ring(): cur = lax.ppermute(cur, ('dp', 'seq'), perm)  40.5 us
    ppermute x14, waiting for transfers between devices, per_device(): arrived = lax.ppermute(buf, 'seq', perm)  38 us
    pallas_call x1, Pallas kernels, head_pass(): pl.pallas_call(head_kernel, grid_spec=grid_spec, out_shape=[jax.ShapeDtyp...  36.9 us
    all_to_all x1, waiting for transfers between devices, per_device(): lax.all_to_all(sent, 'seq', split_axis=0, concat_axis=1, tiled=True)[0]  33.9 us
    ppermute x20, waiting for transfers between devices, ring(): cur = lax.ppermute(cur, ('dp', 'seq'), perm)  33.3 us
    ppermute x14, starting transfers between devices, per_device(): arrived = lax.ppermute(buf, 'seq', perm)  20.3 us
    ppermute x6, waiting for transfers between devices, direct_sum(): lax.ppermute(lax.dynamic_index_in_dim(pieces, (mine + d) % size, 0, keepd...  12.6 us
  transfers between devices with their start and end apart: 46, of which 24 were waited for; matrix products, arithmetic and copies ran while one was open for 13% of the time, Pallas kernels for 0%

profile of v12, /device:TPU:1, one launch (start us, length us, event | category | flops | bytes accessed | tf_op | source)
XLA Modules:
  0.0 403.1 jit_solution(13345890518219814817)
XLA Ops:
  2.4 4.0 %collective-permute-start.10 = (bf16[64,1280]{1,0:T(8,128)(2,1)S(1)}, bf16[64,1280]{1,0:T(8,128)(2,1)S(1)}, u32[]{:S(2)}, u32[]{:S(2)}) collective-permute-start(bf16[64,1280]{1,0:T(8,128)(2,1)S(1)} %get-tuple-element.40), channel_id=1, source_target_pairs={{32,40},{33,41},{34,42},{35,43},{36,44},{37,45},{38,46},{39,47},{4... | collective-permute-start | bytes 491528 | tf_op jit(solution)/shard_map/ppermute | solution.py:182
  7.1 3.4 collective-permute-start.12
  11.2 1.9 collective-permute-start.11
  13.9 4.6 %collective-permute-done.11 = bf16[64,1280]{1,0:T(8,128)(2,1)S(1)} collective-permute-done((bf16[64,1280]{1,0:T(8,128)(2,1)S(1)}, bf16[64,1280]{1,0:T(8,128)(2,1)S(1)}, u32[]{:S(2)}, u32[]{:S(2)}) %collective-permute-start.11) | collective-permute-done | bytes 163872 | tf_op jit(solution)/shard_map/ppermute | solution.py:182
  19.4 3.5 collective-permute-start.13
  22.9 5.9 %collective-permute-start.17 = (bf16[4,64,1280]{2,1,0:T(8,128)(2,1)}, bf16[4,64,1280]{2,1,0:T(8,128)(2,1)}, u32[]{:S(2)}, u32[]{:S(2)}) collective-permute-start(bf16[4,64,1280]{2,1,0:T(8,128)(2,1)} %pad_maximum_fusion.4), channel_id=1, source_target_pairs={{32,39},{33,32},{34,33},{35,34},{36,35},{37,36},{38,37},{39,38},{4... | collective-permute-start | bytes 1966088 | tf_op jit(solution)/shard_map/ppermute | solution.py:182
  31.0 5.9 %collective-permute-done.13 = bf16[4,64,1280]{2,1,0:T(8,128)(2,1)} collective-permute-done((bf16[4,64,1280]{2,1,0:T(8,128)(2,1)}, bf16[4,64,1280]{2,1,0:T(8,128)(2,1)}, u32[]{:S(2)}, u32[]{:S(2)}) %collective-permute-start.13) | collective-permute-done | bytes 655392 | tf_op jit(solution)/shard_map/ppermute | solution.py:182
  36.9 1.9 collective-permute-start.14
  39.6 11.5 %collective-permute-done.14 = bf16[4,64,1280]{2,1,0:T(8,128)(2,1)} collective-permute-done((bf16[4,64,1280]{2,1,0:T(8,128)(2,1)}, bf16[4,64,1280]{2,1,0:T(8,128)(2,1)}, u32[]{:S(2)}, u32[]{:S(2)}) %collective-permute-start.14) | collective-permute-done | bytes 655392 | tf_op jit(solution)/shard_map/ppermute | solution.py:182
  51.1 1.9 collective-permute-start.15
  53.9 4.6 %collective-permute-start.18 = (bf16[4,64,1280]{2,1,0:T(8,128)(2,1)}, bf16[4,64,1280]{2,1,0:T(8,128)(2,1)S(1)}, u32[]{:S(2)}, u32[]{:S(2)}) collective-permute-start(bf16[4,64,1280]{2,1,0:T(8,128)(2,1)} %collective-permute-done.17), channel_id=1, source_target_pairs={{32,39},{33,32},{34,33},{35,34},{36,35},{37,36},{38,37},{39,38},{4... | collective-permute-start | bytes 1966088 | tf_op jit(solution)/shard_map/ppermute | solution.py:182
  59.6 4.6 %collective-permute-done.15 = bf16[4,64,1280]{2,1,0:T(8,128)(2,1)S(1)} collective-permute-done((bf16[4,64,1280]{2,1,0:T(8,128)(2,1)}, bf16[4,64,1280]{2,1,0:T(8,128)(2,1)S(1)}, u32[]{:S(2)}, u32[]{:S(2)}) %collective-permute-start.15) | collective-permute-done | bytes 655392 | tf_op jit(solution)/shard_map/ppermute | solution.py:182
  64.2 1.9 collective-permute-start.16
  67.2 4.6 %collective-permute-start.19 = (bf16[4,64,1280]{2,1,0:T(8,128)(2,1)S(1)}, bf16[4,64,1280]{2,1,0:T(8,128)(2,1)S(1)}, u32[]{:S(2)}, u32[]{:S(2)}) collective-permute-start(bf16[4,64,1280]{2,1,0:T(8,128)(2,1)S(1)} %collective-permute-done.18), channel_id=1, source_target_pairs={{32,39},{33,32},{34,33},{35,34},{36,35},{37,36},{38,37},{39,38},{4... | collective-permute-start | bytes 1966088 | tf_op jit(solution)/shard_map/ppermute | solution.py:182
  72.6 4.4 %collective-permute-done.16 = bf16[4,64,1280]{2,1,0:T(8,128)(2,1)S(1)} collective-permute-done((bf16[4,64,1280]{2,1,0:T(8,128)(2,1)S(1)}, bf16[4,64,1280]{2,1,0:T(8,128)(2,1)S(1)}, u32[]{:S(2)}, u32[]{:S(2)}) %collective-permute-start.16) | collective-permute-done | bytes 655392 | tf_op jit(solution)/shard_map/ppermute | solution.py:182
  77.0 2.3 collective-permute-done.19
  80.6 3.9 pad_maximum_fusion
  84.5 4.1 %bitcast_select_fusion.1 = bf16[2048,1280]{1,0:T(8,128)(2,1)} fusion(bf16[8,4,64,1280]{3,2,1,0:T(8,128)(2,1)S(1)} %bitcast_dynamic-update-slice_fusion, bf16[4,8,64,1280]{3,2,1,0:T(8,128)(2,1)S(1)} %get-tuple-element.45, pred[]{:T(512)S(6)} %eq.27), kind=kLoop, calls=%fused_computation.12 | loop fusion | flops 2621440 | bytes 15728641 | tf_op jit(solution)/shard_map/jit(_where)/select_n | solution.py:228
  88.6 7.7 %collective-permute-start.20 = (bf16[2048,1280]{1,0:T(8,128)(2,1)}, bf16[2048,1280]{1,0:T(8,128)(2,1)}, u32[]{:S(2)}, u32[]{:S(2)}) collective-permute-start(bf16[2048,1280]{1,0:T(8,128)(2,1)} %bitcast_select_fusion.1), channel_id=1, source_target_pairs={{0,32},{32,0},{64,96},{96,64},{128,160},{160,128},{192,224},{224,1... | collective-permute-start | bytes 15728648 | tf_op jit(solution)/shard_map/ppermute | solution.py:229
  97.3 5.9 %all-to-all-start.1 = ((bf16[32,128,64]{1,2,0:T(8,128)(2,1)}), bf16[32,128,64]{1,2,0:T(8,128)(2,1)S(1)}, u32[]{:S(2)}, u32[]{:S(2)}) async-start(bf16[32,128,64]{1,2,0:T(8,128)(2,1)} %bitcast.40), calls=%async_computation.1 | async-start | bytes 1048576 | tf_op jit(solution)/shard_map/all_to_all | solution.py:224
  105.5 3.4 convolution_convert_fusion.1
  109.3 3.4 convolution_convert_fusion
  114.5 3.6 all-to-all-done.1
  118.1 7.6 %all-to-all-start = ((bf16[32,128,192]{1,2,0:T(8,128)(2,1)}), bf16[32,128,192]{1,2,0:T(8,128)(2,1)S(1)}, u32[]{:S(2)}, u32[]{:S(2)}) async-start(bf16[32,128,192]{1,2,0:T(8,128)(2,1)} %pad_maximum_fusion.3), calls=%async_computation | async-start | bytes 3145728 | tf_op jit(solution)/shard_map/all_to_all | solution.py:252
  127.0 1.3 copy.61.g_ref
  128.3 33.9 %all-to-all-done = bf16[32,128,192]{1,2,0:T(8,128)(2,1)S(1)} async-done(((bf16[32,128,192]{1,2,0:T(8,128)(2,1)}), bf16[32,128,192]{1,2,0:T(8,128)(2,1)S(1)}, u32[]{:S(2)}, u32[]{:S(2)}) %all-to-all-start) | async-done | bytes 1572896 | tf_op jit(solution)/shard_map/all_to_all | solution.py:252
  165.3 1.4 copy.60
  166.7 36.9 %shard_map.110 = (bf16[32,128,64]{2,1,0:T(8,128)(2,1)}, bf16[32,128,64]{2,1,0:T(8,128)(2,1)}, bf16[32,128,64]{2,1,0:T(8,128)(2,1)}, bf16[32,128,64]{2,1,0:T(8,128)(2,1)}) custom-call(s32[224]{0:T(256)} %reshape.328.table_ref, s32[1]{0:T(128)} %dynamic_slice.35.count_ref, bf16[32,128,64]{2,1,0:T(8,128)(2,1)} %bitcast.190, bf16[32,128,64]{2,1,0:T(8,128)(2,1)} %copy.61.g_ref, ...), custom_call_target="tpu_custom_call" | custom-call | flops 2818572288 | bytes 5242880 | tf_op jit(solution)/shard_map/pallas_call | solution.py:93
  203.6 4.8 %pad_maximum_fusion.2 = bf16[32,128,256]{2,1,0:T(8,128)(2,1)} fusion(bf16[32,128,64]{2,1,0:T(8,128)(2,1)} %get-tuple-element.18, bf16[32,128,64]{2,1,0:T(8,128)(2,1)} %get-tuple-element.17, bf16[32,128,64]{2,1,0:T(8,128)(2,1)} %get-tuple-element.16, bf16[32,128,64]{2,1,0:T(8,128)(2,1)} %get-tuple-element.15), kind=kLoop, calls=%fused_computation.24 | loop fusion | flops 8388608 | bytes 4194304 | tf_op jit(solution)/shard_map/concatenate | solution.py:261
  208.4 7.9 %all-to-all-start.2 = ((bf16[32,128,256]{2,1,0:T(8,128)(2,1)}), bf16[32,128,256]{2,1,0:T(8,128)(2,1)S(1)}, u32[]{:S(2)}, u32[]{:S(2)}) async-start(bf16[32,128,256]{2,1,0:T(8,128)(2,1)} %pad_maximum_fusion.2), calls=%async_computation.2 | async-start | bytes 4194304 | tf_op jit(solution)/shard_map/all_to_all | solution.py:269
  217.0 1.4 gather_fusion.6
  218.5 1.3 broadcast_select_fusion
  219.9 45.1 %all-to-all-done.2 = bf16[32,128,256]{2,1,0:T(8,128)(2,1)S(1)} async-done(((bf16[32,128,256]{2,1,0:T(8,128)(2,1)}), bf16[32,128,256]{2,1,0:T(8,128)(2,1)S(1)}, u32[]{:S(2)}, u32[]{:S(2)}) %all-to-all-start.2) | async-done | bytes 2097184 | tf_op jit(solution)/shard_map/all_to_all | solution.py:269
  267.3 1.9 slice_bitcast_fusion.2
  269.1 1.6 copy.63
  272.8 2.7 pad_maximum_fusion.1
  275.5 2.4 collective-permute-start.21
  280.0 7.0 %bitcast_select_fusion = bf16[32,64,1280]{2,1,0:T(8,128)(2,1)} fusion(bf16[8,4,64,1280]{3,2,1,0:T(8,128)(2,1)} %copy-done.2, bf16[4,8,64,1280]{3,2,1,0:T(8,128)(2,1)} %copy-done.3, pred[]{:T(512)S(6)} %eq.27), kind=kLoop, calls=%fused_computation.11 | loop fusion | flops 2621440 | bytes 15728641 | tf_op jit(solution)/shard_map/jit(_where)/select_n | solution.py:228
  286.9 4.0 fusion.8
  291.6 4.0 fusion.6
  299.5 4.0 %slice_bitcast_fusion.1 = (bf16[640,2048]{1,0:T(8,128)(2,1)S(1)}, bf16[640,2048]{1,0:T(8,128)(2,1)S(1)}) fusion(bf16[2,640,2048]{2,1,0:T(8,128)(2,1)} %collective-permute-done.21), kind=kLoop, calls=%fused_computation.21 | loop fusion | bytes 10485760 | tf_op jit(solution)/shard_map/squeeze | solution.py:327
  305.5 7.7 %collective-permute-done.29 = bf16[640,256]{1,0:T(8,128)(2,1)S(1)} collective-permute-done((bf16[640,256]{1,0:T(8,128)(2,1)S(1)}, bf16[640,256]{1,0:T(8,128)(2,1)S(1)}, u32[]{:S(2)}, u32[]{:S(2)}) %collective-permute-start.29) | collective-permute-done | bytes 327712 | tf_op jit(solution)/shard_map/ppermute | solution.py:332
  313.3 1.8 collective-permute-start.30
  315.4 6.5 %collective-permute-done.30 = bf16[640,256]{1,0:T(8,128)(2,1)S(1)} collective-permute-done((bf16[640,256]{1,0:T(8,128)(2,1)S(1)}, bf16[640,256]{1,0:T(8,128)(2,1)S(1)}, u32[]{:S(2)}, u32[]{:S(2)}) %collective-permute-start.30) | collective-permute-done | bytes 327712 | tf_op jit(solution)/shard_map/ppermute | solution.py:332
  322.1 3.0 collective-permute-start.31
  325.3 5.0 %collective-permute-done.31 = bf16[640,256]{1,0:T(8,128)(2,1)S(1)} collective-permute-done((bf16[640,256]{1,0:T(8,128)(2,1)S(1)}, bf16[640,256]{1,0:T(8,128)(2,1)S(1)}, u32[]{:S(2)}, u32[]{:S(2)}) %collective-permute-start.31) | collective-permute-done | bytes 327712 | tf_op jit(solution)/shard_map/ppermute | solution.py:332
  330.6 3.7 collective-permute-start.32
  334.5 4.1 %collective-permute-done.32 = bf16[640,256]{1,0:T(8,128)(2,1)S(1)} collective-permute-done((bf16[640,256]{1,0:T(8,128)(2,1)S(1)}, bf16[640,256]{1,0:T(8,128)(2,1)S(1)}, u32[]{:S(2)}, u32[]{:S(2)}) %collective-permute-start.32) | collective-permute-done | bytes 327712 | tf_op jit(solution)/shard_map/ppermute | solution.py:332
  338.8 3.5 collective-permute-start.33
  342.6 3.7 collective-permute-done.33
  346.5 3.2 collective-permute-start.34
  350.0 3.8 collective-permute-done.34
  354.0 3.2 collective-permute-start.35
  358.4 4.0 collective-permute-done.35
  363.6 2.9 collective-permute-done.28
  368.0 2.4 collective-permute-start.38
  371.6 2.9 collective-permute-done.38
  374.4 1.8 collective-permute-done.37
  376.2 1.7 collective-permute-done.36
  377.9 2.6 collective-permute-start.41
  381.6 2.9 collective-permute-done.41
  384.5 1.8 collective-permute-done.40
  386.3 1.7 collective-permute-done.39
  388.8 10.3 %collective-permute-start.42 = (bf16[64,1280]{1,0:T(8,128)(2,1)S(1)}, bf16[64,1280]{1,0:T(8,128)(2,1)S(1)}, u32[]{:S(2)}, u32[]{:S(2)}) collective-permute-start(bf16[64,1280]{1,0:T(8,128)(2,1)S(1)} %select_reduce_fusion), channel_id=1, source_target_pairs={{0,32},{32,0},{64,96},{96,64},{128,160},{160,128},{192,224},{224,1... | collective-permute-start | bytes 491528 | tf_op jit(solution)/shard_map/ppermute | solution.py:347
  (194 shorter events, 49.2 us)
Async XLA Ops:
  0.6 125.0 %copy-start = (s32[32,32,7]{1,0,2:T(8,128)S(1)}, s32[32,32,7]{1,0,2:T(8,128)}, u32[]{:S(2)}) copy-start(s32[32,32,7]{1,0,2:T(8,128)} %param.17) | copy-start | bytes 86020
  1.7 8.8 %collective-permute-start = (bf16[64,1280]{1,0:T(8,128)(2,1)S(1)}, bf16[64,1280]{1,0:T(8,128)(2,1)S(1)}, u32[]{:S(2)}, u32[]{:S(2)}) collective-permute-start(bf16[64,1280]{1,0:T(8,128)(2,1)S(1)} %get-tuple-element.40), channel_id=1, source_target_pairs={{0,1},{1,2},{2,3},{3,4},{4,5},{5,6},{6,7},{7,0},{8,9},{9,10},{10,1... | collective-permute-start | bytes 491528 | tf_op jit(solution)/shard_map/ppermute | solution.py:182
  2.4 8.8 %collective-permute-start.10 = (bf16[64,1280]{1,0:T(8,128)(2,1)S(1)}, bf16[64,1280]{1,0:T(8,128)(2,1)S(1)}, u32[]{:S(2)}, u32[]{:S(2)}) collective-permute-start(bf16[64,1280]{1,0:T(8,128)(2,1)S(1)} %get-tuple-element.40), channel_id=1, source_target_pairs={{32,40},{33,41},{34,42},{35,43},{36,44},{37,45},{38,46},{39,47},{4... | collective-permute-start | bytes 491528 | tf_op jit(solution)/shard_map/ppermute | solution.py:182
  6.5 6.7 %collective-permute-start.4 = (bf16[64,1280]{1,0:T(8,128)(2,1)S(1)}, bf16[64,1280]{1,0:T(8,128)(2,1)S(1)}, u32[]{:S(2)}, u32[]{:S(2)}) collective-permute-start(bf16[64,1280]{1,0:T(8,128)(2,1)S(1)} %get-tuple-element.40), channel_id=1, source_target_pairs={{0,7},{1,0},{2,1},{3,2},{4,3},{5,4},{6,5},{7,6},{8,15},{9,8},{10,9... | collective-permute-start | bytes 491528 | tf_op jit(solution)/shard_map/ppermute | solution.py:182
  7.1 6.7 %collective-permute-start.12 = (bf16[64,1280]{1,0:T(8,128)(2,1)S(1)}, bf16[64,1280]{1,0:T(8,128)(2,1)S(1)}, u32[]{:S(2)}, u32[]{:S(2)}) collective-permute-start(bf16[64,1280]{1,0:T(8,128)(2,1)S(1)} %get-tuple-element.40), channel_id=1, source_target_pairs={{32,56},{33,57},{34,58},{35,59},{36,60},{37,61},{38,62},{39,63},{4... | collective-permute-start | bytes 491528 | tf_op jit(solution)/shard_map/ppermute | solution.py:182
  10.5 18.3 %collective-permute-start.1 = (bf16[64,1280]{1,0:T(8,128)(2,1)S(1)}, bf16[64,1280]{1,0:T(8,128)(2,1)S(1)}, u32[]{:S(2)}, u32[]{:S(2)}) collective-permute-start(bf16[64,1280]{1,0:T(8,128)(2,1)S(1)} %collective-permute-done), channel_id=1, source_target_pairs={{0,1},{1,2},{2,3},{3,4},{4,5},{5,6},{6,7},{7,0},{8,9},{9,10},{10,1... | collective-permute-start | bytes 491528 | tf_op jit(solution)/shard_map/ppermute | solution.py:182
  11.2 7.3 %collective-permute-start.11 = (bf16[64,1280]{1,0:T(8,128)(2,1)S(1)}, bf16[64,1280]{1,0:T(8,128)(2,1)S(1)}, u32[]{:S(2)}, u32[]{:S(2)}) collective-permute-start(bf16[64,1280]{1,0:T(8,128)(2,1)S(1)} %collective-permute-done.10), channel_id=1, source_target_pairs={{32,40},{33,41},{34,42},{35,43},{36,44},{37,45},{38,46},{39,47},{4... | collective-permute-start | bytes 491528 | tf_op jit(solution)/shard_map/ppermute | solution.py:182
  13.2 16.3 %collective-permute-start.5 = (bf16[64,1280]{1,0:T(8,128)(2,1)S(1)}, bf16[64,1280]{1,0:T(8,128)(2,1)S(1)}, u32[]{:S(2)}, u32[]{:S(2)}) collective-permute-start(bf16[64,1280]{1,0:T(8,128)(2,1)S(1)} %collective-permute-done.4), channel_id=1, source_target_pairs={{0,7},{1,0},{2,1},{3,2},{4,3},{5,4},{6,5},{7,6},{8,15},{9,8},{10,9... | collective-permute-start | bytes 491528 | tf_op jit(solution)/shard_map/ppermute | solution.py:182
  19.4 17.5 %collective-permute-start.13 = (bf16[4,64,1280]{2,1,0:T(8,128)(2,1)}, bf16[4,64,1280]{2,1,0:T(8,128)(2,1)}, u32[]{:S(2)}, u32[]{:S(2)}) collective-permute-start(bf16[4,64,1280]{2,1,0:T(8,128)(2,1)} %pad_maximum_fusion.4), channel_id=1, source_target_pairs={{32,33},{33,34},{34,35},{35,36},{36,37},{37,38},{38,39},{39,32},{4... | collective-permute-start | bytes 1966088 | tf_op jit(solution)/shard_map/ppermute | solution.py:182
  22.9 30.9 %collective-permute-start.17 = (bf16[4,64,1280]{2,1,0:T(8,128)(2,1)}, bf16[4,64,1280]{2,1,0:T(8,128)(2,1)}, u32[]{:S(2)}, u32[]{:S(2)}) collective-permute-start(bf16[4,64,1280]{2,1,0:T(8,128)(2,1)} %pad_maximum_fusion.4), channel_id=1, source_target_pairs={{32,39},{33,32},{34,33},{35,34},{36,35},{37,36},{38,37},{39,38},{4... | collective-permute-start | bytes 1966088 | tf_op jit(solution)/shard_map/ppermute | solution.py:182
  28.8 1.4 collective-permute-start.2
  29.5 1.4 collective-permute-start.6
  30.2 0.7 collective-permute-start.3
  36.9 14.2 %collective-permute-start.14 = (bf16[4,64,1280]{2,1,0:T(8,128)(2,1)}, bf16[4,64,1280]{2,1,0:T(8,128)(2,1)}, u32[]{:S(2)}, u32[]{:S(2)}) collective-permute-start(bf16[4,64,1280]{2,1,0:T(8,128)(2,1)} %collective-permute-done.13), channel_id=1, source_target_pairs={{32,33},{33,34},{34,35},{35,36},{36,37},{37,38},{38,39},{39,32},{4... | collective-permute-start | bytes 1966088 | tf_op jit(solution)/shard_map/ppermute | solution.py:182
  38.9 33.0 %collective-permute-start.7 = (bf16[8,64,1280]{2,1,0:T(8,128)(2,1)S(1)}, bf16[8,64,1280]{2,1,0:T(8,128)(2,1)S(1)}, u32[]{:S(2)}, u32[]{:S(2)}) collective-permute-start(bf16[8,64,1280]{2,1,0:T(8,128)(2,1)S(1)} %bitcast_dynamic-update-slice_fusion.8), channel_id=1, source_target_pairs={{0,8},{1,9},{2,10},{3,11},{4,12},{5,13},{6,14},{7,15},{8,16},{9,17... | collective-permute-start | bytes 3932168 | tf_op jit(solution)/shard_map/ppermute | solution.py:182
  51.1 13.0 %collective-permute-start.15 = (bf16[4,64,1280]{2,1,0:T(8,128)(2,1)}, bf16[4,64,1280]{2,1,0:T(8,128)(2,1)S(1)}, u32[]{:S(2)}, u32[]{:S(2)}) collective-permute-start(bf16[4,64,1280]{2,1,0:T(8,128)(2,1)} %collective-permute-done.14), channel_id=1, source_target_pairs={{32,33},{33,34},{34,35},{35,36},{36,37},{37,38},{38,39},{39,32},{4... | collective-permute-start | bytes 1966088 | tf_op jit(solution)/shard_map/ppermute | solution.py:182
  53.1 27.5 %collective-permute-start.9 = (bf16[8,64,1280]{2,1,0:T(8,128)(2,1)S(1)}, bf16[8,64,1280]{2,1,0:T(8,128)(2,1)S(1)}, u32[]{:S(2)}, u32[]{:S(2)}) collective-permute-start(bf16[8,64,1280]{2,1,0:T(8,128)(2,1)S(1)} %bitcast_dynamic-update-slice_fusion.8), channel_id=1, source_target_pairs={{0,24},{1,25},{2,26},{3,27},{4,28},{5,29},{6,30},{7,31},{8,0},{9,1... | collective-permute-start | bytes 3932168 | tf_op jit(solution)/shard_map/ppermute | solution.py:182
  53.9 13.4 %collective-permute-start.18 = (bf16[4,64,1280]{2,1,0:T(8,128)(2,1)}, bf16[4,64,1280]{2,1,0:T(8,128)(2,1)S(1)}, u32[]{:S(2)}, u32[]{:S(2)}) collective-permute-start(bf16[4,64,1280]{2,1,0:T(8,128)(2,1)} %collective-permute-done.17), channel_id=1, source_target_pairs={{32,39},{33,32},{34,33},{35,34},{36,35},{37,36},{38,37},{39,38},{4... | collective-permute-start | bytes 1966088 | tf_op jit(solution)/shard_map/ppermute | solution.py:182
  64.2 12.8 %collective-permute-start.16 = (bf16[4,64,1280]{2,1,0:T(8,128)(2,1)S(1)}, bf16[4,64,1280]{2,1,0:T(8,128)(2,1)S(1)}, u32[]{:S(2)}, u32[]{:S(2)}) collective-permute-start(bf16[4,64,1280]{2,1,0:T(8,128)(2,1)S(1)} %collective-permute-done.15), channel_id=1, source_target_pairs={{32,33},{33,34},{34,35},{35,36},{36,37},{37,38},{38,39},{39,32},{4... | collective-permute-start | bytes 1966088 | tf_op jit(solution)/shard_map/ppermute | solution.py:182
  67.2 12.1 %collective-permute-start.19 = (bf16[4,64,1280]{2,1,0:T(8,128)(2,1)S(1)}, bf16[4,64,1280]{2,1,0:T(8,128)(2,1)S(1)}, u32[]{:S(2)}, u32[]{:S(2)}) collective-permute-start(bf16[4,64,1280]{2,1,0:T(8,128)(2,1)S(1)} %collective-permute-done.18), channel_id=1, source_target_pairs={{32,39},{33,32},{34,33},{35,34},{36,35},{37,36},{38,37},{39,38},{4... | collective-permute-start | bytes 1966088 | tf_op jit(solution)/shard_map/ppermute | solution.py:182
  71.8 8.8 %collective-permute-start.8 = (bf16[8,64,1280]{2,1,0:T(8,128)(2,1)S(1)}, bf16[8,64,1280]{2,1,0:T(8,128)(2,1)S(1)}, u32[]{:S(2)}, u32[]{:S(2)}) collective-permute-start(bf16[8,64,1280]{2,1,0:T(8,128)(2,1)S(1)} %collective-permute-done.7), channel_id=1, source_target_pairs={{0,8},{1,9},{2,10},{3,11},{4,12},{5,13},{6,14},{7,15},{8,16},{9,17... | collective-permute-start | bytes 3932168 | tf_op jit(solution)/shard_map/ppermute | solution.py:182
  80.6 3.9 copy-start.2
  84.5 4.1 %copy-start.3 = (bf16[4,8,64,1280]{3,2,1,0:T(8,128)(2,1)}, bf16[4,8,64,1280]{3,2,1,0:T(8,128)(2,1)S(1)}, u32[]{:S(2)}) copy-start(bf16[4,8,64,1280]{3,2,1,0:T(8,128)(2,1)S(1)} %get-tuple-element.45) | copy-start | bytes 15728644
  84.5 11.8 %copy-start.15 = (bf16[1,128,2048]{2,1,0:T(8,128)(2,1)S(1)}, bf16[1,128,2048]{2,1,0:T(8,128)(2,1)}, u32[]{:S(2)}) copy-start(bf16[1,128,2048]{2,1,0:T(8,128)(2,1)} %param.19) | copy-start | bytes 1572868
  84.5 18.8 %copy-start.16 = (bf16[1,128,2048]{2,1,0:T(8,128)(2,1)S(1)}, bf16[1,128,2048]{2,1,0:T(8,128)(2,1)}, u32[]{:S(2)}) copy-start(bf16[1,128,2048]{2,1,0:T(8,128)(2,1)} %param.13) | copy-start | bytes 1572868
  88.6 20.7 %collective-permute-start.20 = (bf16[2048,1280]{1,0:T(8,128)(2,1)}, bf16[2048,1280]{1,0:T(8,128)(2,1)}, u32[]{:S(2)}, u32[]{:S(2)}) collective-permute-start(bf16[2048,1280]{1,0:T(8,128)(2,1)} %bitcast_select_fusion.1), channel_id=1, source_target_pairs={{0,32},{32,0},{64,96},{96,64},{128,160},{160,128},{192,224},{224,1... | collective-permute-start | bytes 15728648 | tf_op jit(solution)/shard_map/ppermute | solution.py:229
  97.3 20.8 %all-to-all-start.1 = ((bf16[32,128,64]{1,2,0:T(8,128)(2,1)}), bf16[32,128,64]{1,2,0:T(8,128)(2,1)S(1)}, u32[]{:S(2)}, u32[]{:S(2)}) async-start(bf16[32,128,64]{1,2,0:T(8,128)(2,1)} %bitcast.40), calls=%async_computation.1 | async-start | bytes 1048576 | tf_op jit(solution)/shard_map/all_to_all | solution.py:224
  113.2 13.2 %copy-start.17 = (s32[32]{0:T(128)S(1)}, s32[32]{0:T(128)}, u32[]{:S(2)}) copy-start(s32[32]{0:T(128)} %param.18) | copy-start | bytes 388
  118.1 44.1 %all-to-all-start = ((bf16[32,128,192]{1,2,0:T(8,128)(2,1)}), bf16[32,128,192]{1,2,0:T(8,128)(2,1)S(1)}, u32[]{:S(2)}, u32[]{:S(2)}) async-start(bf16[32,128,192]{1,2,0:T(8,128)(2,1)} %pad_maximum_fusion.3), calls=%async_computation | async-start | bytes 3145728 | tf_op jit(solution)/shard_map/all_to_all | solution.py:252
  208.4 56.6 %all-to-all-start.2 = ((bf16[32,128,256]{2,1,0:T(8,128)(2,1)}), bf16[32,128,256]{2,1,0:T(8,128)(2,1)S(1)}, u32[]{:S(2)}, u32[]{:S(2)}) async-start(bf16[32,128,256]{2,1,0:T(8,128)(2,1)} %pad_maximum_fusion.2), calls=%async_computation.2 | async-start | bytes 4194304 | tf_op jit(solution)/shard_map/all_to_all | solution.py:269
  218.5 52.5 %copy-start.9 = (bf16[8,128,4,64]{1,3,2,0:T(8,128)(2,1)}, bf16[8,128,4,64]{1,3,2,0:T(8,128)(2,1)S(1)}, u32[]{:S(2)}) copy-start(bf16[8,128,4,64]{1,3,2,0:T(8,128)(2,1)S(1)} %broadcast_select_fusion.1) | copy-start | bytes 1572868
  219.9 52.0 %copy-start.11 = (bf16[8,128,4,64]{1,3,2,0:T(8,128)(2,1)}, bf16[8,128,4,64]{1,3,2,0:T(8,128)(2,1)S(1)}, u32[]{:S(2)}) copy-start(bf16[8,128,4,64]{1,3,2,0:T(8,128)(2,1)S(1)} %broadcast_select_fusion) | copy-start | bytes 1572868
  271.0 20.6 %copy-start.7 = (bf16[128,2560]{1,0:T(8,128)(2,1)}, bf16[128,2560]{1,0:T(8,128)(2,1)S(1)}, u32[]{:S(2)}) copy-start(bf16[128,2560]{1,0:T(8,128)(2,1)S(1)} %pad_maximum_fusion.5) | copy-start | bytes 1966084
  275.5 23.9 %collective-permute-start.21 = (bf16[2,640,2048]{2,1,0:T(8,128)(2,1)}, bf16[2,640,2048]{2,1,0:T(8,128)(2,1)}, u32[]{:S(2)}, u32[]{:S(2)}) collective-permute-start(bf16[2,640,2048]{2,1,0:T(8,128)(2,1)} %pad_maximum_fusion.1), channel_id=1, source_target_pairs={{0,32},{32,0},{64,96},{96,64},{128,160},{160,128},{192,224},{224,1... | collective-permute-start | bytes 15728648 | tf_op jit(solution)/shard_map/ppermute | solution.py:316
  296.2 1.1 copy-start.8
  296.2 1.4 copy-start.10
  296.2 2.3 copy-start.12
  298.5 59.0 %copy-start.5 = (bf16[640,2048]{1,0:T(8,128)(2,1)}, bf16[640,2048]{1,0:T(8,128)(2,1)S(1)}, u32[]{:S(2)}) copy-start(bf16[640,2048]{1,0:T(8,128)(2,1)S(1)} %multiply_convert_fusion.3) | copy-start | bytes 7864324
  299.4 54.4 %copy-start.6 = (bf16[640,2048]{1,0:T(8,128)(2,1)}, bf16[640,2048]{1,0:T(8,128)(2,1)S(1)}, u32[]{:S(2)}) copy-start(bf16[640,2048]{1,0:T(8,128)(2,1)S(1)} %multiply_convert_fusion.2) | copy-start | bytes 7864324
  303.5 50.3 %copy-start.4 = (bf16[640,2048]{1,0:T(8,128)(2,1)}, bf16[640,2048]{1,0:T(8,128)(2,1)S(1)}, u32[]{:S(2)}) copy-start(bf16[640,2048]{1,0:T(8,128)(2,1)S(1)} %get-tuple-element.44) | copy-start | bytes 7864324
  303.7 9.4 %collective-permute-start.29 = (bf16[640,256]{1,0:T(8,128)(2,1)S(1)}, bf16[640,256]{1,0:T(8,128)(2,1)S(1)}, u32[]{:S(2)}, u32[]{:S(2)}) collective-permute-start(bf16[640,256]{1,0:T(8,128)(2,1)S(1)} %add_convert_fusion.14), channel_id=1, source_target_pairs={{1,0},{2,1},{3,2},{4,3},{5,4},{6,5},{7,6},{0,7},{9,8},{10,9},{11,1... | collective-permute-start | bytes 983048 | tf_op jit(solution)/shard_map/ppermute | solution.py:332
  304.4 10.7 %collective-permute-start.22 = (bf16[640,256]{1,0:T(8,128)(2,1)S(1)}, bf16[640,256]{1,0:T(8,128)(2,1)S(1)}, u32[]{:S(2)}, u32[]{:S(2)}) collective-permute-start(bf16[640,256]{1,0:T(8,128)(2,1)S(1)} %add_convert_fusion.29), channel_id=1, source_target_pairs={{0,1},{1,2},{2,3},{3,4},{4,5},{5,6},{6,7},{7,0},{8,9},{9,10},{10,1... | collective-permute-start | bytes 983048 | tf_op jit(solution)/shard_map/ppermute | solution.py:332
  313.3 8.5 %collective-permute-start.30 = (bf16[640,256]{1,0:T(8,128)(2,1)S(1)}, bf16[640,256]{1,0:T(8,128)(2,1)S(1)}, u32[]{:S(2)}, u32[]{:S(2)}) collective-permute-start(bf16[640,256]{1,0:T(8,128)(2,1)S(1)} %add_convert_fusion.12), channel_id=1, source_target_pairs={{1,0},{2,1},{3,2},{4,3},{5,4},{6,5},{7,6},{0,7},{9,8},{10,9},{11,1... | collective-permute-start | bytes 983048 | tf_op jit(solution)/shard_map/ppermute | solution.py:332
  315.3 9.8 %collective-permute-start.23 = (bf16[640,256]{1,0:T(8,128)(2,1)S(1)}, bf16[640,256]{1,0:T(8,128)(2,1)S(1)}, u32[]{:S(2)}, u32[]{:S(2)}) collective-permute-start(bf16[640,256]{1,0:T(8,128)(2,1)S(1)} %add_convert_fusion.27), channel_id=1, source_target_pairs={{0,1},{1,2},{2,3},{3,4},{4,5},{5,6},{6,7},{7,0},{8,9},{9,10},{10,1... | collective-permute-start | bytes 983048 | tf_op jit(solution)/shard_map/ppermute | solution.py:332
  322.1 8.3 %collective-permute-start.31 = (bf16[640,256]{1,0:T(8,128)(2,1)S(1)}, bf16[640,256]{1,0:T(8,128)(2,1)S(1)}, u32[]{:S(2)}, u32[]{:S(2)}) collective-permute-start(bf16[640,256]{1,0:T(8,128)(2,1)S(1)} %add_convert_fusion.10), channel_id=1, source_target_pairs={{1,0},{2,1},{3,2},{4,3},{5,4},{6,5},{7,6},{0,7},{9,8},{10,9},{11,1... | collective-permute-start | bytes 983048 | tf_op jit(solution)/shard_map/ppermute | solution.py:332
  325.2 9.0 %collective-permute-start.24 = (bf16[640,256]{1,0:T(8,128)(2,1)S(1)}, bf16[640,256]{1,0:T(8,128)(2,1)S(1)}, u32[]{:S(2)}, u32[]{:S(2)}) collective-permute-start(bf16[640,256]{1,0:T(8,128)(2,1)S(1)} %add_convert_fusion.25), channel_id=1, source_target_pairs={{0,1},{1,2},{2,3},{3,4},{4,5},{5,6},{6,7},{7,0},{8,9},{9,10},{10,1... | collective-permute-start | bytes 983048 | tf_op jit(solution)/shard_map/ppermute | solution.py:332
  330.6 8.1 %collective-permute-start.32 = (bf16[640,256]{1,0:T(8,128)(2,1)S(1)}, bf16[640,256]{1,0:T(8,128)(2,1)S(1)}, u32[]{:S(2)}, u32[]{:S(2)}) collective-permute-start(bf16[640,256]{1,0:T(8,128)(2,1)S(1)} %add_convert_fusion.8), channel_id=1, source_target_pairs={{1,0},{2,1},{3,2},{4,3},{5,4},{6,5},{7,6},{0,7},{9,8},{10,9},{11,1... | collective-permute-start | bytes 983048 | tf_op jit(solution)/shard_map/ppermute | solution.py:332
  334.4 7.9 %collective-permute-start.25 = (bf16[640,256]{1,0:T(8,128)(2,1)S(1)}, bf16[640,256]{1,0:T(8,128)(2,1)S(1)}, u32[]{:S(2)}, u32[]{:S(2)}) collective-permute-start(bf16[640,256]{1,0:T(8,128)(2,1)S(1)} %add_convert_fusion.23), channel_id=1, source_target_pairs={{0,1},{1,2},{2,3},{3,4},{4,5},{5,6},{6,7},{7,0},{8,9},{9,10},{10,1... | collective-permute-start | bytes 983048 | tf_op jit(solution)/shard_map/ppermute | solution.py:332
  338.8 7.5 %collective-permute-start.33 = (bf16[640,256]{1,0:T(8,128)(2,1)S(1)}, bf16[640,256]{1,0:T(8,128)(2,1)S(1)}, u32[]{:S(2)}, u32[]{:S(2)}) collective-permute-start(bf16[640,256]{1,0:T(8,128)(2,1)S(1)} %add_convert_fusion.6), channel_id=1, source_target_pairs={{1,0},{2,1},{3,2},{4,3},{5,4},{6,5},{7,6},{0,7},{9,8},{10,9},{11,1... | collective-permute-start | bytes 983048 | tf_op jit(solution)/shard_map/ppermute | solution.py:332
  342.5 7.2 %collective-permute-start.26 = (bf16[640,256]{1,0:T(8,128)(2,1)S(1)}, bf16[640,256]{1,0:T(8,128)(2,1)S(1)}, u32[]{:S(2)}, u32[]{:S(2)}) collective-permute-start(bf16[640,256]{1,0:T(8,128)(2,1)S(1)} %add_convert_fusion.21), channel_id=1, source_target_pairs={{0,1},{1,2},{2,3},{3,4},{4,5},{5,6},{6,7},{7,0},{8,9},{9,10},{10,1... | collective-permute-start | bytes 983048 | tf_op jit(solution)/shard_map/ppermute | solution.py:332
  346.5 7.3 %collective-permute-start.34 = (bf16[640,256]{1,0:T(8,128)(2,1)S(1)}, bf16[640,256]{1,0:T(8,128)(2,1)S(1)}, u32[]{:S(2)}, u32[]{:S(2)}) collective-permute-start(bf16[640,256]{1,0:T(8,128)(2,1)S(1)} %add_convert_fusion.4), channel_id=1, source_target_pairs={{1,0},{2,1},{3,2},{4,3},{5,4},{6,5},{7,6},{0,7},{9,8},{10,9},{11,1... | collective-permute-start | bytes 983048 | tf_op jit(solution)/shard_map/ppermute | solution.py:332
  349.9 7.6 %collective-permute-start.27 = (bf16[640,256]{1,0:T(8,128)(2,1)S(1)}, bf16[640,256]{1,0:T(8,128)(2,1)S(1)}, u32[]{:S(2)}, u32[]{:S(2)}) collective-permute-start(bf16[640,256]{1,0:T(8,128)(2,1)S(1)} %add_convert_fusion.19), channel_id=1, source_target_pairs={{0,1},{1,2},{2,3},{3,4},{4,5},{5,6},{6,7},{7,0},{8,9},{9,10},{10,1... | collective-permute-start | bytes 983048 | tf_op jit(solution)/shard_map/ppermute | solution.py:332
  354.0 8.4 %collective-permute-start.35 = (bf16[640,256]{1,0:T(8,128)(2,1)S(1)}, bf16[640,256]{1,0:T(8,128)(2,1)S(1)}, u32[]{:S(2)}, u32[]{:S(2)}) collective-permute-start(bf16[640,256]{1,0:T(8,128)(2,1)S(1)} %add_convert_fusion.2), channel_id=1, source_target_pairs={{1,0},{2,1},{3,2},{4,3},{5,4},{6,5},{7,6},{0,7},{9,8},{10,9},{11,1... | collective-permute-start | bytes 983048 | tf_op jit(solution)/shard_map/ppermute | solution.py:332
  358.4 8.0 %collective-permute-start.28 = (bf16[640,256]{1,0:T(8,128)(2,1)}, bf16[640,256]{1,0:T(8,128)(2,1)}, u32[]{:S(2)}, u32[]{:S(2)}) collective-permute-start(bf16[640,256]{1,0:T(8,128)(2,1)} %add_convert_fusion.17), channel_id=1, source_target_pairs={{0,1},{1,2},{2,3},{3,4},{4,5},{5,6},{6,7},{7,0},{8,9},{9,10},{10,1... | collective-permute-start | bytes 983048 | tf_op jit(solution)/shard_map/ppermute | solution.py:332
  367.9 31.2 %copy-start.13 = (bf16[128,32,64]{2,0,1:T(8,128)(2,1)S(1)}, bf16[128,32,64]{2,0,1:T(8,128)(2,1)}, u32[]{:S(2)}) copy-start(bf16[128,32,64]{2,0,1:T(8,128)(2,1)} %get-tuple-element.48) | copy-start | bytes 1572868
  368.0 6.4 %collective-permute-start.38 = (bf16[64,1280]{1,0:T(8,128)(2,1)S(1)}, bf16[64,1280]{1,0:T(8,128)(2,1)S(1)}, u32[]{:S(2)}, u32[]{:S(2)}) collective-permute-start(bf16[64,1280]{1,0:T(8,128)(2,1)S(1)} %get-tuple-element.53), channel_id=1, source_target_pairs={{0,24},{1,25},{2,26},{3,27},{4,28},{5,29},{6,30},{7,31},{8,0},{9,1... | collective-permute-start | bytes 491528 | tf_op jit(solution)/shard_map/ppermute | solution.py:153
  370.4 5.8 %collective-permute-start.37 = (bf16[64,1280]{1,0:T(8,128)(2,1)S(1)}, bf16[64,1280]{1,0:T(8,128)(2,1)S(1)}, u32[]{:S(2)}, u32[]{:S(2)}) collective-permute-start(bf16[64,1280]{1,0:T(8,128)(2,1)S(1)} %get-tuple-element.54), channel_id=1, source_target_pairs={{0,16},{1,17},{2,18},{3,19},{4,20},{5,21},{6,22},{7,23},{8,24},{9,... | collective-permute-start | bytes 491528 | tf_op jit(solution)/shard_map/ppermute | solution.py:153
  371.0 6.9 %collective-permute-start.36 = (bf16[64,1280]{1,0:T(8,128)(2,1)S(1)}, bf16[64,1280]{1,0:T(8,128)(2,1)S(1)}, u32[]{:S(2)}, u32[]{:S(2)}) collective-permute-start(bf16[64,1280]{1,0:T(8,128)(2,1)S(1)} %get-tuple-element.52), channel_id=1, source_target_pairs={{0,8},{1,9},{2,10},{3,11},{4,12},{5,13},{6,14},{7,15},{8,16},{9,17... | collective-permute-start | bytes 491528 | tf_op jit(solution)/shard_map/ppermute | solution.py:153
  377.9 6.6 %collective-permute-start.41 = (bf16[64,1280]{1,0:T(8,128)(2,1)S(1)}, bf16[64,1280]{1,0:T(8,128)(2,1)S(1)}, u32[]{:S(2)}, u32[]{:S(2)}) collective-permute-start(bf16[64,1280]{1,0:T(8,128)(2,1)S(1)} %fusion.5), channel_id=1, source_target_pairs={{0,192},{32,224},{64,0},{96,32},{128,64},{160,96},{192,128},{224,1... | collective-permute-start | bytes 491528 | tf_op jit(solution)/shard_map/ppermute | solution.py:153
  380.5 5.8 %collective-permute-start.40 = (bf16[64,1280]{1,0:T(8,128)(2,1)S(1)}, bf16[64,1280]{1,0:T(8,128)(2,1)S(1)}, u32[]{:S(2)}, u32[]{:S(2)}) collective-permute-start(bf16[64,1280]{1,0:T(8,128)(2,1)S(1)} %fusion.5), channel_id=1, source_target_pairs={{0,128},{32,160},{64,192},{96,224},{128,0},{160,32},{192,64},{224,... | collective-permute-start | bytes 491528 | tf_op jit(solution)/shard_map/ppermute | solution.py:153
  381.0 6.9 %collective-permute-start.39 = (bf16[64,1280]{1,0:T(8,128)(2,1)S(1)}, bf16[64,1280]{1,0:T(8,128)(2,1)S(1)}, u32[]{:S(2)}, u32[]{:S(2)}) collective-permute-start(bf16[64,1280]{1,0:T(8,128)(2,1)S(1)} %fusion.5), channel_id=1, source_target_pairs={{0,64},{32,96},{64,128},{96,160},{128,192},{160,224},{192,0},{224,... | collective-permute-start | bytes 491528 | tf_op jit(solution)/shard_map/ppermute | solution.py:153
  388.0 12.5 %copy-start.14 = (bf16[128,32,64]{0,2,1:T(8,128)(2,1)S(1)}, bf16[128,32,64]{0,2,1:T(8,128)(2,1)}, u32[]{:S(2)}) copy-start(bf16[128,32,64]{0,2,1:T(8,128)(2,1)} %fusion.2) | copy-start | bytes 1572868
  388.7 14.3 %copy-start.1 = (s32[32,32,7]{1,0,2:T(8,128)S(1)}, s32[32,32,7]{1,0,2:T(8,128)}, u32[]{:S(2)}) copy-start(s32[32,32,7]{1,0,2:T(8,128)} %param.17) | copy-start | bytes 86020
  388.8 12.8 %collective-permute-start.42 = (bf16[64,1280]{1,0:T(8,128)(2,1)S(1)}, bf16[64,1280]{1,0:T(8,128)(2,1)S(1)}, u32[]{:S(2)}, u32[]{:S(2)}) collective-permute-start(bf16[64,1280]{1,0:T(8,128)(2,1)S(1)} %select_reduce_fusion), channel_id=1, source_target_pairs={{0,32},{32,0},{64,96},{96,64},{128,160},{160,128},{192,224},{224,1... | collective-permute-start | bytes 491528 | tf_op jit(solution)/shard_map/ppermute | solution.py:347
